TPU v7x, 32 devices: a whole 2x2x4 slice. The times are simulated.
32 devices in a mesh: expert: 8 (over z, y), shard: 4 (over x, core).
Axes of the slice: x: 2, y: 2, z: 4, core: 2. Of those that a mesh axis runs over, the one named last changes fastest.
Arguments:
- tokens: float32 [25216, 512], P(('expert', 'shard')), may hold values from -6 to 6
- routes: int32 [25216, 2], P(('expert', 'shard')), may hold values from 0 to 7, all different within a row; in each aligned block of 394 rows (0 to 393, 394 to 787, ...) at most 192 rows name the same one
- priority: int32 [25216], P(('expert', 'shard')), may hold values from 0 to 393, as said below
- norm_gain: bfloat16 [2, 2, 512], P(None, None, 'shard'), may hold values from 0.5 to 1.5
- norm_bias: bfloat16 [2, 2, 512], P(None, None, 'shard'), may hold values from -1 to 1
- w_qkv: bfloat16 [2, 512, 1536], P(None, 'shard'), may hold values from -0.25 to 0.25
- w_proj: bfloat16 [2, 512, 512], P(None, 'shard'), may hold values from -2 to 2
- w_router: bfloat16 [2, 512, 8], P(None, 'shard'), may hold values from -0.1875 to 0.1875
- exp_in: bfloat16 [2, 8, 512, 2048], P(None, 'expert', 'shard'), may hold values from -0.25 to 0.25
- exp_out: bfloat16 [2, 8, 2048, 512], P(None, 'expert', 'shard'), may hold values from -0.875 to 0.875
- cotangent: float32 [25216, 512], P(('expert', 'shard')), may hold values from -6 to 6
Outputs:
- activations: float32 [25216, 512], P(('expert', 'shard'))
- d_tokens: float32 [25216, 512], P(('expert', 'shard'))
- grad_gain: float32 [2, 2, 512], P(None, None, 'shard')
- grad_bias: float32 [2, 2, 512], P(None, None, 'shard')
- grad_qkv: float32 [2, 512, 1536], P(None, 'shard')
- grad_proj: float32 [2, 512, 512], P(None, 'shard')
- grad_router: float32 [2, 512, 8], P(None, 'shard')
- grad_exp_in: float32 [2, 8, 512, 2048], P(None, 'expert', 'shard')
- grad_exp_out: float32 [2, 8, 2048, 512], P(None, 'expert', 'shard')
Inputs may be any that keep to these rules, and one draw needn't show every extreme that they name: `routes`: each row names 2 different experts; in each aligned block of 394 rows no expert is named by more than 192 rows. `priority`: in each aligned block of 394 rows the values are a permutation of 0 to 393.
All inputs are finite; a program needn't handle non-finite values.
Results may differ from a plain program's by a relative error of at most 0.025.
Values may be sent and summed in bfloat16 or wider, within the bound.
No kernel may reach another device: no remote copies, remote signals or barrier semaphores. Data moves between devices by JAX's collectives and lax.ppermute only.
A program may use at most 256 MiB of HBM per device.

v0:
```python
import jax
import jax.numpy as jnp
from jax import lax
from jax.sharding import PartitionSpec as P

D = 512
HEADS = 8
HEAD = 64
HIDDEN_SIZE = 2048
EXP_DEV = 1
SEQ = 197
MICRO = 2
LAYERS = 2
TOP = 2
TOK_MB = 394


norm_eps = 1e-06


def layer_norm(values, norm_scale, norm_shift):
    centre = values - jnp.mean(values, axis=-1, keepdims=True)
    spread = jnp.mean(centre * centre, axis=-1, keepdims=True)
    return centre * lax.rsqrt(spread + norm_eps) * norm_scale + norm_shift


def gelu_tanh(values):
    return jax.nn.gelu(values, approximate=True)


def dot_first(left, right):
    return lax.dot_general(
        left, right, (((0,), (0,)), ((), ())), preferred_element_type=jnp.float32
    )


def dot_last(left, right):
    return lax.dot_general(
        left, right, (((1,), (1,)), ((), ())), preferred_element_type=jnp.float32
    )


def slot_tables(route_ids, prio_rank, experts, capacity):
    tok_count = route_ids.shape[0]
    order_key = jnp.concatenate([prio_rank, prio_rank + tok_count])
    pair_expert = jnp.concatenate([route_ids[:, 0], route_ids[:, 1]])
    same_expert = pair_expert[:, None] == pair_expert[None, :]
    earlier = order_key[None, :] < order_key[:, None]
    position = jnp.sum((same_expert & earlier).astype(jnp.int32), axis=1)
    kept_mask = position < capacity
    flat_slot = jnp.where(kept_mask, pair_expert * capacity + position, experts * capacity)
    pair_ids = jnp.arange(2 * tok_count, dtype=jnp.int32)
    slot_pair = (
        jnp.full((experts * capacity + 1,), 2 * tok_count, jnp.int32).at[flat_slot].set(pair_ids)
    )
    slot_pair = slot_pair[: experts * capacity]
    slot_token = jnp.where(slot_pair < 2 * tok_count, slot_pair % tok_count, tok_count)
    return (flat_slot, slot_pair, slot_token, kept_mask)


def forward_layer(residual, route_ids, prio_rank, weights, experts, capacity):
    norm_gains, norm_shifts, qkv_w, proj_w, router_w, in_w, out_w = weights
    tok_count = residual.shape[0]
    seq_count = tok_count // SEQ
    score_scale = HEAD ** (-0.5)
    norm_scale = norm_gains.astype(jnp.float32)
    norm_shift = norm_shifts.astype(jnp.float32)
    normed = layer_norm(residual, norm_scale[0], norm_shift[0]).astype(jnp.bfloat16)
    qkv_rows = jnp.dot(normed, qkv_w, preferred_element_type=jnp.float32).astype(jnp.bfloat16)
    heads = qkv_rows.reshape(seq_count, SEQ, 3, HEADS, HEAD)
    scores = (
        jnp.einsum(
            "sqhd,skhd->shqk", heads[:, :, 0], heads[:, :, 1], preferred_element_type=jnp.float32
        )
        * score_scale
    )
    row_top = jnp.max(scores, axis=-1, keepdims=True)
    scores_exp = jnp.exp(scores - row_top)
    row_total = jnp.sum(scores_exp, axis=-1, keepdims=True)
    soft_scores = scores_exp / row_total
    log_total = row_top + jnp.log(row_total)
    mixed_heads = jnp.einsum(
        "shqk,skhd->sqhd",
        soft_scores.astype(jnp.bfloat16),
        heads[:, :, 2],
        preferred_element_type=jnp.float32,
    )
    mixed_heads = mixed_heads.astype(jnp.bfloat16).reshape(tok_count, D)
    middle = residual + jnp.dot(mixed_heads, proj_w, preferred_element_type=jnp.float32)
    normed_two = layer_norm(middle, norm_scale[1], norm_shift[1]).astype(jnp.bfloat16)
    gate_probs = jax.nn.softmax(
        jnp.dot(normed_two, router_w, preferred_element_type=jnp.float32), axis=-1
    )
    flat_slot, slot_pair, slot_token, kept_mask = slot_tables(
        route_ids, prio_rank, experts, capacity
    )
    padded = jnp.concatenate([normed_two, jnp.zeros((1, D), jnp.bfloat16)])
    sending = padded[slot_token].reshape(experts, capacity, D)
    received = lax.all_to_all(sending, "expert", split_axis=0, concat_axis=0, tiled=True)
    sources = received.shape[0]
    item_count = received.shape[1]
    row_block = received.reshape(sources * item_count, D)
    hidden_pre = jnp.dot(row_block, in_w[0], preferred_element_type=jnp.float32)
    hidden_act = gelu_tanh(hidden_pre).astype(jnp.bfloat16)
    expert_rows = jnp.dot(hidden_act, out_w[0], preferred_element_type=jnp.float32).astype(
        jnp.bfloat16
    )
    returned = lax.all_to_all(
        expert_rows.reshape(sources, item_count, D),
        "expert",
        split_axis=0,
        concat_axis=0,
        tiled=True,
    )
    returned, received, hidden_pre = (
        returned,
        received,
        hidden_pre.reshape(sources, item_count, HIDDEN_SIZE),
    )
    back_rows = jnp.concatenate(
        [returned.reshape(experts * capacity, D), jnp.zeros((1, D), jnp.bfloat16)]
    )
    pair_rows = back_rows[flat_slot].astype(jnp.float32).reshape(TOP, tok_count, D)
    route_hot = (
        route_ids[:, :, None] == jnp.arange(experts, dtype=jnp.int32)[None, None, :]
    ).astype(jnp.float32)
    chosen = jnp.sum(route_hot * gate_probs[:, None, :], axis=-1)
    kept_gate = kept_mask.astype(jnp.float32).reshape(TOP, tok_count)
    weight_pair = kept_gate * chosen.T
    combined = jnp.sum(weight_pair[:, :, None] * pair_rows, axis=0)
    output = middle + combined
    saved_state = (
        residual,
        normed,
        heads,
        log_total,
        mixed_heads,
        middle,
        normed_two,
        gate_probs,
        route_hot,
        kept_gate,
        weight_pair,
        flat_slot,
        slot_pair,
        pair_rows,
        received,
        hidden_pre,
    )
    return (output, saved_state)


def backward_layer(d_output, saved_state, weights, experts, capacity):
    (
        residual,
        normed,
        heads,
        log_total,
        mixed_heads,
        middle,
        normed_two,
        gate_probs,
        route_hot,
        kept_gate,
        weight_pair,
        flat_slot,
        slot_pair,
        pair_rows,
        received,
        hidden_pre,
    ) = saved_state
    norm_gains, norm_shifts, qkv_w, proj_w, router_w, in_w, out_w = weights
    tok_count = residual.shape[0]
    seq_count = tok_count // SEQ
    score_scale = HEAD ** (-0.5)
    norm_scale = norm_gains.astype(jnp.float32)
    norm_shift = norm_shifts.astype(jnp.float32)
    d_gate_pair = kept_gate * jnp.sum(d_output[None] * pair_rows, axis=-1)
    d_gates = jnp.sum(route_hot * d_gate_pair.T[:, :, None], axis=1)
    d_logits = (
        gate_probs * (d_gates - jnp.sum(gate_probs * d_gates, axis=-1, keepdims=True))
    ).astype(jnp.bfloat16)
    g_router = dot_first(normed_two, d_logits)
    d_normed_two = dot_last(d_logits, router_w)
    d_pairs = (
        (weight_pair[:, :, None] * d_output[None]).astype(jnp.bfloat16).reshape(TOP * tok_count, D)
    )
    d_slots = jnp.concatenate([d_pairs, jnp.zeros((1, D), jnp.bfloat16)])[slot_pair].reshape(
        experts, capacity, D
    )
    d_expert_out = lax.all_to_all(d_slots, "expert", split_axis=0, concat_axis=0, tiled=True)
    flat_out = d_expert_out.reshape(experts * capacity, D)
    hidden_flat = hidden_pre.reshape(experts * capacity, HIDDEN_SIZE)
    hidden_act = gelu_tanh(hidden_flat).astype(jnp.bfloat16)
    g_out = dot_first(hidden_act, flat_out)
    d_act = dot_last(flat_out, out_w[0])
    d_pre = jax.vjp(gelu_tanh, hidden_flat)[1](d_act)[0].astype(jnp.bfloat16)
    g_in = dot_first(received.reshape(experts * capacity, D), d_pre)
    d_rows = dot_last(d_pre, in_w[0]).astype(jnp.bfloat16).reshape(experts, capacity, D)
    d_back = lax.all_to_all(d_rows, "expert", split_axis=0, concat_axis=0, tiled=True)
    d_pair_in = jnp.concatenate(
        [d_back.reshape(experts * capacity, D), jnp.zeros((1, D), jnp.bfloat16)]
    )[flat_slot]
    d_pair_in = d_pair_in.astype(jnp.float32).reshape(TOP, tok_count, D)
    d_normed_two = d_normed_two + jnp.sum(d_pair_in, axis=0)
    pulled_two = jax.vjp(layer_norm, middle, norm_scale[1], norm_shift[1])[1](d_normed_two)
    d_middle = d_output + pulled_two[0]
    d_branch = d_middle.astype(jnp.bfloat16)
    g_proj = dot_first(mixed_heads, d_branch)
    d_mixed = dot_last(d_branch, proj_w).astype(jnp.bfloat16).reshape(seq_count, SEQ, HEADS, HEAD)
    query_heads = heads[:, :, 0]
    key_heads = heads[:, :, 1]
    value_heads = heads[:, :, 2]
    scores = (
        jnp.einsum("sqhd,skhd->shqk", query_heads, key_heads, preferred_element_type=jnp.float32)
        * score_scale
    )
    soft_scores = jnp.exp(scores - log_total)
    d_soft = jnp.einsum("sqhd,skhd->shqk", d_mixed, value_heads, preferred_element_type=jnp.float32)
    d_values = jnp.einsum(
        "shqk,sqhd->skhd",
        soft_scores.astype(jnp.bfloat16),
        d_mixed,
        preferred_element_type=jnp.float32,
    )
    d_scores = (
        soft_scores * (d_soft - jnp.sum(soft_scores * d_soft, axis=-1, keepdims=True))
    ).astype(jnp.bfloat16)
    d_query = (
        jnp.einsum("shqk,skhd->sqhd", d_scores, key_heads, preferred_element_type=jnp.float32)
        * score_scale
    )
    d_keys = (
        jnp.einsum("shqk,sqhd->skhd", d_scores, query_heads, preferred_element_type=jnp.float32)
        * score_scale
    )
    d_qkv = (
        jnp.stack([d_query, d_keys, d_values], axis=2)
        .reshape(tok_count, 3 * D)
        .astype(jnp.bfloat16)
    )
    g_qkv = dot_first(normed, d_qkv)
    d_normed = dot_last(d_qkv, qkv_w)
    pulled_one = jax.vjp(layer_norm, residual, norm_scale[0], norm_shift[0])[1](d_normed)
    d_residual = d_middle + pulled_one[0]
    g_gain = jnp.stack([pulled_one[1], pulled_two[1]])
    g_shift = jnp.stack([pulled_one[2], pulled_two[2]])
    return (d_residual, (g_gain, g_shift, g_qkv, g_proj, g_router, g_in[None], g_out[None]))


def local(
    tokens,
    routes,
    priority,
    norm_gain,
    norm_bias,
    w_qkv,
    w_proj,
    w_router,
    exp_in,
    exp_out,
    cotangent,
):
    experts = lax.axis_size("expert") * EXP_DEV
    capacity = max(8, (5 * TOK_MB // (2 * experts) + 7) // 8 * 8)
    totals = []
    for layer_index in range(LAYERS):
        totals.append(None)
    out_blocks = []
    grad_blocks = []
    for micro_index in range(MICRO):
        row_start = micro_index * TOK_MB
        residual = tokens[row_start : row_start + TOK_MB]
        route_ids = routes[row_start : row_start + TOK_MB]
        prio_rank = priority[row_start : row_start + TOK_MB]
        saved_list = []
        for layer_index in range(LAYERS):
            weights = (
                lax.all_gather(norm_gain[layer_index], "shard", axis=1, tiled=True),
                lax.all_gather(norm_bias[layer_index], "shard", axis=1, tiled=True),
                lax.all_gather(w_qkv[layer_index], "shard", axis=0, tiled=True),
                lax.all_gather(w_proj[layer_index], "shard", axis=0, tiled=True),
                lax.all_gather(w_router[layer_index], "shard", axis=0, tiled=True),
                lax.all_gather(exp_in[layer_index], "shard", axis=1, tiled=True),
                lax.all_gather(exp_out[layer_index], "shard", axis=1, tiled=True),
            )
            residual, saved_state = forward_layer(
                residual, route_ids, prio_rank, weights, experts, capacity
            )
            saved_list.append(saved_state)
        out_blocks.append(residual)
        d_residual = cotangent[row_start : row_start + TOK_MB]
        for layer_index in reversed(range(LAYERS)):
            weights = (
                lax.all_gather(norm_gain[layer_index], "shard", axis=1, tiled=True),
                lax.all_gather(norm_bias[layer_index], "shard", axis=1, tiled=True),
                lax.all_gather(w_qkv[layer_index], "shard", axis=0, tiled=True),
                lax.all_gather(w_proj[layer_index], "shard", axis=0, tiled=True),
                lax.all_gather(w_router[layer_index], "shard", axis=0, tiled=True),
                lax.all_gather(exp_in[layer_index], "shard", axis=1, tiled=True),
                lax.all_gather(exp_out[layer_index], "shard", axis=1, tiled=True),
            )
            d_residual, layer_grads = backward_layer(
                d_residual, saved_list[layer_index], weights, experts, capacity
            )
            if totals[layer_index] is None:
                totals[layer_index] = layer_grads
            else:
                totals[layer_index] = tuple(
                    (
                        old_sum + new_term
                        for old_sum, new_term in zip(totals[layer_index], layer_grads)
                    )
                )
        grad_blocks.append(d_residual)
    stacked = tuple(
        (
            jnp.stack([totals[layer_index][kind_index] for layer_index in range(LAYERS)])
            for kind_index in range(7)
        )
    )
    scattered = (
        lax.psum_scatter(
            stacked[0].astype(jnp.bfloat16), "shard", scatter_dimension=2, tiled=True
        ).astype(jnp.float32),
        lax.psum_scatter(
            stacked[1].astype(jnp.bfloat16), "shard", scatter_dimension=2, tiled=True
        ).astype(jnp.float32),
        lax.psum_scatter(
            stacked[2].astype(jnp.bfloat16), "shard", scatter_dimension=1, tiled=True
        ).astype(jnp.float32),
        lax.psum_scatter(
            stacked[3].astype(jnp.bfloat16), "shard", scatter_dimension=1, tiled=True
        ).astype(jnp.float32),
        lax.psum_scatter(
            stacked[4].astype(jnp.bfloat16), "shard", scatter_dimension=1, tiled=True
        ).astype(jnp.float32),
        lax.psum_scatter(
            stacked[5].astype(jnp.bfloat16), "shard", scatter_dimension=2, tiled=True
        ).astype(jnp.float32),
        lax.psum_scatter(
            stacked[6].astype(jnp.bfloat16), "shard", scatter_dimension=2, tiled=True
        ).astype(jnp.float32),
    )
    replicated = (
        lax.psum(scattered[0].astype(jnp.bfloat16), "expert").astype(jnp.float32),
        lax.psum(scattered[1].astype(jnp.bfloat16), "expert").astype(jnp.float32),
        lax.psum(scattered[2].astype(jnp.bfloat16), "expert").astype(jnp.float32),
        lax.psum(scattered[3].astype(jnp.bfloat16), "expert").astype(jnp.float32),
        lax.psum(scattered[4].astype(jnp.bfloat16), "expert").astype(jnp.float32),
    )
    activations = jnp.concatenate(out_blocks, axis=0)
    d_tokens = jnp.concatenate(grad_blocks, axis=0)
    return (
        activations,
        d_tokens,
        replicated[0],
        replicated[1],
        replicated[2],
        replicated[3],
        replicated[4],
        scattered[5],
        scattered[6],
    )


def solution(mesh):
    return jax.shard_map(
        local,
        mesh=mesh,
        in_specs=(
            P(("expert", "shard"), None),
            P(("expert", "shard"), None),
            P(("expert", "shard")),
            P(None, None, "shard"),
            P(None, None, "shard"),
            P(None, "shard", None),
            P(None, "shard", None),
            P(None, "shard", None),
            P(None, "expert", "shard", None),
            P(None, "expert", "shard", None),
            P(("expert", "shard"), None),
        ),
        out_specs=(
            P(("expert", "shard"), None),
            P(("expert", "shard"), None),
            P(None, None, "shard"),
            P(None, None, "shard"),
            P(None, "shard", None),
            P(None, "shard", None),
            P(None, "shard", None),
            P(None, "expert", "shard", None),
            P(None, "expert", "shard", None),
        ),
        check_vma=False,
    )
```

profile of v0, /device:TPU:0, one launch (start us, length us, event | category | flops | bytes accessed | tf_op | source)
XLA Modules:
  0.0 1039.3 jit_solution(6262433277946074067)
XLA Ops:
  14.2 6.0 all-gather
  26.5 8.2 all-gather.3
  116.0 8.7 all-to-all-done.4
  129.0 7.2 all-gather.10
  141.8 7.6 fusion.80
  149.5 7.7 fusion.125
  163.2 8.9 multiply_convert_fusion.3
  177.4 12.0 %all-to-all-done.5 = bf16[8,128,512]{2,1,0:T(8,128)(2,1)} async-done(((bf16[8,128,512]{2,1,0:T(8,128)(2,1)}), bf16[8,128,512]{2,1,0:T(8,128)(2,1)}, u32[]{:S(2)}, u32[]{:S(2)}) %all-to-all-start.5) | async-done | bytes 1048608 | tf_op jit(solution)/shard_map/all_to_all | solution.py:108
  207.8 11.5 %all-to-all-done.1 = bf16[8,128,512]{2,1,0:T(8,128)(2,1)} async-done(((bf16[8,128,512]{2,1,0:T(8,128)(2,1)}), bf16[8,128,512]{2,1,0:T(8,128)(2,1)}, u32[]{:S(2)}, u32[]{:S(2)}) %all-to-all-start.1) | async-done | bytes 1048608 | tf_op jit(solution)/shard_map/all_to_all | solution.py:108
  315.1 18.7 %all-to-all-done.8 = bf16[8,128,512]{2,1,0:T(8,128)(2,1)} async-done(((bf16[8,128,512]{2,1,0:T(8,128)(2,1)}), bf16[8,128,512]{2,1,0:T(8,128)(2,1)}, u32[]{:S(2)}, u32[]{:S(2)}) %all-to-all-start.8) | async-done | bytes 1048608 | tf_op jit(solution)/shard_map/all_to_all | solution.py:191
  349.9 13.5 %all-to-all-done.6 = bf16[8,128,512]{2,1,0:T(8,128)(2,1)} async-done(((bf16[8,128,512]{2,1,0:T(8,128)(2,1)}), bf16[8,128,512]{2,1,0:T(8,128)(2,1)}, u32[]{:S(2)}, u32[]{:S(2)}) %all-to-all-start.6) | async-done | bytes 1048608 | tf_op jit(solution)/shard_map/all_to_all | solution.py:99
  368.7 9.9 multiply_convert_fusion.2
  378.6 6.2 fusion.134
  384.8 8.3 all-to-all-done.12
  397.7 9.7 fusion.13
  412.7 11.0 %all-to-all-done.3 = bf16[8,128,512]{2,1,0:T(8,128)(2,1)S(1)} async-done(((bf16[8,128,512]{2,1,0:T(8,128)(2,1)}), bf16[8,128,512]{2,1,0:T(8,128)(2,1)S(1)}, u32[]{:S(2)}, u32[]{:S(2)}) %all-to-all-start.3) | async-done | bytes 1048608 | tf_op jit(solution)/shard_map/all_to_all | solution.py:108
  443.6 10.1 all-to-all-done.9
  457.3 9.7 fusion.27
  472.3 10.8 %all-to-all-done.7 = bf16[8,128,512]{2,1,0:T(8,128)(2,1)S(1)} async-done(((bf16[8,128,512]{2,1,0:T(8,128)(2,1)}), bf16[8,128,512]{2,1,0:T(8,128)(2,1)S(1)}, u32[]{:S(2)}, u32[]{:S(2)}) %all-to-all-start.7) | async-done | bytes 1048608 | tf_op jit(solution)/shard_map/all_to_all | solution.py:108
  586.3 6.0 all-to-all-start.10
  610.2 7.3 all-to-all-done.10
  621.2 9.7 fusion.6
  636.4 10.6 %all-to-all-done.14 = bf16[8,128,512]{2,1,0:T(8,128)(2,1)S(1)} async-done(((bf16[8,128,512]{2,1,0:T(8,128)(2,1)}), bf16[8,128,512]{2,1,0:T(8,128)(2,1)S(1)}, u32[]{:S(2)}, u32[]{:S(2)}) %all-to-all-start.14) | async-done | bytes 1048608 | tf_op jit(solution)/shard_map/all_to_all | solution.py:191
  651.6 9.7 fusion.20
  666.6 11.0 %all-to-all-done.11 = bf16[8,128,512]{2,1,0:T(8,128)(2,1)S(1)} async-done(((bf16[8,128,512]{2,1,0:T(8,128)(2,1)}), bf16[8,128,512]{2,1,0:T(8,128)(2,1)S(1)}, u32[]{:S(2)}, u32[]{:S(2)}) %all-to-all-start.11) | async-done | bytes 1048608 | tf_op jit(solution)/shard_map/all_to_all | solution.py:200
  701.7 6.8 all-to-all-done.15
  776.2 9.7 fusion.39
  834.6 17.8 %reduce-scatter.22.cloned.1.call-done = bf16[128,4]{1,0:T(8,128)(2,1)} async-done(((bf16[512,4]{1,0:T(8,128)(2,1)}), bf16[128,4]{1,0:T(8,128)(2,1)}) %reduce-scatter.22.cloned.1.call-update) | async-done | bytes 1040
  853.3 21.6 %all-reduce.16 = (bf16[2,2,128]{2,1,0:T(2,128)(2,1)S(1)}, bf16[2,2,128]{2,1,0:T(2,128)(2,1)S(1)}, bf16[2,128,8]{1,2,0:T(8,128)(2,1)S(1)}) all-reduce(bf16[2,2,128]{2,1,0:T(2,128)(2,1)S(1)} %copy.259, bf16[2,2,128]{2,1,0:T(2,128)(2,1)S(1)} %copy.261, bf16[2,128,8]{1,2,0:T(8,128)(2,1)S(1)} %copy.263), channel_id=1, replica_groups=mesh['expert'=8,'shard'=4] {'expert'}, use_global_device_ids=true, to_apply=%region_89.90 | all-reduce | flops 3072 | bytes 12288 | tf_op jit(solution)/shard_map/psum | solution.py:346
  876.7 22.7 %reduce-scatter.20.cloned.1.call-done = bf16[2,1,512,512]{3,2,1,0:T(8,128)(2,1)} async-done(((bf16[2,1,2048,512]{3,2,1,0:T(8,128)(2,1)}), bf16[2,1,512,512]{3,2,1,0:T(8,128)(2,1)}) %reduce-scatter.20.cloned.1.call-update) | async-done | bytes 1048592 | tf_op jit(solution)/shard_map/reduce_scatter | solution.py:341
  902.3 44.3 %reduce-scatter.18.cloned.1.call-done = bf16[2,1,128,2048]{3,2,1,0:T(8,128)(2,1)} async-done(((bf16[2,1,512,2048]{3,2,1,0:T(8,128)(2,1)}), bf16[2,1,128,2048]{3,2,1,0:T(8,128)(2,1)}) %reduce-scatter.18.cloned.1.call-update) | async-done | bytes 1048592 | tf_op jit(solution)/shard_map/reduce_scatter | solution.py:338
  949.3 79.0 %all-reduce.20.cloned.1.call-done = (bf16[2,128,1536]{2,1,0:T(8,128)(2,1)}, bf16[2,128,512]{2,1,0:T(8,128)(2,1)}) async-done(((bf16[2,128,1536]{2,1,0:T(8,128)(2,1)}, bf16[2,128,512]{2,1,0:T(8,128)(2,1)}), (bf16[2,128,1536]{2,1,0:T(8,128)(2,1)}, bf16[2,128,512]{2,1,0:T(8,128)(2,1)})) %all-reduce.20.cloned.1.call-update) | async-done | bytes 1048592 | tf_op jit(solution)/shard_map/psum | solution.py:348
  (979 shorter events, 579.5 us)
Async XLA Ops:
  7.2 34.5 %all-gather.21.cloned.1.call-start = ((), (), s32[]{:S(2)}) async-start(), calls=%async_computation.27 | async-start | bytes 1966080 | tf_op jit(solution)/shard_map/all_gather | solution.py:281
  9.5 132.4 %all-gather.23.cloned.1.call-start = ((), (), s32[]{:S(2)}) async-start(), calls=%async_computation.28 | async-start | bytes 2621440 | tf_op jit(solution)/shard_map/all_gather | solution.py:284
  11.8 137.6 %all-gather.25.cloned.1.call-start = ((), (), s32[]{:S(2)}) async-start(), calls=%async_computation.29 | async-start | bytes 2621440 | tf_op jit(solution)/shard_map/all_gather | solution.py:285
  92.8 31.9 %all-to-all-start.4 = ((bf16[8,128,512]{2,1,0:T(8,128)(2,1)}), bf16[8,128,512]{2,1,0:T(8,128)(2,1)}, u32[]{:S(2)}, u32[]{:S(2)}) async-start(bf16[8,128,512]{2,1,0:T(8,128)(2,1)} %bitcast.478), calls=%async_computation.4 | async-start | bytes 2097152 | tf_op jit(solution)/shard_map/all_to_all | solution.py:99
  98.4 132.7 %all-gather.27.cloned.1.call-start = ((), (), s32[]{:S(2)}) async-start(), calls=%async_computation.30 | async-start | bytes 1966080 | tf_op jit(solution)/shard_map/all_gather | solution.py:281
  110.8 156.5 %copy-start.195 = (f32[1,1,512]{2,1,0:T(1,128)}, f32[1,1,512]{2,1,0:T(1,128)S(1)}, u32[]{:S(2)}) copy-start(f32[1,1,512]{2,1,0:T(1,128)S(1)} %get-tuple-element.132) | copy-start | bytes 6148
  110.9 182.5 %copy-start.173 = (s32[1024]{0:T(1024)}, s32[1024]{0:T(1024)S(1)}, u32[]{:S(2)}) copy-start(s32[1024]{0:T(1024)S(1)} %get-tuple-element.96) | copy-start | bytes 12292
  124.7 32.4 %all-to-all-start = ((bf16[8,128,512]{2,1,0:T(8,128)(2,1)}), bf16[8,128,512]{2,1,0:T(8,128)(2,1)}, u32[]{:S(2)}, u32[]{:S(2)}) async-start(bf16[8,128,512]{2,1,0:T(8,128)(2,1)} %bitcast.482), calls=%async_computation | async-start | bytes 2097152 | tf_op jit(solution)/shard_map/all_to_all | solution.py:99
  157.2 32.3 %all-to-all-start.5 = ((bf16[8,128,512]{2,1,0:T(8,128)(2,1)}), bf16[8,128,512]{2,1,0:T(8,128)(2,1)}, u32[]{:S(2)}, u32[]{:S(2)}) async-start(bf16[8,128,512]{2,1,0:T(8,128)(2,1)} %bitcast.496), calls=%async_computation.5 | async-start | bytes 2097152 | tf_op jit(solution)/shard_map/all_to_all | solution.py:108
  189.4 29.8 %all-to-all-start.1 = ((bf16[8,128,512]{2,1,0:T(8,128)(2,1)}), bf16[8,128,512]{2,1,0:T(8,128)(2,1)}, u32[]{:S(2)}, u32[]{:S(2)}) async-start(bf16[8,128,512]{2,1,0:T(8,128)(2,1)} %bitcast.494), calls=%async_computation.1 | async-start | bytes 2097152 | tf_op jit(solution)/shard_map/all_to_all | solution.py:108
  274.4 29.7 %all-to-all-start.2 = ((bf16[8,128,512]{2,1,0:T(8,128)(2,1)}), bf16[8,128,512]{2,1,0:T(8,128)(2,1)}, u32[]{:S(2)}, u32[]{:S(2)}) async-start(bf16[8,128,512]{2,1,0:T(8,128)(2,1)} %bitcast.480), calls=%async_computation.2 | async-start | bytes 2097152 | tf_op jit(solution)/shard_map/all_to_all | solution.py:99
  278.6 90.1 %all-gather.29.cloned.1.call-start = ((), (), s32[]{:S(2)}) async-start(), calls=%async_computation.31 | async-start | bytes 2621440 | tf_op jit(solution)/shard_map/all_gather | solution.py:284
  304.1 29.6 %all-to-all-start.8 = ((bf16[8,128,512]{2,1,0:T(8,128)(2,1)}), bf16[8,128,512]{2,1,0:T(8,128)(2,1)}, u32[]{:S(2)}, u32[]{:S(2)}) async-start(bf16[8,128,512]{2,1,0:T(8,128)(2,1)} %bitcast.483), calls=%async_computation.8 | async-start | bytes 2097152 | tf_op jit(solution)/shard_map/all_to_all | solution.py:191
  308.3 70.3 %all-gather.31.cloned.1.call-start = ((), (), s32[]{:S(2)}) async-start(), calls=%async_computation.32 | async-start | bytes 2621440 | tf_op jit(solution)/shard_map/all_gather | solution.py:285
  333.7 29.6 %all-to-all-start.6 = ((bf16[8,128,512]{2,1,0:T(8,128)(2,1)}), bf16[8,128,512]{2,1,0:T(8,128)(2,1)}, u32[]{:S(2)}, u32[]{:S(2)}) async-start(bf16[8,128,512]{2,1,0:T(8,128)(2,1)} %bitcast.481), calls=%async_computation.6 | async-start | bytes 2097152 | tf_op jit(solution)/shard_map/all_to_all | solution.py:99
  363.4 29.7 %all-to-all-start.12 = ((bf16[8,128,512]{2,1,0:T(8,128)(2,1)}), bf16[8,128,512]{2,1,0:T(8,128)(2,1)S(1)}, u32[]{:S(2)}, u32[]{:S(2)}) async-start(bf16[8,128,512]{2,1,0:T(8,128)(2,1)} %bitcast.484), calls=%async_computation.12 | async-start | bytes 2097152 | tf_op jit(solution)/shard_map/all_to_all | solution.py:191
  394.1 29.6 %all-to-all-start.3 = ((bf16[8,128,512]{2,1,0:T(8,128)(2,1)}), bf16[8,128,512]{2,1,0:T(8,128)(2,1)S(1)}, u32[]{:S(2)}, u32[]{:S(2)}) async-start(bf16[8,128,512]{2,1,0:T(8,128)(2,1)} %bitcast.497), calls=%async_computation.3 | async-start | bytes 2097152 | tf_op jit(solution)/shard_map/all_to_all | solution.py:108
  423.7 30.0 %all-to-all-start.9 = ((bf16[8,128,512]{2,1,0:T(8,128)(2,1)}), bf16[8,128,512]{2,1,0:T(8,128)(2,1)}, u32[]{:S(2)}, u32[]{:S(2)}) async-start(bf16[8,128,512]{2,1,0:T(8,128)(2,1)} %bitcast.495), calls=%async_computation.9 | async-start | bytes 2097152 | tf_op jit(solution)/shard_map/all_to_all | solution.py:200
  453.7 29.4 %all-to-all-start.7 = ((bf16[8,128,512]{2,1,0:T(8,128)(2,1)}), bf16[8,128,512]{2,1,0:T(8,128)(2,1)S(1)}, u32[]{:S(2)}, u32[]{:S(2)}) async-start(bf16[8,128,512]{2,1,0:T(8,128)(2,1)} %bitcast.498), calls=%async_computation.7 | async-start | bytes 2097152 | tf_op jit(solution)/shard_map/all_to_all | solution.py:108
  483.1 34.0 %all-to-all-start.13 = ((bf16[8,128,512]{2,1,0:T(8,128)(2,1)}), bf16[8,128,512]{2,1,0:T(8,128)(2,1)}, u32[]{:S(2)}, u32[]{:S(2)}) async-start(bf16[8,128,512]{2,1,0:T(8,128)(2,1)} %bitcast.493), calls=%async_computation.13 | async-start | bytes 2097152 | tf_op jit(solution)/shard_map/all_to_all | solution.py:200
  586.3 31.2 %all-to-all-start.10 = ((bf16[8,128,512]{2,1,0:T(8,128)(2,1)}), bf16[8,128,512]{2,1,0:T(8,128)(2,1)}, u32[]{:S(2)}, u32[]{:S(2)}) async-start(bf16[8,128,512]{2,1,0:T(8,128)(2,1)} %bitcast.477), calls=%async_computation.10 | async-start | bytes 2097152 | tf_op jit(solution)/shard_map/all_to_all | solution.py:191
  617.5 29.5 %all-to-all-start.14 = ((bf16[8,128,512]{2,1,0:T(8,128)(2,1)}), bf16[8,128,512]{2,1,0:T(8,128)(2,1)S(1)}, u32[]{:S(2)}, u32[]{:S(2)}) async-start(bf16[8,128,512]{2,1,0:T(8,128)(2,1)} %bitcast.479), calls=%async_computation.14 | async-start | bytes 2097152 | tf_op jit(solution)/shard_map/all_to_all | solution.py:191
  648.0 29.6 %all-to-all-start.11 = ((bf16[8,128,512]{2,1,0:T(8,128)(2,1)}), bf16[8,128,512]{2,1,0:T(8,128)(2,1)S(1)}, u32[]{:S(2)}, u32[]{:S(2)}) async-start(bf16[8,128,512]{2,1,0:T(8,128)(2,1)} %bitcast.499), calls=%async_computation.11 | async-start | bytes 2097152 | tf_op jit(solution)/shard_map/all_to_all | solution.py:200
  678.5 30.0 %all-to-all-start.15 = ((bf16[8,128,512]{2,1,0:T(8,128)(2,1)}), bf16[8,128,512]{2,1,0:T(8,128)(2,1)}, u32[]{:S(2)}, u32[]{:S(2)}) async-start(bf16[8,128,512]{2,1,0:T(8,128)(2,1)} %bitcast.492), calls=%async_computation.15 | async-start | bytes 2097152 | tf_op jit(solution)/shard_map/all_to_all | solution.py:200
  682.9 143.7 %reduce-scatter.26.cloned.1.call-start = ((), (), s32[]{:S(2)}) async-start(), calls=%async_computation.35 | async-start | bytes 163840
  688.8 142.0 %reduce-scatter.16.cloned.1.call-start = ((), (), s32[]{:S(2)}) async-start(), calls=%async_computation.24 | async-start | bytes 1310720 | tf_op jit(solution)/shard_map/reduce_scatter | solution.py:332
  744.1 86.7 %reduce-scatter.14.cloned.1.call-start = ((), (), s32[]{:S(2)}) async-start(), calls=%async_computation.23 | async-start | bytes 3932160 | tf_op jit(solution)/shard_map/reduce_scatter | solution.py:329
  770.7 63.0 %reduce-scatter.24.cloned.1.call-start = ((), (), s32[]{:S(2)}) async-start(), calls=%async_computation.34 | async-start | bytes 163840
  799.1 53.3 %reduce-scatter.22.cloned.1.call-start = ((), (), s32[]{:S(2)}) async-start(), calls=%async_computation.33 | async-start | bytes 163840
  800.4 99.0 %reduce-scatter.20.cloned.1.call-start = ((), (), s32[]{:S(2)}) async-start(), calls=%async_computation.26 | async-start | bytes 5242880 | tf_op jit(solution)/shard_map/reduce_scatter | solution.py:341
  805.1 141.4 %reduce-scatter.18.cloned.1.call-start = ((), (), s32[]{:S(2)}) async-start(), calls=%async_computation.25 | async-start | bytes 5242880 | tf_op jit(solution)/shard_map/reduce_scatter | solution.py:338
  823.9 204.4 %all-reduce.20.cloned.1.call-start = ((), (), s32[]{:S(2)}) async-start(), calls=%async_computation.36 | async-start | bytes 2097152 | tf_op jit(solution)/shard_map/psum | solution.py:348
  (280 other events, 2750.1 us)
Sparse Core Ops, SparseCore 0:
  10.1 23.2 all-gather.20
  35.6 21.9 all-gather.22
  59.8 22.5 all-gather.24
  100.4 20.5 all-gather.26
  280.7 23.2 all-gather.28
  310.4 23.2 all-gather.30
  688.9 20.3 reduce-scatter.25
  744.2 23.0 reduce-scatter.15
  770.9 36.8 reduce-scatter.13
  810.1 19.6 reduce-scatter.23
  832.7 19.6 reduce-scatter.21
  854.8 44.5 reduce-scatter.19
  901.9 44.5 reduce-scatter.17
  949.9 78.2 all-reduce.19
where the time goes:
time: 1050 us; the launch traced here: 1040 us
  waiting for transfers between devices  311 us (30%)
  local copies, waits for them, and re-layouts  258 us (25%)
  matrix products  229 us (22%)
  other arithmetic  82.1 us (8%)
  starting transfers between devices  71.9 us (7%)
  blocking collectives  69.1 us (7%)
  between operations  18.1 us (2%)
    psum x1, waiting for transfers between devices, local(): lax.psum(scattered[2].astype(jnp.bfloat16), 'expert').astype(jnp.float32)  79 us
    dot_general x20, matrix products, dot_last(): lax.dot_general(left, right, (((1,), (1,)), ((), ())), preferred_element_...  70.6 us
    dot_general x20, matrix products, dot_first(): lax.dot_general(left, right, (((0,), (0,)), ((), ())), preferred_element_...  57.3 us
    unnamed x588, local copies, waits for them, and re-layouts  53.8 us
    all_to_all x4, waiting for transfers between devices, forward_layer(): lax.all_to_all(expert_rows.reshape(sources, item_count, D), 'expert', spl...  45.3 us
    all_to_all x4, waiting for transfers between devices, backward_layer(): lax.all_to_all(d_slots, 'expert', split_axis=0, concat_axis=0, tiled=True)  45 us
    reduce_scatter x1, waiting for transfers between devices, local(): lax.psum_scatter(stacked[5].astype(jnp.bfloat16), 'shard', scatter_dimens...  44.3 us
    dot_general x4, matrix products, forward_layer(): hidden_pre = jnp.dot(row_block, in_w[0], preferred_element_type=jnp.float32)  30.8 us
  transfers between devices with their start and end apart: 30, of which 18 were waited for; matrix products, arithmetic and copies ran while one was open for 41% of the time, Pallas kernels for 0%

commit v1 on v0

v1 whole, which is shorter than its diff:
```python
import jax
import jax.numpy as jnp
from jax import lax
from jax.sharding import PartitionSpec as P

D = 512
HEADS = 8
HEAD = 64
HIDDEN_SIZE = 2048
EXP_DEV = 1
SEQ = 197
MICRO = 2
LAYERS = 2
TOP = 2
TOK_MB = 394


norm_eps = 1e-06


def layer_norm(values, norm_scale, norm_shift):
    centre = values - jnp.mean(values, axis=-1, keepdims=True)
    spread = jnp.mean(centre * centre, axis=-1, keepdims=True)
    return centre * lax.rsqrt(spread + norm_eps) * norm_scale + norm_shift


def gelu_tanh(values):
    return jax.nn.gelu(values, approximate=True)


def dot_first(left, right):
    return lax.dot_general(
        left, right, (((0,), (0,)), ((), ())), preferred_element_type=jnp.float32
    )


def dot_last(left, right):
    return lax.dot_general(
        left, right, (((1,), (1,)), ((), ())), preferred_element_type=jnp.float32
    )


def slot_tables(route_ids, prio_rank, experts, capacity):
    tok_count = route_ids.shape[0]
    order_key = jnp.concatenate([prio_rank, prio_rank + tok_count])
    pair_expert = jnp.concatenate([route_ids[:, 0], route_ids[:, 1]])
    same_expert = pair_expert[:, None] == pair_expert[None, :]
    earlier = order_key[None, :] < order_key[:, None]
    position = jnp.sum((same_expert & earlier).astype(jnp.int32), axis=1)
    kept_mask = position < capacity
    flat_slot = jnp.where(kept_mask, pair_expert * capacity + position, experts * capacity)
    pair_ids = jnp.arange(2 * tok_count, dtype=jnp.int32)
    slot_pair = (
        jnp.full((experts * capacity + 1,), 2 * tok_count, jnp.int32).at[flat_slot].set(pair_ids)
    )
    slot_pair = slot_pair[: experts * capacity]
    slot_token = jnp.where(slot_pair < 2 * tok_count, slot_pair % tok_count, tok_count)
    return (flat_slot, slot_pair, slot_token, kept_mask)


def block_tables(route_ids, prio_rank, experts, capacity):
    blocks, tok_count = prio_rank.shape
    flat_slot, slot_pair, slot_token, kept_mask = jax.vmap(
        lambda r, p: slot_tables(r, p, experts, capacity)
    )(route_ids, prio_rank)
    block_ids = jnp.arange(blocks, dtype=jnp.int32)
    send_index = (block_ids[:, None] * (tok_count + 1) + slot_token).reshape(
        blocks, experts, capacity
    ).transpose(1, 0, 2)
    pair_index = (block_ids[:, None] * (2 * tok_count + 1) + slot_pair).reshape(
        blocks, experts, capacity
    ).transpose(1, 0, 2)
    slot_e = flat_slot // capacity
    slot_c = flat_slot % capacity
    back_index = jnp.where(
        kept_mask,
        (slot_e * blocks + block_ids[:, None]) * capacity + slot_c,
        experts * blocks * capacity,
    )
    return send_index, pair_index, back_index, kept_mask


def forward_layer(residual, route_hot, tables, weights, experts, capacity):
    norm_gains, norm_shifts, qkv_w, proj_w, router_w, in_w, out_w = weights
    send_index, pair_index, back_index, kept_mask = tables
    tok_count = residual.shape[0]
    blocks = back_index.shape[0]
    tok_block = tok_count // blocks
    seq_count = tok_count // SEQ
    score_scale = HEAD ** (-0.5)
    norm_scale = norm_gains.astype(jnp.float32)
    norm_shift = norm_shifts.astype(jnp.float32)
    normed = layer_norm(residual, norm_scale[0], norm_shift[0]).astype(jnp.bfloat16)
    qkv_rows = jnp.dot(normed, qkv_w, preferred_element_type=jnp.float32).astype(jnp.bfloat16)
    heads = qkv_rows.reshape(seq_count, SEQ, 3, HEADS, HEAD)
    scores = (
        jnp.einsum(
            "sqhd,skhd->shqk", heads[:, :, 0], heads[:, :, 1], preferred_element_type=jnp.float32
        )
        * score_scale
    )
    row_top = jnp.max(scores, axis=-1, keepdims=True)
    scores_exp = jnp.exp(scores - row_top)
    row_total = jnp.sum(scores_exp, axis=-1, keepdims=True)
    soft_scores = scores_exp / row_total
    log_total = row_top + jnp.log(row_total)
    mixed_heads = jnp.einsum(
        "shqk,skhd->sqhd",
        soft_scores.astype(jnp.bfloat16),
        heads[:, :, 2],
        preferred_element_type=jnp.float32,
    )
    mixed_heads = mixed_heads.astype(jnp.bfloat16).reshape(tok_count, D)
    middle = residual + jnp.dot(mixed_heads, proj_w, preferred_element_type=jnp.float32)
    normed_two = layer_norm(middle, norm_scale[1], norm_shift[1]).astype(jnp.bfloat16)
    gate_probs = jax.nn.softmax(
        jnp.dot(normed_two, router_w, preferred_element_type=jnp.float32), axis=-1
    )
    padded = jnp.concatenate(
        [normed_two.reshape(blocks, tok_block, D), jnp.zeros((blocks, 1, D), jnp.bfloat16)],
        axis=1,
    ).reshape(blocks * (tok_block + 1), D)
    sending = padded[send_index]
    received = lax.all_to_all(sending, "expert", split_axis=0, concat_axis=0, tiled=True)
    row_block = received.reshape(experts * blocks * capacity, D)
    hidden_pre = jnp.dot(row_block, in_w[0], preferred_element_type=jnp.float32)
    hidden_act = gelu_tanh(hidden_pre).astype(jnp.bfloat16)
    expert_rows = jnp.dot(hidden_act, out_w[0], preferred_element_type=jnp.float32).astype(
        jnp.bfloat16
    )
    returned = lax.all_to_all(
        expert_rows.reshape(experts, blocks, capacity, D),
        "expert",
        split_axis=0,
        concat_axis=0,
        tiled=True,
    )
    back_rows = jnp.concatenate(
        [returned.reshape(experts * blocks * capacity, D), jnp.zeros((1, D), jnp.bfloat16)]
    )
    pair_rows = (
        back_rows[back_index].astype(jnp.float32).reshape(blocks, TOP, tok_block, D)
    )
    probs_block = gate_probs.reshape(blocks, tok_block, experts)
    chosen = jnp.sum(route_hot * probs_block[:, :, None, :], axis=-1)
    kept_gate = kept_mask.astype(jnp.float32).reshape(blocks, TOP, tok_block)
    weight_pair = kept_gate * chosen.transpose(0, 2, 1)
    combined = jnp.sum(weight_pair[..., None] * pair_rows, axis=1)
    output = middle + combined.reshape(tok_count, D)
    saved_state = (
        residual,
        normed,
        heads,
        log_total,
        mixed_heads,
        middle,
        normed_two,
        gate_probs,
        kept_gate,
        weight_pair,
        pair_rows,
        row_block,
        hidden_pre,
    )
    return (output, saved_state)


def backward_layer(d_output, saved_state, route_hot, tables, weights, experts, capacity):
    (
        residual,
        normed,
        heads,
        log_total,
        mixed_heads,
        middle,
        normed_two,
        gate_probs,
        kept_gate,
        weight_pair,
        pair_rows,
        row_block,
        hidden_pre,
    ) = saved_state
    send_index, pair_index, back_index, kept_mask = tables
    norm_gains, norm_shifts, qkv_w, proj_w, router_w, in_w, out_w = weights
    tok_count = residual.shape[0]
    blocks = back_index.shape[0]
    tok_block = tok_count // blocks
    seq_count = tok_count // SEQ
    score_scale = HEAD ** (-0.5)
    norm_scale = norm_gains.astype(jnp.float32)
    norm_shift = norm_shifts.astype(jnp.float32)
    d_block = d_output.reshape(blocks, 1, tok_block, D)
    d_gate_pair = kept_gate * jnp.sum(d_block * pair_rows, axis=-1)
    d_gates = jnp.sum(route_hot * d_gate_pair.transpose(0, 2, 1)[..., None], axis=2)
    d_gates = d_gates.reshape(tok_count, experts)
    d_logits = (
        gate_probs * (d_gates - jnp.sum(gate_probs * d_gates, axis=-1, keepdims=True))
    ).astype(jnp.bfloat16)
    g_router = dot_first(normed_two, d_logits)
    d_normed_two = dot_last(d_logits, router_w)
    d_pairs = (weight_pair[..., None] * d_block).astype(jnp.bfloat16).reshape(
        blocks, TOP * tok_block, D
    )
    d_pairs = jnp.concatenate(
        [d_pairs, jnp.zeros((blocks, 1, D), jnp.bfloat16)], axis=1
    ).reshape(blocks * (TOP * tok_block + 1), D)
    d_slots = d_pairs[pair_index]
    d_expert_out = lax.all_to_all(d_slots, "expert", split_axis=0, concat_axis=0, tiled=True)
    flat_out = d_expert_out.reshape(experts * blocks * capacity, D)
    hidden_act = gelu_tanh(hidden_pre).astype(jnp.bfloat16)
    g_out = dot_first(hidden_act, flat_out)
    d_act = dot_last(flat_out, out_w[0])
    d_pre = jax.vjp(gelu_tanh, hidden_pre)[1](d_act)[0].astype(jnp.bfloat16)
    g_in = dot_first(row_block, d_pre)
    d_rows = dot_last(d_pre, in_w[0]).astype(jnp.bfloat16).reshape(experts, blocks, capacity, D)
    d_back = lax.all_to_all(d_rows, "expert", split_axis=0, concat_axis=0, tiled=True)
    d_pair_in = jnp.concatenate(
        [d_back.reshape(experts * blocks * capacity, D), jnp.zeros((1, D), jnp.bfloat16)]
    )[back_index]
    d_pair_in = d_pair_in.astype(jnp.float32).reshape(blocks, TOP, tok_block, D)
    d_normed_two = d_normed_two + jnp.sum(d_pair_in, axis=1).reshape(tok_count, D)
    pulled_two = jax.vjp(layer_norm, middle, norm_scale[1], norm_shift[1])[1](d_normed_two)
    d_middle = d_output + pulled_two[0]
    d_branch = d_middle.astype(jnp.bfloat16)
    g_proj = dot_first(mixed_heads, d_branch)
    d_mixed = dot_last(d_branch, proj_w).astype(jnp.bfloat16).reshape(seq_count, SEQ, HEADS, HEAD)
    query_heads = heads[:, :, 0]
    key_heads = heads[:, :, 1]
    value_heads = heads[:, :, 2]
    scores = (
        jnp.einsum("sqhd,skhd->shqk", query_heads, key_heads, preferred_element_type=jnp.float32)
        * score_scale
    )
    soft_scores = jnp.exp(scores - log_total)
    d_soft = jnp.einsum("sqhd,skhd->shqk", d_mixed, value_heads, preferred_element_type=jnp.float32)
    d_values = jnp.einsum(
        "shqk,sqhd->skhd",
        soft_scores.astype(jnp.bfloat16),
        d_mixed,
        preferred_element_type=jnp.float32,
    )
    d_scores = (
        soft_scores * (d_soft - jnp.sum(soft_scores * d_soft, axis=-1, keepdims=True))
    ).astype(jnp.bfloat16)
    d_query = (
        jnp.einsum("shqk,skhd->sqhd", d_scores, key_heads, preferred_element_type=jnp.float32)
        * score_scale
    )
    d_keys = (
        jnp.einsum("shqk,sqhd->skhd", d_scores, query_heads, preferred_element_type=jnp.float32)
        * score_scale
    )
    d_qkv = (
        jnp.stack([d_query, d_keys, d_values], axis=2)
        .reshape(tok_count, 3 * D)
        .astype(jnp.bfloat16)
    )
    g_qkv = dot_first(normed, d_qkv)
    d_normed = dot_last(d_qkv, qkv_w)
    pulled_one = jax.vjp(layer_norm, residual, norm_scale[0], norm_shift[0])[1](d_normed)
    d_residual = d_middle + pulled_one[0]
    g_gain = jnp.stack([pulled_one[1], pulled_two[1]])
    g_shift = jnp.stack([pulled_one[2], pulled_two[2]])
    return (d_residual, (g_gain, g_shift, g_qkv, g_proj, g_router, g_in[None], g_out[None]))


SCATTER_DIMS = (1, 1, 0, 0, 0, 1, 1)


def reduce_layer(layer_grads):
    scattered = [
        lax.psum_scatter(
            grad.astype(jnp.bfloat16), "shard", scatter_dimension=dim, tiled=True
        ).astype(jnp.float32)
        for grad, dim in zip(layer_grads, SCATTER_DIMS)
    ]
    replicated = [
        lax.psum(part.astype(jnp.bfloat16), "expert").astype(jnp.float32)
        for part in scattered[:5]
    ]
    return replicated + scattered[5:]


def local(
    tokens,
    routes,
    priority,
    norm_gain,
    norm_bias,
    w_qkv,
    w_proj,
    w_router,
    exp_in,
    exp_out,
    cotangent,
):
    experts = lax.axis_size("expert") * EXP_DEV
    capacity = max(8, (5 * TOK_MB // (2 * experts) + 7) // 8 * 8)
    tok_count = tokens.shape[0]
    blocks = tok_count // TOK_MB
    route_ids = routes.reshape(blocks, TOK_MB, TOP)
    prio_rank = priority.reshape(blocks, TOK_MB)
    tables = block_tables(route_ids, prio_rank, experts, capacity)
    route_hot = (
        route_ids[..., None] == jnp.arange(experts, dtype=jnp.int32)
    ).astype(jnp.float32)
    all_weights = []
    for layer_index in range(LAYERS):
        all_weights.append(
            (
                lax.all_gather(norm_gain[layer_index], "shard", axis=1, tiled=True),
                lax.all_gather(norm_bias[layer_index], "shard", axis=1, tiled=True),
                lax.all_gather(w_qkv[layer_index], "shard", axis=0, tiled=True),
                lax.all_gather(w_proj[layer_index], "shard", axis=0, tiled=True),
                lax.all_gather(w_router[layer_index], "shard", axis=0, tiled=True),
                lax.all_gather(exp_in[layer_index], "shard", axis=1, tiled=True),
                lax.all_gather(exp_out[layer_index], "shard", axis=1, tiled=True),
            )
        )
    residual = tokens
    saved_list = []
    for layer_index in range(LAYERS):
        residual, saved_state = forward_layer(
            residual, route_hot, tables, all_weights[layer_index], experts, capacity
        )
        saved_list.append(saved_state)
    activations = residual
    d_residual = cotangent
    reduced = [None] * LAYERS
    for layer_index in reversed(range(LAYERS)):
        d_residual, layer_grads = backward_layer(
            d_residual,
            saved_list[layer_index],
            route_hot,
            tables,
            all_weights[layer_index],
            experts,
            capacity,
        )
        reduced[layer_index] = reduce_layer(layer_grads)
    outs = [jnp.stack([reduced[l][k] for l in range(LAYERS)]) for k in range(7)]
    return (activations, d_residual, *outs)


def solution(mesh):
    return jax.shard_map(
        local,
        mesh=mesh,
        in_specs=(
            P(("expert", "shard"), None),
            P(("expert", "shard"), None),
            P(("expert", "shard")),
            P(None, None, "shard"),
            P(None, None, "shard"),
            P(None, "shard", None),
            P(None, "shard", None),
            P(None, "shard", None),
            P(None, "expert", "shard", None),
            P(None, "expert", "shard", None),
            P(("expert", "shard"), None),
        ),
        out_specs=(
            P(("expert", "shard"), None),
            P(("expert", "shard"), None),
            P(None, None, "shard"),
            P(None, None, "shard"),
            P(None, "shard", None),
            P(None, "shard", None),
            P(None, "shard", None),
            P(None, "expert", "shard", None),
            P(None, "expert", "shard", None),
        ),
        check_vma=False,
    )
```

time: 1050 us -> 1180 us (1.12)
  waiting for transfers between devices: 311 us -> 502 us
  blocking collectives: 69.1 us -> 123 us
  local copies, waits for them, and re-layouts: 258 us -> 218 us
  starting transfers between devices: 71.9 us -> 33.5 us
  matrix products: 229 us -> 207 us
    reduce_scatter x4 -> x8, waiting for transfers between devices: 67 us -> 147 us  [reduce_layer(): lax.psum_scatter(grad.astype(jnp.bfloat16), 'shard', scatter_dimension=di...]
    all_to_all x0 -> x1, blocking collectives: none -> 52.1 us  [backward_layer(): lax.all_to_all(d_slots, 'expert', split_axis=0, concat_axis=0, tiled=True)]
    all_to_all x4 -> x2, waiting for transfers between devices: 27.8 us -> 70.2 us  [backward_layer(): lax.all_to_all(d_rows, 'expert', split_axis=0, concat_axis=0, tiled=True)]
    all_to_all x4 -> x2, waiting for transfers between devices: 27.8 us -> 69.8 us  [forward_layer(): lax.all_to_all(sending, 'expert', split_axis=0, concat_axis=0, tiled=True)]
    unnamed x17 -> x27, waiting for transfers between devices: 19.5 us -> 42.1 us
    all_to_all x4 -> x1, waiting for transfers between devices: 45 us -> 22.4 us  [backward_layer(): lax.all_to_all(d_slots, 'expert', split_axis=0, concat_axis=0, tiled=True)]
    reduce_sum x2 -> x1, other arithmetic: 1.32 us -> 16.5 us  [slot_tables(): position = jnp.sum((same_expert & earlier).astype(jnp.int32), axis=1)]
    all_to_all x4 -> x2, waiting for transfers between devices: 45.3 us -> 60.4 us  [forward_layer(): lax.all_to_all(expert_rows.reshape(experts, blocks, capacity, D), 'expert...]
  transfers between devices with their start and end apart: 30 -> 28, of which waited for: 18 -> 17; matrix products, arithmetic and copies ran while one was open for 41% -> 25% of each run, Pallas kernels for 0% -> 0%
where the time goes in v1:
time: 1180 us; the launch traced here: 1170 us
  waiting for transfers between devices  502 us (43%)
  local copies, waits for them, and re-layouts  218 us (18%)
  matrix products  207 us (18%)
  blocking collectives  123 us (10%)
  other arithmetic  72.7 us (6%)
  starting transfers between devices  33.5 us (3%)
  between operations  16.4 us (1%)
    reduce_scatter x8, waiting for transfers between devices, reduce_layer(): lax.psum_scatter(grad.astype(jnp.bfloat16), 'shard', scatter_dimension=di...  147 us
    psum x1, waiting for transfers between devices, reduce_layer(): lax.psum(part.astype(jnp.bfloat16), 'expert').astype(jnp.float32)  79.6 us
    all_to_all x2, waiting for transfers between devices, backward_layer(): lax.all_to_all(d_rows, 'expert', split_axis=0, concat_axis=0, tiled=True)  70.2 us
    all_to_all x2, waiting for transfers between devices, forward_layer(): lax.all_to_all(sending, 'expert', split_axis=0, concat_axis=0, tiled=True)  69.8 us
    all_to_all x2, waiting for transfers between devices, forward_layer(): lax.all_to_all(expert_rows.reshape(experts, blocks, capacity, D), 'expert...  60.4 us
    dot_general x10, matrix products, dot_last(): lax.dot_general(left, right, (((1,), (1,)), ((), ())), preferred_element_...  58.6 us
    dot_general x10, matrix products, dot_first(): lax.dot_general(left, right, (((0,), (0,)), ((), ())), preferred_element_...  57.7 us
    all_to_all x1, blocking collectives, backward_layer(): lax.all_to_all(d_slots, 'expert', split_axis=0, concat_axis=0, tiled=True)  52.1 us
  transfers between devices with their start and end apart: 28, of which 17 were waited for; matrix products, arithmetic and copies ran while one was open for 25% of the time, Pallas kernels for 0%

profile of v1, /device:TPU:0, one launch (start us, length us, event | category | flops | bytes accessed | tf_op | source)
XLA Modules:
  0.0 1172.1 jit_solution(14263850944963940253)
XLA Ops:
  24.2 16.5 %fusion.16 = s32[2,788]{0,1:T(8,128)S(1)} fusion(s32[2,788]{0,1:T(8,128)S(1)} %copy.267, s32[2,788]{1,0:T(2,128)S(1)} %get-tuple-element.105, s32[2,788]{1,0:T(2,128)S(1)} %get-tuple-element.104, s32[2,788]{0,1:T(8,128)S(1)} %copy.266), kind=kLoop, calls=%fused_computation.42 | loop fusion | flops 6207864 | bytes 31520 | tf_op jit(solution)/shard_map/vmap()/reduce_sum | solution.py:49
  98.3 9.2 gather_fusion
  115.2 47.3 %all-to-all-done = bf16[8,2,128,512]{3,2,1,0:T(8,128)(2,1)} async-done(((bf16[8,2,128,512]{3,2,1,0:T(8,128)(2,1)}), bf16[8,2,128,512]{3,2,1,0:T(8,128)(2,1)}, u32[]{:S(2)}, u32[]{:S(2)}) %all-to-all-start) | async-done | bytes 2097184 | tf_op jit(solution)/shard_map/all_to_all | solution.py:124
  162.5 14.2 %multiply_convert_fusion.1 = (bf16[2048,2048]{1,0:T(8,128)(2,1)}, f32[2048,2048]{1,0:T(8,128)}) fusion(bf16[2048,512]{1,0:T(8,128)(2,1)} %bitcast.20, bf16[1,1,512,2048]{3,2,1,0:T(8,128)(2,1)} %all-gather.23.cloned.1.call-done), kind=kOutput, calls=%fused_computation.28 | convolution fusion | flops 4332716032 | bytes 29360128 | tf_op jit(solution)/shard_map/dot_general | solution.py:126
  176.7 9.8 convolution_convert_fusion.11
  218.4 20.5 %all-to-all-done.1 = bf16[8,2,128,512]{3,2,1,0:T(8,128)(2,1)} async-done(((bf16[8,2,128,512]{3,2,1,0:T(8,128)(2,1)}), bf16[8,2,128,512]{3,2,1,0:T(8,128)(2,1)}, u32[]{:S(2)}, u32[]{:S(2)}) %all-to-all-start.1) | async-done | bytes 2097184 | tf_op jit(solution)/shard_map/all_to_all | solution.py:131
  293.5 9.2 gather_fusion.2
  332.4 22.5 %all-to-all-done.2 = bf16[8,2,128,512]{3,2,1,0:T(8,128)(2,1)} async-done(((bf16[8,2,128,512]{3,2,1,0:T(8,128)(2,1)}), bf16[8,2,128,512]{3,2,1,0:T(8,128)(2,1)}, u32[]{:S(2)}, u32[]{:S(2)}) %all-to-all-start.2) | async-done | bytes 2097184 | tf_op jit(solution)/shard_map/all_to_all | solution.py:124
  359.1 14.7 %multiply_convert_fusion = (bf16[2048,2048]{1,0:T(8,128)(2,1)}, f32[2048,2048]{1,0:T(8,128)}) fusion(bf16[2048,512]{1,0:T(8,128)(2,1)} %bitcast.38, bf16[1,1,512,2048]{3,2,1,0:T(8,128)(2,1)} %all-gather.29.cloned.1.call-done), kind=kOutput, calls=%fused_computation.27 | convolution fusion | flops 4332716032 | bytes 29360128 | tf_op jit(solution)/shard_map/dot_general | solution.py:126
  373.8 10.8 all-gather.31.cloned.1.call-done
  384.6 22.4 %all-to-all-done.4 = bf16[8,2,128,512]{3,2,1,0:T(8,128)(2,1)S(1)} async-done(((bf16[8,2,128,512]{3,2,1,0:T(8,128)(2,1)}), bf16[8,2,128,512]{3,2,1,0:T(8,128)(2,1)S(1)}, u32[]{:S(2)}, u32[]{:S(2)}) %all-to-all-start.4) | async-done | bytes 2097184 | tf_op jit(solution)/shard_map/all_to_all | solution.py:209
  407.0 17.1 %fusion.13 = bf16[2048,2048]{1,0:T(8,128)(2,1)S(1)} fusion(f32[2048,2048]{1,0:T(8,128)} %get-tuple-element.95, bf16[2048,512]{1,0:T(8,128)(2,1)S(1)} %bitcast.301, bf16[1,1,2048,512]{3,2,1,0:T(8,128)(2,1)} %all-gather.31.cloned.1.call-done), kind=kOutput, calls=%fused_computation.26 | convolution fusion | flops 4378853376 | bytes 29360128 | tf_op jit(solution)/shard_map/dot_general | solution.py:38
  433.8 9.8 convolution_convert_fusion.10
  443.6 38.6 %all-to-all-done.5 = bf16[8,2,128,512]{3,2,1,0:T(8,128)(2,1)S(1)} async-done(((bf16[8,2,128,512]{3,2,1,0:T(8,128)(2,1)}), bf16[8,2,128,512]{3,2,1,0:T(8,128)(2,1)S(1)}, u32[]{:S(2)}, u32[]{:S(2)}) %all-to-all-start.5) | async-done | bytes 2097184 | tf_op jit(solution)/shard_map/all_to_all | solution.py:217
  496.0 39.9 %all-to-all-done.3 = bf16[8,2,128,512]{3,2,1,0:T(8,128)(2,1)} async-done(((bf16[8,2,128,512]{3,2,1,0:T(8,128)(2,1)}), bf16[8,2,128,512]{3,2,1,0:T(8,128)(2,1)}, u32[]{:S(2)}, u32[]{:S(2)}) %all-to-all-start.3) | async-done | bytes 2097184 | tf_op jit(solution)/shard_map/all_to_all | solution.py:131
  608.7 9.2 gather_fusion.6
  617.9 52.1 %all_to_all.40 = bf16[8,2,128,512]{3,2,1,0:T(8,128)(2,1)S(1)} all-to-all(bf16[8,2,128,512]{3,2,1,0:T(8,128)(2,1)} %bitcast.299), channel_id=1, replica_groups=mesh['expert'=8,'shard'=4] {'expert'}, dimensions={0} | all-to-all | bytes 4194304 | tf_op jit(solution)/shard_map/all_to_all | solution.py:209
  670.0 17.5 %fusion.6 = bf16[2048,2048]{1,0:T(8,128)(2,1)S(1)} fusion(f32[2048,2048]{1,0:T(8,128)} %get-tuple-element.85, bf16[2048,512]{1,0:T(8,128)(2,1)S(1)} %bitcast.303, bf16[1,1,2048,512]{3,2,1,0:T(8,128)(2,1)S(1)} %copy-done.103), kind=kOutput, calls=%fused_computation.19 | convolution fusion | flops 4378853376 | bytes 29360128 | tf_op jit(solution)/shard_map/dot_general | solution.py:38
  713.9 31.6 %all-to-all-done.7 = bf16[8,2,128,512]{3,2,1,0:T(8,128)(2,1)} async-done(((bf16[8,2,128,512]{3,2,1,0:T(8,128)(2,1)}), bf16[8,2,128,512]{3,2,1,0:T(8,128)(2,1)}, u32[]{:S(2)}, u32[]{:S(2)}) %all-to-all-start.7) | async-done | bytes 2097184 | tf_op jit(solution)/shard_map/all_to_all | solution.py:217
  814.1 9.9 fusion.32
  824.0 10.0 fusion.31
  834.3 9.9 fusion.30
  844.3 9.9 fusion.29
  868.6 30.5 %reduce-scatter.27.cloned.1.call-done = bf16[128,1536]{1,0:T(8,128)(2,1)} async-done(((bf16[512,1536]{1,0:T(8,128)(2,1)}), bf16[128,1536]{1,0:T(8,128)(2,1)}) %reduce-scatter.27.cloned.1.call-update) | async-done | bytes 393232 | tf_op jit(solution)/shard_map/reduce_scatter | solution.py:273
  902.0 19.1 %reduce-scatter.47.cloned.1.call-done = bf16[128,2]{1,0:T(8,128)(2,1)} async-done(((bf16[512,2]{1,0:T(8,128)(2,1)}), bf16[128,2]{1,0:T(8,128)(2,1)}) %reduce-scatter.47.cloned.1.call-update) | async-done | bytes 528
  921.9 21.1 %reduce-scatter.43.cloned.1.call-done = bf16[128,2]{1,0:T(8,128)(2,1)} async-done(((bf16[512,2]{1,0:T(8,128)(2,1)}), bf16[128,2]{1,0:T(8,128)(2,1)}) %reduce-scatter.43.cloned.1.call-update) | async-done | bytes 528
  943.8 21.6 %all-reduce.8 = (bf16[1,2,128]{2,1,0:T(2,128)(2,1)S(1)}, bf16[1,2,128]{2,1,0:T(2,128)(2,1)S(1)}, bf16[1,2,128]{2,1,0:T(2,128)(2,1)S(1)}, bf16[1,2,128]{2,1,0:T(2...) all-reduce(bf16[1,2,128]{2,1,0:T(2,128)(2,1)S(1)} %bitcast.346, ...), channel_id=1, replica_groups=mesh['expert'=8,'shard'=4] {'expert'}, use_global_device_ids=true, to_apply=%region_47.48 | all-reduce | flops 3072 | bytes 12288 | tf_op jit(solution)/shard_map/psum | solution.py:279
  967.2 10.0 reduce-scatter.41.cloned.1.call-done
  977.2 33.6 %reduce-scatter.39.cloned.1.call-done = bf16[1,512,512]{2,1,0:T(8,128)(2,1)} async-done(((bf16[1,2048,512]{2,1,0:T(8,128)(2,1)}), bf16[1,512,512]{2,1,0:T(8,128)(2,1)}) %reduce-scatter.39.cloned.1.call-update) | async-done | bytes 524304 | tf_op jit(solution)/shard_map/reduce_scatter | solution.py:273
  1013.4 31.7 %reduce-scatter.37.cloned.1.call-done = bf16[1,128,2048]{2,1,0:T(8,128)(2,1)} async-done(((bf16[1,512,2048]{2,1,0:T(8,128)(2,1)}), bf16[1,128,2048]{2,1,0:T(8,128)(2,1)}) %reduce-scatter.37.cloned.1.call-update) | async-done | bytes 524304 | tf_op jit(solution)/shard_map/reduce_scatter | solution.py:273
  1045.1 33.6 %reduce-scatter.35.cloned.1.call-done = bf16[1,128,2048]{2,1,0:T(8,128)(2,1)} async-done(((bf16[1,512,2048]{2,1,0:T(8,128)(2,1)}), bf16[1,128,2048]{2,1,0:T(8,128)(2,1)}) %reduce-scatter.35.cloned.1.call-update) | async-done | bytes 524304 | tf_op jit(solution)/shard_map/reduce_scatter | solution.py:273
  1081.3 79.6 %all-reduce.12.cloned.1.call-done = (bf16[1,128,1536]{2,1,0:T(8,128)(2,1)}, bf16[1,128,1536]{2,1,0:T(8,128)(2,1)}, bf16[1,128,512]{2,1,0:T(8,128)(2,1)}, bf16[1,128,512]{2,1,0:T(8,128)(2,1)}) async-done(((bf16[1,128,1536]{2,1,0:T(8,128)(2,1)}, bf16[1,128,1536]{2,1,0:T(8,128)(2,1)}, bf16[1,128,512]{2,1,0:T(8,128)(2,1)}, bf16[1,128,512]{2,1,0:T(8,128)(2,1)}), (bf16[1,128,1536]{2,1,0:T(8,128)(2,1)}, ...) | async-done | bytes 1048592 | tf_op jit(solution)/shard_map/psum | solution.py:279
  (533 shorter events, 422.3 us)
Async XLA Ops:
  7.2 53.7 %all-gather.21.cloned.1.call-start = ((), (), s32[]{:S(2)}) async-start(), calls=%async_computation.30 | async-start | bytes 1966080 | tf_op jit(solution)/shard_map/all_gather | solution.py:314
  9.5 105.7 %all-gather.23.cloned.1.call-start = ((), (), s32[]{:S(2)}) async-start(), calls=%async_computation.31 | async-start | bytes 2621440 | tf_op jit(solution)/shard_map/all_gather | solution.py:317
  22.1 74.7 %copy-start.81 = (f32[1,1,512]{2,1,0:T(1,128)}, f32[1,1,512]{2,1,0:T(1,128)S(1)}, u32[]{:S(2)}) copy-start(f32[1,1,512]{2,1,0:T(1,128)S(1)} %get-tuple-element.72) | copy-start | bytes 6148
  97.9 118.8 %copy-start.24 = (bf16[788,512]{1,0:T(8,128)(2,1)}, bf16[788,512]{1,0:T(8,128)(2,1)S(1)}, u32[]{:S(2)}) copy-start(bf16[788,512]{1,0:T(8,128)(2,1)S(1)} %add_convert_fusion.2) | copy-start | bytes 2420740
  107.5 54.9 %all-to-all-start = ((bf16[8,2,128,512]{3,2,1,0:T(8,128)(2,1)}), bf16[8,2,128,512]{3,2,1,0:T(8,128)(2,1)}, u32[]{:S(2)}, u32[]{:S(2)}) async-start(bf16[8,2,128,512]{3,2,1,0:T(8,128)(2,1)} %bitcast.298), calls=%async_computation | async-start | bytes 4194304 | tf_op jit(solution)/shard_map/all_to_all | solution.py:124
  113.6 63.0 %all-gather.25.cloned.1.call-start = ((), (), s32[]{:S(2)}) async-start(), calls=%async_computation.32 | async-start | bytes 2621440 | tf_op jit(solution)/shard_map/all_gather | solution.py:318
  186.5 52.4 %all-to-all-start.1 = ((bf16[8,2,128,512]{3,2,1,0:T(8,128)(2,1)}), bf16[8,2,128,512]{3,2,1,0:T(8,128)(2,1)}, u32[]{:S(2)}, u32[]{:S(2)}) async-start(bf16[8,2,128,512]{3,2,1,0:T(8,128)(2,1)} %bitcast.306), calls=%async_computation.1 | async-start | bytes 4194304 | tf_op jit(solution)/shard_map/all_to_all | solution.py:131
  191.0 65.8 %all-gather.27.cloned.1.call-start = ((), (), s32[]{:S(2)}) async-start(), calls=%async_computation.33 | async-start | bytes 1966080 | tf_op jit(solution)/shard_map/all_gather | solution.py:314
  302.8 52.2 %all-to-all-start.2 = ((bf16[8,2,128,512]{3,2,1,0:T(8,128)(2,1)}), bf16[8,2,128,512]{3,2,1,0:T(8,128)(2,1)}, u32[]{:S(2)}, u32[]{:S(2)}) async-start(bf16[8,2,128,512]{3,2,1,0:T(8,128)(2,1)} %bitcast.296), calls=%async_computation.2 | async-start | bytes 4194304 | tf_op jit(solution)/shard_map/all_to_all | solution.py:124
  307.1 52.0 %all-gather.29.cloned.1.call-start = ((), (), s32[]{:S(2)}) async-start(), calls=%async_computation.34 | async-start | bytes 2621440 | tf_op jit(solution)/shard_map/all_gather | solution.py:317
  354.9 52.0 %all-to-all-start.4 = ((bf16[8,2,128,512]{3,2,1,0:T(8,128)(2,1)}), bf16[8,2,128,512]{3,2,1,0:T(8,128)(2,1)S(1)}, u32[]{:S(2)}, u32[]{:S(2)}) async-start(bf16[8,2,128,512]{3,2,1,0:T(8,128)(2,1)} %bitcast.297), calls=%async_computation.4 | async-start | bytes 4194304 | tf_op jit(solution)/shard_map/all_to_all | solution.py:209
  358.5 26.1 %all-gather.31.cloned.1.call-start = ((), (), s32[]{:S(2)}) async-start(), calls=%async_computation.35 | async-start | bytes 2621440 | tf_op jit(solution)/shard_map/all_gather | solution.py:318
  430.2 52.1 %all-to-all-start.5 = ((bf16[8,2,128,512]{3,2,1,0:T(8,128)(2,1)}), bf16[8,2,128,512]{3,2,1,0:T(8,128)(2,1)S(1)}, u32[]{:S(2)}, u32[]{:S(2)}) async-start(bf16[8,2,128,512]{3,2,1,0:T(8,128)(2,1)} %bitcast.308), calls=%async_computation.5 | async-start | bytes 4194304 | tf_op jit(solution)/shard_map/all_to_all | solution.py:217
  483.6 52.3 %all-to-all-start.3 = ((bf16[8,2,128,512]{3,2,1,0:T(8,128)(2,1)}), bf16[8,2,128,512]{3,2,1,0:T(8,128)(2,1)}, u32[]{:S(2)}, u32[]{:S(2)}) async-start(bf16[8,2,128,512]{3,2,1,0:T(8,128)(2,1)} %bitcast.307), calls=%async_computation.3 | async-start | bytes 4194304 | tf_op jit(solution)/shard_map/all_to_all | solution.py:131
  617.9 52.1 %copy-start.103 = (bf16[1,1,2048,512]{3,2,1,0:T(8,128)(2,1)S(1)}, bf16[1,1,2048,512]{3,2,1,0:T(8,128)(2,1)}, u32[]{:S(2)}) copy-start(bf16[1,1,2048,512]{3,2,1,0:T(8,128)(2,1)} %all-gather.25.cloned.1.call-done) | copy-start | bytes 6291460
  693.6 51.9 %all-to-all-start.7 = ((bf16[8,2,128,512]{3,2,1,0:T(8,128)(2,1)}), bf16[8,2,128,512]{3,2,1,0:T(8,128)(2,1)}, u32[]{:S(2)}, u32[]{:S(2)}) async-start(bf16[8,2,128,512]{3,2,1,0:T(8,128)(2,1)} %bitcast.305), calls=%async_computation.7 | async-start | bytes 4194304 | tf_op jit(solution)/shard_map/all_to_all | solution.py:217
  698.2 156.1 %reduce-scatter.49.cloned.1.call-start = ((), (), s32[]{:S(2)}) async-start(), calls=%async_computation.39 | async-start | bytes 163840
  699.2 156.0 %reduce-scatter.45.cloned.1.call-start = ((), (), s32[]{:S(2)}) async-start(), calls=%async_computation.37 | async-start | bytes 163840
  700.1 155.9 %reduce-scatter.53.cloned.1.call-start = ((), (), s32[]{:S(2)}) async-start(), calls=%async_computation.41 | async-start | bytes 163840
  703.3 153.6 %reduce-scatter.51.cloned.1.call-start = ((), (), s32[]{:S(2)}) async-start(), calls=%async_computation.40 | async-start | bytes 163840
  705.8 155.2 %reduce-scatter.33.cloned.1.call-start = ((), (), s32[]{:S(2)}) async-start(), calls=%async_computation.25 | async-start | bytes 655360 | tf_op jit(solution)/shard_map/reduce_scatter | solution.py:273
  708.6 152.4 %reduce-scatter.29.cloned.1.call-start = ((), (), s32[]{:S(2)}) async-start(), calls=%async_computation.23 | async-start | bytes 1966080 | tf_op jit(solution)/shard_map/reduce_scatter | solution.py:273
  713.9 154.7 %reduce-scatter.31.cloned.1.call-start = ((), (), s32[]{:S(2)}) async-start(), calls=%async_computation.24 | async-start | bytes 655360 | tf_op jit(solution)/shard_map/reduce_scatter | solution.py:273
  780.3 118.8 %reduce-scatter.27.cloned.1.call-start = ((), (), s32[]{:S(2)}) async-start(), calls=%async_computation.22 | async-start | bytes 1966080 | tf_op jit(solution)/shard_map/reduce_scatter | solution.py:273
  806.9 114.2 %reduce-scatter.47.cloned.1.call-start = ((), (), s32[]{:S(2)}) async-start(), calls=%async_computation.38 | async-start | bytes 163840
  812.8 130.2 %reduce-scatter.43.cloned.1.call-start = ((), (), s32[]{:S(2)}) async-start(), calls=%async_computation.36 | async-start | bytes 163840
  813.7 163.5 %reduce-scatter.41.cloned.1.call-start = ((), (), s32[]{:S(2)}) async-start(), calls=%async_computation.29 | async-start | bytes 2621440 | tf_op jit(solution)/shard_map/reduce_scatter | solution.py:273
  824.0 186.8 %reduce-scatter.39.cloned.1.call-start = ((), (), s32[]{:S(2)}) async-start(), calls=%async_computation.28 | async-start | bytes 2621440 | tf_op jit(solution)/shard_map/reduce_scatter | solution.py:273
  834.1 211.0 %reduce-scatter.37.cloned.1.call-start = ((), (), s32[]{:S(2)}) async-start(), calls=%async_computation.27 | async-start | bytes 2621440 | tf_op jit(solution)/shard_map/reduce_scatter | solution.py:273
  844.3 234.4 %reduce-scatter.35.cloned.1.call-start = ((), (), s32[]{:S(2)}) async-start(), calls=%async_computation.26 | async-start | bytes 2621440 | tf_op jit(solution)/shard_map/reduce_scatter | solution.py:273
  854.3 306.6 %all-reduce.12.cloned.1.call-start = ((), (), s32[]{:S(2)}) async-start(), calls=%async_computation.42 | async-start | bytes 2097152 | tf_op jit(solution)/shard_map/psum | solution.py:279
  857.7 41.4 %copy-start.15 = (f32[788,512]{1,0:T(8,128)S(1)}, f32[788,512]{1,0:T(8,128)}, u32[]{:S(2)}) copy-start(f32[788,512]{1,0:T(8,128)} %copy-done.14) | copy-start | bytes 4841476
  (109 other events, 837.4 us)
Sparse Core Ops, SparseCore 0:
  10.2 22.3 all-gather.20
  34.7 22.5 all-gather.22
  116.6 23.9 all-gather.24
  193.0 22.2 all-gather.26
  309.7 23.8 all-gather.28
  360.6 23.9 all-gather.30
  701.5 20.9 reduce-scatter.48
  724.9 19.6 reduce-scatter.44
  747.0 19.6 reduce-scatter.52
  768.9 19.6 reduce-scatter.50
  791.7 21.6 reduce-scatter.32
  816.4 28.0 reduce-scatter.28
  847.0 21.6 reduce-scatter.30
  871.0 28.0 reduce-scatter.26
  901.4 19.6 reduce-scatter.46
  923.3 19.6 reduce-scatter.42
  945.9 31.1 reduce-scatter.40
  979.6 31.1 reduce-scatter.38
  1013.9 31.1 reduce-scatter.36
  1047.5 31.1 reduce-scatter.34
  1082.5 78.3 all-reduce.11

commit v2 on v1

--- a/solution.py
+++ b/solution.py
@@ -265,21 +265,57 @@
     return (d_residual, (g_gain, g_shift, g_qkv, g_proj, g_router, g_in[None], g_out[None]))
 
 
-SCATTER_DIMS = (1, 1, 0, 0, 0, 1, 1)
+def halving_scatter(grad, axis_name):
+    size = lax.axis_size(axis_name)
+    me = lax.axis_index(axis_name)
+    chunk = grad.shape[0] // size
+    rest = grad.shape[1:]
+    total = grad.astype(jnp.float32).reshape(size, chunk, *rest)
+    bit = 1
+    while bit < size:
+        pairs = total.reshape(total.shape[0] // 2, 2, chunk, *rest)
+        mine = (me // bit) % 2
+        keep = lax.dynamic_index_in_dim(pairs, mine, axis=1, keepdims=False)
+        give = lax.dynamic_index_in_dim(pairs, 1 - mine, axis=1, keepdims=False)
+        got = lax.ppermute(
+            give.astype(jnp.bfloat16), axis_name, [(i, i ^ bit) for i in range(size)]
+        )
+        total = keep + got.astype(jnp.float32)
+        bit *= 2
+    return total.reshape(chunk, *rest)
+
+
+def doubling_sum(part, axis_name):
+    size = lax.axis_size(axis_name)
+    total = part.astype(jnp.float32)
+    bit = 1
+    while bit < size:
+        own = lax.reduce_precision(total, exponent_bits=8, mantissa_bits=7)
+        got = lax.ppermute(
+            own.astype(jnp.bfloat16), axis_name, [(i, i ^ bit) for i in range(size)]
+        )
+        total = own + got.astype(jnp.float32)
+        bit *= 2
+    return total
 
 
 def reduce_layer(layer_grads):
-    scattered = [
-        lax.psum_scatter(
-            grad.astype(jnp.bfloat16), "shard", scatter_dimension=dim, tiled=True
-        ).astype(jnp.float32)
-        for grad, dim in zip(layer_grads, SCATTER_DIMS)
+    g_gain, g_shift, g_qkv, g_proj, g_router, g_in, g_out = layer_grads
+    qkv_cols = g_qkv.shape[1]
+    proj_cols = g_proj.shape[1]
+    small = jnp.concatenate([g_gain.T, g_shift.T, g_router], axis=1)
+    shared = jnp.concatenate([g_qkv, g_proj, small], axis=1)
+    shared = doubling_sum(halving_scatter(shared, "shard"), "expert")
+    tail = shared[:, qkv_cols + proj_cols :]
+    return [
+        tail[:, 0:2].T,
+        tail[:, 2:4].T,
+        shared[:, :qkv_cols],
+        shared[:, qkv_cols : qkv_cols + proj_cols],
+        tail[:, 4:],
+        halving_scatter(g_in[0], "shard")[None],
+        halving_scatter(g_out[0], "shard")[None],
     ]
-    replicated = [
-        lax.psum(part.astype(jnp.bfloat16), "expert").astype(jnp.float32)
-        for part in scattered[:5]
-    ]
-    return replicated + scattered[5:]
 
 
 def local(
@@ -299,12 +335,16 @@
     capacity = max(8, (5 * TOK_MB // (2 * experts) + 7) // 8 * 8)
     tok_count = tokens.shape[0]
     blocks = tok_count // TOK_MB
-    route_ids = routes.reshape(blocks, TOK_MB, TOP)
-    prio_rank = priority.reshape(blocks, TOK_MB)
-    tables = block_tables(route_ids, prio_rank, experts, capacity)
-    route_hot = (
-        route_ids[..., None] == jnp.arange(experts, dtype=jnp.int32)
-    ).astype(jnp.float32)
+    streams = []
+    for block in range(blocks):
+        rows = slice(block * TOK_MB, (block + 1) * TOK_MB)
+        route_ids = routes[rows].reshape(1, TOK_MB, TOP)
+        prio_rank = priority[rows].reshape(1, TOK_MB)
+        tables = block_tables(route_ids, prio_rank, experts, capacity)
+        route_hot = (
+            route_ids[..., None] == jnp.arange(experts, dtype=jnp.int32)
+        ).astype(jnp.float32)
+        streams.append((rows, tables, route_hot))
     all_weights = []
     for layer_index in range(LAYERS):
         all_weights.append(
@@ -318,29 +358,36 @@
                 lax.all_gather(exp_out[layer_index], "shard", axis=1, tiled=True),
             )
         )
-    residual = tokens
-    saved_list = []
+    residuals = [tokens[rows] for rows, _, _ in streams]
+    saved = [[None] * LAYERS for _ in streams]
     for layer_index in range(LAYERS):
-        residual, saved_state = forward_layer(
-            residual, route_hot, tables, all_weights[layer_index], experts, capacity
-        )
-        saved_list.append(saved_state)
-    activations = residual
-    d_residual = cotangent
+        for block, (rows, tables, route_hot) in enumerate(streams):
+            residuals[block], saved[block][layer_index] = forward_layer(
+                residuals[block], route_hot, tables, all_weights[layer_index], experts, capacity
+            )
+    activations = jnp.concatenate(residuals, axis=0)
+    d_residuals = [cotangent[rows] for rows, _, _ in streams]
     reduced = [None] * LAYERS
     for layer_index in reversed(range(LAYERS)):
-        d_residual, layer_grads = backward_layer(
-            d_residual,
-            saved_list[layer_index],
-            route_hot,
-            tables,
-            all_weights[layer_index],
-            experts,
-            capacity,
-        )
-        reduced[layer_index] = reduce_layer(layer_grads)
+        layer_sum = None
+        for block, (rows, tables, route_hot) in enumerate(streams):
+            d_residuals[block], layer_grads = backward_layer(
+                d_residuals[block],
+                saved[block][layer_index],
+                route_hot,
+                tables,
+                all_weights[layer_index],
+                experts,
+                capacity,
+            )
+            if layer_sum is None:
+                layer_sum = layer_grads
+            else:
+                layer_sum = tuple(old + new for old, new in zip(layer_sum, layer_grads))
+        reduced[layer_index] = reduce_layer(layer_sum)
     outs = [jnp.stack([reduced[l][k] for l in range(LAYERS)]) for k in range(7)]
-    return (activations, d_residual, *outs)
+    d_tokens = jnp.concatenate(d_residuals, axis=0)
+    return (activations, d_tokens, *outs)
 
 
 def solution(mesh):

time: 1180 us -> 1040 us (0.88)
  waiting for transfers between devices: 502 us -> 184 us
  local copies, waits for them, and re-layouts: 218 us -> 301 us
  blocking collectives: 123 us -> 46.9 us
  starting transfers between devices: 33.5 us -> 96.6 us
  other arithmetic: 72.7 us -> 135 us
  matrix products: 207 us -> 244 us
    reduce_scatter x8 -> x0, waiting for transfers between devices: 147 us -> none  [reduce_layer(): lax.psum_scatter(grad.astype(jnp.bfloat16), 'shard', scatter_dimension=di...]
    ppermute x0 -> x18, waiting for transfers between devices: none -> 111 us  [the longest x6 88.9 us: doubling_sum(): lax.ppermute(own.astype(jnp.bfloat16), axis_name, [(i, i ^ bit) for i in...]
    psum x1 -> x0, waiting for transfers between devices: 79.6 us -> none  [reduce_layer(): lax.psum(part.astype(jnp.bfloat16), 'expert').astype(jnp.float32)]
    all_to_all x2 -> x4, waiting for transfers between devices: 70.2 us -> 0.3 us  [backward_layer(): lax.all_to_all(d_rows, 'expert', split_axis=0, concat_axis=0, tiled=True)]
    all_to_all x2 -> x4, waiting for transfers between devices: 69.8 us -> 11.5 us  [forward_layer(): lax.all_to_all(sending, 'expert', split_axis=0, concat_axis=0, tiled=True)]
    all_to_all x1 -> x0, blocking collectives: 52.1 us -> none  [backward_layer(): lax.all_to_all(d_slots, 'expert', split_axis=0, concat_axis=0, tiled=True)]
    unnamed x27 -> x6, waiting for transfers between devices: 42.1 us -> 1.63 us
    reduce_sum x1 -> x2, other arithmetic: 16.5 us -> 38.9 us  [slot_tables(): position = jnp.sum((same_expert & earlier).astype(jnp.int32), axis=1)]
  transfers between devices with their start and end apart: 28 -> 40, of which waited for: 17 -> 20; matrix products, arithmetic and copies ran while one was open for 25% -> 56% of each run, Pallas kernels for 0% -> 0%
where the time goes in v2:
time: 1040 us; the launch traced here: 1030 us
  local copies, waits for them, and re-layouts  301 us (29%)
  matrix products  244 us (23%)
  waiting for transfers between devices  184 us (18%)
  other arithmetic  135 us (13%)
  starting transfers between devices  96.6 us (9%)
  blocking collectives  46.9 us (5%)
  between operations  18.9 us (2%)
    ppermute x6, waiting for transfers between devices, doubling_sum(): lax.ppermute(own.astype(jnp.bfloat16), axis_name, [(i, i ^ bit) for i in...  88.9 us
    dot_general x20, matrix products, dot_first(): lax.dot_general(left, right, (((0,), (0,)), ((), ())), preferred_element_...  74.9 us
    dot_general x20, matrix products, dot_last(): lax.dot_general(left, right, (((1,), (1,)), ((), ())), preferred_element_...  70.3 us
    unnamed x677, local copies, waits for them, and re-layouts  48.3 us
    all_to_all x4, waiting for transfers between devices, forward_layer(): lax.all_to_all(expert_rows.reshape(experts, blocks, capacity, D), 'expert...  42 us
    reduce_sum x2, other arithmetic, slot_tables(): position = jnp.sum((same_expert & earlier).astype(jnp.int32), axis=1)  38.9 us
    dot_general x4, matrix products, forward_layer(): hidden_pre = jnp.dot(row_block, in_w[0], preferred_element_type=jnp.float32)  30.8 us
    ppermute x12, waiting for transfers between devices, halving_scatter(): lax.ppermute(give.astype(jnp.bfloat16), axis_name, [(i, i ^ bit) for i in...  22.3 us
  transfers between devices with their start and end apart: 40, of which 20 were waited for; matrix products, arithmetic and copies ran while one was open for 56% of the time, Pallas kernels for 0%

profile of v2, /device:TPU:0, one launch (start us, length us, event | category | flops | bytes accessed | tf_op | source)
XLA Modules:
  0.0 1026.4 jit_solution(2170580123527098327)
XLA Ops:
  29.9 7.4 all-gather.3
  37.7 19.5 %fusion.33 = s32[788]{0:T(1024)S(1)} fusion(s32[788]{0:T(1024)S(1)} %add_reduce_fusion.3, s32[788]{0:T(1024)S(1)} %add_reduce_fusion.2), kind=kLoop, calls=%fused_computation.95 | loop fusion | flops 3103932 | bytes 9456 | tf_op jit(solution)/shard_map/vmap()/reduce_sum | solution.py:49
  120.9 19.5 %fusion.32 = s32[788]{0:T(1024)S(1)} fusion(s32[788]{0:T(1024)S(1)} %copy-done.221, s32[788]{0:T(1024)S(1)} %copy-done.220), kind=kLoop, calls=%fused_computation.94 | loop fusion | flops 3103932 | bytes 9456 | tf_op jit(solution)/shard_map/vmap()/reduce_sum | solution.py:49
  158.2 7.6 all-gather.10
  176.6 7.6 fusion.74
  184.2 7.7 fusion.119
  198.5 8.9 multiply_convert_fusion.3
  212.7 11.6 %all-to-all-done.5 = bf16[8,1,128,512]{3,2,1,0:T(8,128)(2,1)} async-done(((bf16[8,1,128,512]{3,2,1,0:T(8,128)(2,1)}), bf16[8,1,128,512]{3,2,1,0:T(8,128)(2,1)}, u32[]{:S(2)}, u32[]{:S(2)}) %all-to-all-start.5) | async-done | bytes 1048608 | tf_op jit(solution)/shard_map/all_to_all | solution.py:131
  242.8 11.3 %all-to-all-done.1 = bf16[8,1,128,512]{3,2,1,0:T(8,128)(2,1)} async-done(((bf16[8,1,128,512]{3,2,1,0:T(8,128)(2,1)}), bf16[8,1,128,512]{3,2,1,0:T(8,128)(2,1)}, u32[]{:S(2)}, u32[]{:S(2)}) %all-to-all-start.1) | async-done | bytes 1048608 | tf_op jit(solution)/shard_map/all_to_all | solution.py:131
  345.9 9.9 multiply_convert_fusion.2
  355.9 6.2 fusion.128
  362.1 9.7 all-to-all-done.6
  390.8 10.8 %all-to-all-done.3 = bf16[8,1,128,512]{3,2,1,0:T(8,128)(2,1)} async-done(((bf16[8,1,128,512]{3,2,1,0:T(8,128)(2,1)}), bf16[8,1,128,512]{3,2,1,0:T(8,128)(2,1)}, u32[]{:S(2)}, u32[]{:S(2)}) %all-to-all-start.3) | async-done | bytes 1048608 | tf_op jit(solution)/shard_map/all_to_all | solution.py:131
  423.1 8.2 all-to-all-done.7
  454.3 6.8 all-to-all-done.8
  464.7 9.7 fusion.13
  495.6 8.7 convolution_add_fusion.2
  504.5 8.9 fusion.27
  524.8 6.4 all-to-all-start.13
  541.6 7.9 collective-permute-done.13
  682.4 6.4 all-to-all-start.14
  705.2 9.8 all-to-all-done.14
  715.0 9.2 convolution_add_fusion.3
  726.5 9.4 fusion.6
  739.5 8.8 fusion.20
  771.3 22.2 %collective-permute-done.8 = bf16[128,2060]{0,1:T(8,128)(2,1)S(1)} collective-permute-done((bf16[128,2060]{0,1:T(8,128)(2,1)S(1)}, bf16[128,2060]{0,1:T(8,128)(2,1)S(1)}, u32[]{:S(2)}, u32[]{:S(2)}) %collective-permute-start.8) | collective-permute-done | bytes 527392 | tf_op jit(solution)/shard_map/ppermute | solution.py:294
  809.7 23.4 %collective-permute-done.9 = bf16[128,2060]{0,1:T(8,128)(2,1)} collective-permute-done((bf16[128,2060]{0,1:T(8,128)(2,1)}, bf16[128,2060]{0,1:T(8,128)(2,1)}, u32[]{:S(2)}, u32[]{:S(2)}) %collective-permute-start.9) | collective-permute-done | bytes 527392 | tf_op jit(solution)/shard_map/ppermute | solution.py:294
  944.4 10.5 %collective-permute-done.1 = bf16[1,128,2060]{1,2,0:T(8,128)(2,1)S(1)} collective-permute-done((bf16[1,128,2060]{1,2,0:T(8,128)(2,1)S(1)}, bf16[1,128,2060]{1,2,0:T(8,128)(2,1)S(1)}, u32[]{:S(2)}, u32[]{:S(2)}) %collective-permute-start.1) | collective-permute-done | bytes 527392 | tf_op jit(solution)/shard_map/ppermute | solution.py:280
  954.9 8.4 fusion.185
  966.6 10.6 %collective-permute-done.2 = bf16[128,2060]{0,1:T(8,128)(2,1)S(1)} collective-permute-done((bf16[128,2060]{0,1:T(8,128)(2,1)S(1)}, bf16[128,2060]{0,1:T(8,128)(2,1)S(1)}, u32[]{:S(2)}, u32[]{:S(2)}) %collective-permute-start.2) | collective-permute-done | bytes 527392 | tf_op jit(solution)/shard_map/ppermute | solution.py:294
  978.3 11.7 %collective-permute-done.3 = bf16[128,2060]{0,1:T(8,128)(2,1)S(1)} collective-permute-done((bf16[128,2060]{0,1:T(8,128)(2,1)S(1)}, bf16[128,2060]{0,1:T(8,128)(2,1)S(1)}, u32[]{:S(2)}, u32[]{:S(2)}) %collective-permute-start.3) | collective-permute-done | bytes 527392 | tf_op jit(solution)/shard_map/ppermute | solution.py:294
  993.3 21.1 %collective-permute-done.4 = bf16[128,2060]{0,1:T(8,128)(2,1)S(1)} collective-permute-done((bf16[128,2060]{0,1:T(8,128)(2,1)S(1)}, bf16[128,2060]{0,1:T(8,128)(2,1)S(1)}, u32[]{:S(2)}, u32[]{:S(2)}) %collective-permute-start.4) | collective-permute-done | bytes 527392 | tf_op jit(solution)/shard_map/ppermute | solution.py:294
  (1139 shorter events, 661.7 us)
Async XLA Ops:
  7.2 58.6 %all-gather.21.cloned.1.call-start = ((), (), s32[]{:S(2)}) async-start(), calls=%async_computation.16 | async-start | bytes 1966080 | tf_op jit(solution)/shard_map/all_gather | solution.py:354
  9.4 167.2 %all-gather.23.cloned.1.call-start = ((), (), s32[]{:S(2)}) async-start(), calls=%async_computation.17 | async-start | bytes 2621440 | tf_op jit(solution)/shard_map/all_gather | solution.py:357
  11.9 172.3 %all-gather.25.cloned.1.call-start = ((), (), s32[]{:S(2)}) async-start(), calls=%async_computation.18 | async-start | bytes 2621440 | tf_op jit(solution)/shard_map/all_gather | solution.py:358
  13.0 252.9 %all-gather.27.cloned.1.call-start = ((), (), s32[]{:S(2)}) async-start(), calls=%async_computation.19 | async-start | bytes 1966080 | tf_op jit(solution)/shard_map/all_gather | solution.py:354
  13.6 332.3 %all-gather.29.cloned.1.call-start = ((), (), s32[]{:S(2)}) async-start(), calls=%async_computation.20 | async-start | bytes 2621440 | tf_op jit(solution)/shard_map/all_gather | solution.py:357
  14.2 341.7 %all-gather.31.cloned.1.call-start = ((), (), s32[]{:S(2)}) async-start(), calls=%async_computation.21 | async-start | bytes 2621440 | tf_op jit(solution)/shard_map/all_gather | solution.py:358
  114.9 37.3 %all-to-all-start.4 = ((bf16[8,1,128,512]{3,2,1,0:T(8,128)(2,1)}), bf16[8,1,128,512]{3,2,1,0:T(8,128)(2,1)}, u32[]{:S(2)}, u32[]{:S(2)}) async-start(bf16[8,1,128,512]{3,2,1,0:T(8,128)(2,1)} %bitcast.694), calls=%async_computation.4 | async-start | bytes 2097152 | tf_op jit(solution)/shard_map/all_to_all | solution.py:124
  152.2 39.7 %all-to-all-start = ((bf16[8,1,128,512]{3,2,1,0:T(8,128)(2,1)}), bf16[8,1,128,512]{3,2,1,0:T(8,128)(2,1)}, u32[]{:S(2)}, u32[]{:S(2)}) async-start(bf16[8,1,128,512]{3,2,1,0:T(8,128)(2,1)} %bitcast.695), calls=%async_computation | async-start | bytes 2097152 | tf_op jit(solution)/shard_map/all_to_all | solution.py:124
  191.9 32.4 %all-to-all-start.5 = ((bf16[8,1,128,512]{3,2,1,0:T(8,128)(2,1)}), bf16[8,1,128,512]{3,2,1,0:T(8,128)(2,1)}, u32[]{:S(2)}, u32[]{:S(2)}) async-start(bf16[8,1,128,512]{3,2,1,0:T(8,128)(2,1)} %bitcast.709), calls=%async_computation.5 | async-start | bytes 2097152 | tf_op jit(solution)/shard_map/all_to_all | solution.py:131
  224.3 29.8 %all-to-all-start.1 = ((bf16[8,1,128,512]{3,2,1,0:T(8,128)(2,1)}), bf16[8,1,128,512]{3,2,1,0:T(8,128)(2,1)}, u32[]{:S(2)}, u32[]{:S(2)}) async-start(bf16[8,1,128,512]{3,2,1,0:T(8,128)(2,1)} %bitcast.706), calls=%async_computation.1 | async-start | bytes 2097152 | tf_op jit(solution)/shard_map/all_to_all | solution.py:131
  311.2 29.7 %all-to-all-start.2 = ((bf16[8,1,128,512]{3,2,1,0:T(8,128)(2,1)}), bf16[8,1,128,512]{3,2,1,0:T(8,128)(2,1)}, u32[]{:S(2)}, u32[]{:S(2)}) async-start(bf16[8,1,128,512]{3,2,1,0:T(8,128)(2,1)} %bitcast.49), calls=%async_computation.2 | async-start | bytes 2097152 | tf_op jit(solution)/shard_map/all_to_all | solution.py:124
  340.9 30.8 %all-to-all-start.6 = ((bf16[8,1,128,512]{3,2,1,0:T(8,128)(2,1)}), bf16[8,1,128,512]{3,2,1,0:T(8,128)(2,1)}, u32[]{:S(2)}, u32[]{:S(2)}) async-start(bf16[8,1,128,512]{3,2,1,0:T(8,128)(2,1)} %bitcast.696), calls=%async_computation.6 | async-start | bytes 2097152 | tf_op jit(solution)/shard_map/all_to_all | solution.py:124
  371.8 29.9 %all-to-all-start.3 = ((bf16[8,1,128,512]{3,2,1,0:T(8,128)(2,1)}), bf16[8,1,128,512]{3,2,1,0:T(8,128)(2,1)}, u32[]{:S(2)}, u32[]{:S(2)}) async-start(bf16[8,1,128,512]{3,2,1,0:T(8,128)(2,1)} %bitcast.710), calls=%async_computation.3 | async-start | bytes 2097152 | tf_op jit(solution)/shard_map/all_to_all | solution.py:131
  401.6 29.7 %all-to-all-start.7 = ((bf16[8,1,128,512]{3,2,1,0:T(8,128)(2,1)}), bf16[8,1,128,512]{3,2,1,0:T(8,128)(2,1)}, u32[]{:S(2)}, u32[]{:S(2)}) async-start(bf16[8,1,128,512]{3,2,1,0:T(8,128)(2,1)} %bitcast.92), calls=%async_computation.7 | async-start | bytes 2097152 | tf_op jit(solution)/shard_map/all_to_all | solution.py:131
  431.3 29.8 %all-to-all-start.8 = ((bf16[8,1,128,512]{3,2,1,0:T(8,128)(2,1)}), bf16[8,1,128,512]{3,2,1,0:T(8,128)(2,1)}, u32[]{:S(2)}, u32[]{:S(2)}) async-start(bf16[8,1,128,512]{3,2,1,0:T(8,128)(2,1)} %bitcast.693), calls=%async_computation.8 | async-start | bytes 2097152 | tf_op jit(solution)/shard_map/all_to_all | solution.py:209
  461.1 29.3 %all-to-all-start.12 = ((bf16[8,1,128,512]{3,2,1,0:T(8,128)(2,1)}), bf16[8,1,128,512]{3,2,1,0:T(8,128)(2,1)S(1)}, u32[]{:S(2)}, u32[]{:S(2)}) async-start(bf16[8,1,128,512]{3,2,1,0:T(8,128)(2,1)} %bitcast.135), calls=%async_computation.12 | async-start | bytes 2097152 | tf_op jit(solution)/shard_map/all_to_all | solution.py:209
  490.5 34.3 %all-to-all-start.9 = ((bf16[8,1,128,512]{3,2,1,0:T(8,128)(2,1)}), bf16[8,1,128,512]{3,2,1,0:T(8,128)(2,1)S(1)}, u32[]{:S(2)}, u32[]{:S(2)}) async-start(bf16[8,1,128,512]{3,2,1,0:T(8,128)(2,1)} %bitcast.104), calls=%async_computation.9 | async-start | bytes 2097152 | tf_op jit(solution)/shard_map/all_to_all | solution.py:217
  504.4 16.9 %collective-permute-start.16 = (bf16[2,512,512]{2,1,0:T(8,128)(2,1)S(1)}, bf16[2,512,512]{2,1,0:T(8,128)(2,1)S(1)}, u32[]{:S(2)}, u32[]{:S(2)}) collective-permute-start(bf16[2,512,512]{2,1,0:T(8,128)(2,1)S(1)} %fusion.189), channel_id=1, source_target_pairs={{0,1},{1,0},{2,3},{3,2},{4,5},{5,4},{6,7},{7,6},{8,9},{9,8},{10,11... | collective-permute-start | bytes 3145736 | tf_op jit(solution)/shard_map/ppermute | solution.py:280
  524.0 15.1 %collective-permute-start.17 = (bf16[1,512,512]{2,1,0:T(8,128)(2,1)}, bf16[1,512,512]{2,1,0:T(8,128)(2,1)}, u32[]{:S(2)}, u32[]{:S(2)}) collective-permute-start(bf16[1,512,512]{2,1,0:T(8,128)(2,1)} %dynamic-slice_convert_fusion.4), channel_id=1, source_target_pairs={{0,2},{1,3},{2,0},{3,1},{4,6},{5,7},{6,4},{7,5},{8,10},{9,11},{10,... | collective-permute-start | bytes 1572872 | tf_op jit(solution)/shard_map/ppermute | solution.py:280
  524.8 32.3 %all-to-all-start.13 = ((bf16[8,1,128,512]{3,2,1,0:T(8,128)(2,1)}), bf16[8,1,128,512]{3,2,1,0:T(8,128)(2,1)}, u32[]{:S(2)}, u32[]{:S(2)}) async-start(bf16[8,1,128,512]{3,2,1,0:T(8,128)(2,1)} %bitcast.704), calls=%async_computation.13 | async-start | bytes 2097152 | tf_op jit(solution)/shard_map/all_to_all | solution.py:217
  634.1 48.2 %all-to-all-start.10 = ((bf16[8,1,128,512]{3,2,1,0:T(8,128)(2,1)}), bf16[8,1,128,512]{3,2,1,0:T(8,128)(2,1)}, u32[]{:S(2)}, u32[]{:S(2)}) async-start(bf16[8,1,128,512]{3,2,1,0:T(8,128)(2,1)} %bitcast.117), calls=%async_computation.10 | async-start | bytes 2097152 | tf_op jit(solution)/shard_map/all_to_all | solution.py:209
  682.4 32.6 %all-to-all-start.14 = ((bf16[8,1,128,512]{3,2,1,0:T(8,128)(2,1)}), bf16[8,1,128,512]{3,2,1,0:T(8,128)(2,1)}, u32[]{:S(2)}, u32[]{:S(2)}) async-start(bf16[8,1,128,512]{3,2,1,0:T(8,128)(2,1)} %bitcast.692), calls=%async_computation.14 | async-start | bytes 2097152 | tf_op jit(solution)/shard_map/all_to_all | solution.py:209
  697.5 64.6 %collective-permute-start.7 = (bf16[128,2060]{0,1:T(8,128)(2,1)S(1)}, bf16[128,2060]{0,1:T(8,128)(2,1)}, u32[]{:S(2)}, u32[]{:S(2)}) collective-permute-start(bf16[128,2060]{0,1:T(8,128)(2,1)S(1)} %bitcast_convert_fusion.5), channel_id=1, source_target_pairs={{0,4},{4,0},{8,12},{12,8},{16,20},{20,16},{24,28},{28,24},{1,5},{5... | collective-permute-start | bytes 1582088 | tf_op jit(solution)/shard_map/ppermute | solution.py:294
  725.4 71.5 %collective-permute-start.14 = (bf16[2,512,512]{2,1,0:T(8,128)(2,1)}, bf16[2,512,512]{2,1,0:T(8,128)(2,1)}, u32[]{:S(2)}, u32[]{:S(2)}) collective-permute-start(bf16[2,512,512]{2,1,0:T(8,128)(2,1)} %fusion.188), channel_id=1, source_target_pairs={{0,1},{1,0},{2,3},{3,2},{4,5},{5,4},{6,7},{7,6},{8,9},{9,8},{10,11... | collective-permute-start | bytes 3145736 | tf_op jit(solution)/shard_map/ppermute | solution.py:280
  754.4 47.6 %collective-permute-start.10 = (bf16[2,128,2048]{2,1,0:T(8,128)(2,1)}, bf16[2,128,2048]{2,1,0:T(8,128)(2,1)}, u32[]{:S(2)}, u32[]{:S(2)}) collective-permute-start(bf16[2,128,2048]{2,1,0:T(8,128)(2,1)} %fusion.186), channel_id=1, source_target_pairs={{0,1},{1,0},{2,3},{3,2},{4,5},{5,4},{6,7},{7,6},{8,9},{9,8},{10,11... | collective-permute-start | bytes 3145736 | tf_op jit(solution)/shard_map/ppermute | solution.py:280
  757.8 45.7 %all-to-all-start.11 = ((bf16[8,1,128,512]{3,2,1,0:T(8,128)(2,1)}), bf16[8,1,128,512]{3,2,1,0:T(8,128)(2,1)}, u32[]{:S(2)}, u32[]{:S(2)}) async-start(bf16[8,1,128,512]{3,2,1,0:T(8,128)(2,1)} %bitcast.120), calls=%async_computation.11 | async-start | bytes 2097152 | tf_op jit(solution)/shard_map/all_to_all | solution.py:217
  763.7 29.8 %collective-permute-start.8 = (bf16[128,2060]{0,1:T(8,128)(2,1)S(1)}, bf16[128,2060]{0,1:T(8,128)(2,1)S(1)}, u32[]{:S(2)}, u32[]{:S(2)}) collective-permute-start(bf16[128,2060]{0,1:T(8,128)(2,1)S(1)} %get-tuple-element.97), channel_id=1, source_target_pairs={{0,8},{4,12},{8,0},{12,4},{16,24},{20,28},{24,16},{28,20},{1,9},{5... | collective-permute-start | bytes 1582088 | tf_op jit(solution)/shard_map/ppermute | solution.py:294
  794.4 38.7 %collective-permute-start.9 = (bf16[128,2060]{0,1:T(8,128)(2,1)}, bf16[128,2060]{0,1:T(8,128)(2,1)}, u32[]{:S(2)}, u32[]{:S(2)}) collective-permute-start(bf16[128,2060]{0,1:T(8,128)(2,1)} %fusion.191), channel_id=1, source_target_pairs={{0,16},{4,20},{8,24},{12,28},{16,0},{20,4},{24,8},{28,12},{1,17},{... | collective-permute-start | bytes 1582088 | tf_op jit(solution)/shard_map/ppermute | solution.py:294
  800.7 140.9 %collective-permute-start.15 = (bf16[1,512,512]{2,1,0:T(8,128)(2,1)}, bf16[1,512,512]{2,1,0:T(8,128)(2,1)}, u32[]{:S(2)}, u32[]{:S(2)}) collective-permute-start(bf16[1,512,512]{2,1,0:T(8,128)(2,1)} %dynamic-slice_convert_fusion.5), channel_id=1, source_target_pairs={{0,2},{1,3},{2,0},{3,1},{4,6},{5,7},{6,4},{7,5},{8,10},{9,11},{10,... | collective-permute-start | bytes 1572872 | tf_op jit(solution)/shard_map/ppermute | solution.py:280
  803.5 39.5 %all-to-all-start.15 = ((bf16[8,1,128,512]{3,2,1,0:T(8,128)(2,1)}), bf16[8,1,128,512]{3,2,1,0:T(8,128)(2,1)}, u32[]{:S(2)}, u32[]{:S(2)}) async-start(bf16[8,1,128,512]{3,2,1,0:T(8,128)(2,1)} %bitcast.705), calls=%async_computation.15 | async-start | bytes 2097152 | tf_op jit(solution)/shard_map/all_to_all | solution.py:217
  808.9 117.7 %collective-permute-start.11 = (bf16[1,128,2048]{2,1,0:T(8,128)(2,1)}, bf16[1,128,2048]{2,1,0:T(8,128)(2,1)}, u32[]{:S(2)}, u32[]{:S(2)}) collective-permute-start(bf16[1,128,2048]{2,1,0:T(8,128)(2,1)} %dynamic-slice_convert_fusion.7), channel_id=1, source_target_pairs={{0,2},{1,3},{2,0},{3,1},{4,6},{5,7},{6,4},{7,5},{8,10},{9,11},{10,... | collective-permute-start | bytes 1572872 | tf_op jit(solution)/shard_map/ppermute | solution.py:280
  990.2 24.1 %collective-permute-start.4 = (bf16[128,2060]{0,1:T(8,128)(2,1)S(1)}, bf16[128,2060]{0,1:T(8,128)(2,1)S(1)}, u32[]{:S(2)}, u32[]{:S(2)}) collective-permute-start(bf16[128,2060]{0,1:T(8,128)(2,1)S(1)} %fusion.190), channel_id=1, source_target_pairs={{0,16},{4,20},{8,24},{12,28},{16,0},{20,4},{24,8},{28,12},{1,17},{... | collective-permute-start | bytes 1582088 | tf_op jit(solution)/shard_map/ppermute | solution.py:294
  (338 other events, 4106.7 us)
Sparse Core Ops, SparseCore 0:
  10.1 22.3 all-gather.20
  34.7 22.5 all-gather.22
  59.4 22.5 all-gather.24
  83.4 19.6 all-gather.26
  104.5 22.5 all-gather.28
  128.5 22.5 all-gather.30

commit v3 on v2

--- a/solution.py
+++ b/solution.py
@@ -40,52 +40,29 @@
     )
 
 
-def slot_tables(route_ids, prio_rank, experts, capacity):
+def slot_onehot(route_ids, prio_rank, experts, capacity):
     tok_count = route_ids.shape[0]
     order_key = jnp.concatenate([prio_rank, prio_rank + tok_count])
     pair_expert = jnp.concatenate([route_ids[:, 0], route_ids[:, 1]])
-    same_expert = pair_expert[:, None] == pair_expert[None, :]
-    earlier = order_key[None, :] < order_key[:, None]
-    position = jnp.sum((same_expert & earlier).astype(jnp.int32), axis=1)
+    expert_hot = (pair_expert[:, None] == jnp.arange(experts, dtype=jnp.int32)[None, :]).astype(
+        jnp.bfloat16
+    )
+    earlier = (order_key[:, None] < order_key[None, :]).astype(jnp.bfloat16)
+    counts = dot_first(expert_hot, earlier)
+    position = jnp.sum(counts.T * expert_hot.astype(jnp.float32), axis=1).astype(jnp.int32)
     kept_mask = position < capacity
     flat_slot = jnp.where(kept_mask, pair_expert * capacity + position, experts * capacity)
-    pair_ids = jnp.arange(2 * tok_count, dtype=jnp.int32)
-    slot_pair = (
-        jnp.full((experts * capacity + 1,), 2 * tok_count, jnp.int32).at[flat_slot].set(pair_ids)
-    )
-    slot_pair = slot_pair[: experts * capacity]
-    slot_token = jnp.where(slot_pair < 2 * tok_count, slot_pair % tok_count, tok_count)
-    return (flat_slot, slot_pair, slot_token, kept_mask)
-
-
-def block_tables(route_ids, prio_rank, experts, capacity):
-    blocks, tok_count = prio_rank.shape
-    flat_slot, slot_pair, slot_token, kept_mask = jax.vmap(
-        lambda r, p: slot_tables(r, p, experts, capacity)
-    )(route_ids, prio_rank)
-    block_ids = jnp.arange(blocks, dtype=jnp.int32)
-    send_index = (block_ids[:, None] * (tok_count + 1) + slot_token).reshape(
-        blocks, experts, capacity
-    ).transpose(1, 0, 2)
-    pair_index = (block_ids[:, None] * (2 * tok_count + 1) + slot_pair).reshape(
-        blocks, experts, capacity
-    ).transpose(1, 0, 2)
-    slot_e = flat_slot // capacity
-    slot_c = flat_slot % capacity
-    back_index = jnp.where(
-        kept_mask,
-        (slot_e * blocks + block_ids[:, None]) * capacity + slot_c,
-        experts * blocks * capacity,
-    )
-    return send_index, pair_index, back_index, kept_mask
+    pair_hot = (
+        flat_slot[:, None] == jnp.arange(experts * capacity, dtype=jnp.int32)[None, :]
+    ).astype(jnp.bfloat16)
+    token_hot = pair_hot[:tok_count] + pair_hot[tok_count:]
+    return pair_hot, token_hot, kept_mask
 
 
 def forward_layer(residual, route_hot, tables, weights, experts, capacity):
     norm_gains, norm_shifts, qkv_w, proj_w, router_w, in_w, out_w = weights
-    send_index, pair_index, back_index, kept_mask = tables
+    pair_hot, token_hot, kept_mask = tables
     tok_count = residual.shape[0]
-    blocks = back_index.shape[0]
-    tok_block = tok_count // blocks
     seq_count = tok_count // SEQ
     score_scale = HEAD ** (-0.5)
     norm_scale = norm_gains.astype(jnp.float32)
@@ -116,37 +93,31 @@
     gate_probs = jax.nn.softmax(
         jnp.dot(normed_two, router_w, preferred_element_type=jnp.float32), axis=-1
     )
-    padded = jnp.concatenate(
-        [normed_two.reshape(blocks, tok_block, D), jnp.zeros((blocks, 1, D), jnp.bfloat16)],
-        axis=1,
-    ).reshape(blocks * (tok_block + 1), D)
-    sending = padded[send_index]
-    received = lax.all_to_all(sending, "expert", split_axis=0, concat_axis=0, tiled=True)
-    row_block = received.reshape(experts * blocks * capacity, D)
+    sending = dot_first(token_hot, normed_two).astype(jnp.bfloat16)
+    received = lax.all_to_all(
+        sending.reshape(experts, capacity, D), "expert", split_axis=0, concat_axis=0, tiled=True
+    )
+    row_block = received.reshape(experts * capacity, D)
     hidden_pre = jnp.dot(row_block, in_w[0], preferred_element_type=jnp.float32)
     hidden_act = gelu_tanh(hidden_pre).astype(jnp.bfloat16)
     expert_rows = jnp.dot(hidden_act, out_w[0], preferred_element_type=jnp.float32).astype(
         jnp.bfloat16
     )
     returned = lax.all_to_all(
-        expert_rows.reshape(experts, blocks, capacity, D),
+        expert_rows.reshape(experts, capacity, D),
         "expert",
         split_axis=0,
         concat_axis=0,
         tiled=True,
     )
-    back_rows = jnp.concatenate(
-        [returned.reshape(experts * blocks * capacity, D), jnp.zeros((1, D), jnp.bfloat16)]
-    )
-    pair_rows = (
-        back_rows[back_index].astype(jnp.float32).reshape(blocks, TOP, tok_block, D)
-    )
-    probs_block = gate_probs.reshape(blocks, tok_block, experts)
-    chosen = jnp.sum(route_hot * probs_block[:, :, None, :], axis=-1)
-    kept_gate = kept_mask.astype(jnp.float32).reshape(blocks, TOP, tok_block)
-    weight_pair = kept_gate * chosen.transpose(0, 2, 1)
-    combined = jnp.sum(weight_pair[..., None] * pair_rows, axis=1)
-    output = middle + combined.reshape(tok_count, D)
+    pair_rows = jnp.dot(
+        pair_hot, returned.reshape(experts * capacity, D), preferred_element_type=jnp.float32
+    ).reshape(TOP, tok_count, D)
+    chosen = jnp.sum(route_hot * gate_probs[:, None, :], axis=-1)
+    kept_gate = kept_mask.astype(jnp.float32).reshape(TOP, tok_count)
+    weight_pair = kept_gate * chosen.T
+    combined = jnp.sum(weight_pair[..., None] * pair_rows, axis=0)
+    output = middle + combined
     saved_state = (
         residual,
         normed,
@@ -181,45 +152,37 @@
         row_block,
         hidden_pre,
     ) = saved_state
-    send_index, pair_index, back_index, kept_mask = tables
+    pair_hot, token_hot, kept_mask = tables
     norm_gains, norm_shifts, qkv_w, proj_w, router_w, in_w, out_w = weights
     tok_count = residual.shape[0]
-    blocks = back_index.shape[0]
-    tok_block = tok_count // blocks
     seq_count = tok_count // SEQ
     score_scale = HEAD ** (-0.5)
     norm_scale = norm_gains.astype(jnp.float32)
     norm_shift = norm_shifts.astype(jnp.float32)
-    d_block = d_output.reshape(blocks, 1, tok_block, D)
-    d_gate_pair = kept_gate * jnp.sum(d_block * pair_rows, axis=-1)
-    d_gates = jnp.sum(route_hot * d_gate_pair.transpose(0, 2, 1)[..., None], axis=2)
-    d_gates = d_gates.reshape(tok_count, experts)
+    d_gate_pair = kept_gate * jnp.sum(d_output[None] * pair_rows, axis=-1)
+    d_gates = jnp.sum(route_hot * d_gate_pair.T[:, :, None], axis=1)
     d_logits = (
         gate_probs * (d_gates - jnp.sum(gate_probs * d_gates, axis=-1, keepdims=True))
     ).astype(jnp.bfloat16)
     g_router = dot_first(normed_two, d_logits)
     d_normed_two = dot_last(d_logits, router_w)
-    d_pairs = (weight_pair[..., None] * d_block).astype(jnp.bfloat16).reshape(
-        blocks, TOP * tok_block, D
-    )
-    d_pairs = jnp.concatenate(
-        [d_pairs, jnp.zeros((blocks, 1, D), jnp.bfloat16)], axis=1
-    ).reshape(blocks * (TOP * tok_block + 1), D)
-    d_slots = d_pairs[pair_index]
+    d_pairs = (
+        (weight_pair[:, :, None] * d_output[None]).astype(jnp.bfloat16).reshape(TOP * tok_count, D)
+    )
+    d_slots = dot_first(pair_hot, d_pairs).astype(jnp.bfloat16).reshape(experts, capacity, D)
     d_expert_out = lax.all_to_all(d_slots, "expert", split_axis=0, concat_axis=0, tiled=True)
-    flat_out = d_expert_out.reshape(experts * blocks * capacity, D)
+    flat_out = d_expert_out.reshape(experts * capacity, D)
     hidden_act = gelu_tanh(hidden_pre).astype(jnp.bfloat16)
     g_out = dot_first(hidden_act, flat_out)
     d_act = dot_last(flat_out, out_w[0])
     d_pre = jax.vjp(gelu_tanh, hidden_pre)[1](d_act)[0].astype(jnp.bfloat16)
     g_in = dot_first(row_block, d_pre)
-    d_rows = dot_last(d_pre, in_w[0]).astype(jnp.bfloat16).reshape(experts, blocks, capacity, D)
+    d_rows = dot_last(d_pre, in_w[0]).astype(jnp.bfloat16).reshape(experts, capacity, D)
     d_back = lax.all_to_all(d_rows, "expert", split_axis=0, concat_axis=0, tiled=True)
-    d_pair_in = jnp.concatenate(
-        [d_back.reshape(experts * blocks * capacity, D), jnp.zeros((1, D), jnp.bfloat16)]
-    )[back_index]
-    d_pair_in = d_pair_in.astype(jnp.float32).reshape(blocks, TOP, tok_block, D)
-    d_normed_two = d_normed_two + jnp.sum(d_pair_in, axis=1).reshape(tok_count, D)
+    d_pair_in = jnp.dot(
+        pair_hot, d_back.reshape(experts * capacity, D), preferred_element_type=jnp.float32
+    ).reshape(TOP, tok_count, D)
+    d_normed_two = d_normed_two + jnp.sum(d_pair_in, axis=0)
     pulled_two = jax.vjp(layer_norm, middle, norm_scale[1], norm_shift[1])[1](d_normed_two)
     d_middle = d_output + pulled_two[0]
     d_branch = d_middle.astype(jnp.bfloat16)
@@ -338,22 +301,40 @@
     streams = []
     for block in range(blocks):
         rows = slice(block * TOK_MB, (block + 1) * TOK_MB)
-        route_ids = routes[rows].reshape(1, TOK_MB, TOP)
-        prio_rank = priority[rows].reshape(1, TOK_MB)
-        tables = block_tables(route_ids, prio_rank, experts, capacity)
+        route_ids = routes[rows]
+        tables = slot_onehot(route_ids, priority[rows], experts, capacity)
         route_hot = (
             route_ids[..., None] == jnp.arange(experts, dtype=jnp.int32)
         ).astype(jnp.float32)
         streams.append((rows, tables, route_hot))
+    layer_count = norm_gain.shape[0]
+    small = jnp.concatenate(
+        [
+            norm_gain.reshape(layer_count * 2, -1).T,
+            norm_bias.reshape(layer_count * 2, -1).T,
+            w_router.transpose(1, 0, 2).reshape(w_router.shape[1], -1),
+        ],
+        axis=1,
+    )
+    small = lax.all_gather(small, "shard", axis=0, tiled=True)
+    qkv_cols = w_qkv.shape[2]
     all_weights = []
     for layer_index in range(LAYERS):
+        attn = lax.all_gather(
+            jnp.concatenate([w_qkv[layer_index], w_proj[layer_index]], axis=1),
+            "shard",
+            axis=0,
+            tiled=True,
+        )
+        shift_at = 2 * layer_count + 2 * layer_index
+        router_at = 4 * layer_count + experts * layer_index
         all_weights.append(
             (
-                lax.all_gather(norm_gain[layer_index], "shard", axis=1, tiled=True),
-                lax.all_gather(norm_bias[layer_index], "shard", axis=1, tiled=True),
-                lax.all_gather(w_qkv[layer_index], "shard", axis=0, tiled=True),
-                lax.all_gather(w_proj[layer_index], "shard", axis=0, tiled=True),
-                lax.all_gather(w_router[layer_index], "shard", axis=0, tiled=True),
+                small[:, 2 * layer_index : 2 * layer_index + 2].T,
+                small[:, shift_at : shift_at + 2].T,
+                attn[:, :qkv_cols],
+                attn[:, qkv_cols:],
+                small[:, router_at : router_at + experts],
                 lax.all_gather(exp_in[layer_index], "shard", axis=1, tiled=True),
                 lax.all_gather(exp_out[layer_index], "shard", axis=1, tiled=True),
             )

time: 1040 us -> 979 us (0.941)
  local copies, waits for them, and re-layouts: 301 us -> 195 us
  waiting for transfers between devices: 184 us -> 285 us
  other arithmetic: 135 us -> 70.2 us
  matrix products: 244 us -> 307 us
  blocking collectives: 46.9 us -> 6.14 us
    gather x16 -> x0, local copies, waits for them, and re-layouts: 71.2 us -> none  [the longest x4 20.7 us: forward_layer(): sending = padded[send_index]]
    reduce_sum x20 -> x10, other arithmetic: 54.3 us -> 2.24 us  [the longest x2 2.11 us: backward_layer(): d_gate_pair = kept_gate * jnp.sum(d_output[None] * pair_rows, axis=-1)]
    all_to_all x8, waiting for transfers between devices: 53.5 us -> 98.7 us  [the longest x4 59 us: forward_layer(): lax.all_to_all(sending.reshape(experts, capacity, D), 'expert', split_axi...]
    all_gather x8 -> x1, blocking collectives: 46.9 us -> 6.14 us  [local(): small = lax.all_gather(small, 'shard', axis=0, tiled=True)]
    all_to_all x4, waiting for transfers between devices: 0.3 us -> 35 us  [backward_layer(): lax.all_to_all(d_rows, 'expert', split_axis=0, concat_axis=0, tiled=True)]
    dot_general x0 -> x8, matrix products: none -> 23 us  [the longest x4 13.9 us: forward_layer(): jnp.dot(pair_hot, returned.reshape(experts * capacity, D), preferred_elem...]
    dot_general x20 -> x30, matrix products: 74.9 us -> 95.2 us  [dot_first(): lax.dot_general(left, right, (((0,), (0,)), ((), ())), preferred_element_...]
    all_to_all x4, waiting for transfers between devices: 17.7 us -> 35.4 us  [backward_layer(): lax.all_to_all(d_slots, 'expert', split_axis=0, concat_axis=0, tiled=True)]
  transfers between devices with their start and end apart: 40 -> 40, of which waited for: 20 -> 21; matrix products, arithmetic and copies ran while one was open for 56% -> 42% of each run, Pallas kernels for 0% -> 0%
where the time goes in v3:
time: 979 us; the launch traced here: 968 us
  matrix products  307 us (31%)
  waiting for transfers between devices  285 us (29%)
  local copies, waits for them, and re-layouts  195 us (20%)
  starting transfers between devices  86.4 us (9%)
  other arithmetic  70.2 us (7%)
  between operations  18.5 us (2%)
    dot_general x30, matrix products, dot_first(): lax.dot_general(left, right, (((0,), (0,)), ((), ())), preferred_element_...  95.2 us
    ppermute x6, waiting for transfers between devices, doubling_sum(): lax.ppermute(own.astype(jnp.bfloat16), axis_name, [(i, i ^ bit) for i in...  89.3 us
    dot_general x20, matrix products, dot_last(): lax.dot_general(left, right, (((1,), (1,)), ((), ())), preferred_element_...  77.4 us
    all_to_all x4, waiting for transfers between devices, forward_layer(): lax.all_to_all(sending.reshape(experts, capacity, D), 'expert', split_axi...  59 us
    unnamed x599, local copies, waits for them, and re-layouts  48.7 us
    all_to_all x4, waiting for transfers between devices, forward_layer(): lax.all_to_all(expert_rows.reshape(experts, capacity, D), 'expert', split...  39.7 us
    all_to_all x4, waiting for transfers between devices, backward_layer(): lax.all_to_all(d_slots, 'expert', split_axis=0, concat_axis=0, tiled=True)  35.4 us
    all_to_all x4, waiting for transfers between devices, backward_layer(): lax.all_to_all(d_rows, 'expert', split_axis=0, concat_axis=0, tiled=True)  35 us
  transfers between devices with their start and end apart: 40, of which 21 were waited for; matrix products, arithmetic and copies ran while one was open for 42% of the time, Pallas kernels for 0%

profile of v3, /device:TPU:0, one launch (start us, length us, event | category | flops | bytes accessed | tf_op | source)
XLA Modules:
  0.0 968.2 jit_solution(11255564962332810747)
XLA Ops:
  27.4 9.8 %all-gather.11.cloned.1.call-done = bf16[512,2048]{1,0:T(8,128)(2,1)} async-done(((bf16[128,2048]{1,0:T(8,128)(2,1)}), bf16[512,2048]{1,0:T(8,128)(2,1)}) %all-gather.11.cloned.1.call-update) | async-done | bytes 2097168 | tf_op jit(solution)/shard_map/all_gather | solution.py:323
  96.6 18.6 %all-to-all-done.4 = bf16[8,128,512]{2,1,0:T(8,128)(2,1)S(1)} async-done(((bf16[8,128,512]{2,1,0:T(8,128)(2,1)}), bf16[8,128,512]{2,1,0:T(8,128)(2,1)S(1)}, u32[]{:S(2)}, u32[]{:S(2)}) %all-to-all-start.4) | async-done | bytes 1048608 | tf_op jit(solution)/shard_map/all_to_all | solution.py:97
  120.9 7.6 fusion.100
  128.6 7.7 fusion.149
  136.3 9.7 %all-to-all-done = bf16[8,128,512]{2,1,0:T(8,128)(2,1)S(1)} async-done(((bf16[8,128,512]{2,1,0:T(8,128)(2,1)}), bf16[8,128,512]{2,1,0:T(8,128)(2,1)S(1)}, u32[]{:S(2)}, u32[]{:S(2)}) %all-to-all-start) | async-done | bytes 1048608 | tf_op jit(solution)/shard_map/all_to_all | solution.py:97
  150.5 7.7 multiply_convert_fusion.3
  163.5 12.3 %all-to-all-done.5 = bf16[8,128,512]{2,1,0:T(8,128)(2,1)} async-done(((bf16[8,128,512]{2,1,0:T(8,128)(2,1)}), bf16[8,128,512]{2,1,0:T(8,128)(2,1)}, u32[]{:S(2)}, u32[]{:S(2)}) %all-to-all-start.5) | async-done | bytes 1048608 | tf_op jit(solution)/shard_map/all_to_all | solution.py:106
  184.8 20.8 %all-to-all-done.1 = bf16[8,128,512]{2,1,0:T(8,128)(2,1)S(1)} async-done(((bf16[8,128,512]{2,1,0:T(8,128)(2,1)}), bf16[8,128,512]{2,1,0:T(8,128)(2,1)S(1)}, u32[]{:S(2)}, u32[]{:S(2)}) %all-to-all-start.1) | async-done | bytes 1048608 | tf_op jit(solution)/shard_map/all_to_all | solution.py:106
  273.8 11.6 %all-to-all-done.2 = bf16[8,128,512]{2,1,0:T(8,128)(2,1)} async-done(((bf16[8,128,512]{2,1,0:T(8,128)(2,1)}), bf16[8,128,512]{2,1,0:T(8,128)(2,1)}, u32[]{:S(2)}, u32[]{:S(2)}) %all-to-all-start.2) | async-done | bytes 1048608 | tf_op jit(solution)/shard_map/all_to_all | solution.py:97
  301.0 14.1 %all-to-all-done.8 = bf16[8,128,512]{2,1,0:T(8,128)(2,1)} async-done(((bf16[8,128,512]{2,1,0:T(8,128)(2,1)}), bf16[8,128,512]{2,1,0:T(8,128)(2,1)}, u32[]{:S(2)}, u32[]{:S(2)}) %all-to-all-start.8) | async-done | bytes 1048608 | tf_op jit(solution)/shard_map/all_to_all | solution.py:173
  325.7 19.2 %all-to-all-done.6 = bf16[8,128,512]{2,1,0:T(8,128)(2,1)} async-done(((bf16[8,128,512]{2,1,0:T(8,128)(2,1)}), bf16[8,128,512]{2,1,0:T(8,128)(2,1)}, u32[]{:S(2)}, u32[]{:S(2)}) %all-to-all-start.6) | async-done | bytes 1048608 | tf_op jit(solution)/shard_map/all_to_all | solution.py:97
  349.3 8.8 multiply_convert_fusion.2
  358.1 7.7 fusion.80
  384.0 9.0 convolution_add_fusion.2
  394.2 11.1 %fusion.27 = bf16[1024,2048]{1,0:T(8,128)(2,1)S(1)} fusion(f32[1024,2048]{1,0:T(8,128)} %fusion.80, bf16[1024,512]{1,0:T(8,128)(2,1)} %bitcast.98, bf16[1,1,2048,512]{3,2,1,0:T(8,128)(2,1)S(1)} %copy-done.283), kind=kOutput, calls=%fused_computation.35 | convolution fusion | flops 2189426688 | bytes 15728640 | tf_op jit(solution)/shard_map/dot_general | solution.py:38
  405.3 9.6 fusion.13
  435.0 7.9 fusion.161
  450.0 11.5 %all-to-all-done.9 = bf16[8,128,512]{2,1,0:T(8,128)(2,1)} async-done(((bf16[8,128,512]{2,1,0:T(8,128)(2,1)}), bf16[8,128,512]{2,1,0:T(8,128)(2,1)}, u32[]{:S(2)}, u32[]{:S(2)}) %all-to-all-start.9) | async-done | bytes 1048608 | tf_op jit(solution)/shard_map/all_to_all | solution.py:181
  484.9 6.5 all-to-all-done.7
  502.9 18.5 %all-to-all-done.13 = bf16[8,128,512]{2,1,0:T(8,128)(2,1)} async-done(((bf16[8,128,512]{2,1,0:T(8,128)(2,1)}), bf16[8,128,512]{2,1,0:T(8,128)(2,1)}, u32[]{:S(2)}, u32[]{:S(2)}) %all-to-all-start.13) | async-done | bytes 1048608 | tf_op jit(solution)/shard_map/all_to_all | solution.py:181
  628.2 8.4 all-to-all-done.10
  653.6 12.8 %all-to-all-done.14 = bf16[8,128,512]{2,1,0:T(8,128)(2,1)} async-done(((bf16[8,128,512]{2,1,0:T(8,128)(2,1)}), bf16[8,128,512]{2,1,0:T(8,128)(2,1)}, u32[]{:S(2)}, u32[]{:S(2)}) %all-to-all-start.14) | async-done | bytes 1048608 | tf_op jit(solution)/shard_map/all_to_all | solution.py:173
  666.4 9.1 convolution_add_fusion.3
  677.9 9.4 fusion.6
  689.7 9.0 fusion.20
  719.5 22.2 %collective-permute-done.8 = bf16[128,2060]{0,1:T(8,128)(2,1)S(1)} collective-permute-done((bf16[128,2060]{0,1:T(8,128)(2,1)S(1)}, bf16[128,2060]{0,1:T(8,128)(2,1)S(1)}, u32[]{:S(2)}, u32[]{:S(2)}) %collective-permute-start.8) | collective-permute-done | bytes 527392 | tf_op jit(solution)/shard_map/ppermute | solution.py:257
  757.4 23.7 %collective-permute-done.9 = bf16[128,2060]{0,1:T(8,128)(2,1)S(1)} collective-permute-done((bf16[128,2060]{0,1:T(8,128)(2,1)}, bf16[128,2060]{0,1:T(8,128)(2,1)S(1)}, u32[]{:S(2)}, u32[]{:S(2)}) %collective-permute-start.9) | collective-permute-done | bytes 527392 | tf_op jit(solution)/shard_map/ppermute | solution.py:257
  885.1 11.2 %collective-permute-done.1 = bf16[1,128,2060]{1,2,0:T(8,128)(2,1)S(1)} collective-permute-done((bf16[1,128,2060]{1,2,0:T(8,128)(2,1)S(1)}, bf16[1,128,2060]{1,2,0:T(8,128)(2,1)S(1)}, u32[]{:S(2)}, u32[]{:S(2)}) %collective-permute-start.1) | collective-permute-done | bytes 527392 | tf_op jit(solution)/shard_map/ppermute | solution.py:243
  896.4 8.5 fusion.243
  908.1 10.6 %collective-permute-done.2 = bf16[128,2060]{0,1:T(8,128)(2,1)S(1)} collective-permute-done((bf16[128,2060]{0,1:T(8,128)(2,1)S(1)}, bf16[128,2060]{0,1:T(8,128)(2,1)S(1)}, u32[]{:S(2)}, u32[]{:S(2)}) %collective-permute-start.2) | collective-permute-done | bytes 527392 | tf_op jit(solution)/shard_map/ppermute | solution.py:257
  919.9 11.7 %collective-permute-done.3 = bf16[128,2060]{0,1:T(8,128)(2,1)S(1)} collective-permute-done((bf16[128,2060]{0,1:T(8,128)(2,1)S(1)}, bf16[128,2060]{0,1:T(8,128)(2,1)S(1)}, u32[]{:S(2)}, u32[]{:S(2)}) %collective-permute-start.3) | collective-permute-done | bytes 527392 | tf_op jit(solution)/shard_map/ppermute | solution.py:257
  934.8 21.2 %collective-permute-done.4 = bf16[128,2060]{0,1:T(8,128)(2,1)S(1)} collective-permute-done((bf16[128,2060]{0,1:T(8,128)(2,1)S(1)}, bf16[128,2060]{0,1:T(8,128)(2,1)S(1)}, u32[]{:S(2)}, u32[]{:S(2)}) %collective-permute-start.4) | collective-permute-done | bytes 527392 | tf_op jit(solution)/shard_map/ppermute | solution.py:257
  (1003 shorter events, 562.4 us)
Async XLA Ops:
  7.2 30.0 %all-gather.11.cloned.1.call-start = ((), (), s32[]{:S(2)}) async-start(), calls=%async_computation.16 | async-start | bytes 2621440 | tf_op jit(solution)/shard_map/all_gather | solution.py:323
  11.7 109.2 %all-gather.15.cloned.1.call-start = ((), (), s32[]{:S(2)}) async-start(), calls=%async_computation.18 | async-start | bytes 2621440 | tf_op jit(solution)/shard_map/all_gather | solution.py:338
  12.9 115.6 %all-gather.17.cloned.1.call-start = ((), (), s32[]{:S(2)}) async-start(), calls=%async_computation.19 | async-start | bytes 2621440 | tf_op jit(solution)/shard_map/all_gather | solution.py:339
  83.4 31.8 %all-to-all-start.4 = ((bf16[8,128,512]{2,1,0:T(8,128)(2,1)}), bf16[8,128,512]{2,1,0:T(8,128)(2,1)S(1)}, u32[]{:S(2)}, u32[]{:S(2)}) async-start(bf16[8,128,512]{2,1,0:T(8,128)(2,1)} %bitcast.582), calls=%async_computation.4 | async-start | bytes 2097152 | tf_op jit(solution)/shard_map/all_to_all | solution.py:97
  89.0 121.0 %all-gather.13.cloned.1.call-start = ((), (), s32[]{:S(2)}) async-start(), calls=%async_computation.17 | async-start | bytes 2621440 | tf_op jit(solution)/shard_map/all_gather | solution.py:323
  116.2 29.8 %all-to-all-start = ((bf16[8,128,512]{2,1,0:T(8,128)(2,1)}), bf16[8,128,512]{2,1,0:T(8,128)(2,1)S(1)}, u32[]{:S(2)}, u32[]{:S(2)}) async-start(bf16[8,128,512]{2,1,0:T(8,128)(2,1)} %bitcast.583), calls=%async_computation | async-start | bytes 2097152 | tf_op jit(solution)/shard_map/all_to_all | solution.py:97
  146.0 29.8 %all-to-all-start.5 = ((bf16[8,128,512]{2,1,0:T(8,128)(2,1)}), bf16[8,128,512]{2,1,0:T(8,128)(2,1)}, u32[]{:S(2)}, u32[]{:S(2)}) async-start(bf16[8,128,512]{2,1,0:T(8,128)(2,1)} %bitcast.592), calls=%async_computation.5 | async-start | bytes 2097152 | tf_op jit(solution)/shard_map/all_to_all | solution.py:106
  175.8 29.8 %all-to-all-start.1 = ((bf16[8,128,512]{2,1,0:T(8,128)(2,1)}), bf16[8,128,512]{2,1,0:T(8,128)(2,1)S(1)}, u32[]{:S(2)}, u32[]{:S(2)}) async-start(bf16[8,128,512]{2,1,0:T(8,128)(2,1)} %bitcast.589), calls=%async_computation.1 | async-start | bytes 2097152 | tf_op jit(solution)/shard_map/all_to_all | solution.py:106
  255.6 29.8 %all-to-all-start.2 = ((bf16[8,128,512]{2,1,0:T(8,128)(2,1)}), bf16[8,128,512]{2,1,0:T(8,128)(2,1)}, u32[]{:S(2)}, u32[]{:S(2)}) async-start(bf16[8,128,512]{2,1,0:T(8,128)(2,1)} %bitcast.584), calls=%async_computation.2 | async-start | bytes 2097152 | tf_op jit(solution)/shard_map/all_to_all | solution.py:97
  259.9 89.4 %all-gather.19.cloned.1.call-start = ((), (), s32[]{:S(2)}) async-start(), calls=%async_computation.20 | async-start | bytes 2621440 | tf_op jit(solution)/shard_map/all_gather | solution.py:338
  285.5 29.7 %all-to-all-start.8 = ((bf16[8,128,512]{2,1,0:T(8,128)(2,1)}), bf16[8,128,512]{2,1,0:T(8,128)(2,1)}, u32[]{:S(2)}, u32[]{:S(2)}) async-start(bf16[8,128,512]{2,1,0:T(8,128)(2,1)} %bitcast.577), calls=%async_computation.8 | async-start | bytes 2097152 | tf_op jit(solution)/shard_map/all_to_all | solution.py:173
  289.8 81.7 %all-gather.21.cloned.1.call-start = ((), (), s32[]{:S(2)}) async-start(), calls=%async_computation.21 | async-start | bytes 2621440 | tf_op jit(solution)/shard_map/all_gather | solution.py:339
  315.2 29.6 %all-to-all-start.6 = ((bf16[8,128,512]{2,1,0:T(8,128)(2,1)}), bf16[8,128,512]{2,1,0:T(8,128)(2,1)}, u32[]{:S(2)}, u32[]{:S(2)}) async-start(bf16[8,128,512]{2,1,0:T(8,128)(2,1)} %bitcast.587), calls=%async_computation.6 | async-start | bytes 2097152 | tf_op jit(solution)/shard_map/all_to_all | solution.py:97
  344.8 32.8 %all-to-all-start.12 = ((bf16[8,128,512]{2,1,0:T(8,128)(2,1)}), bf16[8,128,512]{2,1,0:T(8,128)(2,1)}, u32[]{:S(2)}, u32[]{:S(2)}) async-start(bf16[8,128,512]{2,1,0:T(8,128)(2,1)} %bitcast.590), calls=%async_computation.12 | async-start | bytes 2097152 | tf_op jit(solution)/shard_map/all_to_all | solution.py:173
  377.6 51.3 %all-to-all-start.3 = ((bf16[8,128,512]{2,1,0:T(8,128)(2,1)}), bf16[8,128,512]{2,1,0:T(8,128)(2,1)}, u32[]{:S(2)}, u32[]{:S(2)}) async-start(bf16[8,128,512]{2,1,0:T(8,128)(2,1)} %bitcast.585), calls=%async_computation.3 | async-start | bytes 2097152 | tf_op jit(solution)/shard_map/all_to_all | solution.py:106
  394.2 48.7 %collective-permute-start.16 = (bf16[2,512,512]{2,1,0:T(8,128)(2,1)}, bf16[2,512,512]{2,1,0:T(8,128)(2,1)}, u32[]{:S(2)}, u32[]{:S(2)}) collective-permute-start(bf16[2,512,512]{2,1,0:T(8,128)(2,1)} %fusion.247), channel_id=1, source_target_pairs={{0,1},{1,0},{2,3},{3,2},{4,5},{5,4},{6,7},{7,6},{8,9},{9,8},{10,11... | collective-permute-start | bytes 3145736 | tf_op jit(solution)/shard_map/ppermute | solution.py:243
  428.9 32.5 %all-to-all-start.9 = ((bf16[8,128,512]{2,1,0:T(8,128)(2,1)}), bf16[8,128,512]{2,1,0:T(8,128)(2,1)}, u32[]{:S(2)}, u32[]{:S(2)}) async-start(bf16[8,128,512]{2,1,0:T(8,128)(2,1)} %bitcast.588), calls=%async_computation.9 | async-start | bytes 2097152 | tf_op jit(solution)/shard_map/all_to_all | solution.py:181
  446.7 27.1 %collective-permute-start.17 = (bf16[1,512,512]{2,1,0:T(8,128)(2,1)}, bf16[1,512,512]{2,1,0:T(8,128)(2,1)}, u32[]{:S(2)}, u32[]{:S(2)}) collective-permute-start(bf16[1,512,512]{2,1,0:T(8,128)(2,1)} %dynamic-slice_convert_fusion.4), channel_id=1, source_target_pairs={{0,2},{1,3},{2,0},{3,1},{4,6},{5,7},{6,4},{7,5},{8,10},{9,11},{10,... | collective-permute-start | bytes 1572872 | tf_op jit(solution)/shard_map/ppermute | solution.py:243
  461.5 29.9 %all-to-all-start.7 = ((bf16[8,128,512]{2,1,0:T(8,128)(2,1)}), bf16[8,128,512]{2,1,0:T(8,128)(2,1)}, u32[]{:S(2)}, u32[]{:S(2)}) async-start(bf16[8,128,512]{2,1,0:T(8,128)(2,1)} %bitcast.580), calls=%async_computation.7 | async-start | bytes 2097152 | tf_op jit(solution)/shard_map/all_to_all | solution.py:106
  491.4 30.0 %all-to-all-start.13 = ((bf16[8,128,512]{2,1,0:T(8,128)(2,1)}), bf16[8,128,512]{2,1,0:T(8,128)(2,1)}, u32[]{:S(2)}, u32[]{:S(2)}) async-start(bf16[8,128,512]{2,1,0:T(8,128)(2,1)} %bitcast.579), calls=%async_computation.13 | async-start | bytes 2097152 | tf_op jit(solution)/shard_map/all_to_all | solution.py:181
  606.9 29.7 %all-to-all-start.10 = ((bf16[8,128,512]{2,1,0:T(8,128)(2,1)}), bf16[8,128,512]{2,1,0:T(8,128)(2,1)}, u32[]{:S(2)}, u32[]{:S(2)}) async-start(bf16[8,128,512]{2,1,0:T(8,128)(2,1)} %bitcast.578), calls=%async_computation.10 | async-start | bytes 2097152 | tf_op jit(solution)/shard_map/all_to_all | solution.py:173
  636.6 29.8 %all-to-all-start.14 = ((bf16[8,128,512]{2,1,0:T(8,128)(2,1)}), bf16[8,128,512]{2,1,0:T(8,128)(2,1)}, u32[]{:S(2)}, u32[]{:S(2)}) async-start(bf16[8,128,512]{2,1,0:T(8,128)(2,1)} %bitcast.581), calls=%async_computation.14 | async-start | bytes 2097152 | tf_op jit(solution)/shard_map/all_to_all | solution.py:173
  645.9 64.4 %collective-permute-start.7 = (bf16[128,2060]{0,1:T(8,128)(2,1)S(1)}, bf16[128,2060]{0,1:T(8,128)(2,1)}, u32[]{:S(2)}, u32[]{:S(2)}) collective-permute-start(bf16[128,2060]{0,1:T(8,128)(2,1)S(1)} %bitcast_convert_fusion.5), channel_id=1, source_target_pairs={{0,4},{4,0},{8,12},{12,8},{16,20},{20,16},{24,28},{28,24},{1,5},{5... | collective-permute-start | bytes 1582088 | tf_op jit(solution)/shard_map/ppermute | solution.py:257
  676.8 68.4 %collective-permute-start.14 = (bf16[2,512,512]{2,1,0:T(8,128)(2,1)}, bf16[2,512,512]{2,1,0:T(8,128)(2,1)}, u32[]{:S(2)}, u32[]{:S(2)}) collective-permute-start(bf16[2,512,512]{2,1,0:T(8,128)(2,1)} %fusion.246), channel_id=1, source_target_pairs={{0,1},{1,0},{2,3},{3,2},{4,5},{5,4},{6,7},{7,6},{8,9},{9,8},{10,11... | collective-permute-start | bytes 3145736 | tf_op jit(solution)/shard_map/ppermute | solution.py:243
  702.7 45.5 %collective-permute-start.10 = (bf16[2,128,2048]{2,1,0:T(8,128)(2,1)}, bf16[2,128,2048]{2,1,0:T(8,128)(2,1)}, u32[]{:S(2)}, u32[]{:S(2)}) collective-permute-start(bf16[2,128,2048]{2,1,0:T(8,128)(2,1)} %fusion.244), channel_id=1, source_target_pairs={{0,1},{1,0},{2,3},{3,2},{4,5},{5,4},{6,7},{7,6},{8,9},{9,8},{10,11... | collective-permute-start | bytes 3145736 | tf_op jit(solution)/shard_map/ppermute | solution.py:243
  706.0 47.5 %all-to-all-start.11 = ((bf16[8,128,512]{2,1,0:T(8,128)(2,1)}), bf16[8,128,512]{2,1,0:T(8,128)(2,1)}, u32[]{:S(2)}, u32[]{:S(2)}) async-start(bf16[8,128,512]{2,1,0:T(8,128)(2,1)} %bitcast.87), calls=%async_computation.11 | async-start | bytes 2097152 | tf_op jit(solution)/shard_map/all_to_all | solution.py:181
  711.9 29.8 %collective-permute-start.8 = (bf16[128,2060]{0,1:T(8,128)(2,1)S(1)}, bf16[128,2060]{0,1:T(8,128)(2,1)S(1)}, u32[]{:S(2)}, u32[]{:S(2)}) collective-permute-start(bf16[128,2060]{0,1:T(8,128)(2,1)S(1)} %get-tuple-element.97), channel_id=1, source_target_pairs={{0,8},{4,12},{8,0},{12,4},{16,24},{20,28},{24,16},{28,20},{1,9},{5... | collective-permute-start | bytes 1582088 | tf_op jit(solution)/shard_map/ppermute | solution.py:257
  742.6 38.6 %collective-permute-start.9 = (bf16[128,2060]{0,1:T(8,128)(2,1)}, bf16[128,2060]{0,1:T(8,128)(2,1)S(1)}, u32[]{:S(2)}, u32[]{:S(2)}) collective-permute-start(bf16[128,2060]{0,1:T(8,128)(2,1)} %fusion.265), channel_id=1, source_target_pairs={{0,16},{4,20},{8,24},{12,28},{16,0},{20,4},{24,8},{28,12},{1,17},{... | collective-permute-start | bytes 1582088 | tf_op jit(solution)/shard_map/ppermute | solution.py:257
  747.7 134.7 %collective-permute-start.15 = (bf16[1,512,512]{2,1,0:T(8,128)(2,1)}, bf16[1,512,512]{2,1,0:T(8,128)(2,1)}, u32[]{:S(2)}, u32[]{:S(2)}) collective-permute-start(bf16[1,512,512]{2,1,0:T(8,128)(2,1)} %dynamic-slice_convert_fusion.5), channel_id=1, source_target_pairs={{0,2},{1,3},{2,0},{3,1},{4,6},{5,7},{6,4},{7,5},{8,10},{9,11},{10,... | collective-permute-start | bytes 1572872 | tf_op jit(solution)/shard_map/ppermute | solution.py:243
  752.0 116.1 %collective-permute-start.11 = (bf16[1,128,2048]{2,1,0:T(8,128)(2,1)}, bf16[1,128,2048]{2,1,0:T(8,128)(2,1)}, u32[]{:S(2)}, u32[]{:S(2)}) collective-permute-start(bf16[1,128,2048]{2,1,0:T(8,128)(2,1)} %dynamic-slice_convert_fusion.7), channel_id=1, source_target_pairs={{0,2},{1,3},{2,0},{3,1},{4,6},{5,7},{6,4},{7,5},{8,10},{9,11},{10,... | collective-permute-start | bytes 1572872 | tf_op jit(solution)/shard_map/ppermute | solution.py:243
  753.6 37.5 %all-to-all-start.15 = ((bf16[8,128,512]{2,1,0:T(8,128)(2,1)}), bf16[8,128,512]{2,1,0:T(8,128)(2,1)S(1)}, u32[]{:S(2)}, u32[]{:S(2)}) async-start(bf16[8,128,512]{2,1,0:T(8,128)(2,1)} %bitcast.111), calls=%async_computation.15 | async-start | bytes 2097152 | tf_op jit(solution)/shard_map/all_to_all | solution.py:181
  931.8 24.1 %collective-permute-start.4 = (bf16[128,2060]{0,1:T(8,128)(2,1)S(1)}, bf16[128,2060]{0,1:T(8,128)(2,1)S(1)}, u32[]{:S(2)}, u32[]{:S(2)}) collective-permute-start(bf16[128,2060]{0,1:T(8,128)(2,1)S(1)} %fusion.264), channel_id=1, source_target_pairs={{0,16},{4,20},{8,24},{12,28},{16,0},{20,4},{24,8},{28,12},{1,17},{... | collective-permute-start | bytes 1582088 | tf_op jit(solution)/shard_map/ppermute | solution.py:257
  (299 other events, 3992.5 us)
Sparse Core Ops, SparseCore 0:
  11.9 25.2 all-gather.10
  39.3 22.5 all-gather.14
  63.5 22.5 all-gather.16
  91.1 23.0 all-gather.12
  261.9 22.9 all-gather.18
  291.8 22.9 all-gather.20

commit v4 on v3

--- a/solution.py
+++ b/solution.py
@@ -51,12 +51,24 @@
     counts = dot_first(expert_hot, earlier)
     position = jnp.sum(counts.T * expert_hot.astype(jnp.float32), axis=1).astype(jnp.int32)
     kept_mask = position < capacity
-    flat_slot = jnp.where(kept_mask, pair_expert * capacity + position, experts * capacity)
+    own = lax.axis_index("expert")
+    flat_slot = jnp.where(
+        kept_mask, (pair_expert ^ own) * capacity + position, experts * capacity
+    )
     pair_hot = (
         flat_slot[:, None] == jnp.arange(experts * capacity, dtype=jnp.int32)[None, :]
     ).astype(jnp.bfloat16)
     token_hot = pair_hot[:tok_count] + pair_hot[tok_count:]
     return pair_hot, token_hot, kept_mask
+
+
+def exchange(blocks, axis_name):
+    size = blocks.shape[0]
+    moved = [blocks[0]] + [
+        lax.ppermute(blocks[k], axis_name, [(i, i ^ k) for i in range(size)])
+        for k in range(1, size)
+    ]
+    return jnp.stack(moved)
 
 
 def forward_layer(residual, route_hot, tables, weights, experts, capacity):
@@ -94,22 +106,14 @@
         jnp.dot(normed_two, router_w, preferred_element_type=jnp.float32), axis=-1
     )
     sending = dot_first(token_hot, normed_two).astype(jnp.bfloat16)
-    received = lax.all_to_all(
-        sending.reshape(experts, capacity, D), "expert", split_axis=0, concat_axis=0, tiled=True
-    )
+    received = exchange(sending.reshape(experts, capacity, D), "expert")
     row_block = received.reshape(experts * capacity, D)
     hidden_pre = jnp.dot(row_block, in_w[0], preferred_element_type=jnp.float32)
     hidden_act = gelu_tanh(hidden_pre).astype(jnp.bfloat16)
     expert_rows = jnp.dot(hidden_act, out_w[0], preferred_element_type=jnp.float32).astype(
         jnp.bfloat16
     )
-    returned = lax.all_to_all(
-        expert_rows.reshape(experts, capacity, D),
-        "expert",
-        split_axis=0,
-        concat_axis=0,
-        tiled=True,
-    )
+    returned = exchange(expert_rows.reshape(experts, capacity, D), "expert")
     pair_rows = jnp.dot(
         pair_hot, returned.reshape(experts * capacity, D), preferred_element_type=jnp.float32
     ).reshape(TOP, tok_count, D)
@@ -170,7 +174,7 @@
         (weight_pair[:, :, None] * d_output[None]).astype(jnp.bfloat16).reshape(TOP * tok_count, D)
     )
     d_slots = dot_first(pair_hot, d_pairs).astype(jnp.bfloat16).reshape(experts, capacity, D)
-    d_expert_out = lax.all_to_all(d_slots, "expert", split_axis=0, concat_axis=0, tiled=True)
+    d_expert_out = exchange(d_slots, "expert")
     flat_out = d_expert_out.reshape(experts * capacity, D)
     hidden_act = gelu_tanh(hidden_pre).astype(jnp.bfloat16)
     g_out = dot_first(hidden_act, flat_out)
@@ -178,7 +182,7 @@
     d_pre = jax.vjp(gelu_tanh, hidden_pre)[1](d_act)[0].astype(jnp.bfloat16)
     g_in = dot_first(row_block, d_pre)
     d_rows = dot_last(d_pre, in_w[0]).astype(jnp.bfloat16).reshape(experts, capacity, D)
-    d_back = lax.all_to_all(d_rows, "expert", split_axis=0, concat_axis=0, tiled=True)
+    d_back = exchange(d_rows, "expert")
     d_pair_in = jnp.dot(
         pair_hot, d_back.reshape(experts * capacity, D), preferred_element_type=jnp.float32
     ).reshape(TOP, tok_count, D)

time: 979 us -> 1020 us (1.042)
  starting transfers between devices: 86.4 us -> 221 us
  waiting for transfers between devices: 285 us -> 226 us
  matrix products: 307 us -> 250 us
  local copies, waits for them, and re-layouts: 195 us -> 215 us
    ppermute x0 -> x112, starting transfers between devices: none -> 211 us  [exchange(): lax.ppermute(blocks[k], axis_name, [(i, i ^ k) for i in range(size)])]
    all_to_all x16 -> x0, waiting for transfers between devices: 169 us -> none  [the longest x4 59 us: forward_layer(): lax.all_to_all(sending.reshape(experts, capacity, D), 'expert', split_axi...]
    ppermute x0 -> x112, waiting for transfers between devices: none -> 116 us  [exchange(): lax.ppermute(blocks[k], axis_name, [(i, i ^ k) for i in range(size)])]
    all_to_all x16 -> x0, starting transfers between devices: 72.7 us -> none  [the longest x4 18.8 us: forward_layer(): lax.all_to_all(expert_rows.reshape(experts, capacity, D), 'expert', split...]
    ppermute x12, waiting for transfers between devices: 15.4 us -> 51.8 us  [halving_scatter(): lax.ppermute(give.astype(jnp.bfloat16), axis_name, [(i, i ^ bit) for i in...]
    ppermute x6, waiting for transfers between devices: 89.3 us -> 57.2 us  [doubling_sum(): lax.ppermute(own.astype(jnp.bfloat16), axis_name, [(i, i ^ bit) for i in...]
    unnamed x599 -> x737, local copies, waits for them, and re-layouts: 48.7 us -> 79.8 us
    dot_general x30, matrix products: 95.2 us -> 66.1 us  [dot_first(): lax.dot_general(left, right, (((0,), (0,)), ((), ())), preferred_element_...]
  transfers between devices with their start and end apart: 40 -> 136, of which waited for: 21 -> 43; matrix products, arithmetic and copies ran while one was open for 42% -> 48% of each run, Pallas kernels for 0% -> 0%
where the time goes in v4:
time: 1020 us; the launch traced here: 1010 us
  matrix products  250 us (25%)
  waiting for transfers between devices  226 us (22%)
  starting transfers between devices  221 us (22%)
  local copies, waits for them, and re-layouts  215 us (21%)
  other arithmetic  68.1 us (7%)
  between operations  20 us (2%)
    ppermute x112, starting transfers between devices, exchange(): lax.ppermute(blocks[k], axis_name, [(i, i ^ k) for i in range(size)])  211 us
    ppermute x112, waiting for transfers between devices, exchange(): lax.ppermute(blocks[k], axis_name, [(i, i ^ k) for i in range(size)])  116 us
    unnamed x737, local copies, waits for them, and re-layouts  79.8 us
    dot_general x30, matrix products, dot_first(): lax.dot_general(left, right, (((0,), (0,)), ((), ())), preferred_element_...  66.1 us
    dot_general x20, matrix products, dot_last(): lax.dot_general(left, right, (((1,), (1,)), ((), ())), preferred_element_...  64.9 us
    ppermute x6, waiting for transfers between devices, doubling_sum(): lax.ppermute(own.astype(jnp.bfloat16), axis_name, [(i, i ^ bit) for i in...  57.2 us
    ppermute x12, waiting for transfers between devices, halving_scatter(): lax.ppermute(give.astype(jnp.bfloat16), axis_name, [(i, i ^ bit) for i in...  51.8 us
    dot_general x4, matrix products, forward_layer(): jnp.dot(hidden_act, out_w[0], preferred_element_type=jnp.float32)  29.1 us
  transfers between devices with their start and end apart: 136, of which 43 were waited for; matrix products, arithmetic and copies ran while one was open for 48% of the time, Pallas kernels for 0%

profile of v4, /device:TPU:0, one launch (start us, length us, event | category | flops | bytes accessed | tf_op | source)
XLA Modules:
  0.0 1006.6 jit_solution(2051286043216994570)
XLA Ops:
  17.7 6.1 all_gather.21
  119.9 7.5 fusion.102
  127.4 18.3 %fusion.146 = bf16[1024,512]{1,0:T(8,128)(2,1)S(1)} fusion(bf16[1,1,2048,512]{3,2,1,0:T(8,128)(2,1)} %all-gather.17.cloned.1.call-done, f32[1024,2048]{1,0:T(8,128)} %fusion.102), kind=kOutput, calls=%fused_computation.209 | convolution fusion | flops 2166882304 | bytes 11534336 | tf_op jit(solution)/shard_map/dot_general | solution.py:113
  163.6 5.8 multiply_convert_fusion.1
  284.8 7.0 collective-permute-done.46
  295.3 7.3 collective-permute-start.88
  324.9 9.9 multiply_convert_fusion
  334.9 9.9 fusion.27
  366.4 5.6 fusion.82
  380.5 8.9 fusion.13
  391.9 6.1 fusion.158
  402.0 5.8 fusion.422
  416.3 6.6 convolution_add_fusion.2
  439.4 7.2 collective-permute-done.52
  448.4 8.3 collective-permute-done.53
  457.0 7.1 collective-permute-done.54
  466.8 6.0 collective-permute-done.55
  491.7 9.9 collective-permute-start.67
  657.1 9.4 fusion.20
  674.9 7.4 collective-permute-done.73
  690.0 7.6 fusion.6
  727.0 5.7 collective-permute-done.108
  868.9 12.3 %collective-permute-done.129 = bf16[1,512,512]{2,1,0:T(8,128)(2,1)S(1)} collective-permute-done((bf16[1,512,512]{2,1,0:T(8,128)(2,1)S(1)}, bf16[1,512,512]{2,1,0:T(8,128)(2,1)S(1)}, u32[]{:S(2)}, u32[]{:S(2)}) %collective-permute-start.129) | collective-permute-done | bytes 524320 | tf_op jit(solution)/shard_map/ppermute | solution.py:247
  881.6 11.0 %collective-permute-done.118 = bf16[1,128,2060]{1,2,0:T(8,128)(2,1)S(1)} collective-permute-done((bf16[1,128,2060]{1,2,0:T(8,128)(2,1)S(1)}, bf16[1,128,2060]{1,2,0:T(8,128)(2,1)S(1)}, u32[]{:S(2)}, u32[]{:S(2)}) %collective-permute-start.118) | collective-permute-done | bytes 527392 | tf_op jit(solution)/shard_map/ppermute | solution.py:247
  893.5 10.3 %collective-permute-done.123 = bf16[1,128,2048]{2,1,0:T(8,128)(2,1)S(1)} collective-permute-done((bf16[1,128,2048]{2,1,0:T(8,128)(2,1)S(1)}, bf16[1,128,2048]{2,1,0:T(8,128)(2,1)S(1)}, u32[]{:S(2)}, u32[]{:S(2)}) %collective-permute-start.123) | collective-permute-done | bytes 524320 | tf_op jit(solution)/shard_map/ppermute | solution.py:247
  903.9 11.1 %collective-permute-done.127 = bf16[1,512,512]{2,1,0:T(8,128)(2,1)S(1)} collective-permute-done((bf16[1,512,512]{2,1,0:T(8,128)(2,1)S(1)}, bf16[1,512,512]{2,1,0:T(8,128)(2,1)S(1)}, u32[]{:S(2)}, u32[]{:S(2)}) %collective-permute-start.127) | collective-permute-done | bytes 524320 | tf_op jit(solution)/shard_map/ppermute | solution.py:247
  918.1 7.1 collective-permute-done.113
  925.3 8.4 fusion.243
  934.9 11.9 %collective-permute-done.114 = bf16[128,2060]{0,1:T(8,128)(2,1)S(1)} collective-permute-done((bf16[128,2060]{0,1:T(8,128)(2,1)S(1)}, bf16[128,2060]{0,1:T(8,128)(2,1)S(1)}, u32[]{:S(2)}, u32[]{:S(2)}) %collective-permute-start.114) | collective-permute-done | bytes 527392 | tf_op jit(solution)/shard_map/ppermute | solution.py:261
  949.2 19.9 %collective-permute-done.115 = bf16[128,2060]{0,1:T(8,128)(2,1)S(1)} collective-permute-done((bf16[128,2060]{0,1:T(8,128)(2,1)S(1)}, bf16[128,2060]{0,1:T(8,128)(2,1)S(1)}, u32[]{:S(2)}, u32[]{:S(2)}) %collective-permute-start.115) | collective-permute-done | bytes 527392 | tf_op jit(solution)/shard_map/ppermute | solution.py:261
  969.4 15.1 %collective-permute-done.121 = bf16[128,2060]{0,1:T(8,128)(2,1)S(1)} collective-permute-done((bf16[128,2060]{0,1:T(8,128)(2,1)S(1)}, bf16[128,2060]{0,1:T(8,128)(2,1)S(1)}, u32[]{:S(2)}, u32[]{:S(2)}) %collective-permute-start.121) | collective-permute-done | bytes 527392 | tf_op jit(solution)/shard_map/ppermute | solution.py:261
  984.8 9.7 collective-permute-done.116
  (1365 shorter events, 696.4 us)
Async XLA Ops:
  10.4 109.5 %all-gather.15.cloned.1.call-start = ((), (), s32[]{:S(2)}) async-start(), calls=%async_computation.2 | async-start | bytes 2621440 | tf_op jit(solution)/shard_map/all_gather | solution.py:342
  11.6 115.8 %all-gather.17.cloned.1.call-start = ((), (), s32[]{:S(2)}) async-start(), calls=%async_computation.3 | async-start | bytes 2621440 | tf_op jit(solution)/shard_map/all_gather | solution.py:343
  12.7 195.6 %all-gather.13.cloned.1.call-start = ((), (), s32[]{:S(2)}) async-start(), calls=%async_computation.1 | async-start | bytes 2621440 | tf_op jit(solution)/shard_map/all_gather | solution.py:327
  13.7 311.3 %all-gather.19.cloned.1.call-start = ((), (), s32[]{:S(2)}) async-start(), calls=%async_computation.4 | async-start | bytes 2621440 | tf_op jit(solution)/shard_map/all_gather | solution.py:342
  14.3 320.6 %all-gather.21.cloned.1.call-start = ((), (), s32[]{:S(2)}) async-start(), calls=%async_computation.5 | async-start | bytes 2621440 | tf_op jit(solution)/shard_map/all_gather | solution.py:343
  101.7 44.2 %collective-permute-start.28 = (bf16[128,512]{1,0:T(8,128)(2,1)}, bf16[128,512]{1,0:T(8,128)(2,1)}, u32[]{:S(2)}, u32[]{:S(2)}) collective-permute-start(bf16[128,512]{1,0:T(8,128)(2,1)} %get-tuple-element.256), channel_id=1, source_target_pairs={{0,4},{4,0},{8,12},{12,8},{16,20},{20,16},{24,28},{28,24},{1,5},{5... | collective-permute-start | bytes 393224 | tf_op jit(solution)/shard_map/ppermute | solution.py:68
  105.0 44.2 %collective-permute-start.29 = (bf16[128,512]{1,0:T(8,128)(2,1)}, bf16[128,512]{1,0:T(8,128)(2,1)}, u32[]{:S(2)}, u32[]{:S(2)}) collective-permute-start(bf16[128,512]{1,0:T(8,128)(2,1)} %get-tuple-element.255), channel_id=1, source_target_pairs={{0,8},{4,12},{8,0},{12,4},{16,24},{20,28},{24,16},{28,20},{1,9},{5... | collective-permute-start | bytes 393224 | tf_op jit(solution)/shard_map/ppermute | solution.py:68
  111.2 43.3 %collective-permute-start.30 = (bf16[128,512]{1,0:T(8,128)(2,1)S(1)}, bf16[128,512]{1,0:T(8,128)(2,1)}, u32[]{:S(2)}, u32[]{:S(2)}) collective-permute-start(bf16[128,512]{1,0:T(8,128)(2,1)S(1)} %get-tuple-element.254), channel_id=1, source_target_pairs={{0,12},{4,8},{8,4},{12,0},{16,28},{20,24},{24,20},{28,16},{1,13},{... | collective-permute-start | bytes 393224 | tf_op jit(solution)/shard_map/ppermute | solution.py:68
  113.9 41.6 %collective-permute-start.31 = (bf16[128,512]{1,0:T(8,128)(2,1)S(1)}, bf16[128,512]{1,0:T(8,128)(2,1)}, u32[]{:S(2)}, u32[]{:S(2)}) collective-permute-start(bf16[128,512]{1,0:T(8,128)(2,1)S(1)} %get-tuple-element.253), channel_id=1, source_target_pairs={{0,16},{4,20},{8,24},{12,28},{16,0},{20,4},{24,8},{28,12},{1,17},{... | collective-permute-start | bytes 393224 | tf_op jit(solution)/shard_map/ppermute | solution.py:68
  118.0 38.6 %collective-permute-start.32 = (bf16[128,512]{1,0:T(8,128)(2,1)S(1)}, bf16[128,512]{1,0:T(8,128)(2,1)}, u32[]{:S(2)}, u32[]{:S(2)}) collective-permute-start(bf16[128,512]{1,0:T(8,128)(2,1)S(1)} %get-tuple-element.252), channel_id=1, source_target_pairs={{0,20},{4,16},{8,28},{12,24},{16,4},{20,0},{24,12},{28,8},{1,21},{... | collective-permute-start | bytes 393224 | tf_op jit(solution)/shard_map/ppermute | solution.py:68
  309.6 40.4 %collective-permute-start.14 = (bf16[128,512]{1,0:T(8,128)(2,1)}, bf16[128,512]{1,0:T(8,128)(2,1)}, u32[]{:S(2)}, u32[]{:S(2)}) collective-permute-start(bf16[128,512]{1,0:T(8,128)(2,1)} %get-tuple-element.210), channel_id=1, source_target_pairs={{0,4},{4,0},{8,12},{12,8},{16,20},{20,16},{24,28},{28,24},{1,5},{5... | collective-permute-start | bytes 393224 | tf_op jit(solution)/shard_map/ppermute | solution.py:68
  310.9 40.7 %collective-permute-start.15 = (bf16[128,512]{1,0:T(8,128)(2,1)}, bf16[128,512]{1,0:T(8,128)(2,1)}, u32[]{:S(2)}, u32[]{:S(2)}) collective-permute-start(bf16[128,512]{1,0:T(8,128)(2,1)} %get-tuple-element.209), channel_id=1, source_target_pairs={{0,8},{4,12},{8,0},{12,4},{16,24},{20,28},{24,16},{28,20},{1,9},{5... | collective-permute-start | bytes 393224 | tf_op jit(solution)/shard_map/ppermute | solution.py:68
  314.4 41.6 %collective-permute-start.16 = (bf16[128,512]{1,0:T(8,128)(2,1)}, bf16[128,512]{1,0:T(8,128)(2,1)}, u32[]{:S(2)}, u32[]{:S(2)}) collective-permute-start(bf16[128,512]{1,0:T(8,128)(2,1)} %get-tuple-element.208), channel_id=1, source_target_pairs={{0,12},{4,8},{8,4},{12,0},{16,28},{20,24},{24,20},{28,16},{1,13},{... | collective-permute-start | bytes 393224 | tf_op jit(solution)/shard_map/ppermute | solution.py:68
  315.1 43.2 %collective-permute-start.17 = (bf16[128,512]{1,0:T(8,128)(2,1)}, bf16[128,512]{1,0:T(8,128)(2,1)}, u32[]{:S(2)}, u32[]{:S(2)}) collective-permute-start(bf16[128,512]{1,0:T(8,128)(2,1)} %get-tuple-element.207), channel_id=1, source_target_pairs={{0,16},{4,20},{8,24},{12,28},{16,0},{20,4},{24,8},{28,12},{1,17},{... | collective-permute-start | bytes 393224 | tf_op jit(solution)/shard_map/ppermute | solution.py:68
  319.3 40.1 %collective-permute-start.18 = (bf16[128,512]{1,0:T(8,128)(2,1)}, bf16[128,512]{1,0:T(8,128)(2,1)}, u32[]{:S(2)}, u32[]{:S(2)}) collective-permute-start(bf16[128,512]{1,0:T(8,128)(2,1)} %get-tuple-element.206), channel_id=1, source_target_pairs={{0,20},{4,16},{8,28},{12,24},{16,4},{20,0},{24,12},{28,8},{1,21},{... | collective-permute-start | bytes 393224 | tf_op jit(solution)/shard_map/ppermute | solution.py:68
  407.8 70.7 %collective-permute-start.91 = (bf16[128,512]{1,0:T(8,128)(2,1)S(1)}, bf16[128,512]{1,0:T(8,128)(2,1)S(1)}, u32[]{:S(2)}, u32[]{:S(2)}) collective-permute-start(bf16[128,512]{1,0:T(8,128)(2,1)S(1)} %get-tuple-element.189), channel_id=1, source_target_pairs={{0,4},{4,0},{8,12},{12,8},{16,20},{20,16},{24,28},{28,24},{1,5},{5... | collective-permute-start | bytes 393224 | tf_op jit(solution)/shard_map/ppermute | solution.py:68
  409.3 73.0 %collective-permute-start.92 = (bf16[128,512]{1,0:T(8,128)(2,1)S(1)}, bf16[128,512]{1,0:T(8,128)(2,1)S(1)}, u32[]{:S(2)}, u32[]{:S(2)}) collective-permute-start(bf16[128,512]{1,0:T(8,128)(2,1)S(1)} %get-tuple-element.188), channel_id=1, source_target_pairs={{0,8},{4,12},{8,0},{12,4},{16,24},{20,28},{24,16},{28,20},{1,9},{5... | collective-permute-start | bytes 393224 | tf_op jit(solution)/shard_map/ppermute | solution.py:68
  410.9 74.4 %collective-permute-start.93 = (bf16[128,512]{1,0:T(8,128)(2,1)S(1)}, bf16[128,512]{1,0:T(8,128)(2,1)S(1)}, u32[]{:S(2)}, u32[]{:S(2)}) collective-permute-start(bf16[128,512]{1,0:T(8,128)(2,1)S(1)} %get-tuple-element.187), channel_id=1, source_target_pairs={{0,12},{4,8},{8,4},{12,0},{16,28},{20,24},{24,20},{28,16},{1,13},{... | collective-permute-start | bytes 393224 | tf_op jit(solution)/shard_map/ppermute | solution.py:68
  411.3 74.0 %collective-permute-start.94 = (bf16[128,512]{1,0:T(8,128)(2,1)S(1)}, bf16[128,512]{1,0:T(8,128)(2,1)S(1)}, u32[]{:S(2)}, u32[]{:S(2)}) collective-permute-start(bf16[128,512]{1,0:T(8,128)(2,1)S(1)} %get-tuple-element.186), channel_id=1, source_target_pairs={{0,16},{4,20},{8,24},{12,28},{16,0},{20,4},{24,8},{28,12},{1,17},{... | collective-permute-start | bytes 393224 | tf_op jit(solution)/shard_map/ppermute | solution.py:68
  519.1 333.0 %collective-permute-start.124 = (bf16[2,128,2048]{2,1,0:T(8,128)(2,1)}, bf16[2,128,2048]{2,1,0:T(8,128)(2,1)}, u32[]{:S(2)}, u32[]{:S(2)}) collective-permute-start(bf16[2,128,2048]{2,1,0:T(8,128)(2,1)} %fusion.245), channel_id=1, source_target_pairs={{0,1},{1,0},{2,3},{3,2},{4,5},{5,4},{6,7},{7,6},{8,9},{9,8},{10,11... | collective-permute-start | bytes 3145736 | tf_op jit(solution)/shard_map/ppermute | solution.py:247
  519.2 335.9 %collective-permute-start.128 = (bf16[2,512,512]{2,1,0:T(8,128)(2,1)}, bf16[2,512,512]{2,1,0:T(8,128)(2,1)}, u32[]{:S(2)}, u32[]{:S(2)}) collective-permute-start(bf16[2,512,512]{2,1,0:T(8,128)(2,1)} %fusion.247), channel_id=1, source_target_pairs={{0,1},{1,0},{2,3},{3,2},{4,5},{5,4},{6,7},{7,6},{8,9},{9,8},{10,11... | collective-permute-start | bytes 3145736 | tf_op jit(solution)/shard_map/ppermute | solution.py:247
  597.8 35.9 %collective-permute-start.98 = (bf16[128,512]{1,0:T(8,128)(2,1)}, bf16[128,512]{1,0:T(8,128)(2,1)}, u32[]{:S(2)}, u32[]{:S(2)}) collective-permute-start(bf16[128,512]{1,0:T(8,128)(2,1)} %get-tuple-element.182), channel_id=1, source_target_pairs={{0,4},{4,0},{8,12},{12,8},{16,20},{20,16},{24,28},{28,24},{1,5},{5... | collective-permute-start | bytes 393224 | tf_op jit(solution)/shard_map/ppermute | solution.py:68
  598.7 38.6 %collective-permute-start.99 = (bf16[128,512]{1,0:T(8,128)(2,1)}, bf16[128,512]{1,0:T(8,128)(2,1)}, u32[]{:S(2)}, u32[]{:S(2)}) collective-permute-start(bf16[128,512]{1,0:T(8,128)(2,1)} %get-tuple-element.181), channel_id=1, source_target_pairs={{0,8},{4,12},{8,0},{12,4},{16,24},{20,28},{24,16},{28,20},{1,9},{5... | collective-permute-start | bytes 393224 | tf_op jit(solution)/shard_map/ppermute | solution.py:68
  600.6 39.9 %collective-permute-start.100 = (bf16[128,512]{1,0:T(8,128)(2,1)}, bf16[128,512]{1,0:T(8,128)(2,1)}, u32[]{:S(2)}, u32[]{:S(2)}) collective-permute-start(bf16[128,512]{1,0:T(8,128)(2,1)} %get-tuple-element.180), channel_id=1, source_target_pairs={{0,12},{4,8},{8,4},{12,0},{16,28},{20,24},{24,20},{28,16},{1,13},{... | collective-permute-start | bytes 393224 | tf_op jit(solution)/shard_map/ppermute | solution.py:68
  684.9 172.1 %collective-permute-start.117 = (bf16[2,128,2060]{1,0,2:T(2,128)(2,1)}, bf16[2,128,2060]{1,0,2:T(2,128)(2,1)}, u32[]{:S(2)}, u32[]{:S(2)}) collective-permute-start(bf16[2,128,2060]{1,0,2:T(2,128)(2,1)} %bitcast.259), channel_id=1, source_target_pairs={{0,1},{1,0},{2,3},{3,2},{4,5},{5,4},{6,7},{7,6},{8,9},{9,8},{10,11... | collective-permute-start | bytes 3164168 | tf_op jit(solution)/shard_map/ppermute | solution.py:247
  765.0 95.5 %collective-permute-start.122 = (bf16[2,128,2048]{2,1,0:T(8,128)(2,1)}, bf16[2,128,2048]{2,1,0:T(8,128)(2,1)}, u32[]{:S(2)}, u32[]{:S(2)}) collective-permute-start(bf16[2,128,2048]{2,1,0:T(8,128)(2,1)} %fusion.244), channel_id=1, source_target_pairs={{0,1},{1,0},{2,3},{3,2},{4,5},{5,4},{6,7},{7,6},{8,9},{9,8},{10,11... | collective-permute-start | bytes 3145736 | tf_op jit(solution)/shard_map/ppermute | solution.py:247
  769.6 93.1 %collective-permute-start.126 = (bf16[2,512,512]{2,1,0:T(8,128)(2,1)}, bf16[2,512,512]{2,1,0:T(8,128)(2,1)}, u32[]{:S(2)}, u32[]{:S(2)}) collective-permute-start(bf16[2,512,512]{2,1,0:T(8,128)(2,1)} %fusion.246), channel_id=1, source_target_pairs={{0,1},{1,0},{2,3},{3,2},{4,5},{5,4},{6,7},{7,6},{8,9},{9,8},{10,11... | collective-permute-start | bytes 3145736 | tf_op jit(solution)/shard_map/ppermute | solution.py:247
  862.7 41.0 %collective-permute-start.123 = (bf16[1,128,2048]{2,1,0:T(8,128)(2,1)S(1)}, bf16[1,128,2048]{2,1,0:T(8,128)(2,1)S(1)}, u32[]{:S(2)}, u32[]{:S(2)}) collective-permute-start(bf16[1,128,2048]{2,1,0:T(8,128)(2,1)S(1)} %dynamic-slice_convert_fusion.7), channel_id=1, source_target_pairs={{0,2},{1,3},{2,0},{3,1},{4,6},{5,7},{6,4},{7,5},{8,10},{9,11},{10,... | collective-permute-start | bytes 1572872 | tf_op jit(solution)/shard_map/ppermute | solution.py:247
  866.0 49.0 %collective-permute-start.127 = (bf16[1,512,512]{2,1,0:T(8,128)(2,1)S(1)}, bf16[1,512,512]{2,1,0:T(8,128)(2,1)S(1)}, u32[]{:S(2)}, u32[]{:S(2)}) collective-permute-start(bf16[1,512,512]{2,1,0:T(8,128)(2,1)S(1)} %dynamic-slice_convert_fusion.5), channel_id=1, source_target_pairs={{0,2},{1,3},{2,0},{3,1},{4,6},{5,7},{6,4},{7,5},{8,10},{9,11},{10,... | collective-permute-start | bytes 1572872 | tf_op jit(solution)/shard_map/ppermute | solution.py:247
  881.2 44.1 %collective-permute-start.113 = (bf16[1,128,2060]{1,2,0:T(8,128)(2,1)S(1)}, bf16[1,128,2060]{1,2,0:T(8,128)(2,1)S(1)}, u32[]{:S(2)}, u32[]{:S(2)}) collective-permute-start(bf16[1,128,2060]{1,2,0:T(8,128)(2,1)S(1)} %copy.500), channel_id=1, source_target_pairs={{0,2},{1,3},{2,0},{3,1},{4,6},{5,7},{6,4},{7,5},{8,10},{9,11},{10,... | collective-permute-start | bytes 1582088 | tf_op jit(solution)/shard_map/ppermute | solution.py:247
  892.6 41.9 %collective-permute-start.119 = (bf16[128,2060]{0,1:T(8,128)(2,1)S(1)}, bf16[128,2060]{0,1:T(8,128)(2,1)S(1)}, u32[]{:S(2)}, u32[]{:S(2)}) collective-permute-start(bf16[128,2060]{0,1:T(8,128)(2,1)S(1)} %bitcast_convert_fusion.5), channel_id=1, source_target_pairs={{0,4},{4,0},{8,12},{12,8},{16,20},{20,16},{24,28},{28,24},{1,5},{5... | collective-permute-start | bytes 1582088 | tf_op jit(solution)/shard_map/ppermute | solution.py:261
  947.7 36.8 %collective-permute-start.121 = (bf16[128,2060]{0,1:T(8,128)(2,1)S(1)}, bf16[128,2060]{0,1:T(8,128)(2,1)S(1)}, u32[]{:S(2)}, u32[]{:S(2)}) collective-permute-start(bf16[128,2060]{0,1:T(8,128)(2,1)S(1)} %fusion.265), channel_id=1, source_target_pairs={{0,16},{4,20},{8,24},{12,28},{16,0},{20,4},{24,8},{28,12},{1,17},{... | collective-permute-start | bytes 1582088 | tf_op jit(solution)/shard_map/ppermute | solution.py:261
  (408 other events, 4513.9 us)
Sparse Core Ops, SparseCore 0:
  10.5 25.3 all-gather.10
  37.4 22.6 all-gather.14
  61.7 22.5 all-gather.16
  85.7 22.5 all-gather.12
  109.8 22.5 all-gather.18
  133.8 22.5 all-gather.20

commit v5 on v3

--- a/solution.py
+++ b/solution.py
@@ -262,13 +262,36 @@
     return total
 
 
-def reduce_layer(layer_grads):
+def doubling_gather(part, axis_name):
+    size = lax.axis_size(axis_name)
+    me = lax.axis_index(axis_name)
+    held = part[None]
+    bit = size // 2
+    steps = 0
+    while bit >= 1:
+        got = lax.ppermute(held, axis_name, [(i, i ^ bit) for i in range(size)])
+        low = (me // bit) % 2 == 0
+        held = jnp.where(low, jnp.concatenate([held, got]), jnp.concatenate([got, held]))
+        bit //= 2
+        steps += 1
+    held = held.reshape((2,) * steps + part.shape)
+    held = held.transpose(tuple(reversed(range(steps))) + tuple(range(steps, held.ndim)))
+    return held.reshape((size * part.shape[0],) + part.shape[1:])
+
+
+def reduce_layer(layer_grads, late):
     g_gain, g_shift, g_qkv, g_proj, g_router, g_in, g_out = layer_grads
     qkv_cols = g_qkv.shape[1]
     proj_cols = g_proj.shape[1]
     small = jnp.concatenate([g_gain.T, g_shift.T, g_router], axis=1)
     shared = jnp.concatenate([g_qkv, g_proj, small], axis=1)
-    shared = doubling_sum(halving_scatter(shared, "shard"), "expert")
+    shared = halving_scatter(shared, "shard")
+    if late:
+        owned = halving_scatter(shared, "expert")
+        owned = lax.reduce_precision(owned, exponent_bits=8, mantissa_bits=7)
+        shared = doubling_gather(owned.astype(jnp.bfloat16), "expert").astype(jnp.float32)
+    else:
+        shared = lax.psum(shared.astype(jnp.bfloat16), "expert").astype(jnp.float32)
     tail = shared[:, qkv_cols + proj_cols :]
     return [
         tail[:, 0:2].T,
@@ -365,7 +388,7 @@
                 layer_sum = layer_grads
             else:
                 layer_sum = tuple(old + new for old, new in zip(layer_sum, layer_grads))
-        reduced[layer_index] = reduce_layer(layer_sum)
+        reduced[layer_index] = reduce_layer(layer_sum, layer_index == 0)
     outs = [jnp.stack([reduced[l][k] for l in range(LAYERS)]) for k in range(7)]
     d_tokens = jnp.concatenate(d_residuals, axis=0)
     return (activations, d_tokens, *outs)

time: 979 us -> 938 us (0.958)
  waiting for transfers between devices: 285 us -> 252 us
    ppermute x6 -> x3, waiting for transfers between devices: 89.3 us -> 13.6 us  [doubling_gather(): got = lax.ppermute(held, axis_name, [(i, i ^ bit) for i in range(size)])]
    ppermute x12 -> x15, waiting for transfers between devices: 15.4 us -> 31.4 us  [halving_scatter(): lax.ppermute(give.astype(jnp.bfloat16), axis_name, [(i, i ^ bit) for i in...]
    all_to_all x4, waiting for transfers between devices: 35 us -> 48.9 us  [backward_layer(): lax.all_to_all(d_rows, 'expert', split_axis=0, concat_axis=0, tiled=True)]
    psum x0 -> x1, waiting for transfers between devices: none -> 10.4 us  [reduce_layer(): shared = lax.psum(shared.astype(jnp.bfloat16), 'expert').astype(jnp.float32)]
    unnamed x599 -> x594, local copies, waits for them, and re-layouts: 48.7 us -> 57.4 us
  transfers between devices with their start and end apart: 40 -> 41, of which waited for: 21 -> 26; matrix products, arithmetic and copies ran while one was open for 42% -> 44% of each run, Pallas kernels for 0% -> 0%
where the time goes in v5:
time: 938 us; the launch traced here: 927 us
  matrix products  311 us (33%)
  waiting for transfers between devices  252 us (27%)
  local copies, waits for them, and re-layouts  195 us (21%)
  starting transfers between devices  81 us (9%)
  other arithmetic  63.3 us (7%)
  between operations  18.5 us (2%)
    dot_general x30, matrix products, dot_first(): lax.dot_general(left, right, (((0,), (0,)), ((), ())), preferred_element_...  101 us
    dot_general x20, matrix products, dot_last(): lax.dot_general(left, right, (((1,), (1,)), ((), ())), preferred_element_...  75.7 us
    all_to_all x4, waiting for transfers between devices, forward_layer(): lax.all_to_all(sending.reshape(experts, capacity, D), 'expert', split_axi...  59 us
    unnamed x594, local copies, waits for them, and re-layouts  57.4 us
    all_to_all x4, waiting for transfers between devices, backward_layer(): lax.all_to_all(d_rows, 'expert', split_axis=0, concat_axis=0, tiled=True)  48.9 us
    all_to_all x4, waiting for transfers between devices, forward_layer(): lax.all_to_all(expert_rows.reshape(experts, capacity, D), 'expert', split...  39.7 us
    all_to_all x4, waiting for transfers between devices, backward_layer(): lax.all_to_all(d_slots, 'expert', split_axis=0, concat_axis=0, tiled=True)  37.8 us
    dot_general x4, matrix products, forward_layer(): hidden_pre = jnp.dot(row_block, in_w[0], preferred_element_type=jnp.float32)  31.8 us
  transfers between devices with their start and end apart: 41, of which 26 were waited for; matrix products, arithmetic and copies ran while one was open for 44% of the time, Pallas kernels for 0%

profile of v5, /device:TPU:0, one launch (start us, length us, event | category | flops | bytes accessed | tf_op | source)
XLA Modules:
  0.0 926.7 jit_solution(18168053945592269285)
XLA Ops:
  27.4 9.7 %all-gather.11.cloned.1.call-done = bf16[512,2048]{1,0:T(8,128)(2,1)} async-done(((bf16[128,2048]{1,0:T(8,128)(2,1)}), bf16[512,2048]{1,0:T(8,128)(2,1)}) %all-gather.11.cloned.1.call-update) | async-done | bytes 2097168 | tf_op jit(solution)/shard_map/all_gather | solution.py:346
  96.6 18.5 %all-to-all-done.4 = bf16[8,128,512]{2,1,0:T(8,128)(2,1)S(1)} async-done(((bf16[8,128,512]{2,1,0:T(8,128)(2,1)}), bf16[8,128,512]{2,1,0:T(8,128)(2,1)S(1)}, u32[]{:S(2)}, u32[]{:S(2)}) %all-to-all-start.4) | async-done | bytes 1048608 | tf_op jit(solution)/shard_map/all_to_all | solution.py:97
  120.9 7.6 fusion.100
  128.5 7.7 fusion.149
  136.2 9.7 %all-to-all-done = bf16[8,128,512]{2,1,0:T(8,128)(2,1)S(1)} async-done(((bf16[8,128,512]{2,1,0:T(8,128)(2,1)}), bf16[8,128,512]{2,1,0:T(8,128)(2,1)S(1)}, u32[]{:S(2)}, u32[]{:S(2)}) %all-to-all-start) | async-done | bytes 1048608 | tf_op jit(solution)/shard_map/all_to_all | solution.py:97
  150.5 7.7 multiply_convert_fusion.3
  163.4 12.3 %all-to-all-done.5 = bf16[8,128,512]{2,1,0:T(8,128)(2,1)} async-done(((bf16[8,128,512]{2,1,0:T(8,128)(2,1)}), bf16[8,128,512]{2,1,0:T(8,128)(2,1)}, u32[]{:S(2)}, u32[]{:S(2)}) %all-to-all-start.5) | async-done | bytes 1048608 | tf_op jit(solution)/shard_map/all_to_all | solution.py:106
  184.6 20.9 %all-to-all-done.1 = bf16[8,128,512]{2,1,0:T(8,128)(2,1)S(1)} async-done(((bf16[8,128,512]{2,1,0:T(8,128)(2,1)}), bf16[8,128,512]{2,1,0:T(8,128)(2,1)S(1)}, u32[]{:S(2)}, u32[]{:S(2)}) %all-to-all-start.1) | async-done | bytes 1048608 | tf_op jit(solution)/shard_map/all_to_all | solution.py:106
  273.6 11.6 %all-to-all-done.2 = bf16[8,128,512]{2,1,0:T(8,128)(2,1)} async-done(((bf16[8,128,512]{2,1,0:T(8,128)(2,1)}), bf16[8,128,512]{2,1,0:T(8,128)(2,1)}, u32[]{:S(2)}, u32[]{:S(2)}) %all-to-all-start.2) | async-done | bytes 1048608 | tf_op jit(solution)/shard_map/all_to_all | solution.py:97
  300.9 14.1 %all-to-all-done.8 = bf16[8,128,512]{2,1,0:T(8,128)(2,1)} async-done(((bf16[8,128,512]{2,1,0:T(8,128)(2,1)}), bf16[8,128,512]{2,1,0:T(8,128)(2,1)}, u32[]{:S(2)}, u32[]{:S(2)}) %all-to-all-start.8) | async-done | bytes 1048608 | tf_op jit(solution)/shard_map/all_to_all | solution.py:173
  325.4 19.2 %all-to-all-done.6 = bf16[8,128,512]{2,1,0:T(8,128)(2,1)} async-done(((bf16[8,128,512]{2,1,0:T(8,128)(2,1)}), bf16[8,128,512]{2,1,0:T(8,128)(2,1)}, u32[]{:S(2)}, u32[]{:S(2)}) %all-to-all-start.6) | async-done | bytes 1048608 | tf_op jit(solution)/shard_map/all_to_all | solution.py:97
  349.1 8.8 multiply_convert_fusion.2
  357.9 7.7 fusion.80
  371.2 6.2 fusion.158
  377.4 6.3 all-to-all-start.3
  383.7 9.1 convolution_add_fusion.2
  393.9 11.1 %fusion.27 = bf16[1024,2048]{1,0:T(8,128)(2,1)S(1)} fusion(f32[1024,2048]{1,0:T(8,128)} %fusion.80, bf16[1024,512]{1,0:T(8,128)(2,1)} %bitcast.98, bf16[1,1,2048,512]{3,2,1,0:T(8,128)(2,1)S(1)} %copy-done.280), kind=kOutput, calls=%fused_computation.35 | convolution fusion | flops 2189426688 | bytes 15728640 | tf_op jit(solution)/shard_map/dot_general | solution.py:38
  405.1 9.6 %fusion.13 = bf16[1024,2048]{1,0:T(8,128)(2,1)S(1)} fusion(f32[1024,2048]{1,0:T(8,128)S(1)} %bitcast.660, bf16[1024,512]{1,0:T(8,128)(2,1)} %bitcast.74, bf16[1,1,2048,512]{3,2,1,0:T(8,128)(2,1)S(1)} %copy-done.280), kind=kOutput, calls=%fused_computation.21 | convolution fusion | flops 2189426688 | bytes 15728640 | tf_op jit(solution)/shard_map/dot_general | solution.py:38
  434.7 7.9 fusion.161
  449.8 11.5 %all-to-all-done.9 = bf16[8,128,512]{2,1,0:T(8,128)(2,1)} async-done(((bf16[8,128,512]{2,1,0:T(8,128)(2,1)}), bf16[8,128,512]{2,1,0:T(8,128)(2,1)}, u32[]{:S(2)}, u32[]{:S(2)}) %all-to-all-start.9) | async-done | bytes 1048608 | tf_op jit(solution)/shard_map/all_to_all | solution.py:181
  467.4 6.3 fusion.155
  484.7 6.5 all-to-all-done.7
  502.7 18.5 %all-to-all-done.13 = bf16[8,128,512]{2,1,0:T(8,128)(2,1)} async-done(((bf16[8,128,512]{2,1,0:T(8,128)(2,1)}), bf16[8,128,512]{2,1,0:T(8,128)(2,1)}, u32[]{:S(2)}, u32[]{:S(2)}) %all-to-all-start.13) | async-done | bytes 1048608 | tf_op jit(solution)/shard_map/all_to_all | solution.py:181
  647.1 6.9 fusion.397
  654.0 18.0 %all-to-all-done.14 = bf16[8,128,512]{2,1,0:T(8,128)(2,1)} async-done(((bf16[8,128,512]{2,1,0:T(8,128)(2,1)}), bf16[8,128,512]{2,1,0:T(8,128)(2,1)}, u32[]{:S(2)}, u32[]{:S(2)}) %all-to-all-start.14) | async-done | bytes 1048608 | tf_op jit(solution)/shard_map/all_to_all | solution.py:173
  672.0 9.1 convolution_add_fusion.3
  683.5 9.6 %fusion.6 = bf16[1024,2048]{1,0:T(8,128)(2,1)S(1)} fusion(f32[1024,2048]{1,0:T(8,128)} %get-tuple-element.191, bf16[1024,512]{1,0:T(8,128)(2,1)} %bitcast.86, bf16[1,1,2048,512]{3,2,1,0:T(8,128)(2,1)S(1)} %copy-done.277), kind=kOutput, calls=%fused_computation.14 | convolution fusion | flops 2189426688 | bytes 15728640 | tf_op jit(solution)/shard_map/dot_general | solution.py:38
  705.0 9.4 %fusion.20 = bf16[1024,2048]{1,0:T(8,128)(2,1)S(1)} fusion(f32[1024,2048]{1,0:T(8,128)} %fusion.100, bf16[1024,512]{1,0:T(8,128)(2,1)} %bitcast.110, bf16[1,1,2048,512]{3,2,1,0:T(8,128)(2,1)S(1)} %copy-done.277), kind=kOutput, calls=%fused_computation.28 | convolution fusion | flops 2189426688 | bytes 15728640 | tf_op jit(solution)/shard_map/dot_general | solution.py:38
  722.7 10.4 %all-reduce.2.cloned.1.call-done = bf16[128,2060]{0,1:T(8,128)(2,1)} async-done(((bf16[128,2060]{0,1:T(8,128)(2,1)}), bf16[128,2060]{0,1:T(8,128)(2,1)}) %all-reduce.2.cloned.1.call-update) | async-done | bytes 527376 | tf_op jit(solution)/shard_map/psum | solution.py:294
  748.8 17.4 %all-to-all-done.15 = bf16[8,128,512]{2,1,0:T(8,128)(2,1)} async-done(((bf16[8,128,512]{2,1,0:T(8,128)(2,1)}), bf16[8,128,512]{2,1,0:T(8,128)(2,1)}, u32[]{:S(2)}, u32[]{:S(2)}) %all-to-all-start.15) | async-done | bytes 1048608 | tf_op jit(solution)/shard_map/all_to_all | solution.py:181
  866.5 6.4 collective-permute-done.1
  877.3 6.9 collective-permute-done.2
  (1008 shorter events, 565.8 us)
Async XLA Ops:
  7.2 30.0 %all-gather.11.cloned.1.call-start = ((), (), s32[]{:S(2)}) async-start(), calls=%async_computation.16 | async-start | bytes 2621440 | tf_op jit(solution)/shard_map/all_gather | solution.py:346
  11.7 109.1 %all-gather.15.cloned.1.call-start = ((), (), s32[]{:S(2)}) async-start(), calls=%async_computation.19 | async-start | bytes 2621440 | tf_op jit(solution)/shard_map/all_gather | solution.py:361
  12.9 115.6 %all-gather.17.cloned.1.call-start = ((), (), s32[]{:S(2)}) async-start(), calls=%async_computation.20 | async-start | bytes 2621440 | tf_op jit(solution)/shard_map/all_gather | solution.py:362
  83.4 31.8 %all-to-all-start.4 = ((bf16[8,128,512]{2,1,0:T(8,128)(2,1)}), bf16[8,128,512]{2,1,0:T(8,128)(2,1)S(1)}, u32[]{:S(2)}, u32[]{:S(2)}) async-start(bf16[8,128,512]{2,1,0:T(8,128)(2,1)} %bitcast.592), calls=%async_computation.4 | async-start | bytes 2097152 | tf_op jit(solution)/shard_map/all_to_all | solution.py:97
  89.0 121.0 %all-gather.13.cloned.1.call-start = ((), (), s32[]{:S(2)}) async-start(), calls=%async_computation.17 | async-start | bytes 2621440 | tf_op jit(solution)/shard_map/all_gather | solution.py:346
  116.1 29.8 %all-to-all-start = ((bf16[8,128,512]{2,1,0:T(8,128)(2,1)}), bf16[8,128,512]{2,1,0:T(8,128)(2,1)S(1)}, u32[]{:S(2)}, u32[]{:S(2)}) async-start(bf16[8,128,512]{2,1,0:T(8,128)(2,1)} %bitcast.594), calls=%async_computation | async-start | bytes 2097152 | tf_op jit(solution)/shard_map/all_to_all | solution.py:97
  145.9 29.8 %all-to-all-start.5 = ((bf16[8,128,512]{2,1,0:T(8,128)(2,1)}), bf16[8,128,512]{2,1,0:T(8,128)(2,1)}, u32[]{:S(2)}, u32[]{:S(2)}) async-start(bf16[8,128,512]{2,1,0:T(8,128)(2,1)} %bitcast.602), calls=%async_computation.5 | async-start | bytes 2097152 | tf_op jit(solution)/shard_map/all_to_all | solution.py:106
  175.7 29.8 %all-to-all-start.1 = ((bf16[8,128,512]{2,1,0:T(8,128)(2,1)}), bf16[8,128,512]{2,1,0:T(8,128)(2,1)S(1)}, u32[]{:S(2)}, u32[]{:S(2)}) async-start(bf16[8,128,512]{2,1,0:T(8,128)(2,1)} %bitcast.600), calls=%async_computation.1 | async-start | bytes 2097152 | tf_op jit(solution)/shard_map/all_to_all | solution.py:106
  255.4 29.8 %all-to-all-start.2 = ((bf16[8,128,512]{2,1,0:T(8,128)(2,1)}), bf16[8,128,512]{2,1,0:T(8,128)(2,1)}, u32[]{:S(2)}, u32[]{:S(2)}) async-start(bf16[8,128,512]{2,1,0:T(8,128)(2,1)} %bitcast.595), calls=%async_computation.2 | async-start | bytes 2097152 | tf_op jit(solution)/shard_map/all_to_all | solution.py:97
  259.7 89.4 %all-gather.19.cloned.1.call-start = ((), (), s32[]{:S(2)}) async-start(), calls=%async_computation.21 | async-start | bytes 2621440 | tf_op jit(solution)/shard_map/all_gather | solution.py:361
  285.2 29.7 %all-to-all-start.8 = ((bf16[8,128,512]{2,1,0:T(8,128)(2,1)}), bf16[8,128,512]{2,1,0:T(8,128)(2,1)}, u32[]{:S(2)}, u32[]{:S(2)}) async-start(bf16[8,128,512]{2,1,0:T(8,128)(2,1)} %bitcast.586), calls=%async_computation.8 | async-start | bytes 2097152 | tf_op jit(solution)/shard_map/all_to_all | solution.py:173
  289.5 81.7 %all-gather.21.cloned.1.call-start = ((), (), s32[]{:S(2)}) async-start(), calls=%async_computation.22 | async-start | bytes 2621440 | tf_op jit(solution)/shard_map/all_gather | solution.py:362
  315.0 29.6 %all-to-all-start.6 = ((bf16[8,128,512]{2,1,0:T(8,128)(2,1)}), bf16[8,128,512]{2,1,0:T(8,128)(2,1)}, u32[]{:S(2)}, u32[]{:S(2)}) async-start(bf16[8,128,512]{2,1,0:T(8,128)(2,1)} %bitcast.598), calls=%async_computation.6 | async-start | bytes 2097152 | tf_op jit(solution)/shard_map/all_to_all | solution.py:97
  344.6 32.8 %all-to-all-start.12 = ((bf16[8,128,512]{2,1,0:T(8,128)(2,1)}), bf16[8,128,512]{2,1,0:T(8,128)(2,1)}, u32[]{:S(2)}, u32[]{:S(2)}) async-start(bf16[8,128,512]{2,1,0:T(8,128)(2,1)} %bitcast.601), calls=%async_computation.12 | async-start | bytes 2097152 | tf_op jit(solution)/shard_map/all_to_all | solution.py:173
  377.4 51.3 %all-to-all-start.3 = ((bf16[8,128,512]{2,1,0:T(8,128)(2,1)}), bf16[8,128,512]{2,1,0:T(8,128)(2,1)}, u32[]{:S(2)}, u32[]{:S(2)}) async-start(bf16[8,128,512]{2,1,0:T(8,128)(2,1)} %bitcast.596), calls=%async_computation.3 | async-start | bytes 2097152 | tf_op jit(solution)/shard_map/all_to_all | solution.py:106
  393.9 48.7 %collective-permute-start.16 = (bf16[2,512,512]{2,1,0:T(8,128)(2,1)}, bf16[2,512,512]{2,1,0:T(8,128)(2,1)}, u32[]{:S(2)}, u32[]{:S(2)}) collective-permute-start(bf16[2,512,512]{2,1,0:T(8,128)(2,1)} %fusion.243), channel_id=1, source_target_pairs={{0,1},{1,0},{2,3},{3,2},{4,5},{5,4},{6,7},{7,6},{8,9},{9,8},{10,11... | collective-permute-start | bytes 3145736 | tf_op jit(solution)/shard_map/ppermute | solution.py:243
  425.4 21.6 %collective-permute-start.12 = (bf16[2,128,2048]{2,1,0:T(8,128)(2,1)}, bf16[2,128,2048]{2,1,0:T(8,128)(2,1)}, u32[]{:S(2)}, u32[]{:S(2)}) collective-permute-start(bf16[2,128,2048]{2,1,0:T(8,128)(2,1)} %fusion.241), channel_id=1, source_target_pairs={{0,1},{1,0},{2,3},{3,2},{4,5},{5,4},{6,7},{7,6},{8,9},{9,8},{10,11... | collective-permute-start | bytes 3145736 | tf_op jit(solution)/shard_map/ppermute | solution.py:243
  428.7 32.5 %all-to-all-start.9 = ((bf16[8,128,512]{2,1,0:T(8,128)(2,1)}), bf16[8,128,512]{2,1,0:T(8,128)(2,1)}, u32[]{:S(2)}, u32[]{:S(2)}) async-start(bf16[8,128,512]{2,1,0:T(8,128)(2,1)} %bitcast.599), calls=%async_computation.9 | async-start | bytes 2097152 | tf_op jit(solution)/shard_map/all_to_all | solution.py:181
  446.5 27.1 %collective-permute-start.17 = (bf16[1,512,512]{2,1,0:T(8,128)(2,1)}, bf16[1,512,512]{2,1,0:T(8,128)(2,1)}, u32[]{:S(2)}, u32[]{:S(2)}) collective-permute-start(bf16[1,512,512]{2,1,0:T(8,128)(2,1)} %dynamic-slice_convert_fusion.4), channel_id=1, source_target_pairs={{0,2},{1,3},{2,0},{3,1},{4,6},{5,7},{6,4},{7,5},{8,10},{9,11},{10,... | collective-permute-start | bytes 1572872 | tf_op jit(solution)/shard_map/ppermute | solution.py:243
  461.3 29.9 %all-to-all-start.7 = ((bf16[8,128,512]{2,1,0:T(8,128)(2,1)}), bf16[8,128,512]{2,1,0:T(8,128)(2,1)}, u32[]{:S(2)}, u32[]{:S(2)}) async-start(bf16[8,128,512]{2,1,0:T(8,128)(2,1)} %bitcast.589), calls=%async_computation.7 | async-start | bytes 2097152 | tf_op jit(solution)/shard_map/all_to_all | solution.py:106
  491.1 30.0 %all-to-all-start.13 = ((bf16[8,128,512]{2,1,0:T(8,128)(2,1)}), bf16[8,128,512]{2,1,0:T(8,128)(2,1)}, u32[]{:S(2)}, u32[]{:S(2)}) async-start(bf16[8,128,512]{2,1,0:T(8,128)(2,1)} %bitcast.588), calls=%async_computation.13 | async-start | bytes 2097152 | tf_op jit(solution)/shard_map/all_to_all | solution.py:181
  606.7 29.9 %all-to-all-start.10 = ((bf16[8,128,512]{2,1,0:T(8,128)(2,1)}), bf16[8,128,512]{2,1,0:T(8,128)(2,1)}, u32[]{:S(2)}, u32[]{:S(2)}) async-start(bf16[8,128,512]{2,1,0:T(8,128)(2,1)} %bitcast.587), calls=%async_computation.10 | async-start | bytes 2097152 | tf_op jit(solution)/shard_map/all_to_all | solution.py:173
  630.4 14.7 %collective-permute-start.9 = (bf16[1,128,2060]{1,2,0:T(8,128)(2,1)}, bf16[1,128,2060]{1,2,0:T(8,128)(2,1)}, u32[]{:S(2)}, u32[]{:S(2)}) collective-permute-start(bf16[1,128,2060]{1,2,0:T(8,128)(2,1)} %dynamic-slice_convert_fusion.2), channel_id=1, source_target_pairs={{0,2},{1,3},{2,0},{3,1},{4,6},{5,7},{6,4},{7,5},{8,10},{9,11},{10,... | collective-permute-start | bytes 1582088 | tf_op jit(solution)/shard_map/ppermute | solution.py:243
  636.5 35.4 %all-to-all-start.14 = ((bf16[8,128,512]{2,1,0:T(8,128)(2,1)}), bf16[8,128,512]{2,1,0:T(8,128)(2,1)}, u32[]{:S(2)}, u32[]{:S(2)}) async-start(bf16[8,128,512]{2,1,0:T(8,128)(2,1)} %bitcast.590), calls=%async_computation.14 | async-start | bytes 2097152 | tf_op jit(solution)/shard_map/all_to_all | solution.py:173
  640.8 92.3 %all-reduce.2.cloned.1.call-start = ((), (), s32[]{:S(2)}) async-start(), calls=%async_computation.18 | async-start | bytes 1056768 | tf_op jit(solution)/shard_map/psum | solution.py:294
  682.4 161.5 %collective-permute-start.14 = (bf16[2,512,512]{2,1,0:T(8,128)(2,1)}, bf16[2,512,512]{2,1,0:T(8,128)(2,1)}, u32[]{:S(2)}, u32[]{:S(2)}) collective-permute-start(bf16[2,512,512]{2,1,0:T(8,128)(2,1)} %fusion.242), channel_id=1, source_target_pairs={{0,1},{1,0},{2,3},{3,2},{4,5},{5,4},{6,7},{7,6},{8,9},{9,8},{10,11... | collective-permute-start | bytes 3145736 | tf_op jit(solution)/shard_map/ppermute | solution.py:243
  701.0 35.4 %all-to-all-start.11 = ((bf16[8,128,512]{2,1,0:T(8,128)(2,1)}), bf16[8,128,512]{2,1,0:T(8,128)(2,1)S(1)}, u32[]{:S(2)}, u32[]{:S(2)}) async-start(bf16[8,128,512]{2,1,0:T(8,128)(2,1)} %bitcast.87), calls=%async_computation.11 | async-start | bytes 2097152 | tf_op jit(solution)/shard_map/all_to_all | solution.py:181
  719.2 23.8 %collective-permute-start.10 = (bf16[2,128,2048]{2,1,0:T(8,128)(2,1)S(1)}, bf16[2,128,2048]{2,1,0:T(8,128)(2,1)}, u32[]{:S(2)}, u32[]{:S(2)}) collective-permute-start(bf16[2,128,2048]{2,1,0:T(8,128)(2,1)S(1)} %fusion.240), channel_id=1, source_target_pairs={{0,1},{1,0},{2,3},{3,2},{4,5},{5,4},{6,7},{7,6},{8,9},{9,8},{10,11... | collective-permute-start | bytes 3145736 | tf_op jit(solution)/shard_map/ppermute | solution.py:243
  736.3 29.9 %all-to-all-start.15 = ((bf16[8,128,512]{2,1,0:T(8,128)(2,1)}), bf16[8,128,512]{2,1,0:T(8,128)(2,1)}, u32[]{:S(2)}, u32[]{:S(2)}) async-start(bf16[8,128,512]{2,1,0:T(8,128)(2,1)} %bitcast.593), calls=%async_computation.15 | async-start | bytes 2097152 | tf_op jit(solution)/shard_map/all_to_all | solution.py:181
  747.4 100.1 %collective-permute-start.11 = (bf16[1,128,2048]{2,1,0:T(8,128)(2,1)}, bf16[1,128,2048]{2,1,0:T(8,128)(2,1)}, u32[]{:S(2)}, u32[]{:S(2)}) collective-permute-start(bf16[1,128,2048]{2,1,0:T(8,128)(2,1)} %dynamic-slice_convert_fusion.7), channel_id=1, source_target_pairs={{0,2},{1,3},{2,0},{3,1},{4,6},{5,7},{6,4},{7,5},{8,10},{9,11},{10,... | collective-permute-start | bytes 1572872 | tf_op jit(solution)/shard_map/ppermute | solution.py:243
  847.1 15.1 %collective-permute-start.15 = (bf16[1,512,512]{2,1,0:T(8,128)(2,1)}, bf16[1,512,512]{2,1,0:T(8,128)(2,1)}, u32[]{:S(2)}, u32[]{:S(2)}) collective-permute-start(bf16[1,512,512]{2,1,0:T(8,128)(2,1)} %dynamic-slice_convert_fusion.5), channel_id=1, source_target_pairs={{0,2},{1,3},{2,0},{3,1},{4,6},{5,7},{6,4},{7,5},{8,10},{9,11},{10,... | collective-permute-start | bytes 1572872 | tf_op jit(solution)/shard_map/ppermute | solution.py:243
  855.6 17.4 %collective-permute-start.1 = (bf16[1,128,2060]{1,2,0:T(8,128)(2,1)S(1)}, bf16[1,128,2060]{1,2,0:T(8,128)(2,1)S(1)}, u32[]{:S(2)}, u32[]{:S(2)}) collective-permute-start(bf16[1,128,2060]{1,2,0:T(8,128)(2,1)S(1)} %dynamic-slice_convert_fusion.3), channel_id=1, source_target_pairs={{0,2},{1,3},{2,0},{3,1},{4,6},{5,7},{6,4},{7,5},{8,10},{9,11},{10,... | collective-permute-start | bytes 1582088 | tf_op jit(solution)/shard_map/ppermute | solution.py:243
  (296 other events, 3861.4 us)
Sparse Core Ops, SparseCore 0:
  11.8 25.2 all-gather.10
  39.3 22.5 all-gather.14
  63.5 22.5 all-gather.16
  91.0 23.0 all-gather.12
  261.7 22.9 all-gather.18
  291.6 22.9 all-gather.20
  647.2 85.8 all-reduce.1

commit v6 on v5

--- a/solution.py
+++ b/solution.py
@@ -3,13 +3,12 @@
 from jax import lax
 from jax.sharding import PartitionSpec as P
 
+
 D = 512
 HEADS = 8
 HEAD = 64
-HIDDEN_SIZE = 2048
 EXP_DEV = 1
 SEQ = 197
-MICRO = 2
 LAYERS = 2
 TOP = 2
 TOK_MB = 394
@@ -59,9 +58,13 @@
     return pair_hot, token_hot, kept_mask
 
 
-def forward_layer(residual, route_hot, tables, weights, experts, capacity):
-    norm_gains, norm_shifts, qkv_w, proj_w, router_w, in_w, out_w = weights
-    pair_hot, token_hot, kept_mask = tables
+def exchange(blocks, axis_name):
+    return lax.all_to_all(blocks, axis_name, split_axis=0, concat_axis=0, tiled=True)
+
+
+def forward_attend(residual, tables, weights):
+    norm_gains, norm_shifts, qkv_w, proj_w, router_w, _, _ = weights
+    _, token_hot, _ = tables
     tok_count = residual.shape[0]
     seq_count = tok_count // SEQ
     score_scale = HEAD ** (-0.5)
@@ -94,22 +97,29 @@
         jnp.dot(normed_two, router_w, preferred_element_type=jnp.float32), axis=-1
     )
     sending = dot_first(token_hot, normed_two).astype(jnp.bfloat16)
-    received = lax.all_to_all(
-        sending.reshape(experts, capacity, D), "expert", split_axis=0, concat_axis=0, tiled=True
-    )
+    carry = (residual, normed, heads, log_total, mixed_heads, middle, normed_two, gate_probs)
+    return carry, sending
+
+
+def forward_expert(carry, sending, route_hot, tables, weights, experts, capacity):
+    _, _, _, _, _, in_w, out_w = weights
+    received = exchange(sending.reshape(experts, capacity, D), "expert")
     row_block = received.reshape(experts * capacity, D)
     hidden_pre = jnp.dot(row_block, in_w[0], preferred_element_type=jnp.float32)
     hidden_act = gelu_tanh(hidden_pre).astype(jnp.bfloat16)
     expert_rows = jnp.dot(hidden_act, out_w[0], preferred_element_type=jnp.float32).astype(
         jnp.bfloat16
     )
-    returned = lax.all_to_all(
-        expert_rows.reshape(experts, capacity, D),
-        "expert",
-        split_axis=0,
-        concat_axis=0,
-        tiled=True,
-    )
+    returned = exchange(expert_rows.reshape(experts, capacity, D), "expert")
+    return forward_combine(
+        carry, returned, row_block, hidden_pre, route_hot, tables, experts, capacity
+    )
+
+
+def forward_combine(carry, returned, row_block, hidden_pre, route_hot, tables, experts, capacity):
+    residual, normed, heads, log_total, mixed_heads, middle, normed_two, gate_probs = carry
+    pair_hot, _, kept_mask = tables
+    tok_count = residual.shape[0]
     pair_rows = jnp.dot(
         pair_hot, returned.reshape(experts * capacity, D), preferred_element_type=jnp.float32
     ).reshape(TOP, tok_count, D)
@@ -137,28 +147,33 @@
 
 
 def backward_layer(d_output, saved_state, route_hot, tables, weights, experts, capacity):
+    (_, _, _, _, _, _, _, _, _, _, _, row_block, hidden_pre) = saved_state
+    _, _, _, _, router_w, in_w, out_w = weights
+    d_slots, g_router, d_normed_two = backward_route(
+        d_output, saved_state, tables, route_hot, router_w, experts, capacity
+    )
+    d_expert_out = exchange(d_slots, "expert")
+    flat_out = d_expert_out.reshape(experts * capacity, D)
+    hidden_act = gelu_tanh(hidden_pre).astype(jnp.bfloat16)
+    g_out = dot_first(hidden_act, flat_out)
+    d_act = dot_last(flat_out, out_w[0])
+    d_pre = jax.vjp(gelu_tanh, hidden_pre)[1](d_act)[0].astype(jnp.bfloat16)
+    g_in = dot_first(row_block, d_pre)
+    d_rows = dot_last(d_pre, in_w[0]).astype(jnp.bfloat16).reshape(experts, capacity, D)
+    d_back = exchange(d_rows, "expert")
+    d_residual, grads = backward_attend(
+        d_output, saved_state, d_back, d_normed_two, tables, weights, experts, capacity
+    )
+    g_gain, g_shift, g_qkv, g_proj = grads
+    return (d_residual, (g_gain, g_shift, g_qkv, g_proj, g_router, g_in[None], g_out[None]))
+
+
+def backward_route(d_output, saved_state, tables, route_hot, router_w, experts, capacity):
     (
-        residual,
-        normed,
-        heads,
-        log_total,
-        mixed_heads,
-        middle,
-        normed_two,
-        gate_probs,
-        kept_gate,
-        weight_pair,
-        pair_rows,
-        row_block,
-        hidden_pre,
+        residual, _, _, _, _, _, normed_two, gate_probs, kept_gate, weight_pair, pair_rows, _, _
     ) = saved_state
-    pair_hot, token_hot, kept_mask = tables
-    norm_gains, norm_shifts, qkv_w, proj_w, router_w, in_w, out_w = weights
+    pair_hot, _, _ = tables
     tok_count = residual.shape[0]
-    seq_count = tok_count // SEQ
-    score_scale = HEAD ** (-0.5)
-    norm_scale = norm_gains.astype(jnp.float32)
-    norm_shift = norm_shifts.astype(jnp.float32)
     d_gate_pair = kept_gate * jnp.sum(d_output[None] * pair_rows, axis=-1)
     d_gates = jnp.sum(route_hot * d_gate_pair.T[:, :, None], axis=1)
     d_logits = (
@@ -170,15 +185,18 @@
         (weight_pair[:, :, None] * d_output[None]).astype(jnp.bfloat16).reshape(TOP * tok_count, D)
     )
     d_slots = dot_first(pair_hot, d_pairs).astype(jnp.bfloat16).reshape(experts, capacity, D)
-    d_expert_out = lax.all_to_all(d_slots, "expert", split_axis=0, concat_axis=0, tiled=True)
-    flat_out = d_expert_out.reshape(experts * capacity, D)
-    hidden_act = gelu_tanh(hidden_pre).astype(jnp.bfloat16)
-    g_out = dot_first(hidden_act, flat_out)
-    d_act = dot_last(flat_out, out_w[0])
-    d_pre = jax.vjp(gelu_tanh, hidden_pre)[1](d_act)[0].astype(jnp.bfloat16)
-    g_in = dot_first(row_block, d_pre)
-    d_rows = dot_last(d_pre, in_w[0]).astype(jnp.bfloat16).reshape(experts, capacity, D)
-    d_back = lax.all_to_all(d_rows, "expert", split_axis=0, concat_axis=0, tiled=True)
+    return d_slots, g_router, d_normed_two
+
+
+def backward_attend(d_output, saved_state, d_back, d_normed_two, tables, weights, experts, capacity):
+    (residual, normed, heads, log_total, mixed_heads, middle, _, _, _, _, _, _, _) = saved_state
+    pair_hot, _, _ = tables
+    norm_gains, norm_shifts, qkv_w, proj_w, _, _, _ = weights
+    tok_count = residual.shape[0]
+    seq_count = tok_count // SEQ
+    score_scale = HEAD ** (-0.5)
+    norm_scale = norm_gains.astype(jnp.float32)
+    norm_shift = norm_shifts.astype(jnp.float32)
     d_pair_in = jnp.dot(
         pair_hot, d_back.reshape(experts * capacity, D), preferred_element_type=jnp.float32
     ).reshape(TOP, tok_count, D)
@@ -225,7 +243,7 @@
     d_residual = d_middle + pulled_one[0]
     g_gain = jnp.stack([pulled_one[1], pulled_two[1]])
     g_shift = jnp.stack([pulled_one[2], pulled_two[2]])
-    return (d_residual, (g_gain, g_shift, g_qkv, g_proj, g_router, g_in[None], g_out[None]))
+    return d_residual, (g_gain, g_shift, g_qkv, g_proj)
 
 
 def halving_scatter(grad, axis_name):
@@ -246,20 +264,6 @@
         total = keep + got.astype(jnp.float32)
         bit *= 2
     return total.reshape(chunk, *rest)
-
-
-def doubling_sum(part, axis_name):
-    size = lax.axis_size(axis_name)
-    total = part.astype(jnp.float32)
-    bit = 1
-    while bit < size:
-        own = lax.reduce_precision(total, exponent_bits=8, mantissa_bits=7)
-        got = lax.ppermute(
-            own.astype(jnp.bfloat16), axis_name, [(i, i ^ bit) for i in range(size)]
-        )
-        total = own + got.astype(jnp.float32)
-        bit *= 2
-    return total
 
 
 def doubling_gather(part, axis_name):
@@ -365,9 +369,16 @@
     residuals = [tokens[rows] for rows, _, _ in streams]
     saved = [[None] * LAYERS for _ in streams]
     for layer_index in range(LAYERS):
+        staged = []
         for block, (rows, tables, route_hot) in enumerate(streams):
-            residuals[block], saved[block][layer_index] = forward_layer(
-                residuals[block], route_hot, tables, all_weights[layer_index], experts, capacity
+            own_weights, own_rows = lax.optimization_barrier(
+                (all_weights[layer_index], residuals[block])
+            )
+            staged.append(forward_attend(own_rows, tables, own_weights))
+        for block, (rows, tables, route_hot) in enumerate(streams):
+            carry, sending = staged[block]
+            residuals[block], saved[block][layer_index] = forward_expert(
+                carry, sending, route_hot, tables, all_weights[layer_index], experts, capacity
             )
     activations = jnp.concatenate(residuals, axis=0)
     d_residuals = [cotangent[rows] for rows, _, _ in streams]

time: 938 us -> 915 us (0.975)
  matrix products: 311 us -> 293 us
  waiting for transfers between devices: 252 us -> 240 us
    all_to_all x16, waiting for transfers between devices: 185 us -> 142 us  [exchange(): lax.all_to_all(blocks, axis_name, split_axis=0, concat_axis=0, tiled=True)]
    all_gather x2, waiting for transfers between devices: 0.01 us -> 24.2 us  [local(): lax.all_gather(exp_out[layer_index], 'shard', axis=1, tiled=True)]
    all_gather x2, waiting for transfers between devices: 0.02 us -> 19 us  [local(): lax.all_gather(exp_in[layer_index], 'shard', axis=1, tiled=True)]
    dot_general x52, matrix products: 135 us -> 119 us  [the longest x4 26 us: forward_expert(): hidden_pre = jnp.dot(row_block, in_w[0], preferred_element_type=jnp.float32)]
    slice x7 -> x17, local copies, waits for them, and re-layouts: 11.9 us -> 22.7 us  [the longest x4 11.2 us: forward_attend(): heads[:, :, 2]]
    all_gather x2, waiting for transfers between devices: 9.77 us -> 0.01 us  [local(): lax.all_gather(jnp.concatenate([w_qkv[layer_index], w_proj[layer_index]],...]
    unnamed x594 -> x638, local copies, waits for them, and re-layouts: 57.4 us -> 60.6 us
  transfers between devices with their start and end apart: 41 -> 41, of which waited for: 26 -> 26; matrix products, arithmetic and copies ran while one was open for 44% -> 48% of each run, Pallas kernels for 0% -> 0%
where the time goes in v6:
time: 915 us; the launch traced here: 901 us
  matrix products  293 us (32%)
  waiting for transfers between devices  240 us (26%)
  local copies, waits for them, and re-layouts  194 us (21%)
  starting transfers between devices  82.1 us (9%)
  other arithmetic  68 us (7%)
  between operations  18.5 us (2%)
    all_to_all x16, waiting for transfers between devices, exchange(): lax.all_to_all(blocks, axis_name, split_axis=0, concat_axis=0, tiled=True)  142 us
    dot_general x30, matrix products, dot_first(): lax.dot_general(left, right, (((0,), (0,)), ((), ())), preferred_element_...  97.8 us
    dot_general x20, matrix products, dot_last(): lax.dot_general(left, right, (((1,), (1,)), ((), ())), preferred_element_...  76.5 us
    all_to_all x16, starting transfers between devices, exchange(): lax.all_to_all(blocks, axis_name, split_axis=0, concat_axis=0, tiled=True)  73.8 us
    unnamed x638, local copies, waits for them, and re-layouts  60.6 us
    ppermute x15, waiting for transfers between devices, halving_scatter(): lax.ppermute(give.astype(jnp.bfloat16), axis_name, [(i, i ^ bit) for i in...  30 us
    dot_general x4, matrix products, forward_expert(): hidden_pre = jnp.dot(row_block, in_w[0], preferred_element_type=jnp.float32)  26 us
    all_gather x2, waiting for transfers between devices, local(): lax.all_gather(exp_out[layer_index], 'shard', axis=1, tiled=True)  24.2 us
  transfers between devices with their start and end apart: 41, of which 26 were waited for; matrix products, arithmetic and copies ran while one was open for 48% of the time, Pallas kernels for 0%

profile of v6, /device:TPU:0, one launch (start us, length us, event | category | flops | bytes accessed | tf_op | source)
XLA Modules:
  0.0 901.2 jit_solution(15492749084757228983)
XLA Ops:
  14.8 6.1 all_gather.21
  41.6 18.9 %all-gather.19.cloned.1.call-done = bf16[1,1,512,2048]{3,2,1,0:T(8,128)(2,1)} async-done(((bf16[1,1,128,2048]{3,2,1,0:T(8,128)(2,1)}), bf16[1,1,512,2048]{3,2,1,0:T(8,128)(2,1)}) %all-gather.19.cloned.1.call-update) | async-done | bytes 2097168 | tf_op jit(solution)/shard_map/all_gather | solution.py:365
  60.6 24.2 %all-gather.21.cloned.1.call-done = bf16[1,1,2048,512]{3,2,1,0:T(8,128)(2,1)} async-done(((bf16[1,1,512,512]{3,2,1,0:T(8,128)(2,1)}), bf16[1,1,2048,512]{3,2,1,0:T(8,128)(2,1)}) %all-gather.21.cloned.1.call-update) | async-done | bytes 2097168 | tf_op jit(solution)/shard_map/all_gather | solution.py:366
  143.3 6.1 all-to-all-start.4
  149.5 7.8 multiply_convert_fusion.3
  162.6 12.6 %all-to-all-done.4 = bf16[8,128,512]{2,1,0:T(8,128)(2,1)} async-done(((bf16[8,128,512]{2,1,0:T(8,128)(2,1)}), bf16[8,128,512]{2,1,0:T(8,128)(2,1)}, u32[]{:S(2)}, u32[]{:S(2)}) %all-to-all-start.4) | async-done | bytes 1048608 | tf_op jit(solution)/shard_map/all_to_all | solution.py:62
  196.3 8.8 all-to-all-done.1
  237.4 6.2 all-to-all-start.2
  281.9 16.2 %all-to-all-done.8 = bf16[8,128,512]{2,1,0:T(8,128)(2,1)} async-done(((bf16[8,128,512]{2,1,0:T(8,128)(2,1)}), bf16[8,128,512]{2,1,0:T(8,128)(2,1)}, u32[]{:S(2)}, u32[]{:S(2)}) %all-to-all-start.8) | async-done | bytes 1048608 | tf_op jit(solution)/shard_map/all_to_all | solution.py:62
  307.9 19.9 %all-to-all-done.6 = bf16[8,128,512]{2,1,0:T(8,128)(2,1)S(1)} async-done(((bf16[8,128,512]{2,1,0:T(8,128)(2,1)}), bf16[8,128,512]{2,1,0:T(8,128)(2,1)S(1)}, u32[]{:S(2)}, u32[]{:S(2)}) %all-to-all-start.6) | async-done | bytes 1048608 | tf_op jit(solution)/shard_map/all_to_all | solution.py:62
  331.5 8.8 multiply_convert_fusion.2
  340.3 5.7 fusion.80
  346.0 5.8 fusion.390
  361.9 8.7 convolution_add_fusion.2
  370.9 10.9 %fusion.27 = bf16[1024,2048]{1,0:T(8,128)(2,1)S(1)} fusion(f32[1024,2048]{1,0:T(8,128)} %fusion.80, bf16[1024,512]{1,0:T(8,128)(2,1)} %bitcast.627, bf16[1,1,2048,512]{3,2,1,0:T(8,128)(2,1)S(1)} %copy-done.302), kind=kOutput, calls=%fused_computation.35 | convolution fusion | flops 2189426688 | bytes 15728640 | tf_op jit(solution)/shard_map/dot_general | solution.py:37
  381.8 9.6 %fusion.13 = bf16[1024,2048]{1,0:T(8,128)(2,1)S(1)} fusion(f32[1024,2048]{1,0:T(8,128)S(1)} %bitcast.691, bf16[1024,512]{1,0:T(8,128)(2,1)} %bitcast.86, bf16[1,1,2048,512]{3,2,1,0:T(8,128)(2,1)S(1)} %copy-done.302), kind=kOutput, calls=%fused_computation.21 | convolution fusion | flops 2189426688 | bytes 15728640 | tf_op jit(solution)/shard_map/dot_general | solution.py:37
  404.2 5.9 all-to-all-start.9
  410.1 7.9 fusion.161
  423.3 13.3 %all-to-all-done.9 = bf16[8,128,512]{2,1,0:T(8,128)(2,1)} async-done(((bf16[8,128,512]{2,1,0:T(8,128)(2,1)}), bf16[8,128,512]{2,1,0:T(8,128)(2,1)}, u32[]{:S(2)}, u32[]{:S(2)}) %all-to-all-start.9) | async-done | bytes 1048608 | tf_op jit(solution)/shard_map/all_to_all | solution.py:62
  442.7 6.2 fusion.155
  459.8 6.7 all-to-all-done.7
  480.0 16.4 %all-to-all-done.13 = bf16[8,128,512]{2,1,0:T(8,128)(2,1)S(1)} async-done(((bf16[8,128,512]{2,1,0:T(8,128)(2,1)}), bf16[8,128,512]{2,1,0:T(8,128)(2,1)S(1)}, u32[]{:S(2)}, u32[]{:S(2)}) %all-to-all-start.13) | async-done | bytes 1048608 | tf_op jit(solution)/shard_map/all_to_all | solution.py:62
  562.1 5.6 concatenate.81
  605.6 5.8 all-to-all-done.10
  621.8 6.9 fusion.389
  628.7 18.2 %all-to-all-done.14 = bf16[8,128,512]{2,1,0:T(8,128)(2,1)} async-done(((bf16[8,128,512]{2,1,0:T(8,128)(2,1)}), bf16[8,128,512]{2,1,0:T(8,128)(2,1)}, u32[]{:S(2)}, u32[]{:S(2)}) %all-to-all-start.14) | async-done | bytes 1048608 | tf_op jit(solution)/shard_map/all_to_all | solution.py:62
  646.9 9.1 %convolution_add_fusion.3 = f32[2048,512]{1,0:T(8,128)S(1)} fusion(f32[2048,512]{1,0:T(8,128)} %fusion.389, bf16[1024,512]{1,0:T(8,128)(2,1)} %bitcast.126, f32[1024,2048]{1,0:T(8,128)} %copy-done.303), kind=kOutput, calls=%fused_computation.83 | convolution fusion | flops 2167406592 | bytes 17825792 | tf_op jit(solution)/shard_map/dot_general | solution.py:31
  658.4 9.7 %fusion.6 = bf16[1024,2048]{1,0:T(8,128)(2,1)S(1)} fusion(f32[1024,2048]{1,0:T(8,128)} %get-tuple-element.242, bf16[1024,512]{1,0:T(8,128)(2,1)} %bitcast.100, bf16[1,1,2048,512]{3,2,1,0:T(8,128)(2,1)S(1)} %copy-done.298), kind=kOutput, calls=%fused_computation.14 | convolution fusion | flops 2189426688 | bytes 15728640 | tf_op jit(solution)/shard_map/dot_general | solution.py:37
  679.7 9.4 %fusion.20 = bf16[1024,2048]{1,0:T(8,128)(2,1)S(1)} fusion(f32[1024,2048]{1,0:T(8,128)} %copy-done.303, bf16[1024,512]{1,0:T(8,128)(2,1)} %bitcast.126, bf16[1,1,2048,512]{3,2,1,0:T(8,128)(2,1)S(1)} %copy-done.298), kind=kOutput, calls=%fused_computation.28 | convolution fusion | flops 2189426688 | bytes 15728640 | tf_op jit(solution)/shard_map/dot_general | solution.py:37
  698.7 9.1 %all-reduce.2.cloned.1.call-done = bf16[128,2060]{0,1:T(8,128)(2,1)} async-done(((bf16[128,2060]{0,1:T(8,128)(2,1)}), bf16[128,2060]{0,1:T(8,128)(2,1)}) %all-reduce.2.cloned.1.call-update) | async-done | bytes 527376 | tf_op jit(solution)/shard_map/psum | solution.py:298
  723.0 18.0 %all-to-all-done.15 = bf16[8,128,512]{2,1,0:T(8,128)(2,1)} async-done(((bf16[8,128,512]{2,1,0:T(8,128)(2,1)}), bf16[8,128,512]{2,1,0:T(8,128)(2,1)}, u32[]{:S(2)}, u32[]{:S(2)}) %all-to-all-start.15) | async-done | bytes 1048608 | tf_op jit(solution)/shard_map/all_to_all | solution.py:62
  841.4 6.4 collective-permute-done.1
  (1065 shorter events, 551.7 us)
Async XLA Ops:
  7.2 30.7 %all-gather.13.cloned.1.call-start = ((), (), s32[]{:S(2)}) async-start(), calls=%async_computation.17 | async-start | bytes 2621440 | tf_op jit(solution)/shard_map/all_gather | solution.py:350
  10.4 50.2 %all-gather.19.cloned.1.call-start = ((), (), s32[]{:S(2)}) async-start(), calls=%async_computation.21 | async-start | bytes 2621440 | tf_op jit(solution)/shard_map/all_gather | solution.py:365
  11.6 73.1 %all-gather.21.cloned.1.call-start = ((), (), s32[]{:S(2)}) async-start(), calls=%async_computation.22 | async-start | bytes 2621440 | tf_op jit(solution)/shard_map/all_gather | solution.py:366
  12.7 168.3 %all-gather.11.cloned.1.call-start = ((), (), s32[]{:S(2)}) async-start(), calls=%async_computation.16 | async-start | bytes 2621440 | tf_op jit(solution)/shard_map/all_gather | solution.py:350
  13.6 199.5 %all-gather.15.cloned.1.call-start = ((), (), s32[]{:S(2)}) async-start(), calls=%async_computation.19 | async-start | bytes 2621440 | tf_op jit(solution)/shard_map/all_gather | solution.py:365
  14.2 198.9 %all-gather.17.cloned.1.call-start = ((), (), s32[]{:S(2)}) async-start(), calls=%async_computation.20 | async-start | bytes 2621440 | tf_op jit(solution)/shard_map/all_gather | solution.py:366
  106.8 36.5 %all-to-all-start = ((bf16[8,128,512]{2,1,0:T(8,128)(2,1)}), bf16[8,128,512]{2,1,0:T(8,128)(2,1)S(1)}, u32[]{:S(2)}, u32[]{:S(2)}) async-start(bf16[8,128,512]{2,1,0:T(8,128)(2,1)} %bitcast.619), calls=%async_computation | async-start | bytes 2097152 | tf_op jit(solution)/shard_map/all_to_all | solution.py:62
  143.3 31.9 %all-to-all-start.4 = ((bf16[8,128,512]{2,1,0:T(8,128)(2,1)}), bf16[8,128,512]{2,1,0:T(8,128)(2,1)}, u32[]{:S(2)}, u32[]{:S(2)}) async-start(bf16[8,128,512]{2,1,0:T(8,128)(2,1)} %bitcast.628), calls=%async_computation.4 | async-start | bytes 2097152 | tf_op jit(solution)/shard_map/all_to_all | solution.py:62
  175.2 29.9 %all-to-all-start.1 = ((bf16[8,128,512]{2,1,0:T(8,128)(2,1)}), bf16[8,128,512]{2,1,0:T(8,128)(2,1)}, u32[]{:S(2)}, u32[]{:S(2)}) async-start(bf16[8,128,512]{2,1,0:T(8,128)(2,1)} %bitcast.34), calls=%async_computation.1 | async-start | bytes 2097152 | tf_op jit(solution)/shard_map/all_to_all | solution.py:62
  205.1 32.2 %all-to-all-start.5 = ((bf16[8,128,512]{2,1,0:T(8,128)(2,1)}), bf16[8,128,512]{2,1,0:T(8,128)(2,1)}, u32[]{:S(2)}, u32[]{:S(2)}) async-start(bf16[8,128,512]{2,1,0:T(8,128)(2,1)} %bitcast.617), calls=%async_computation.5 | async-start | bytes 2097152 | tf_op jit(solution)/shard_map/all_to_all | solution.py:62
  237.4 31.0 %all-to-all-start.2 = ((bf16[8,128,512]{2,1,0:T(8,128)(2,1)}), bf16[8,128,512]{2,1,0:T(8,128)(2,1)}, u32[]{:S(2)}, u32[]{:S(2)}) async-start(bf16[8,128,512]{2,1,0:T(8,128)(2,1)} %bitcast.46), calls=%async_computation.2 | async-start | bytes 2097152 | tf_op jit(solution)/shard_map/all_to_all | solution.py:62
  268.4 29.7 %all-to-all-start.8 = ((bf16[8,128,512]{2,1,0:T(8,128)(2,1)}), bf16[8,128,512]{2,1,0:T(8,128)(2,1)}, u32[]{:S(2)}, u32[]{:S(2)}) async-start(bf16[8,128,512]{2,1,0:T(8,128)(2,1)} %bitcast.625), calls=%async_computation.8 | async-start | bytes 2097152 | tf_op jit(solution)/shard_map/all_to_all | solution.py:62
  298.1 29.7 %all-to-all-start.6 = ((bf16[8,128,512]{2,1,0:T(8,128)(2,1)}), bf16[8,128,512]{2,1,0:T(8,128)(2,1)S(1)}, u32[]{:S(2)}, u32[]{:S(2)}) async-start(bf16[8,128,512]{2,1,0:T(8,128)(2,1)} %bitcast.79), calls=%async_computation.6 | async-start | bytes 2097152 | tf_op jit(solution)/shard_map/all_to_all | solution.py:62
  327.8 29.6 %all-to-all-start.12 = ((bf16[8,128,512]{2,1,0:T(8,128)(2,1)}), bf16[8,128,512]{2,1,0:T(8,128)(2,1)S(1)}, u32[]{:S(2)}, u32[]{:S(2)}) async-start(bf16[8,128,512]{2,1,0:T(8,128)(2,1)} %bitcast.629), calls=%async_computation.12 | async-start | bytes 2097152 | tf_op jit(solution)/shard_map/all_to_all | solution.py:62
  357.4 46.7 %all-to-all-start.3 = ((bf16[8,128,512]{2,1,0:T(8,128)(2,1)}), bf16[8,128,512]{2,1,0:T(8,128)(2,1)}, u32[]{:S(2)}, u32[]{:S(2)}) async-start(bf16[8,128,512]{2,1,0:T(8,128)(2,1)} %bitcast.50), calls=%async_computation.3 | async-start | bytes 2097152 | tf_op jit(solution)/shard_map/all_to_all | solution.py:62
  370.8 47.2 %collective-permute-start.16 = (bf16[2,512,512]{2,1,0:T(8,128)(2,1)S(1)}, bf16[2,512,512]{2,1,0:T(8,128)(2,1)}, u32[]{:S(2)}, u32[]{:S(2)}) collective-permute-start(bf16[2,512,512]{2,1,0:T(8,128)(2,1)S(1)} %fusion.243), channel_id=1, source_target_pairs={{0,1},{1,0},{2,3},{3,2},{4,5},{5,4},{6,7},{7,6},{8,9},{9,8},{10,11... | collective-permute-start | bytes 3145736 | tf_op jit(solution)/shard_map/ppermute | solution.py:261
  400.8 19.6 %collective-permute-start.12 = (bf16[2,128,2048]{2,1,0:T(8,128)(2,1)}, bf16[2,128,2048]{2,1,0:T(8,128)(2,1)}, u32[]{:S(2)}, u32[]{:S(2)}) collective-permute-start(bf16[2,128,2048]{2,1,0:T(8,128)(2,1)} %fusion.241), channel_id=1, source_target_pairs={{0,1},{1,0},{2,3},{3,2},{4,5},{5,4},{6,7},{7,6},{8,9},{9,8},{10,11... | collective-permute-start | bytes 3145736 | tf_op jit(solution)/shard_map/ppermute | solution.py:261
  404.2 32.5 %all-to-all-start.9 = ((bf16[8,128,512]{2,1,0:T(8,128)(2,1)}), bf16[8,128,512]{2,1,0:T(8,128)(2,1)}, u32[]{:S(2)}, u32[]{:S(2)}) async-start(bf16[8,128,512]{2,1,0:T(8,128)(2,1)} %bitcast.87), calls=%async_computation.9 | async-start | bytes 2097152 | tf_op jit(solution)/shard_map/all_to_all | solution.py:62
  419.8 29.1 %collective-permute-start.17 = (bf16[1,512,512]{2,1,0:T(8,128)(2,1)S(1)}, bf16[1,512,512]{2,1,0:T(8,128)(2,1)}, u32[]{:S(2)}, u32[]{:S(2)}) collective-permute-start(bf16[1,512,512]{2,1,0:T(8,128)(2,1)S(1)} %dynamic-slice_convert_fusion.4), channel_id=1, source_target_pairs={{0,2},{1,3},{2,0},{3,1},{4,6},{5,7},{6,4},{7,5},{8,10},{9,11},{10,... | collective-permute-start | bytes 1572872 | tf_op jit(solution)/shard_map/ppermute | solution.py:261
  436.6 29.9 %all-to-all-start.7 = ((bf16[8,128,512]{2,1,0:T(8,128)(2,1)}), bf16[8,128,512]{2,1,0:T(8,128)(2,1)}, u32[]{:S(2)}, u32[]{:S(2)}) async-start(bf16[8,128,512]{2,1,0:T(8,128)(2,1)} %bitcast.620), calls=%async_computation.7 | async-start | bytes 2097152 | tf_op jit(solution)/shard_map/all_to_all | solution.py:62
  466.5 29.9 %all-to-all-start.13 = ((bf16[8,128,512]{2,1,0:T(8,128)(2,1)}), bf16[8,128,512]{2,1,0:T(8,128)(2,1)S(1)}, u32[]{:S(2)}, u32[]{:S(2)}) async-start(bf16[8,128,512]{2,1,0:T(8,128)(2,1)} %bitcast.115), calls=%async_computation.13 | async-start | bytes 2097152 | tf_op jit(solution)/shard_map/all_to_all | solution.py:62
  581.3 30.1 %all-to-all-start.10 = ((bf16[8,128,512]{2,1,0:T(8,128)(2,1)}), bf16[8,128,512]{2,1,0:T(8,128)(2,1)}, u32[]{:S(2)}, u32[]{:S(2)}) async-start(bf16[8,128,512]{2,1,0:T(8,128)(2,1)} %bitcast.618), calls=%async_computation.10 | async-start | bytes 2097152 | tf_op jit(solution)/shard_map/all_to_all | solution.py:62
  605.1 14.7 %collective-permute-start.9 = (bf16[1,128,2060]{1,2,0:T(8,128)(2,1)}, bf16[1,128,2060]{1,2,0:T(8,128)(2,1)}, u32[]{:S(2)}, u32[]{:S(2)}) collective-permute-start(bf16[1,128,2060]{1,2,0:T(8,128)(2,1)} %dynamic-slice_convert_fusion.2), channel_id=1, source_target_pairs={{0,2},{1,3},{2,0},{3,1},{4,6},{5,7},{6,4},{7,5},{8,10},{9,11},{10,... | collective-permute-start | bytes 1582088 | tf_op jit(solution)/shard_map/ppermute | solution.py:261
  611.4 35.5 %all-to-all-start.14 = ((bf16[8,128,512]{2,1,0:T(8,128)(2,1)}), bf16[8,128,512]{2,1,0:T(8,128)(2,1)}, u32[]{:S(2)}, u32[]{:S(2)}) async-start(bf16[8,128,512]{2,1,0:T(8,128)(2,1)} %bitcast.621), calls=%async_computation.14 | async-start | bytes 2097152 | tf_op jit(solution)/shard_map/all_to_all | solution.py:62
  615.6 92.2 %all-reduce.2.cloned.1.call-start = ((), (), s32[]{:S(2)}) async-start(), calls=%async_computation.18 | async-start | bytes 1056768 | tf_op jit(solution)/shard_map/psum | solution.py:298
  657.3 161.5 %collective-permute-start.14 = (bf16[2,512,512]{2,1,0:T(8,128)(2,1)}, bf16[2,512,512]{2,1,0:T(8,128)(2,1)}, u32[]{:S(2)}, u32[]{:S(2)}) collective-permute-start(bf16[2,512,512]{2,1,0:T(8,128)(2,1)} %fusion.242), channel_id=1, source_target_pairs={{0,1},{1,0},{2,3},{3,2},{4,5},{5,4},{6,7},{7,6},{8,9},{9,8},{10,11... | collective-permute-start | bytes 3145736 | tf_op jit(solution)/shard_map/ppermute | solution.py:261
  676.0 35.1 %all-to-all-start.11 = ((bf16[8,128,512]{2,1,0:T(8,128)(2,1)}), bf16[8,128,512]{2,1,0:T(8,128)(2,1)S(1)}, u32[]{:S(2)}, u32[]{:S(2)}) async-start(bf16[8,128,512]{2,1,0:T(8,128)(2,1)} %bitcast.101), calls=%async_computation.11 | async-start | bytes 2097152 | tf_op jit(solution)/shard_map/all_to_all | solution.py:62
  695.3 21.9 %collective-permute-start.10 = (bf16[2,128,2048]{2,1,0:T(8,128)(2,1)S(1)}, bf16[2,128,2048]{2,1,0:T(8,128)(2,1)}, u32[]{:S(2)}, u32[]{:S(2)}) collective-permute-start(bf16[2,128,2048]{2,1,0:T(8,128)(2,1)S(1)} %fusion.240), channel_id=1, source_target_pairs={{0,1},{1,0},{2,3},{3,2},{4,5},{5,4},{6,7},{7,6},{8,9},{9,8},{10,11... | collective-permute-start | bytes 3145736 | tf_op jit(solution)/shard_map/ppermute | solution.py:261
  711.0 30.0 %all-to-all-start.15 = ((bf16[8,128,512]{2,1,0:T(8,128)(2,1)}), bf16[8,128,512]{2,1,0:T(8,128)(2,1)}, u32[]{:S(2)}, u32[]{:S(2)}) async-start(bf16[8,128,512]{2,1,0:T(8,128)(2,1)} %bitcast.624), calls=%async_computation.15 | async-start | bytes 2097152 | tf_op jit(solution)/shard_map/all_to_all | solution.py:62
  721.6 100.8 %collective-permute-start.11 = (bf16[1,128,2048]{2,1,0:T(8,128)(2,1)}, bf16[1,128,2048]{2,1,0:T(8,128)(2,1)}, u32[]{:S(2)}, u32[]{:S(2)}) collective-permute-start(bf16[1,128,2048]{2,1,0:T(8,128)(2,1)} %dynamic-slice_convert_fusion.7), channel_id=1, source_target_pairs={{0,2},{1,3},{2,0},{3,1},{4,6},{5,7},{6,4},{7,5},{8,10},{9,11},{10,... | collective-permute-start | bytes 1572872 | tf_op jit(solution)/shard_map/ppermute | solution.py:261
  822.0 15.1 %collective-permute-start.15 = (bf16[1,512,512]{2,1,0:T(8,128)(2,1)}, bf16[1,512,512]{2,1,0:T(8,128)(2,1)}, u32[]{:S(2)}, u32[]{:S(2)}) collective-permute-start(bf16[1,512,512]{2,1,0:T(8,128)(2,1)} %dynamic-slice_convert_fusion.5), channel_id=1, source_target_pairs={{0,2},{1,3},{2,0},{3,1},{4,6},{5,7},{6,4},{7,5},{8,10},{9,11},{10,... | collective-permute-start | bytes 1572872 | tf_op jit(solution)/shard_map/ppermute | solution.py:261
  830.5 17.3 %collective-permute-start.1 = (bf16[1,128,2060]{1,2,0:T(8,128)(2,1)S(1)}, bf16[1,128,2060]{1,2,0:T(8,128)(2,1)S(1)}, u32[]{:S(2)}, u32[]{:S(2)}) collective-permute-start(bf16[1,128,2060]{1,2,0:T(8,128)(2,1)S(1)} %dynamic-slice_convert_fusion.3), channel_id=1, source_target_pairs={{0,2},{1,3},{2,0},{3,1},{4,6},{5,7},{6,4},{7,5},{8,10},{9,11},{10,... | collective-permute-start | bytes 1582088 | tf_op jit(solution)/shard_map/ppermute | solution.py:261
  (318 other events, 2315.6 us)
Sparse Core Ops, SparseCore 0:
  10.5 25.2 all-gather.12
  38.0 22.5 all-gather.18
  62.1 22.5 all-gather.20
  86.2 22.5 all-gather.10
  110.2 22.5 all-gather.14
  134.2 22.5 all-gather.16
  621.9 85.8 all-reduce.1

commit v7 on v6

--- a/solution.py
+++ b/solution.py
@@ -371,9 +371,10 @@
     for layer_index in range(LAYERS):
         staged = []
         for block, (rows, tables, route_hot) in enumerate(streams):
-            own_weights, own_rows = lax.optimization_barrier(
-                (all_weights[layer_index], residuals[block])
+            attn_weights, own_rows = lax.optimization_barrier(
+                (all_weights[layer_index][:5], residuals[block])
             )
+            own_weights = tuple(attn_weights) + tuple(all_weights[layer_index][5:])
             staged.append(forward_attend(own_rows, tables, own_weights))
         for block, (rows, tables, route_hot) in enumerate(streams):
             carry, sending = staged[block]

time: 915 us -> 875 us (0.956)
  waiting for transfers between devices: 240 us -> 189 us
    all_gather x2, waiting for transfers between devices: 24.2 us -> 0.01 us  [local(): lax.all_gather(exp_out[layer_index], 'shard', axis=1, tiled=True)]
    all_gather x2, waiting for transfers between devices: 19 us -> 0.03 us  [local(): lax.all_gather(exp_in[layer_index], 'shard', axis=1, tiled=True)]
    unnamed x638 -> x634, local copies, waits for them, and re-layouts: 60.6 us -> 58.6 us
  transfers between devices with their start and end apart: 41 -> 41, of which waited for: 26 -> 23; matrix products, arithmetic and copies ran while one was open for 48% -> 51% of each run, Pallas kernels for 0% -> 0%
where the time goes in v7:
time: 875 us; the launch traced here: 862 us
  matrix products  300 us (34%)
  local copies, waits for them, and re-layouts  191 us (22%)
  waiting for transfers between devices  189 us (22%)
  starting transfers between devices  88.3 us (10%)
  other arithmetic  68 us (8%)
  between operations  18.5 us (2%)
    all_to_all x16, waiting for transfers between devices, exchange(): lax.all_to_all(blocks, axis_name, split_axis=0, concat_axis=0, tiled=True)  135 us
    dot_general x30, matrix products, dot_first(): lax.dot_general(left, right, (((0,), (0,)), ((), ())), preferred_element_...  97.8 us
    dot_general x20, matrix products, dot_last(): lax.dot_general(left, right, (((1,), (1,)), ((), ())), preferred_element_...  76.6 us
    all_to_all x16, starting transfers between devices, exchange(): lax.all_to_all(blocks, axis_name, split_axis=0, concat_axis=0, tiled=True)  76.2 us
    unnamed x634, local copies, waits for them, and re-layouts  58.6 us
    ppermute x15, waiting for transfers between devices, halving_scatter(): lax.ppermute(give.astype(jnp.bfloat16), axis_name, [(i, i ^ bit) for i in...  29.8 us
    dot_general x4, matrix products, forward_expert(): hidden_pre = jnp.dot(row_block, in_w[0], preferred_element_type=jnp.float32)  26.6 us
    dot_general x4, matrix products, forward_expert(): jnp.dot(hidden_act, out_w[0], preferred_element_type=jnp.float32)  24.5 us
  transfers between devices with their start and end apart: 41, of which 23 were waited for; matrix products, arithmetic and copies ran while one was open for 51% of the time, Pallas kernels for 0%

profile of v7, /device:TPU:0, one launch (start us, length us, event | category | flops | bytes accessed | tf_op | source)
XLA Modules:
  0.0 861.8 jit_solution(17636695094294078390)
XLA Ops:
  14.9 6.1 all_gather.21
  63.7 6.2 all-to-all-start
  101.1 5.9 all-to-all-start.4
  107.1 8.3 multiply_convert_fusion.3
  115.4 6.7 fusion.146
  122.1 10.9 %all-to-all-done.4 = bf16[8,128,512]{2,1,0:T(8,128)(2,1)} async-done(((bf16[8,128,512]{2,1,0:T(8,128)(2,1)}), bf16[8,128,512]{2,1,0:T(8,128)(2,1)}, u32[]{:S(2)}, u32[]{:S(2)}) %all-to-all-start.4) | async-done | bytes 1048608 | tf_op jit(solution)/shard_map/all_to_all | solution.py:62
  154.2 8.8 %all-to-all-done.1 = bf16[8,128,512]{2,1,0:T(8,128)(2,1)} async-done(((bf16[8,128,512]{2,1,0:T(8,128)(2,1)}), bf16[8,128,512]{2,1,0:T(8,128)(2,1)}, u32[]{:S(2)}, u32[]{:S(2)}) %all-to-all-start.1) | async-done | bytes 1048608 | tf_op jit(solution)/shard_map/all_to_all | solution.py:62
  195.3 6.2 all-to-all-start.2
  239.7 16.3 %all-to-all-done.8 = bf16[8,128,512]{2,1,0:T(8,128)(2,1)} async-done(((bf16[8,128,512]{2,1,0:T(8,128)(2,1)}), bf16[8,128,512]{2,1,0:T(8,128)(2,1)}, u32[]{:S(2)}, u32[]{:S(2)}) %all-to-all-start.8) | async-done | bytes 1048608 | tf_op jit(solution)/shard_map/all_to_all | solution.py:62
  265.9 19.9 %all-to-all-done.6 = bf16[8,128,512]{2,1,0:T(8,128)(2,1)S(1)} async-done(((bf16[8,128,512]{2,1,0:T(8,128)(2,1)}), bf16[8,128,512]{2,1,0:T(8,128)(2,1)S(1)}, u32[]{:S(2)}, u32[]{:S(2)}) %all-to-all-start.6) | async-done | bytes 1048608 | tf_op jit(solution)/shard_map/all_to_all | solution.py:62
  289.5 8.8 %multiply_convert_fusion.2 = (bf16[1024,2048]{1,0:T(8,128)(2,1)S(1)}, f32[1024,2048]{1,0:T(8,128)}) fusion(bf16[1024,512]{1,0:T(8,128)(2,1)} %bitcast.43, bf16[1,1,512,2048]{3,2,1,0:T(8,128)(2,1)} %all-gather.19.cloned.1.call-done), kind=kOutput, calls=%fused_computation.38 | convolution fusion | flops 2166358016 | bytes 15728640 | tf_op jit(solution)/shard_map/dot_general | solution.py:108
  298.3 5.7 fusion.80
  309.7 6.2 fusion.158
  315.9 6.2 all-to-all-start.3
  322.1 8.7 %convolution_add_fusion.2 = f32[2048,512]{1,0:T(8,128)S(1)} fusion(f32[2048,512]{1,0:T(8,128)} %fusion.390, bf16[1024,512]{1,0:T(8,128)(2,1)S(1)} %bitcast.621, f32[1024,2048]{1,0:T(8,128)} %fusion.80), kind=kOutput, calls=%fused_computation.82 | convolution fusion | flops 2167406592 | bytes 17825792 | tf_op jit(solution)/shard_map/dot_general | solution.py:31
  331.1 10.9 %fusion.27 = bf16[1024,2048]{1,0:T(8,128)(2,1)S(1)} fusion(f32[1024,2048]{1,0:T(8,128)} %fusion.80, bf16[1024,512]{1,0:T(8,128)(2,1)} %bitcast.622, bf16[1,1,2048,512]{3,2,1,0:T(8,128)(2,1)S(1)} %copy-done.300), kind=kOutput, calls=%fused_computation.35 | convolution fusion | flops 2189426688 | bytes 15728640 | tf_op jit(solution)/shard_map/dot_general | solution.py:37
  342.1 9.6 %fusion.13 = bf16[1024,2048]{1,0:T(8,128)(2,1)S(1)} fusion(f32[1024,2048]{1,0:T(8,128)S(1)} %bitcast.688, bf16[1024,512]{1,0:T(8,128)(2,1)} %bitcast.82, bf16[1,1,2048,512]{3,2,1,0:T(8,128)(2,1)S(1)} %copy-done.300), kind=kOutput, calls=%fused_computation.21 | convolution fusion | flops 2189426688 | bytes 15728640 | tf_op jit(solution)/shard_map/dot_general | solution.py:37
  364.4 6.0 all-to-all-start.9
  370.3 7.9 fusion.161
  384.5 12.4 %all-to-all-done.9 = bf16[8,128,512]{2,1,0:T(8,128)(2,1)} async-done(((bf16[8,128,512]{2,1,0:T(8,128)(2,1)}), bf16[8,128,512]{2,1,0:T(8,128)(2,1)}, u32[]{:S(2)}, u32[]{:S(2)}) %all-to-all-start.9) | async-done | bytes 1048608 | tf_op jit(solution)/shard_map/all_to_all | solution.py:62
  404.0 6.2 fusion.155
  420.1 6.7 all-to-all-done.7
  440.2 16.4 %all-to-all-done.13 = bf16[8,128,512]{2,1,0:T(8,128)(2,1)S(1)} async-done(((bf16[8,128,512]{2,1,0:T(8,128)(2,1)}), bf16[8,128,512]{2,1,0:T(8,128)(2,1)S(1)}, u32[]{:S(2)}, u32[]{:S(2)}) %all-to-all-start.13) | async-done | bytes 1048608 | tf_op jit(solution)/shard_map/all_to_all | solution.py:62
  582.1 6.9 fusion.389
  589.0 18.1 %all-to-all-done.14 = bf16[8,128,512]{2,1,0:T(8,128)(2,1)} async-done(((bf16[8,128,512]{2,1,0:T(8,128)(2,1)}), bf16[8,128,512]{2,1,0:T(8,128)(2,1)}, u32[]{:S(2)}, u32[]{:S(2)}) %all-to-all-start.14) | async-done | bytes 1048608 | tf_op jit(solution)/shard_map/all_to_all | solution.py:62
  607.2 9.1 %convolution_add_fusion.3 = f32[2048,512]{1,0:T(8,128)S(1)} fusion(f32[2048,512]{1,0:T(8,128)} %fusion.389, bf16[1024,512]{1,0:T(8,128)(2,1)} %bitcast.122, f32[1024,2048]{1,0:T(8,128)} %copy-done.301), kind=kOutput, calls=%fused_computation.83 | convolution fusion | flops 2167406592 | bytes 17825792 | tf_op jit(solution)/shard_map/dot_general | solution.py:31
  618.7 9.7 %fusion.6 = bf16[1024,2048]{1,0:T(8,128)(2,1)S(1)} fusion(f32[1024,2048]{1,0:T(8,128)} %get-tuple-element.242, bf16[1024,512]{1,0:T(8,128)(2,1)} %bitcast.96, bf16[1,1,2048,512]{3,2,1,0:T(8,128)(2,1)S(1)} %copy-done.297), kind=kOutput, calls=%fused_computation.14 | convolution fusion | flops 2189426688 | bytes 15728640 | tf_op jit(solution)/shard_map/dot_general | solution.py:37
  640.0 9.4 %fusion.20 = bf16[1024,2048]{1,0:T(8,128)(2,1)S(1)} fusion(f32[1024,2048]{1,0:T(8,128)} %copy-done.301, bf16[1024,512]{1,0:T(8,128)(2,1)} %bitcast.122, bf16[1,1,2048,512]{3,2,1,0:T(8,128)(2,1)S(1)} %copy-done.297), kind=kOutput, calls=%fused_computation.28 | convolution fusion | flops 2189426688 | bytes 15728640 | tf_op jit(solution)/shard_map/dot_general | solution.py:37
  659.0 9.4 %all-reduce.2.cloned.1.call-done = bf16[128,2060]{0,1:T(8,128)(2,1)} async-done(((bf16[128,2060]{0,1:T(8,128)(2,1)}), bf16[128,2060]{0,1:T(8,128)(2,1)}) %all-reduce.2.cloned.1.call-update) | async-done | bytes 527376 | tf_op jit(solution)/shard_map/psum | solution.py:298
  684.4 16.8 %all-to-all-done.15 = bf16[8,128,512]{2,1,0:T(8,128)(2,1)} async-done(((bf16[8,128,512]{2,1,0:T(8,128)(2,1)}), bf16[8,128,512]{2,1,0:T(8,128)(2,1)}, u32[]{:S(2)}, u32[]{:S(2)}) %all-to-all-start.15) | async-done | bytes 1048608 | tf_op jit(solution)/shard_map/all_to_all | solution.py:62
  801.5 6.4 collective-permute-done.1
  825.4 6.2 collective-permute-done.4
  (1061 shorter events, 544.2 us)
Async XLA Ops:
  7.2 30.8 %all-gather.13.cloned.1.call-start = ((), (), s32[]{:S(2)}) async-start(), calls=%async_computation.17 | async-start | bytes 2621440 | tf_op jit(solution)/shard_map/all_gather | solution.py:350
  10.4 96.7 %all-gather.15.cloned.1.call-start = ((), (), s32[]{:S(2)}) async-start(), calls=%async_computation.19 | async-start | bytes 2621440 | tf_op jit(solution)/shard_map/all_gather | solution.py:365
  11.6 103.8 %all-gather.17.cloned.1.call-start = ((), (), s32[]{:S(2)}) async-start(), calls=%async_computation.20 | async-start | bytes 2621440 | tf_op jit(solution)/shard_map/all_gather | solution.py:366
  12.7 126.0 %all-gather.11.cloned.1.call-start = ((), (), s32[]{:S(2)}) async-start(), calls=%async_computation.16 | async-start | bytes 2621440 | tf_op jit(solution)/shard_map/all_gather | solution.py:350
  13.7 275.8 %all-gather.19.cloned.1.call-start = ((), (), s32[]{:S(2)}) async-start(), calls=%async_computation.21 | async-start | bytes 2621440 | tf_op jit(solution)/shard_map/all_gather | solution.py:365
  14.3 295.4 %all-gather.21.cloned.1.call-start = ((), (), s32[]{:S(2)}) async-start(), calls=%async_computation.22 | async-start | bytes 2621440 | tf_op jit(solution)/shard_map/all_gather | solution.py:366
  63.7 37.4 %all-to-all-start = ((bf16[8,128,512]{2,1,0:T(8,128)(2,1)}), bf16[8,128,512]{2,1,0:T(8,128)(2,1)S(1)}, u32[]{:S(2)}, u32[]{:S(2)}) async-start(bf16[8,128,512]{2,1,0:T(8,128)(2,1)} %bitcast.615), calls=%async_computation | async-start | bytes 2097152 | tf_op jit(solution)/shard_map/all_to_all | solution.py:62
  101.1 31.9 %all-to-all-start.4 = ((bf16[8,128,512]{2,1,0:T(8,128)(2,1)}), bf16[8,128,512]{2,1,0:T(8,128)(2,1)}, u32[]{:S(2)}, u32[]{:S(2)}) async-start(bf16[8,128,512]{2,1,0:T(8,128)(2,1)} %bitcast.625), calls=%async_computation.4 | async-start | bytes 2097152 | tf_op jit(solution)/shard_map/all_to_all | solution.py:62
  133.0 30.0 %all-to-all-start.1 = ((bf16[8,128,512]{2,1,0:T(8,128)(2,1)}), bf16[8,128,512]{2,1,0:T(8,128)(2,1)}, u32[]{:S(2)}, u32[]{:S(2)}) async-start(bf16[8,128,512]{2,1,0:T(8,128)(2,1)} %bitcast.30), calls=%async_computation.1 | async-start | bytes 2097152 | tf_op jit(solution)/shard_map/all_to_all | solution.py:62
  163.0 32.2 %all-to-all-start.5 = ((bf16[8,128,512]{2,1,0:T(8,128)(2,1)}), bf16[8,128,512]{2,1,0:T(8,128)(2,1)}, u32[]{:S(2)}, u32[]{:S(2)}) async-start(bf16[8,128,512]{2,1,0:T(8,128)(2,1)} %bitcast.613), calls=%async_computation.5 | async-start | bytes 2097152 | tf_op jit(solution)/shard_map/all_to_all | solution.py:62
  195.3 31.1 %all-to-all-start.2 = ((bf16[8,128,512]{2,1,0:T(8,128)(2,1)}), bf16[8,128,512]{2,1,0:T(8,128)(2,1)}, u32[]{:S(2)}, u32[]{:S(2)}) async-start(bf16[8,128,512]{2,1,0:T(8,128)(2,1)} %bitcast.42), calls=%async_computation.2 | async-start | bytes 2097152 | tf_op jit(solution)/shard_map/all_to_all | solution.py:62
  226.3 29.7 %all-to-all-start.8 = ((bf16[8,128,512]{2,1,0:T(8,128)(2,1)}), bf16[8,128,512]{2,1,0:T(8,128)(2,1)}, u32[]{:S(2)}, u32[]{:S(2)}) async-start(bf16[8,128,512]{2,1,0:T(8,128)(2,1)} %bitcast.624), calls=%async_computation.8 | async-start | bytes 2097152 | tf_op jit(solution)/shard_map/all_to_all | solution.py:62
  256.0 29.7 %all-to-all-start.6 = ((bf16[8,128,512]{2,1,0:T(8,128)(2,1)}), bf16[8,128,512]{2,1,0:T(8,128)(2,1)S(1)}, u32[]{:S(2)}, u32[]{:S(2)}) async-start(bf16[8,128,512]{2,1,0:T(8,128)(2,1)} %bitcast.75), calls=%async_computation.6 | async-start | bytes 2097152 | tf_op jit(solution)/shard_map/all_to_all | solution.py:62
  285.8 30.1 %all-to-all-start.12 = ((bf16[8,128,512]{2,1,0:T(8,128)(2,1)}), bf16[8,128,512]{2,1,0:T(8,128)(2,1)S(1)}, u32[]{:S(2)}, u32[]{:S(2)}) async-start(bf16[8,128,512]{2,1,0:T(8,128)(2,1)} %bitcast.626), calls=%async_computation.12 | async-start | bytes 2097152 | tf_op jit(solution)/shard_map/all_to_all | solution.py:62
  315.9 48.5 %all-to-all-start.3 = ((bf16[8,128,512]{2,1,0:T(8,128)(2,1)}), bf16[8,128,512]{2,1,0:T(8,128)(2,1)}, u32[]{:S(2)}, u32[]{:S(2)}) async-start(bf16[8,128,512]{2,1,0:T(8,128)(2,1)} %bitcast.623), calls=%async_computation.3 | async-start | bytes 2097152 | tf_op jit(solution)/shard_map/all_to_all | solution.py:62
  331.0 47.2 %collective-permute-start.16 = (bf16[2,512,512]{2,1,0:T(8,128)(2,1)S(1)}, bf16[2,512,512]{2,1,0:T(8,128)(2,1)}, u32[]{:S(2)}, u32[]{:S(2)}) collective-permute-start(bf16[2,512,512]{2,1,0:T(8,128)(2,1)S(1)} %fusion.243), channel_id=1, source_target_pairs={{0,1},{1,0},{2,3},{3,2},{4,5},{5,4},{6,7},{7,6},{8,9},{9,8},{10,11... | collective-permute-start | bytes 3145736 | tf_op jit(solution)/shard_map/ppermute | solution.py:261
  361.0 20.7 %collective-permute-start.12 = (bf16[2,128,2048]{2,1,0:T(8,128)(2,1)}, bf16[2,128,2048]{2,1,0:T(8,128)(2,1)}, u32[]{:S(2)}, u32[]{:S(2)}) collective-permute-start(bf16[2,128,2048]{2,1,0:T(8,128)(2,1)} %fusion.241), channel_id=1, source_target_pairs={{0,1},{1,0},{2,3},{3,2},{4,5},{5,4},{6,7},{7,6},{8,9},{9,8},{10,11... | collective-permute-start | bytes 3145736 | tf_op jit(solution)/shard_map/ppermute | solution.py:261
  364.4 32.5 %all-to-all-start.9 = ((bf16[8,128,512]{2,1,0:T(8,128)(2,1)}), bf16[8,128,512]{2,1,0:T(8,128)(2,1)}, u32[]{:S(2)}, u32[]{:S(2)}) async-start(bf16[8,128,512]{2,1,0:T(8,128)(2,1)} %bitcast.83), calls=%async_computation.9 | async-start | bytes 2097152 | tf_op jit(solution)/shard_map/all_to_all | solution.py:62
  380.1 30.2 %collective-permute-start.17 = (bf16[1,512,512]{2,1,0:T(8,128)(2,1)S(1)}, bf16[1,512,512]{2,1,0:T(8,128)(2,1)}, u32[]{:S(2)}, u32[]{:S(2)}) collective-permute-start(bf16[1,512,512]{2,1,0:T(8,128)(2,1)S(1)} %dynamic-slice_convert_fusion.4), channel_id=1, source_target_pairs={{0,2},{1,3},{2,0},{3,1},{4,6},{5,7},{6,4},{7,5},{8,10},{9,11},{10,... | collective-permute-start | bytes 1572872 | tf_op jit(solution)/shard_map/ppermute | solution.py:261
  396.9 29.9 %all-to-all-start.7 = ((bf16[8,128,512]{2,1,0:T(8,128)(2,1)}), bf16[8,128,512]{2,1,0:T(8,128)(2,1)}, u32[]{:S(2)}, u32[]{:S(2)}) async-start(bf16[8,128,512]{2,1,0:T(8,128)(2,1)} %bitcast.616), calls=%async_computation.7 | async-start | bytes 2097152 | tf_op jit(solution)/shard_map/all_to_all | solution.py:62
  426.8 29.9 %all-to-all-start.13 = ((bf16[8,128,512]{2,1,0:T(8,128)(2,1)}), bf16[8,128,512]{2,1,0:T(8,128)(2,1)S(1)}, u32[]{:S(2)}, u32[]{:S(2)}) async-start(bf16[8,128,512]{2,1,0:T(8,128)(2,1)} %bitcast.111), calls=%async_computation.13 | async-start | bytes 2097152 | tf_op jit(solution)/shard_map/all_to_all | solution.py:62
  541.6 30.1 %all-to-all-start.10 = ((bf16[8,128,512]{2,1,0:T(8,128)(2,1)}), bf16[8,128,512]{2,1,0:T(8,128)(2,1)}, u32[]{:S(2)}, u32[]{:S(2)}) async-start(bf16[8,128,512]{2,1,0:T(8,128)(2,1)} %bitcast.614), calls=%async_computation.10 | async-start | bytes 2097152 | tf_op jit(solution)/shard_map/all_to_all | solution.py:62
  565.4 14.7 %collective-permute-start.9 = (bf16[1,128,2060]{1,2,0:T(8,128)(2,1)}, bf16[1,128,2060]{1,2,0:T(8,128)(2,1)}, u32[]{:S(2)}, u32[]{:S(2)}) collective-permute-start(bf16[1,128,2060]{1,2,0:T(8,128)(2,1)} %dynamic-slice_convert_fusion.2), channel_id=1, source_target_pairs={{0,2},{1,3},{2,0},{3,1},{4,6},{5,7},{6,4},{7,5},{8,10},{9,11},{10,... | collective-permute-start | bytes 1582088 | tf_op jit(solution)/shard_map/ppermute | solution.py:261
  571.7 35.5 %all-to-all-start.14 = ((bf16[8,128,512]{2,1,0:T(8,128)(2,1)}), bf16[8,128,512]{2,1,0:T(8,128)(2,1)}, u32[]{:S(2)}, u32[]{:S(2)}) async-start(bf16[8,128,512]{2,1,0:T(8,128)(2,1)} %bitcast.617), calls=%async_computation.14 | async-start | bytes 2097152 | tf_op jit(solution)/shard_map/all_to_all | solution.py:62
  575.9 92.5 %all-reduce.2.cloned.1.call-start = ((), (), s32[]{:S(2)}) async-start(), calls=%async_computation.18 | async-start | bytes 1056768 | tf_op jit(solution)/shard_map/psum | solution.py:298
  617.5 161.3 %collective-permute-start.14 = (bf16[2,512,512]{2,1,0:T(8,128)(2,1)}, bf16[2,512,512]{2,1,0:T(8,128)(2,1)}, u32[]{:S(2)}, u32[]{:S(2)}) collective-permute-start(bf16[2,512,512]{2,1,0:T(8,128)(2,1)} %fusion.242), channel_id=1, source_target_pairs={{0,1},{1,0},{2,3},{3,2},{4,5},{5,4},{6,7},{7,6},{8,9},{9,8},{10,11... | collective-permute-start | bytes 3145736 | tf_op jit(solution)/shard_map/ppermute | solution.py:261
  636.2 35.0 %all-to-all-start.11 = ((bf16[8,128,512]{2,1,0:T(8,128)(2,1)}), bf16[8,128,512]{2,1,0:T(8,128)(2,1)S(1)}, u32[]{:S(2)}, u32[]{:S(2)}) async-start(bf16[8,128,512]{2,1,0:T(8,128)(2,1)} %bitcast.97), calls=%async_computation.11 | async-start | bytes 2097152 | tf_op jit(solution)/shard_map/all_to_all | solution.py:62
  655.6 21.8 %collective-permute-start.10 = (bf16[2,128,2048]{2,1,0:T(8,128)(2,1)S(1)}, bf16[2,128,2048]{2,1,0:T(8,128)(2,1)}, u32[]{:S(2)}, u32[]{:S(2)}) collective-permute-start(bf16[2,128,2048]{2,1,0:T(8,128)(2,1)S(1)} %fusion.240), channel_id=1, source_target_pairs={{0,1},{1,0},{2,3},{3,2},{4,5},{5,4},{6,7},{7,6},{8,9},{9,8},{10,11... | collective-permute-start | bytes 3145736 | tf_op jit(solution)/shard_map/ppermute | solution.py:261
  671.2 29.9 %all-to-all-start.15 = ((bf16[8,128,512]{2,1,0:T(8,128)(2,1)}), bf16[8,128,512]{2,1,0:T(8,128)(2,1)}, u32[]{:S(2)}, u32[]{:S(2)}) async-start(bf16[8,128,512]{2,1,0:T(8,128)(2,1)} %bitcast.620), calls=%async_computation.15 | async-start | bytes 2097152 | tf_op jit(solution)/shard_map/all_to_all | solution.py:62
  681.8 101.9 %collective-permute-start.11 = (bf16[1,128,2048]{2,1,0:T(8,128)(2,1)}, bf16[1,128,2048]{2,1,0:T(8,128)(2,1)}, u32[]{:S(2)}, u32[]{:S(2)}) collective-permute-start(bf16[1,128,2048]{2,1,0:T(8,128)(2,1)} %dynamic-slice_convert_fusion.7), channel_id=1, source_target_pairs={{0,2},{1,3},{2,0},{3,1},{4,6},{5,7},{6,4},{7,5},{8,10},{9,11},{10,... | collective-permute-start | bytes 1572872 | tf_op jit(solution)/shard_map/ppermute | solution.py:261
  782.2 15.1 %collective-permute-start.15 = (bf16[1,512,512]{2,1,0:T(8,128)(2,1)}, bf16[1,512,512]{2,1,0:T(8,128)(2,1)}, u32[]{:S(2)}, u32[]{:S(2)}) collective-permute-start(bf16[1,512,512]{2,1,0:T(8,128)(2,1)} %dynamic-slice_convert_fusion.5), channel_id=1, source_target_pairs={{0,2},{1,3},{2,0},{3,1},{4,6},{5,7},{6,4},{7,5},{8,10},{9,11},{10,... | collective-permute-start | bytes 1572872 | tf_op jit(solution)/shard_map/ppermute | solution.py:261
  791.7 16.3 %collective-permute-start.1 = (bf16[1,128,2060]{1,2,0:T(8,128)(2,1)S(1)}, bf16[1,128,2060]{1,2,0:T(8,128)(2,1)S(1)}, u32[]{:S(2)}, u32[]{:S(2)}) collective-permute-start(bf16[1,128,2060]{1,2,0:T(8,128)(2,1)S(1)} %dynamic-slice_convert_fusion.3), channel_id=1, source_target_pairs={{0,2},{1,3},{2,0},{3,1},{4,6},{5,7},{6,4},{7,5},{8,10},{9,11},{10,... | collective-permute-start | bytes 1582088 | tf_op jit(solution)/shard_map/ppermute | solution.py:261
  (316 other events, 2098.8 us)
Sparse Core Ops, SparseCore 0:
  10.5 25.2 all-gather.12
  37.4 22.5 all-gather.14
  61.6 22.5 all-gather.16
  85.6 22.5 all-gather.10
  109.6 22.5 all-gather.18
  133.6 22.5 all-gather.20
  582.2 86.1 all-reduce.1

commit v8 on v5

--- a/solution.py
+++ b/solution.py
@@ -100,6 +100,7 @@
     row_block = received.reshape(experts * capacity, D)
     hidden_pre = jnp.dot(row_block, in_w[0], preferred_element_type=jnp.float32)
     hidden_act = gelu_tanh(hidden_pre).astype(jnp.bfloat16)
+    slope = jax.vjp(gelu_tanh, hidden_pre)[1](jnp.ones_like(hidden_pre))[0].astype(jnp.bfloat16)
     expert_rows = jnp.dot(hidden_act, out_w[0], preferred_element_type=jnp.float32).astype(
         jnp.bfloat16
     )
@@ -131,7 +132,8 @@
         weight_pair,
         pair_rows,
         row_block,
-        hidden_pre,
+        hidden_act,
+        slope,
     )
     return (output, saved_state)
 
@@ -150,7 +152,8 @@
         weight_pair,
         pair_rows,
         row_block,
-        hidden_pre,
+        hidden_act,
+        slope,
     ) = saved_state
     pair_hot, token_hot, kept_mask = tables
     norm_gains, norm_shifts, qkv_w, proj_w, router_w, in_w, out_w = weights
@@ -172,10 +175,9 @@
     d_slots = dot_first(pair_hot, d_pairs).astype(jnp.bfloat16).reshape(experts, capacity, D)
     d_expert_out = lax.all_to_all(d_slots, "expert", split_axis=0, concat_axis=0, tiled=True)
     flat_out = d_expert_out.reshape(experts * capacity, D)
-    hidden_act = gelu_tanh(hidden_pre).astype(jnp.bfloat16)
     g_out = dot_first(hidden_act, flat_out)
     d_act = dot_last(flat_out, out_w[0])
-    d_pre = jax.vjp(gelu_tanh, hidden_pre)[1](d_act)[0].astype(jnp.bfloat16)
+    d_pre = (d_act * slope.astype(jnp.float32)).astype(jnp.bfloat16)
     g_in = dot_first(row_block, d_pre)
     d_rows = dot_last(d_pre, in_w[0]).astype(jnp.bfloat16).reshape(experts, capacity, D)
     d_back = lax.all_to_all(d_rows, "expert", split_axis=0, concat_axis=0, tiled=True)

time: 938 us -> 937 us (level)
  no operation moved by 1% of the time
where the time goes in v8:
time: 937 us; the launch traced here: 926 us
  matrix products  310 us (33%)
  waiting for transfers between devices  252 us (27%)
  local copies, waits for them, and re-layouts  195 us (21%)
  starting transfers between devices  81 us (9%)
  other arithmetic  63.2 us (7%)
  between operations  18.5 us (2%)
    dot_general x30, matrix products, dot_first(): lax.dot_general(left, right, (((0,), (0,)), ((), ())), preferred_element_...  101 us
    dot_general x20, matrix products, dot_last(): lax.dot_general(left, right, (((1,), (1,)), ((), ())), preferred_element_...  74.5 us
    all_to_all x4, waiting for transfers between devices, forward_layer(): lax.all_to_all(sending.reshape(experts, capacity, D), 'expert', split_axi...  59 us
    unnamed x594, local copies, waits for them, and re-layouts  57.4 us
    all_to_all x4, waiting for transfers between devices, backward_layer(): lax.all_to_all(d_rows, 'expert', split_axis=0, concat_axis=0, tiled=True)  48.8 us
    all_to_all x4, waiting for transfers between devices, forward_layer(): lax.all_to_all(expert_rows.reshape(experts, capacity, D), 'expert', split...  39.7 us
    all_to_all x4, waiting for transfers between devices, backward_layer(): lax.all_to_all(d_slots, 'expert', split_axis=0, concat_axis=0, tiled=True)  37.8 us
    dot_general x4, matrix products, forward_layer(): hidden_pre = jnp.dot(row_block, in_w[0], preferred_element_type=jnp.float32)  31.8 us
  transfers between devices with their start and end apart: 41, of which 26 were waited for; matrix products, arithmetic and copies ran while one was open for 44% of the time, Pallas kernels for 0%

profile of v8, /device:TPU:0, one launch (start us, length us, event | category | flops | bytes accessed | tf_op | source)
XLA Modules:
  0.0 925.9 jit_solution(9465717246666787908)
XLA Ops:
  27.4 9.8 %all-gather.11.cloned.1.call-done = bf16[512,2048]{1,0:T(8,128)(2,1)} async-done(((bf16[128,2048]{1,0:T(8,128)(2,1)}), bf16[512,2048]{1,0:T(8,128)(2,1)}) %all-gather.11.cloned.1.call-update) | async-done | bytes 2097168 | tf_op jit(solution)/shard_map/all_gather | solution.py:348
  96.6 18.5 %all-to-all-done.4 = bf16[8,128,512]{2,1,0:T(8,128)(2,1)S(1)} async-done(((bf16[8,128,512]{2,1,0:T(8,128)(2,1)}), bf16[8,128,512]{2,1,0:T(8,128)(2,1)S(1)}, u32[]{:S(2)}, u32[]{:S(2)}) %all-to-all-start.4) | async-done | bytes 1048608 | tf_op jit(solution)/shard_map/all_to_all | solution.py:97
  120.9 7.6 fusion.88
  128.5 7.7 fusion.137
  136.2 9.7 %all-to-all-done = bf16[8,128,512]{2,1,0:T(8,128)(2,1)S(1)} async-done(((bf16[8,128,512]{2,1,0:T(8,128)(2,1)}), bf16[8,128,512]{2,1,0:T(8,128)(2,1)S(1)}, u32[]{:S(2)}, u32[]{:S(2)}) %all-to-all-start) | async-done | bytes 1048608 | tf_op jit(solution)/shard_map/all_to_all | solution.py:97
  150.5 7.7 multiply_convert_fusion.7
  163.4 12.3 %all-to-all-done.5 = bf16[8,128,512]{2,1,0:T(8,128)(2,1)} async-done(((bf16[8,128,512]{2,1,0:T(8,128)(2,1)}), bf16[8,128,512]{2,1,0:T(8,128)(2,1)}, u32[]{:S(2)}, u32[]{:S(2)}) %all-to-all-start.5) | async-done | bytes 1048608 | tf_op jit(solution)/shard_map/all_to_all | solution.py:107
  184.6 20.9 %all-to-all-done.1 = bf16[8,128,512]{2,1,0:T(8,128)(2,1)S(1)} async-done(((bf16[8,128,512]{2,1,0:T(8,128)(2,1)}), bf16[8,128,512]{2,1,0:T(8,128)(2,1)S(1)}, u32[]{:S(2)}, u32[]{:S(2)}) %all-to-all-start.1) | async-done | bytes 1048608 | tf_op jit(solution)/shard_map/all_to_all | solution.py:107
  273.6 11.6 %all-to-all-done.2 = bf16[8,128,512]{2,1,0:T(8,128)(2,1)} async-done(((bf16[8,128,512]{2,1,0:T(8,128)(2,1)}), bf16[8,128,512]{2,1,0:T(8,128)(2,1)}, u32[]{:S(2)}, u32[]{:S(2)}) %all-to-all-start.2) | async-done | bytes 1048608 | tf_op jit(solution)/shard_map/all_to_all | solution.py:97
  300.9 14.1 %all-to-all-done.8 = bf16[8,128,512]{2,1,0:T(8,128)(2,1)} async-done(((bf16[8,128,512]{2,1,0:T(8,128)(2,1)}), bf16[8,128,512]{2,1,0:T(8,128)(2,1)}, u32[]{:S(2)}, u32[]{:S(2)}) %all-to-all-start.8) | async-done | bytes 1048608 | tf_op jit(solution)/shard_map/all_to_all | solution.py:176
  325.4 19.2 %all-to-all-done.6 = bf16[8,128,512]{2,1,0:T(8,128)(2,1)} async-done(((bf16[8,128,512]{2,1,0:T(8,128)(2,1)}), bf16[8,128,512]{2,1,0:T(8,128)(2,1)}, u32[]{:S(2)}, u32[]{:S(2)}) %all-to-all-start.6) | async-done | bytes 1048608 | tf_op jit(solution)/shard_map/all_to_all | solution.py:97
  349.1 8.8 multiply_convert_fusion.6
  357.9 7.7 fusion.74
  371.2 6.2 fusion.146
  377.4 6.3 all-to-all-start.3
  383.7 9.1 convolution_add_fusion.2
  393.9 10.8 %multiply_convert_fusion.1 = bf16[1024,2048]{1,0:T(8,128)(2,1)S(1)} fusion(bf16[1024,512]{1,0:T(8,128)(2,1)} %bitcast.98, f32[1024,2048]{1,0:T(8,128)} %fusion.74, bf16[1,1,2048,512]{3,2,1,0:T(8,128)(2,1)S(1)} %copy-done.280), kind=kOutput, calls=%fused_computation.37 | convolution fusion | flops 2191523840 | bytes 15728640 | tf_op jit(solution)/shard_map/dot_general | solution.py:38
  404.8 9.3 %multiply_convert_fusion.3 = bf16[1024,2048]{1,0:T(8,128)(2,1)S(1)} fusion(bf16[1024,512]{1,0:T(8,128)(2,1)} %bitcast.74, f32[1024,2048]{1,0:T(8,128)S(1)} %bitcast.652, bf16[1,1,2048,512]{3,2,1,0:T(8,128)(2,1)S(1)} %copy-done.280), kind=kOutput, calls=%fused_computation.39 | convolution fusion | flops 2191523840 | bytes 15728640 | tf_op jit(solution)/shard_map/dot_general | solution.py:38
  434.1 7.9 fusion.149
  449.2 11.5 %all-to-all-done.9 = bf16[8,128,512]{2,1,0:T(8,128)(2,1)} async-done(((bf16[8,128,512]{2,1,0:T(8,128)(2,1)}), bf16[8,128,512]{2,1,0:T(8,128)(2,1)}, u32[]{:S(2)}, u32[]{:S(2)}) %all-to-all-start.9) | async-done | bytes 1048608 | tf_op jit(solution)/shard_map/all_to_all | solution.py:183
  466.8 6.3 fusion.143
  484.1 6.5 all-to-all-done.7
  502.1 18.5 %all-to-all-done.13 = bf16[8,128,512]{2,1,0:T(8,128)(2,1)} async-done(((bf16[8,128,512]{2,1,0:T(8,128)(2,1)}), bf16[8,128,512]{2,1,0:T(8,128)(2,1)}, u32[]{:S(2)}, u32[]{:S(2)}) %all-to-all-start.13) | async-done | bytes 1048608 | tf_op jit(solution)/shard_map/all_to_all | solution.py:183
  646.5 6.9 fusion.385
  653.4 18.0 %all-to-all-done.14 = bf16[8,128,512]{2,1,0:T(8,128)(2,1)} async-done(((bf16[8,128,512]{2,1,0:T(8,128)(2,1)}), bf16[8,128,512]{2,1,0:T(8,128)(2,1)}, u32[]{:S(2)}, u32[]{:S(2)}) %all-to-all-start.14) | async-done | bytes 1048608 | tf_op jit(solution)/shard_map/all_to_all | solution.py:176
  671.4 9.1 convolution_add_fusion.3
  682.9 9.3 %multiply_convert_fusion.2 = bf16[1024,2048]{1,0:T(8,128)(2,1)S(1)} fusion(bf16[1024,512]{1,0:T(8,128)(2,1)} %bitcast.86, f32[1024,2048]{1,0:T(8,128)} %get-tuple-element.191, bf16[1,1,2048,512]{3,2,1,0:T(8,128)(2,1)S(1)} %copy-done.277), kind=kOutput, calls=%fused_computation.38 | convolution fusion | flops 2191523840 | bytes 15728640 | tf_op jit(solution)/shard_map/dot_general | solution.py:38
  704.1 9.1 multiply_convert_fusion
  721.5 10.9 %all-reduce.2.cloned.1.call-done = bf16[128,2060]{0,1:T(8,128)(2,1)} async-done(((bf16[128,2060]{0,1:T(8,128)(2,1)}), bf16[128,2060]{0,1:T(8,128)(2,1)}) %all-reduce.2.cloned.1.call-update) | async-done | bytes 527376 | tf_op jit(solution)/shard_map/psum | solution.py:296
  747.9 17.5 %all-to-all-done.15 = bf16[8,128,512]{2,1,0:T(8,128)(2,1)} async-done(((bf16[8,128,512]{2,1,0:T(8,128)(2,1)}), bf16[8,128,512]{2,1,0:T(8,128)(2,1)}, u32[]{:S(2)}, u32[]{:S(2)}) %all-to-all-start.15) | async-done | bytes 1048608 | tf_op jit(solution)/shard_map/all_to_all | solution.py:183
  865.7 6.4 collective-permute-done.1
  876.5 6.9 collective-permute-done.2
  (1008 shorter events, 565.6 us)
Async XLA Ops:
  7.2 30.0 %all-gather.11.cloned.1.call-start = ((), (), s32[]{:S(2)}) async-start(), calls=%async_computation.16 | async-start | bytes 2621440 | tf_op jit(solution)/shard_map/all_gather | solution.py:348
  11.7 109.1 %all-gather.15.cloned.1.call-start = ((), (), s32[]{:S(2)}) async-start(), calls=%async_computation.19 | async-start | bytes 2621440 | tf_op jit(solution)/shard_map/all_gather | solution.py:363
  12.9 115.6 %all-gather.17.cloned.1.call-start = ((), (), s32[]{:S(2)}) async-start(), calls=%async_computation.20 | async-start | bytes 2621440 | tf_op jit(solution)/shard_map/all_gather | solution.py:364
  83.4 31.8 %all-to-all-start.4 = ((bf16[8,128,512]{2,1,0:T(8,128)(2,1)}), bf16[8,128,512]{2,1,0:T(8,128)(2,1)S(1)}, u32[]{:S(2)}, u32[]{:S(2)}) async-start(bf16[8,128,512]{2,1,0:T(8,128)(2,1)} %bitcast.584), calls=%async_computation.4 | async-start | bytes 2097152 | tf_op jit(solution)/shard_map/all_to_all | solution.py:97
  89.0 121.0 %all-gather.13.cloned.1.call-start = ((), (), s32[]{:S(2)}) async-start(), calls=%async_computation.17 | async-start | bytes 2621440 | tf_op jit(solution)/shard_map/all_gather | solution.py:348
  116.1 29.8 %all-to-all-start = ((bf16[8,128,512]{2,1,0:T(8,128)(2,1)}), bf16[8,128,512]{2,1,0:T(8,128)(2,1)S(1)}, u32[]{:S(2)}, u32[]{:S(2)}) async-start(bf16[8,128,512]{2,1,0:T(8,128)(2,1)} %bitcast.586), calls=%async_computation | async-start | bytes 2097152 | tf_op jit(solution)/shard_map/all_to_all | solution.py:97
  145.9 29.8 %all-to-all-start.5 = ((bf16[8,128,512]{2,1,0:T(8,128)(2,1)}), bf16[8,128,512]{2,1,0:T(8,128)(2,1)}, u32[]{:S(2)}, u32[]{:S(2)}) async-start(bf16[8,128,512]{2,1,0:T(8,128)(2,1)} %bitcast.594), calls=%async_computation.5 | async-start | bytes 2097152 | tf_op jit(solution)/shard_map/all_to_all | solution.py:107
  175.7 29.8 %all-to-all-start.1 = ((bf16[8,128,512]{2,1,0:T(8,128)(2,1)}), bf16[8,128,512]{2,1,0:T(8,128)(2,1)S(1)}, u32[]{:S(2)}, u32[]{:S(2)}) async-start(bf16[8,128,512]{2,1,0:T(8,128)(2,1)} %bitcast.592), calls=%async_computation.1 | async-start | bytes 2097152 | tf_op jit(solution)/shard_map/all_to_all | solution.py:107
  255.4 29.8 %all-to-all-start.2 = ((bf16[8,128,512]{2,1,0:T(8,128)(2,1)}), bf16[8,128,512]{2,1,0:T(8,128)(2,1)}, u32[]{:S(2)}, u32[]{:S(2)}) async-start(bf16[8,128,512]{2,1,0:T(8,128)(2,1)} %bitcast.587), calls=%async_computation.2 | async-start | bytes 2097152 | tf_op jit(solution)/shard_map/all_to_all | solution.py:97
  259.7 89.4 %all-gather.19.cloned.1.call-start = ((), (), s32[]{:S(2)}) async-start(), calls=%async_computation.21 | async-start | bytes 2621440 | tf_op jit(solution)/shard_map/all_gather | solution.py:363
  285.2 29.7 %all-to-all-start.8 = ((bf16[8,128,512]{2,1,0:T(8,128)(2,1)}), bf16[8,128,512]{2,1,0:T(8,128)(2,1)}, u32[]{:S(2)}, u32[]{:S(2)}) async-start(bf16[8,128,512]{2,1,0:T(8,128)(2,1)} %bitcast.578), calls=%async_computation.8 | async-start | bytes 2097152 | tf_op jit(solution)/shard_map/all_to_all | solution.py:176
  289.5 81.7 %all-gather.21.cloned.1.call-start = ((), (), s32[]{:S(2)}) async-start(), calls=%async_computation.22 | async-start | bytes 2621440 | tf_op jit(solution)/shard_map/all_gather | solution.py:364
  315.0 29.6 %all-to-all-start.6 = ((bf16[8,128,512]{2,1,0:T(8,128)(2,1)}), bf16[8,128,512]{2,1,0:T(8,128)(2,1)}, u32[]{:S(2)}, u32[]{:S(2)}) async-start(bf16[8,128,512]{2,1,0:T(8,128)(2,1)} %bitcast.590), calls=%async_computation.6 | async-start | bytes 2097152 | tf_op jit(solution)/shard_map/all_to_all | solution.py:97
  344.6 32.8 %all-to-all-start.12 = ((bf16[8,128,512]{2,1,0:T(8,128)(2,1)}), bf16[8,128,512]{2,1,0:T(8,128)(2,1)}, u32[]{:S(2)}, u32[]{:S(2)}) async-start(bf16[8,128,512]{2,1,0:T(8,128)(2,1)} %bitcast.593), calls=%async_computation.12 | async-start | bytes 2097152 | tf_op jit(solution)/shard_map/all_to_all | solution.py:176
  377.4 50.7 %all-to-all-start.3 = ((bf16[8,128,512]{2,1,0:T(8,128)(2,1)}), bf16[8,128,512]{2,1,0:T(8,128)(2,1)}, u32[]{:S(2)}, u32[]{:S(2)}) async-start(bf16[8,128,512]{2,1,0:T(8,128)(2,1)} %bitcast.588), calls=%async_computation.3 | async-start | bytes 2097152 | tf_op jit(solution)/shard_map/all_to_all | solution.py:107
  393.9 48.1 %collective-permute-start.16 = (bf16[2,512,512]{2,1,0:T(8,128)(2,1)}, bf16[2,512,512]{2,1,0:T(8,128)(2,1)}, u32[]{:S(2)}, u32[]{:S(2)}) collective-permute-start(bf16[2,512,512]{2,1,0:T(8,128)(2,1)} %fusion.231), channel_id=1, source_target_pairs={{0,1},{1,0},{2,3},{3,2},{4,5},{5,4},{6,7},{7,6},{8,9},{9,8},{10,11... | collective-permute-start | bytes 3145736 | tf_op jit(solution)/shard_map/ppermute | solution.py:245
  424.8 21.6 %collective-permute-start.12 = (bf16[2,128,2048]{2,1,0:T(8,128)(2,1)}, bf16[2,128,2048]{2,1,0:T(8,128)(2,1)}, u32[]{:S(2)}, u32[]{:S(2)}) collective-permute-start(bf16[2,128,2048]{2,1,0:T(8,128)(2,1)} %fusion.229), channel_id=1, source_target_pairs={{0,1},{1,0},{2,3},{3,2},{4,5},{5,4},{6,7},{7,6},{8,9},{9,8},{10,11... | collective-permute-start | bytes 3145736 | tf_op jit(solution)/shard_map/ppermute | solution.py:245
  428.1 32.5 %all-to-all-start.9 = ((bf16[8,128,512]{2,1,0:T(8,128)(2,1)}), bf16[8,128,512]{2,1,0:T(8,128)(2,1)}, u32[]{:S(2)}, u32[]{:S(2)}) async-start(bf16[8,128,512]{2,1,0:T(8,128)(2,1)} %bitcast.591), calls=%async_computation.9 | async-start | bytes 2097152 | tf_op jit(solution)/shard_map/all_to_all | solution.py:183
  445.9 27.1 %collective-permute-start.17 = (bf16[1,512,512]{2,1,0:T(8,128)(2,1)}, bf16[1,512,512]{2,1,0:T(8,128)(2,1)}, u32[]{:S(2)}, u32[]{:S(2)}) collective-permute-start(bf16[1,512,512]{2,1,0:T(8,128)(2,1)} %dynamic-slice_convert_fusion.4), channel_id=1, source_target_pairs={{0,2},{1,3},{2,0},{3,1},{4,6},{5,7},{6,4},{7,5},{8,10},{9,11},{10,... | collective-permute-start | bytes 1572872 | tf_op jit(solution)/shard_map/ppermute | solution.py:245
  460.7 29.9 %all-to-all-start.7 = ((bf16[8,128,512]{2,1,0:T(8,128)(2,1)}), bf16[8,128,512]{2,1,0:T(8,128)(2,1)}, u32[]{:S(2)}, u32[]{:S(2)}) async-start(bf16[8,128,512]{2,1,0:T(8,128)(2,1)} %bitcast.581), calls=%async_computation.7 | async-start | bytes 2097152 | tf_op jit(solution)/shard_map/all_to_all | solution.py:107
  490.6 30.0 %all-to-all-start.13 = ((bf16[8,128,512]{2,1,0:T(8,128)(2,1)}), bf16[8,128,512]{2,1,0:T(8,128)(2,1)}, u32[]{:S(2)}, u32[]{:S(2)}) async-start(bf16[8,128,512]{2,1,0:T(8,128)(2,1)} %bitcast.580), calls=%async_computation.13 | async-start | bytes 2097152 | tf_op jit(solution)/shard_map/all_to_all | solution.py:183
  606.1 29.9 %all-to-all-start.10 = ((bf16[8,128,512]{2,1,0:T(8,128)(2,1)}), bf16[8,128,512]{2,1,0:T(8,128)(2,1)}, u32[]{:S(2)}, u32[]{:S(2)}) async-start(bf16[8,128,512]{2,1,0:T(8,128)(2,1)} %bitcast.579), calls=%async_computation.10 | async-start | bytes 2097152 | tf_op jit(solution)/shard_map/all_to_all | solution.py:176
  629.8 14.7 %collective-permute-start.9 = (bf16[1,128,2060]{1,2,0:T(8,128)(2,1)}, bf16[1,128,2060]{1,2,0:T(8,128)(2,1)}, u32[]{:S(2)}, u32[]{:S(2)}) collective-permute-start(bf16[1,128,2060]{1,2,0:T(8,128)(2,1)} %dynamic-slice_convert_fusion.2), channel_id=1, source_target_pairs={{0,2},{1,3},{2,0},{3,1},{4,6},{5,7},{6,4},{7,5},{8,10},{9,11},{10,... | collective-permute-start | bytes 1582088 | tf_op jit(solution)/shard_map/ppermute | solution.py:245
  636.0 35.4 %all-to-all-start.14 = ((bf16[8,128,512]{2,1,0:T(8,128)(2,1)}), bf16[8,128,512]{2,1,0:T(8,128)(2,1)}, u32[]{:S(2)}, u32[]{:S(2)}) async-start(bf16[8,128,512]{2,1,0:T(8,128)(2,1)} %bitcast.582), calls=%async_computation.14 | async-start | bytes 2097152 | tf_op jit(solution)/shard_map/all_to_all | solution.py:176
  640.2 92.2 %all-reduce.2.cloned.1.call-start = ((), (), s32[]{:S(2)}) async-start(), calls=%async_computation.18 | async-start | bytes 1056768 | tf_op jit(solution)/shard_map/psum | solution.py:296
  681.8 161.2 %collective-permute-start.14 = (bf16[2,512,512]{2,1,0:T(8,128)(2,1)}, bf16[2,512,512]{2,1,0:T(8,128)(2,1)}, u32[]{:S(2)}, u32[]{:S(2)}) collective-permute-start(bf16[2,512,512]{2,1,0:T(8,128)(2,1)} %fusion.230), channel_id=1, source_target_pairs={{0,1},{1,0},{2,3},{3,2},{4,5},{5,4},{6,7},{7,6},{8,9},{9,8},{10,11... | collective-permute-start | bytes 3145736 | tf_op jit(solution)/shard_map/ppermute | solution.py:245
  700.1 35.4 %all-to-all-start.11 = ((bf16[8,128,512]{2,1,0:T(8,128)(2,1)}), bf16[8,128,512]{2,1,0:T(8,128)(2,1)S(1)}, u32[]{:S(2)}, u32[]{:S(2)}) async-start(bf16[8,128,512]{2,1,0:T(8,128)(2,1)} %bitcast.87), calls=%async_computation.11 | async-start | bytes 2097152 | tf_op jit(solution)/shard_map/all_to_all | solution.py:183
  718.1 24.1 %collective-permute-start.10 = (bf16[2,128,2048]{2,1,0:T(8,128)(2,1)S(1)}, bf16[2,128,2048]{2,1,0:T(8,128)(2,1)}, u32[]{:S(2)}, u32[]{:S(2)}) collective-permute-start(bf16[2,128,2048]{2,1,0:T(8,128)(2,1)S(1)} %fusion.228), channel_id=1, source_target_pairs={{0,1},{1,0},{2,3},{3,2},{4,5},{5,4},{6,7},{7,6},{8,9},{9,8},{10,11... | collective-permute-start | bytes 3145736 | tf_op jit(solution)/shard_map/ppermute | solution.py:245
  735.5 29.9 %all-to-all-start.15 = ((bf16[8,128,512]{2,1,0:T(8,128)(2,1)}), bf16[8,128,512]{2,1,0:T(8,128)(2,1)}, u32[]{:S(2)}, u32[]{:S(2)}) async-start(bf16[8,128,512]{2,1,0:T(8,128)(2,1)} %bitcast.585), calls=%async_computation.15 | async-start | bytes 2097152 | tf_op jit(solution)/shard_map/all_to_all | solution.py:183
  746.5 100.1 %collective-permute-start.11 = (bf16[1,128,2048]{2,1,0:T(8,128)(2,1)}, bf16[1,128,2048]{2,1,0:T(8,128)(2,1)}, u32[]{:S(2)}, u32[]{:S(2)}) collective-permute-start(bf16[1,128,2048]{2,1,0:T(8,128)(2,1)} %dynamic-slice_convert_fusion.7), channel_id=1, source_target_pairs={{0,2},{1,3},{2,0},{3,1},{4,6},{5,7},{6,4},{7,5},{8,10},{9,11},{10,... | collective-permute-start | bytes 1572872 | tf_op jit(solution)/shard_map/ppermute | solution.py:245
  846.3 15.1 %collective-permute-start.15 = (bf16[1,512,512]{2,1,0:T(8,128)(2,1)}, bf16[1,512,512]{2,1,0:T(8,128)(2,1)}, u32[]{:S(2)}, u32[]{:S(2)}) collective-permute-start(bf16[1,512,512]{2,1,0:T(8,128)(2,1)} %dynamic-slice_convert_fusion.5), channel_id=1, source_target_pairs={{0,2},{1,3},{2,0},{3,1},{4,6},{5,7},{6,4},{7,5},{8,10},{9,11},{10,... | collective-permute-start | bytes 1572872 | tf_op jit(solution)/shard_map/ppermute | solution.py:245
  854.7 17.4 %collective-permute-start.1 = (bf16[1,128,2060]{1,2,0:T(8,128)(2,1)S(1)}, bf16[1,128,2060]{1,2,0:T(8,128)(2,1)S(1)}, u32[]{:S(2)}, u32[]{:S(2)}) collective-permute-start(bf16[1,128,2060]{1,2,0:T(8,128)(2,1)S(1)} %dynamic-slice_convert_fusion.3), channel_id=1, source_target_pairs={{0,2},{1,3},{2,0},{3,1},{4,6},{5,7},{6,4},{7,5},{8,10},{9,11},{10,... | collective-permute-start | bytes 1582088 | tf_op jit(solution)/shard_map/ppermute | solution.py:245
  (296 other events, 3857.9 us)
Sparse Core Ops, SparseCore 0:
  11.8 25.2 all-gather.10
  39.3 22.5 all-gather.14
  63.5 22.5 all-gather.16
  91.0 23.0 all-gather.12
  261.7 22.9 all-gather.18
  291.6 22.9 all-gather.20
  646.6 85.7 all-reduce.1

commit v9 on v5

--- a/solution.py
+++ b/solution.py
@@ -339,16 +339,15 @@
         ],
         axis=1,
     )
-    small = lax.all_gather(small, "shard", axis=0, tiled=True)
+    small = doubling_gather(small, "shard")
     qkv_cols = w_qkv.shape[2]
     all_weights = []
     for layer_index in range(LAYERS):
-        attn = lax.all_gather(
-            jnp.concatenate([w_qkv[layer_index], w_proj[layer_index]], axis=1),
-            "shard",
-            axis=0,
-            tiled=True,
-        )
+        attn = jnp.concatenate([w_qkv[layer_index], w_proj[layer_index]], axis=1)
+        if layer_index == 0:
+            attn = doubling_gather(attn, "shard")
+        else:
+            attn = lax.all_gather(attn, "shard", axis=0, tiled=True)
         shift_at = 2 * layer_count + 2 * layer_index
         router_at = 4 * layer_count + experts * layer_index
         all_weights.append(

time: 938 us -> 939 us (level)
  starting transfers between devices: 81 us -> 94.7 us
    ppermute x3 -> x7, waiting for transfers between devices: 13.6 us -> 29.9 us  [doubling_gather(): got = lax.ppermute(held, axis_name, [(i, i ^ bit) for i in range(size)])]
    all_gather x2 -> x1, waiting for transfers between devices: 9.77 us -> 0.02 us  [local(): attn = lax.all_gather(attn, 'shard', axis=0, tiled=True)]
    unnamed x594 -> x532, local copies, waits for them, and re-layouts: 57.4 us -> 59.3 us
  transfers between devices with their start and end apart: 41 -> 44, of which waited for: 26 -> 27; matrix products, arithmetic and copies ran while one was open for 44% -> 43% of each run, Pallas kernels for 0% -> 0%
where the time goes in v9:
time: 939 us; the launch traced here: 928 us
  matrix products  310 us (33%)
  waiting for transfers between devices  251 us (27%)
  local copies, waits for them, and re-layouts  190 us (20%)
  starting transfers between devices  94.7 us (10%)
  other arithmetic  64.2 us (7%)
  between operations  18.4 us (2%)
    dot_general x30, matrix products, dot_first(): lax.dot_general(left, right, (((0,), (0,)), ((), ())), preferred_element_...  99 us
    dot_general x20, matrix products, dot_last(): lax.dot_general(left, right, (((1,), (1,)), ((), ())), preferred_element_...  77.6 us
    all_to_all x4, waiting for transfers between devices, forward_layer(): lax.all_to_all(sending.reshape(experts, capacity, D), 'expert', split_axi...  60 us
    unnamed x532, local copies, waits for them, and re-layouts  59.3 us
    all_to_all x4, waiting for transfers between devices, backward_layer(): lax.all_to_all(d_rows, 'expert', split_axis=0, concat_axis=0, tiled=True)  43.7 us
    all_to_all x4, waiting for transfers between devices, forward_layer(): lax.all_to_all(expert_rows.reshape(experts, capacity, D), 'expert', split...  38.8 us
    all_to_all x4, waiting for transfers between devices, backward_layer(): lax.all_to_all(d_slots, 'expert', split_axis=0, concat_axis=0, tiled=True)  35.1 us
    dot_general x4, matrix products, forward_layer(): hidden_pre = jnp.dot(row_block, in_w[0], preferred_element_type=jnp.float32)  31.7 us
  transfers between devices with their start and end apart: 44, of which 27 were waited for; matrix products, arithmetic and copies ran while one was open for 43% of the time, Pallas kernels for 0%

profile of v9, /device:TPU:0, one launch (start us, length us, event | category | flops | bytes accessed | tf_op | source)
XLA Modules:
  0.0 927.7 jit_solution(16955638827266925350)
XLA Ops:
  20.4 13.7 %collective-permute-done.2 = bf16[1,128,2048]{2,1,0:T(8,128)(2,1)} collective-permute-done((bf16[1,128,2048]{2,1,0:T(8,128)(2,1)S(1)}, bf16[1,128,2048]{2,1,0:T(8,128)(2,1)}, u32[]{:S(2)}, u32[]{:S(2)}) %collective-permute-start.2) | collective-permute-done | bytes 524320 | tf_op jit(solution)/shard_map/ppermute | solution.py:272
  85.9 6.1 all-to-all-start.4
  99.3 18.7 %all-to-all-done.4 = bf16[8,128,512]{2,1,0:T(8,128)(2,1)S(1)} async-done(((bf16[8,128,512]{2,1,0:T(8,128)(2,1)}), bf16[8,128,512]{2,1,0:T(8,128)(2,1)S(1)}, u32[]{:S(2)}, u32[]{:S(2)}) %all-to-all-start.4) | async-done | bytes 1048608 | tf_op jit(solution)/shard_map/all_to_all | solution.py:97
  123.3 7.6 fusion.100
  130.9 7.7 fusion.149
  138.7 10.2 %all-to-all-done = bf16[8,128,512]{2,1,0:T(8,128)(2,1)S(1)} async-done(((bf16[8,128,512]{2,1,0:T(8,128)(2,1)}), bf16[8,128,512]{2,1,0:T(8,128)(2,1)S(1)}, u32[]{:S(2)}, u32[]{:S(2)}) %all-to-all-start) | async-done | bytes 1048608 | tf_op jit(solution)/shard_map/all_to_all | solution.py:97
  153.5 7.7 multiply_convert_fusion.3
  166.4 12.3 %all-to-all-done.5 = bf16[8,128,512]{2,1,0:T(8,128)(2,1)} async-done(((bf16[8,128,512]{2,1,0:T(8,128)(2,1)}), bf16[8,128,512]{2,1,0:T(8,128)(2,1)}, u32[]{:S(2)}, u32[]{:S(2)}) %all-to-all-start.5) | async-done | bytes 1048608 | tf_op jit(solution)/shard_map/all_to_all | solution.py:106
  187.7 20.9 %all-to-all-done.1 = bf16[8,128,512]{2,1,0:T(8,128)(2,1)S(1)} async-done(((bf16[8,128,512]{2,1,0:T(8,128)(2,1)}), bf16[8,128,512]{2,1,0:T(8,128)(2,1)S(1)}, u32[]{:S(2)}, u32[]{:S(2)}) %all-to-all-start.1) | async-done | bytes 1048608 | tf_op jit(solution)/shard_map/all_to_all | solution.py:106
  276.4 11.8 %all-to-all-done.2 = bf16[8,128,512]{2,1,0:T(8,128)(2,1)} async-done(((bf16[8,128,512]{2,1,0:T(8,128)(2,1)}), bf16[8,128,512]{2,1,0:T(8,128)(2,1)}, u32[]{:S(2)}, u32[]{:S(2)}) %all-to-all-start.2) | async-done | bytes 1048608 | tf_op jit(solution)/shard_map/all_to_all | solution.py:97
  303.6 14.3 %all-to-all-done.8 = bf16[8,128,512]{2,1,0:T(8,128)(2,1)} async-done(((bf16[8,128,512]{2,1,0:T(8,128)(2,1)}), bf16[8,128,512]{2,1,0:T(8,128)(2,1)}, u32[]{:S(2)}, u32[]{:S(2)}) %all-to-all-start.8) | async-done | bytes 1048608 | tf_op jit(solution)/shard_map/all_to_all | solution.py:173
  328.4 19.2 %all-to-all-done.6 = bf16[8,128,512]{2,1,0:T(8,128)(2,1)} async-done(((bf16[8,128,512]{2,1,0:T(8,128)(2,1)}), bf16[8,128,512]{2,1,0:T(8,128)(2,1)}, u32[]{:S(2)}, u32[]{:S(2)}) %all-to-all-start.6) | async-done | bytes 1048608 | tf_op jit(solution)/shard_map/all_to_all | solution.py:97
  352.1 8.8 multiply_convert_fusion.2
  360.9 7.7 fusion.80
  374.2 6.2 fusion.158
  380.4 6.5 all-to-all-start.3
  386.9 9.0 convolution_add_fusion.2
  397.1 11.1 %fusion.27 = bf16[1024,2048]{1,0:T(8,128)(2,1)S(1)} fusion(f32[1024,2048]{1,0:T(8,128)} %fusion.80, bf16[1024,512]{1,0:T(8,128)(2,1)} %bitcast.105, bf16[1,1,2048,512]{3,2,1,0:T(8,128)(2,1)S(1)} %copy-done.249), kind=kOutput, calls=%fused_computation.35 | convolution fusion | flops 2189426688 | bytes 15728640 | tf_op jit(solution)/shard_map/dot_general | solution.py:38
  408.3 9.6 %fusion.13 = bf16[1024,2048]{1,0:T(8,128)(2,1)S(1)} fusion(f32[1024,2048]{1,0:T(8,128)S(1)} %bitcast.683, bf16[1024,512]{1,0:T(8,128)(2,1)} %bitcast.81, bf16[1,1,2048,512]{3,2,1,0:T(8,128)(2,1)S(1)} %copy-done.249), kind=kOutput, calls=%fused_computation.21 | convolution fusion | flops 2189426688 | bytes 15728640 | tf_op jit(solution)/shard_map/dot_general | solution.py:38
  437.9 7.9 fusion.161
  455.0 9.4 %all-to-all-done.9 = bf16[8,128,512]{2,1,0:T(8,128)(2,1)} async-done(((bf16[8,128,512]{2,1,0:T(8,128)(2,1)}), bf16[8,128,512]{2,1,0:T(8,128)(2,1)}, u32[]{:S(2)}, u32[]{:S(2)}) %all-to-all-start.9) | async-done | bytes 1048608 | tf_op jit(solution)/shard_map/all_to_all | solution.py:181
  472.6 6.2 fusion.155
  505.8 18.5 %all-to-all-done.13 = bf16[8,128,512]{2,1,0:T(8,128)(2,1)} async-done(((bf16[8,128,512]{2,1,0:T(8,128)(2,1)}), bf16[8,128,512]{2,1,0:T(8,128)(2,1)}, u32[]{:S(2)}, u32[]{:S(2)}) %all-to-all-start.13) | async-done | bytes 1048608 | tf_op jit(solution)/shard_map/all_to_all | solution.py:181
  650.9 6.9 fusion.397
  657.8 17.1 %all-to-all-done.14 = bf16[8,128,512]{2,1,0:T(8,128)(2,1)} async-done(((bf16[8,128,512]{2,1,0:T(8,128)(2,1)}), bf16[8,128,512]{2,1,0:T(8,128)(2,1)}, u32[]{:S(2)}, u32[]{:S(2)}) %all-to-all-start.14) | async-done | bytes 1048608 | tf_op jit(solution)/shard_map/all_to_all | solution.py:173
  675.0 9.1 convolution_add_fusion.3
  686.4 9.6 %fusion.6 = bf16[1024,2048]{1,0:T(8,128)(2,1)S(1)} fusion(f32[1024,2048]{1,0:T(8,128)} %get-tuple-element.191, bf16[1024,512]{1,0:T(8,128)(2,1)} %bitcast.93, bf16[1,1,2048,512]{3,2,1,0:T(8,128)(2,1)S(1)} %copy-done.246), kind=kOutput, calls=%fused_computation.14 | convolution fusion | flops 2189426688 | bytes 15728640 | tf_op jit(solution)/shard_map/dot_general | solution.py:38
  707.9 9.4 %fusion.20 = bf16[1024,2048]{1,0:T(8,128)(2,1)S(1)} fusion(f32[1024,2048]{1,0:T(8,128)} %fusion.100, bf16[1024,512]{1,0:T(8,128)(2,1)} %bitcast.117, bf16[1,1,2048,512]{3,2,1,0:T(8,128)(2,1)S(1)} %copy-done.246), kind=kOutput, calls=%fused_computation.28 | convolution fusion | flops 2189426688 | bytes 15728640 | tf_op jit(solution)/shard_map/dot_general | solution.py:38
  725.5 11.3 %all-reduce.2.cloned.1.call-done = bf16[128,2060]{0,1:T(8,128)(2,1)} async-done(((bf16[128,2060]{0,1:T(8,128)(2,1)}), bf16[128,2060]{0,1:T(8,128)(2,1)}) %all-reduce.2.cloned.1.call-update) | async-done | bytes 527376 | tf_op jit(solution)/shard_map/psum | solution.py:294
  753.9 15.2 %all-to-all-done.15 = bf16[8,128,512]{2,1,0:T(8,128)(2,1)} async-done(((bf16[8,128,512]{2,1,0:T(8,128)(2,1)}), bf16[8,128,512]{2,1,0:T(8,128)(2,1)}, u32[]{:S(2)}, u32[]{:S(2)}) %all-to-all-start.15) | async-done | bytes 1048608 | tf_op jit(solution)/shard_map/all_to_all | solution.py:181
  867.5 6.7 collective-permute-done.5
  878.1 7.1 collective-permute-done.6
  (957 shorter events, 565.9 us)
Async XLA Ops:
  7.2 116.1 %all-gather.12.cloned.1.call-start = ((), (), s32[]{:S(2)}) async-start(), calls=%async_computation.18 | async-start | bytes 2621440 | tf_op jit(solution)/shard_map/all_gather | solution.py:360
  9.7 121.2 %all-gather.14.cloned.1.call-start = ((), (), s32[]{:S(2)}) async-start(), calls=%async_computation.19 | async-start | bytes 2621440 | tf_op jit(solution)/shard_map/all_gather | solution.py:361
  12.4 21.7 %collective-permute-start.2 = (bf16[1,128,2048]{2,1,0:T(8,128)(2,1)S(1)}, bf16[1,128,2048]{2,1,0:T(8,128)(2,1)}, u32[]{:S(2)}, u32[]{:S(2)}) collective-permute-start(bf16[1,128,2048]{2,1,0:T(8,128)(2,1)S(1)} %maximum_bitcast_fusion), channel_id=1, source_target_pairs={{0,2},{1,3},{2,0},{3,1},{4,6},{5,7},{6,4},{7,5},{8,10},{9,11},{10,... | collective-permute-start | bytes 1572872 | tf_op jit(solution)/shard_map/ppermute | solution.py:272
  15.4 20.1 %collective-permute-start = (bf16[1,128,24]{1,2,0:T(8,128)(2,1)S(1)}, bf16[1,128,24]{1,2,0:T(8,128)(2,1)S(1)}, u32[]{:S(2)}, u32[]{:S(2)}) collective-permute-start(bf16[1,128,24]{1,2,0:T(8,128)(2,1)S(1)} %maximum_bitcast_fusion.1), channel_id=1, source_target_pairs={{0,2},{1,3},{2,0},{3,1},{4,6},{5,7},{6,4},{7,5},{8,10},{9,11},{10,... | collective-permute-start | bytes 18440 | tf_op jit(solution)/shard_map/ppermute | solution.py:272
  85.9 32.1 %all-to-all-start.4 = ((bf16[8,128,512]{2,1,0:T(8,128)(2,1)}), bf16[8,128,512]{2,1,0:T(8,128)(2,1)S(1)}, u32[]{:S(2)}, u32[]{:S(2)}) async-start(bf16[8,128,512]{2,1,0:T(8,128)(2,1)} %bitcast.614), calls=%async_computation.4 | async-start | bytes 2097152 | tf_op jit(solution)/shard_map/all_to_all | solution.py:97
  91.9 120.5 %all-gather.10.cloned.1.call-start = ((), (), s32[]{:S(2)}) async-start(), calls=%async_computation.16 | async-start | bytes 2621440 | tf_op jit(solution)/shard_map/all_gather | solution.py:350
  119.0 29.8 %all-to-all-start = ((bf16[8,128,512]{2,1,0:T(8,128)(2,1)}), bf16[8,128,512]{2,1,0:T(8,128)(2,1)S(1)}, u32[]{:S(2)}, u32[]{:S(2)}) async-start(bf16[8,128,512]{2,1,0:T(8,128)(2,1)} %bitcast.620), calls=%async_computation | async-start | bytes 2097152 | tf_op jit(solution)/shard_map/all_to_all | solution.py:97
  148.9 29.8 %all-to-all-start.5 = ((bf16[8,128,512]{2,1,0:T(8,128)(2,1)}), bf16[8,128,512]{2,1,0:T(8,128)(2,1)}, u32[]{:S(2)}, u32[]{:S(2)}) async-start(bf16[8,128,512]{2,1,0:T(8,128)(2,1)} %bitcast.624), calls=%async_computation.5 | async-start | bytes 2097152 | tf_op jit(solution)/shard_map/all_to_all | solution.py:106
  178.7 29.9 %all-to-all-start.1 = ((bf16[8,128,512]{2,1,0:T(8,128)(2,1)}), bf16[8,128,512]{2,1,0:T(8,128)(2,1)S(1)}, u32[]{:S(2)}, u32[]{:S(2)}) async-start(bf16[8,128,512]{2,1,0:T(8,128)(2,1)} %bitcast.622), calls=%async_computation.1 | async-start | bytes 2097152 | tf_op jit(solution)/shard_map/all_to_all | solution.py:106
  258.4 29.8 %all-to-all-start.2 = ((bf16[8,128,512]{2,1,0:T(8,128)(2,1)}), bf16[8,128,512]{2,1,0:T(8,128)(2,1)}, u32[]{:S(2)}, u32[]{:S(2)}) async-start(bf16[8,128,512]{2,1,0:T(8,128)(2,1)} %bitcast.616), calls=%async_computation.2 | async-start | bytes 2097152 | tf_op jit(solution)/shard_map/all_to_all | solution.py:97
  262.6 89.5 %all-gather.16.cloned.1.call-start = ((), (), s32[]{:S(2)}) async-start(), calls=%async_computation.20 | async-start | bytes 2621440 | tf_op jit(solution)/shard_map/all_gather | solution.py:360
  288.2 29.7 %all-to-all-start.8 = ((bf16[8,128,512]{2,1,0:T(8,128)(2,1)}), bf16[8,128,512]{2,1,0:T(8,128)(2,1)}, u32[]{:S(2)}, u32[]{:S(2)}) async-start(bf16[8,128,512]{2,1,0:T(8,128)(2,1)} %bitcast.608), calls=%async_computation.8 | async-start | bytes 2097152 | tf_op jit(solution)/shard_map/all_to_all | solution.py:173
  292.5 81.8 %all-gather.18.cloned.1.call-start = ((), (), s32[]{:S(2)}) async-start(), calls=%async_computation.21 | async-start | bytes 2621440 | tf_op jit(solution)/shard_map/all_gather | solution.py:361
  317.9 29.6 %all-to-all-start.6 = ((bf16[8,128,512]{2,1,0:T(8,128)(2,1)}), bf16[8,128,512]{2,1,0:T(8,128)(2,1)}, u32[]{:S(2)}, u32[]{:S(2)}) async-start(bf16[8,128,512]{2,1,0:T(8,128)(2,1)} %bitcast.619), calls=%async_computation.6 | async-start | bytes 2097152 | tf_op jit(solution)/shard_map/all_to_all | solution.py:97
  347.6 32.8 %all-to-all-start.12 = ((bf16[8,128,512]{2,1,0:T(8,128)(2,1)}), bf16[8,128,512]{2,1,0:T(8,128)(2,1)}, u32[]{:S(2)}, u32[]{:S(2)}) async-start(bf16[8,128,512]{2,1,0:T(8,128)(2,1)} %bitcast.623), calls=%async_computation.12 | async-start | bytes 2097152 | tf_op jit(solution)/shard_map/all_to_all | solution.py:173
  380.4 51.5 %all-to-all-start.3 = ((bf16[8,128,512]{2,1,0:T(8,128)(2,1)}), bf16[8,128,512]{2,1,0:T(8,128)(2,1)}, u32[]{:S(2)}, u32[]{:S(2)}) async-start(bf16[8,128,512]{2,1,0:T(8,128)(2,1)} %bitcast.617), calls=%async_computation.3 | async-start | bytes 2097152 | tf_op jit(solution)/shard_map/all_to_all | solution.py:106
  397.1 48.7 %collective-permute-start.20 = (bf16[2,512,512]{2,1,0:T(8,128)(2,1)}, bf16[2,512,512]{2,1,0:T(8,128)(2,1)}, u32[]{:S(2)}, u32[]{:S(2)}) collective-permute-start(bf16[2,512,512]{2,1,0:T(8,128)(2,1)} %fusion.243), channel_id=1, source_target_pairs={{0,1},{1,0},{2,3},{3,2},{4,5},{5,4},{6,7},{7,6},{8,9},{9,8},{10,11... | collective-permute-start | bytes 3145736 | tf_op jit(solution)/shard_map/ppermute | solution.py:243
  428.6 23.7 %collective-permute-start.16 = (bf16[2,128,2048]{2,1,0:T(8,128)(2,1)}, bf16[2,128,2048]{2,1,0:T(8,128)(2,1)}, u32[]{:S(2)}, u32[]{:S(2)}) collective-permute-start(bf16[2,128,2048]{2,1,0:T(8,128)(2,1)} %fusion.241), channel_id=1, source_target_pairs={{0,1},{1,0},{2,3},{3,2},{4,5},{5,4},{6,7},{7,6},{8,9},{9,8},{10,11... | collective-permute-start | bytes 3145736 | tf_op jit(solution)/shard_map/ppermute | solution.py:243
  431.9 32.6 %all-to-all-start.9 = ((bf16[8,128,512]{2,1,0:T(8,128)(2,1)}), bf16[8,128,512]{2,1,0:T(8,128)(2,1)}, u32[]{:S(2)}, u32[]{:S(2)}) async-start(bf16[8,128,512]{2,1,0:T(8,128)(2,1)} %bitcast.621), calls=%async_computation.9 | async-start | bytes 2097152 | tf_op jit(solution)/shard_map/all_to_all | solution.py:181
  449.7 29.1 %collective-permute-start.21 = (bf16[1,512,512]{2,1,0:T(8,128)(2,1)}, bf16[1,512,512]{2,1,0:T(8,128)(2,1)}, u32[]{:S(2)}, u32[]{:S(2)}) collective-permute-start(bf16[1,512,512]{2,1,0:T(8,128)(2,1)} %dynamic-slice_convert_fusion.4), channel_id=1, source_target_pairs={{0,2},{1,3},{2,0},{3,1},{4,6},{5,7},{6,4},{7,5},{8,10},{9,11},{10,... | collective-permute-start | bytes 1572872 | tf_op jit(solution)/shard_map/ppermute | solution.py:243
  464.4 29.9 %all-to-all-start.7 = ((bf16[8,128,512]{2,1,0:T(8,128)(2,1)}), bf16[8,128,512]{2,1,0:T(8,128)(2,1)}, u32[]{:S(2)}, u32[]{:S(2)}) async-start(bf16[8,128,512]{2,1,0:T(8,128)(2,1)} %bitcast.611), calls=%async_computation.7 | async-start | bytes 2097152 | tf_op jit(solution)/shard_map/all_to_all | solution.py:106
  494.3 30.0 %all-to-all-start.13 = ((bf16[8,128,512]{2,1,0:T(8,128)(2,1)}), bf16[8,128,512]{2,1,0:T(8,128)(2,1)}, u32[]{:S(2)}, u32[]{:S(2)}) async-start(bf16[8,128,512]{2,1,0:T(8,128)(2,1)} %bitcast.610), calls=%async_computation.13 | async-start | bytes 2097152 | tf_op jit(solution)/shard_map/all_to_all | solution.py:181
  609.8 29.9 %all-to-all-start.10 = ((bf16[8,128,512]{2,1,0:T(8,128)(2,1)}), bf16[8,128,512]{2,1,0:T(8,128)(2,1)}, u32[]{:S(2)}, u32[]{:S(2)}) async-start(bf16[8,128,512]{2,1,0:T(8,128)(2,1)} %bitcast.609), calls=%async_computation.10 | async-start | bytes 2097152 | tf_op jit(solution)/shard_map/all_to_all | solution.py:173
  639.6 35.3 %all-to-all-start.14 = ((bf16[8,128,512]{2,1,0:T(8,128)(2,1)}), bf16[8,128,512]{2,1,0:T(8,128)(2,1)}, u32[]{:S(2)}, u32[]{:S(2)}) async-start(bf16[8,128,512]{2,1,0:T(8,128)(2,1)} %bitcast.612), calls=%async_computation.14 | async-start | bytes 2097152 | tf_op jit(solution)/shard_map/all_to_all | solution.py:173
  643.9 93.0 %all-reduce.2.cloned.1.call-start = ((), (), s32[]{:S(2)}) async-start(), calls=%async_computation.17 | async-start | bytes 1056768 | tf_op jit(solution)/shard_map/psum | solution.py:294
  685.3 159.1 %collective-permute-start.18 = (bf16[2,512,512]{2,1,0:T(8,128)(2,1)}, bf16[2,512,512]{2,1,0:T(8,128)(2,1)}, u32[]{:S(2)}, u32[]{:S(2)}) collective-permute-start(bf16[2,512,512]{2,1,0:T(8,128)(2,1)} %fusion.242), channel_id=1, source_target_pairs={{0,1},{1,0},{2,3},{3,2},{4,5},{5,4},{6,7},{7,6},{8,9},{9,8},{10,11... | collective-permute-start | bytes 3145736 | tf_op jit(solution)/shard_map/ppermute | solution.py:243
  703.8 35.3 %all-to-all-start.11 = ((bf16[8,128,512]{2,1,0:T(8,128)(2,1)}), bf16[8,128,512]{2,1,0:T(8,128)(2,1)S(1)}, u32[]{:S(2)}, u32[]{:S(2)}) async-start(bf16[8,128,512]{2,1,0:T(8,128)(2,1)} %bitcast.94), calls=%async_computation.11 | async-start | bytes 2097152 | tf_op jit(solution)/shard_map/all_to_all | solution.py:181
  722.1 23.8 %collective-permute-start.14 = (bf16[2,128,2048]{2,1,0:T(8,128)(2,1)S(1)}, bf16[2,128,2048]{2,1,0:T(8,128)(2,1)}, u32[]{:S(2)}, u32[]{:S(2)}) collective-permute-start(bf16[2,128,2048]{2,1,0:T(8,128)(2,1)S(1)} %fusion.240), channel_id=1, source_target_pairs={{0,1},{1,0},{2,3},{3,2},{4,5},{5,4},{6,7},{7,6},{8,9},{9,8},{10,11... | collective-permute-start | bytes 3145736 | tf_op jit(solution)/shard_map/ppermute | solution.py:243
  739.1 30.0 %all-to-all-start.15 = ((bf16[8,128,512]{2,1,0:T(8,128)(2,1)}), bf16[8,128,512]{2,1,0:T(8,128)(2,1)}, u32[]{:S(2)}, u32[]{:S(2)}) async-start(bf16[8,128,512]{2,1,0:T(8,128)(2,1)} %bitcast.615), calls=%async_computation.15 | async-start | bytes 2097152 | tf_op jit(solution)/shard_map/all_to_all | solution.py:181
  750.2 100.0 %collective-permute-start.15 = (bf16[1,128,2048]{2,1,0:T(8,128)(2,1)}, bf16[1,128,2048]{2,1,0:T(8,128)(2,1)}, u32[]{:S(2)}, u32[]{:S(2)}) collective-permute-start(bf16[1,128,2048]{2,1,0:T(8,128)(2,1)} %dynamic-slice_convert_fusion.7), channel_id=1, source_target_pairs={{0,2},{1,3},{2,0},{3,1},{4,6},{5,7},{6,4},{7,5},{8,10},{9,11},{10,... | collective-permute-start | bytes 1572872 | tf_op jit(solution)/shard_map/ppermute | solution.py:243
  847.6 15.6 %collective-permute-start.19 = (bf16[1,512,512]{2,1,0:T(8,128)(2,1)}, bf16[1,512,512]{2,1,0:T(8,128)(2,1)}, u32[]{:S(2)}, u32[]{:S(2)}) collective-permute-start(bf16[1,512,512]{2,1,0:T(8,128)(2,1)} %dynamic-slice_convert_fusion.5), channel_id=1, source_target_pairs={{0,2},{1,3},{2,0},{3,1},{4,6},{5,7},{6,4},{7,5},{8,10},{9,11},{10,... | collective-permute-start | bytes 1572872 | tf_op jit(solution)/shard_map/ppermute | solution.py:243
  858.1 16.1 %collective-permute-start.5 = (bf16[1,128,2060]{1,2,0:T(8,128)(2,1)S(1)}, bf16[1,128,2060]{1,2,0:T(8,128)(2,1)S(1)}, u32[]{:S(2)}, u32[]{:S(2)}) collective-permute-start(bf16[1,128,2060]{1,2,0:T(8,128)(2,1)S(1)} %dynamic-slice_convert_fusion.3), channel_id=1, source_target_pairs={{0,2},{1,3},{2,0},{3,1},{4,6},{5,7},{6,4},{7,5},{8,10},{9,11},{10,... | collective-permute-start | bytes 1582088 | tf_op jit(solution)/shard_map/ppermute | solution.py:243
  (268 other events, 2910.0 us)
Sparse Core Ops, SparseCore 0:
  9.8 30.3 all-gather.11
  41.8 24.0 all-gather.13
  94.3 25.0 all-gather.9
  264.7 24.8 all-gather.15
  294.5 24.8 all-gather.17
  651.1 85.7 all-reduce.1

commit v10 on v7

--- a/solution.py
+++ b/solution.py
@@ -400,7 +400,10 @@
                 layer_sum = layer_grads
             else:
                 layer_sum = tuple(old + new for old, new in zip(layer_sum, layer_grads))
-        reduced[layer_index] = reduce_layer(layer_sum, layer_index == 0)
+        if layer_index == 0:
+            reduced[layer_index] = reduce_layer(layer_sum, True)
+        else:
+            reduced[layer_index] = reduce_layer(layer_sum, False)
     outs = [jnp.stack([reduced[l][k] for l in range(LAYERS)]) for k in range(7)]
     d_tokens = jnp.concatenate(d_residuals, axis=0)
     return (activations, d_tokens, *outs)

time: 875 us -> 875 us (level)
  no operation moved by 1% of the time
where the time goes in v10:
time: 875 us; the launch traced here: 862 us
  matrix products  300 us (34%)
  local copies, waits for them, and re-layouts  191 us (22%)
  waiting for transfers between devices  189 us (22%)
  starting transfers between devices  88.3 us (10%)
  other arithmetic  68 us (8%)
  between operations  18.5 us (2%)
    all_to_all x16, waiting for transfers between devices, exchange(): lax.all_to_all(blocks, axis_name, split_axis=0, concat_axis=0, tiled=True)  135 us
    dot_general x30, matrix products, dot_first(): lax.dot_general(left, right, (((0,), (0,)), ((), ())), preferred_element_...  97.8 us
    dot_general x20, matrix products, dot_last(): lax.dot_general(left, right, (((1,), (1,)), ((), ())), preferred_element_...  76.6 us
    all_to_all x16, starting transfers between devices, exchange(): lax.all_to_all(blocks, axis_name, split_axis=0, concat_axis=0, tiled=True)  76.2 us
    unnamed x634, local copies, waits for them, and re-layouts  58.6 us
    ppermute x15, waiting for transfers between devices, halving_scatter(): lax.ppermute(give.astype(jnp.bfloat16), axis_name, [(i, i ^ bit) for i in...  29.8 us
    dot_general x4, matrix products, forward_expert(): hidden_pre = jnp.dot(row_block, in_w[0], preferred_element_type=jnp.float32)  26.6 us
    dot_general x4, matrix products, forward_expert(): jnp.dot(hidden_act, out_w[0], preferred_element_type=jnp.float32)  24.5 us
  transfers between devices with their start and end apart: 41, of which 23 were waited for; matrix products, arithmetic and copies ran while one was open for 51% of the time, Pallas kernels for 0%

profile of v10, /device:TPU:0, one launch (start us, length us, event | category | flops | bytes accessed | tf_op | source)
XLA Modules:
  0.0 861.8 jit_solution(17636695094294078390)
XLA Ops:
  14.9 6.1 all_gather.21
  63.7 6.2 all-to-all-start
  101.1 5.9 all-to-all-start.4
  107.1 8.3 multiply_convert_fusion.3
  115.4 6.7 fusion.146
  122.1 10.9 %all-to-all-done.4 = bf16[8,128,512]{2,1,0:T(8,128)(2,1)} async-done(((bf16[8,128,512]{2,1,0:T(8,128)(2,1)}), bf16[8,128,512]{2,1,0:T(8,128)(2,1)}, u32[]{:S(2)}, u32[]{:S(2)}) %all-to-all-start.4) | async-done | bytes 1048608 | tf_op jit(solution)/shard_map/all_to_all | solution.py:62
  154.2 8.8 %all-to-all-done.1 = bf16[8,128,512]{2,1,0:T(8,128)(2,1)} async-done(((bf16[8,128,512]{2,1,0:T(8,128)(2,1)}), bf16[8,128,512]{2,1,0:T(8,128)(2,1)}, u32[]{:S(2)}, u32[]{:S(2)}) %all-to-all-start.1) | async-done | bytes 1048608 | tf_op jit(solution)/shard_map/all_to_all | solution.py:62
  195.3 6.2 all-to-all-start.2
  239.7 16.3 %all-to-all-done.8 = bf16[8,128,512]{2,1,0:T(8,128)(2,1)} async-done(((bf16[8,128,512]{2,1,0:T(8,128)(2,1)}), bf16[8,128,512]{2,1,0:T(8,128)(2,1)}, u32[]{:S(2)}, u32[]{:S(2)}) %all-to-all-start.8) | async-done | bytes 1048608 | tf_op jit(solution)/shard_map/all_to_all | solution.py:62
  265.9 19.9 %all-to-all-done.6 = bf16[8,128,512]{2,1,0:T(8,128)(2,1)S(1)} async-done(((bf16[8,128,512]{2,1,0:T(8,128)(2,1)}), bf16[8,128,512]{2,1,0:T(8,128)(2,1)S(1)}, u32[]{:S(2)}, u32[]{:S(2)}) %all-to-all-start.6) | async-done | bytes 1048608 | tf_op jit(solution)/shard_map/all_to_all | solution.py:62
  289.5 8.8 %multiply_convert_fusion.2 = (bf16[1024,2048]{1,0:T(8,128)(2,1)S(1)}, f32[1024,2048]{1,0:T(8,128)}) fusion(bf16[1024,512]{1,0:T(8,128)(2,1)} %bitcast.43, bf16[1,1,512,2048]{3,2,1,0:T(8,128)(2,1)} %all-gather.19.cloned.1.call-done), kind=kOutput, calls=%fused_computation.38 | convolution fusion | flops 2166358016 | bytes 15728640 | tf_op jit(solution)/shard_map/dot_general | solution.py:108
  298.3 5.7 fusion.80
  309.7 6.2 fusion.158
  315.9 6.2 all-to-all-start.3
  322.1 8.7 %convolution_add_fusion.2 = f32[2048,512]{1,0:T(8,128)S(1)} fusion(f32[2048,512]{1,0:T(8,128)} %fusion.390, bf16[1024,512]{1,0:T(8,128)(2,1)S(1)} %bitcast.621, f32[1024,2048]{1,0:T(8,128)} %fusion.80), kind=kOutput, calls=%fused_computation.82 | convolution fusion | flops 2167406592 | bytes 17825792 | tf_op jit(solution)/shard_map/dot_general | solution.py:31
  331.1 10.9 %fusion.27 = bf16[1024,2048]{1,0:T(8,128)(2,1)S(1)} fusion(f32[1024,2048]{1,0:T(8,128)} %fusion.80, bf16[1024,512]{1,0:T(8,128)(2,1)} %bitcast.622, bf16[1,1,2048,512]{3,2,1,0:T(8,128)(2,1)S(1)} %copy-done.300), kind=kOutput, calls=%fused_computation.35 | convolution fusion | flops 2189426688 | bytes 15728640 | tf_op jit(solution)/shard_map/dot_general | solution.py:37
  342.1 9.6 %fusion.13 = bf16[1024,2048]{1,0:T(8,128)(2,1)S(1)} fusion(f32[1024,2048]{1,0:T(8,128)S(1)} %bitcast.688, bf16[1024,512]{1,0:T(8,128)(2,1)} %bitcast.82, bf16[1,1,2048,512]{3,2,1,0:T(8,128)(2,1)S(1)} %copy-done.300), kind=kOutput, calls=%fused_computation.21 | convolution fusion | flops 2189426688 | bytes 15728640 | tf_op jit(solution)/shard_map/dot_general | solution.py:37
  364.4 6.0 all-to-all-start.9
  370.3 7.9 fusion.161
  384.5 12.4 %all-to-all-done.9 = bf16[8,128,512]{2,1,0:T(8,128)(2,1)} async-done(((bf16[8,128,512]{2,1,0:T(8,128)(2,1)}), bf16[8,128,512]{2,1,0:T(8,128)(2,1)}, u32[]{:S(2)}, u32[]{:S(2)}) %all-to-all-start.9) | async-done | bytes 1048608 | tf_op jit(solution)/shard_map/all_to_all | solution.py:62
  404.0 6.2 fusion.155
  420.1 6.7 all-to-all-done.7
  440.2 16.4 %all-to-all-done.13 = bf16[8,128,512]{2,1,0:T(8,128)(2,1)S(1)} async-done(((bf16[8,128,512]{2,1,0:T(8,128)(2,1)}), bf16[8,128,512]{2,1,0:T(8,128)(2,1)S(1)}, u32[]{:S(2)}, u32[]{:S(2)}) %all-to-all-start.13) | async-done | bytes 1048608 | tf_op jit(solution)/shard_map/all_to_all | solution.py:62
  582.1 6.9 fusion.389
  589.0 18.1 %all-to-all-done.14 = bf16[8,128,512]{2,1,0:T(8,128)(2,1)} async-done(((bf16[8,128,512]{2,1,0:T(8,128)(2,1)}), bf16[8,128,512]{2,1,0:T(8,128)(2,1)}, u32[]{:S(2)}, u32[]{:S(2)}) %all-to-all-start.14) | async-done | bytes 1048608 | tf_op jit(solution)/shard_map/all_to_all | solution.py:62
  607.2 9.1 %convolution_add_fusion.3 = f32[2048,512]{1,0:T(8,128)S(1)} fusion(f32[2048,512]{1,0:T(8,128)} %fusion.389, bf16[1024,512]{1,0:T(8,128)(2,1)} %bitcast.122, f32[1024,2048]{1,0:T(8,128)} %copy-done.301), kind=kOutput, calls=%fused_computation.83 | convolution fusion | flops 2167406592 | bytes 17825792 | tf_op jit(solution)/shard_map/dot_general | solution.py:31
  618.7 9.7 %fusion.6 = bf16[1024,2048]{1,0:T(8,128)(2,1)S(1)} fusion(f32[1024,2048]{1,0:T(8,128)} %get-tuple-element.242, bf16[1024,512]{1,0:T(8,128)(2,1)} %bitcast.96, bf16[1,1,2048,512]{3,2,1,0:T(8,128)(2,1)S(1)} %copy-done.297), kind=kOutput, calls=%fused_computation.14 | convolution fusion | flops 2189426688 | bytes 15728640 | tf_op jit(solution)/shard_map/dot_general | solution.py:37
  640.0 9.4 %fusion.20 = bf16[1024,2048]{1,0:T(8,128)(2,1)S(1)} fusion(f32[1024,2048]{1,0:T(8,128)} %copy-done.301, bf16[1024,512]{1,0:T(8,128)(2,1)} %bitcast.122, bf16[1,1,2048,512]{3,2,1,0:T(8,128)(2,1)S(1)} %copy-done.297), kind=kOutput, calls=%fused_computation.28 | convolution fusion | flops 2189426688 | bytes 15728640 | tf_op jit(solution)/shard_map/dot_general | solution.py:37
  659.0 9.4 %all-reduce.2.cloned.1.call-done = bf16[128,2060]{0,1:T(8,128)(2,1)} async-done(((bf16[128,2060]{0,1:T(8,128)(2,1)}), bf16[128,2060]{0,1:T(8,128)(2,1)}) %all-reduce.2.cloned.1.call-update) | async-done | bytes 527376 | tf_op jit(solution)/shard_map/psum | solution.py:298
  684.4 16.8 %all-to-all-done.15 = bf16[8,128,512]{2,1,0:T(8,128)(2,1)} async-done(((bf16[8,128,512]{2,1,0:T(8,128)(2,1)}), bf16[8,128,512]{2,1,0:T(8,128)(2,1)}, u32[]{:S(2)}, u32[]{:S(2)}) %all-to-all-start.15) | async-done | bytes 1048608 | tf_op jit(solution)/shard_map/all_to_all | solution.py:62
  801.5 6.4 collective-permute-done.1
  825.4 6.2 collective-permute-done.4
  (1061 shorter events, 544.2 us)
Async XLA Ops:
  7.2 30.8 %all-gather.13.cloned.1.call-start = ((), (), s32[]{:S(2)}) async-start(), calls=%async_computation.17 | async-start | bytes 2621440 | tf_op jit(solution)/shard_map/all_gather | solution.py:350
  10.4 96.7 %all-gather.15.cloned.1.call-start = ((), (), s32[]{:S(2)}) async-start(), calls=%async_computation.19 | async-start | bytes 2621440 | tf_op jit(solution)/shard_map/all_gather | solution.py:365
  11.6 103.8 %all-gather.17.cloned.1.call-start = ((), (), s32[]{:S(2)}) async-start(), calls=%async_computation.20 | async-start | bytes 2621440 | tf_op jit(solution)/shard_map/all_gather | solution.py:366
  12.7 126.0 %all-gather.11.cloned.1.call-start = ((), (), s32[]{:S(2)}) async-start(), calls=%async_computation.16 | async-start | bytes 2621440 | tf_op jit(solution)/shard_map/all_gather | solution.py:350
  13.7 275.8 %all-gather.19.cloned.1.call-start = ((), (), s32[]{:S(2)}) async-start(), calls=%async_computation.21 | async-start | bytes 2621440 | tf_op jit(solution)/shard_map/all_gather | solution.py:365
  14.3 295.4 %all-gather.21.cloned.1.call-start = ((), (), s32[]{:S(2)}) async-start(), calls=%async_computation.22 | async-start | bytes 2621440 | tf_op jit(solution)/shard_map/all_gather | solution.py:366
  63.7 37.4 %all-to-all-start = ((bf16[8,128,512]{2,1,0:T(8,128)(2,1)}), bf16[8,128,512]{2,1,0:T(8,128)(2,1)S(1)}, u32[]{:S(2)}, u32[]{:S(2)}) async-start(bf16[8,128,512]{2,1,0:T(8,128)(2,1)} %bitcast.615), calls=%async_computation | async-start | bytes 2097152 | tf_op jit(solution)/shard_map/all_to_all | solution.py:62
  101.1 31.9 %all-to-all-start.4 = ((bf16[8,128,512]{2,1,0:T(8,128)(2,1)}), bf16[8,128,512]{2,1,0:T(8,128)(2,1)}, u32[]{:S(2)}, u32[]{:S(2)}) async-start(bf16[8,128,512]{2,1,0:T(8,128)(2,1)} %bitcast.625), calls=%async_computation.4 | async-start | bytes 2097152 | tf_op jit(solution)/shard_map/all_to_all | solution.py:62
  133.0 30.0 %all-to-all-start.1 = ((bf16[8,128,512]{2,1,0:T(8,128)(2,1)}), bf16[8,128,512]{2,1,0:T(8,128)(2,1)}, u32[]{:S(2)}, u32[]{:S(2)}) async-start(bf16[8,128,512]{2,1,0:T(8,128)(2,1)} %bitcast.30), calls=%async_computation.1 | async-start | bytes 2097152 | tf_op jit(solution)/shard_map/all_to_all | solution.py:62
  163.0 32.2 %all-to-all-start.5 = ((bf16[8,128,512]{2,1,0:T(8,128)(2,1)}), bf16[8,128,512]{2,1,0:T(8,128)(2,1)}, u32[]{:S(2)}, u32[]{:S(2)}) async-start(bf16[8,128,512]{2,1,0:T(8,128)(2,1)} %bitcast.613), calls=%async_computation.5 | async-start | bytes 2097152 | tf_op jit(solution)/shard_map/all_to_all | solution.py:62
  195.3 31.1 %all-to-all-start.2 = ((bf16[8,128,512]{2,1,0:T(8,128)(2,1)}), bf16[8,128,512]{2,1,0:T(8,128)(2,1)}, u32[]{:S(2)}, u32[]{:S(2)}) async-start(bf16[8,128,512]{2,1,0:T(8,128)(2,1)} %bitcast.42), calls=%async_computation.2 | async-start | bytes 2097152 | tf_op jit(solution)/shard_map/all_to_all | solution.py:62
  226.3 29.7 %all-to-all-start.8 = ((bf16[8,128,512]{2,1,0:T(8,128)(2,1)}), bf16[8,128,512]{2,1,0:T(8,128)(2,1)}, u32[]{:S(2)}, u32[]{:S(2)}) async-start(bf16[8,128,512]{2,1,0:T(8,128)(2,1)} %bitcast.624), calls=%async_computation.8 | async-start | bytes 2097152 | tf_op jit(solution)/shard_map/all_to_all | solution.py:62
  256.0 29.7 %all-to-all-start.6 = ((bf16[8,128,512]{2,1,0:T(8,128)(2,1)}), bf16[8,128,512]{2,1,0:T(8,128)(2,1)S(1)}, u32[]{:S(2)}, u32[]{:S(2)}) async-start(bf16[8,128,512]{2,1,0:T(8,128)(2,1)} %bitcast.75), calls=%async_computation.6 | async-start | bytes 2097152 | tf_op jit(solution)/shard_map/all_to_all | solution.py:62
  285.8 30.1 %all-to-all-start.12 = ((bf16[8,128,512]{2,1,0:T(8,128)(2,1)}), bf16[8,128,512]{2,1,0:T(8,128)(2,1)S(1)}, u32[]{:S(2)}, u32[]{:S(2)}) async-start(bf16[8,128,512]{2,1,0:T(8,128)(2,1)} %bitcast.626), calls=%async_computation.12 | async-start | bytes 2097152 | tf_op jit(solution)/shard_map/all_to_all | solution.py:62
  315.9 48.5 %all-to-all-start.3 = ((bf16[8,128,512]{2,1,0:T(8,128)(2,1)}), bf16[8,128,512]{2,1,0:T(8,128)(2,1)}, u32[]{:S(2)}, u32[]{:S(2)}) async-start(bf16[8,128,512]{2,1,0:T(8,128)(2,1)} %bitcast.623), calls=%async_computation.3 | async-start | bytes 2097152 | tf_op jit(solution)/shard_map/all_to_all | solution.py:62
  331.0 47.2 %collective-permute-start.16 = (bf16[2,512,512]{2,1,0:T(8,128)(2,1)S(1)}, bf16[2,512,512]{2,1,0:T(8,128)(2,1)}, u32[]{:S(2)}, u32[]{:S(2)}) collective-permute-start(bf16[2,512,512]{2,1,0:T(8,128)(2,1)S(1)} %fusion.243), channel_id=1, source_target_pairs={{0,1},{1,0},{2,3},{3,2},{4,5},{5,4},{6,7},{7,6},{8,9},{9,8},{10,11... | collective-permute-start | bytes 3145736 | tf_op jit(solution)/shard_map/ppermute | solution.py:261
  361.0 20.7 %collective-permute-start.12 = (bf16[2,128,2048]{2,1,0:T(8,128)(2,1)}, bf16[2,128,2048]{2,1,0:T(8,128)(2,1)}, u32[]{:S(2)}, u32[]{:S(2)}) collective-permute-start(bf16[2,128,2048]{2,1,0:T(8,128)(2,1)} %fusion.241), channel_id=1, source_target_pairs={{0,1},{1,0},{2,3},{3,2},{4,5},{5,4},{6,7},{7,6},{8,9},{9,8},{10,11... | collective-permute-start | bytes 3145736 | tf_op jit(solution)/shard_map/ppermute | solution.py:261
  364.4 32.5 %all-to-all-start.9 = ((bf16[8,128,512]{2,1,0:T(8,128)(2,1)}), bf16[8,128,512]{2,1,0:T(8,128)(2,1)}, u32[]{:S(2)}, u32[]{:S(2)}) async-start(bf16[8,128,512]{2,1,0:T(8,128)(2,1)} %bitcast.83), calls=%async_computation.9 | async-start | bytes 2097152 | tf_op jit(solution)/shard_map/all_to_all | solution.py:62
  380.1 30.2 %collective-permute-start.17 = (bf16[1,512,512]{2,1,0:T(8,128)(2,1)S(1)}, bf16[1,512,512]{2,1,0:T(8,128)(2,1)}, u32[]{:S(2)}, u32[]{:S(2)}) collective-permute-start(bf16[1,512,512]{2,1,0:T(8,128)(2,1)S(1)} %dynamic-slice_convert_fusion.4), channel_id=1, source_target_pairs={{0,2},{1,3},{2,0},{3,1},{4,6},{5,7},{6,4},{7,5},{8,10},{9,11},{10,... | collective-permute-start | bytes 1572872 | tf_op jit(solution)/shard_map/ppermute | solution.py:261
  396.9 29.9 %all-to-all-start.7 = ((bf16[8,128,512]{2,1,0:T(8,128)(2,1)}), bf16[8,128,512]{2,1,0:T(8,128)(2,1)}, u32[]{:S(2)}, u32[]{:S(2)}) async-start(bf16[8,128,512]{2,1,0:T(8,128)(2,1)} %bitcast.616), calls=%async_computation.7 | async-start | bytes 2097152 | tf_op jit(solution)/shard_map/all_to_all | solution.py:62
  426.8 29.9 %all-to-all-start.13 = ((bf16[8,128,512]{2,1,0:T(8,128)(2,1)}), bf16[8,128,512]{2,1,0:T(8,128)(2,1)S(1)}, u32[]{:S(2)}, u32[]{:S(2)}) async-start(bf16[8,128,512]{2,1,0:T(8,128)(2,1)} %bitcast.111), calls=%async_computation.13 | async-start | bytes 2097152 | tf_op jit(solution)/shard_map/all_to_all | solution.py:62
  541.6 30.1 %all-to-all-start.10 = ((bf16[8,128,512]{2,1,0:T(8,128)(2,1)}), bf16[8,128,512]{2,1,0:T(8,128)(2,1)}, u32[]{:S(2)}, u32[]{:S(2)}) async-start(bf16[8,128,512]{2,1,0:T(8,128)(2,1)} %bitcast.614), calls=%async_computation.10 | async-start | bytes 2097152 | tf_op jit(solution)/shard_map/all_to_all | solution.py:62
  565.4 14.7 %collective-permute-start.9 = (bf16[1,128,2060]{1,2,0:T(8,128)(2,1)}, bf16[1,128,2060]{1,2,0:T(8,128)(2,1)}, u32[]{:S(2)}, u32[]{:S(2)}) collective-permute-start(bf16[1,128,2060]{1,2,0:T(8,128)(2,1)} %dynamic-slice_convert_fusion.2), channel_id=1, source_target_pairs={{0,2},{1,3},{2,0},{3,1},{4,6},{5,7},{6,4},{7,5},{8,10},{9,11},{10,... | collective-permute-start | bytes 1582088 | tf_op jit(solution)/shard_map/ppermute | solution.py:261
  571.7 35.5 %all-to-all-start.14 = ((bf16[8,128,512]{2,1,0:T(8,128)(2,1)}), bf16[8,128,512]{2,1,0:T(8,128)(2,1)}, u32[]{:S(2)}, u32[]{:S(2)}) async-start(bf16[8,128,512]{2,1,0:T(8,128)(2,1)} %bitcast.617), calls=%async_computation.14 | async-start | bytes 2097152 | tf_op jit(solution)/shard_map/all_to_all | solution.py:62
  575.9 92.5 %all-reduce.2.cloned.1.call-start = ((), (), s32[]{:S(2)}) async-start(), calls=%async_computation.18 | async-start | bytes 1056768 | tf_op jit(solution)/shard_map/psum | solution.py:298
  617.5 161.3 %collective-permute-start.14 = (bf16[2,512,512]{2,1,0:T(8,128)(2,1)}, bf16[2,512,512]{2,1,0:T(8,128)(2,1)}, u32[]{:S(2)}, u32[]{:S(2)}) collective-permute-start(bf16[2,512,512]{2,1,0:T(8,128)(2,1)} %fusion.242), channel_id=1, source_target_pairs={{0,1},{1,0},{2,3},{3,2},{4,5},{5,4},{6,7},{7,6},{8,9},{9,8},{10,11... | collective-permute-start | bytes 3145736 | tf_op jit(solution)/shard_map/ppermute | solution.py:261
  636.2 35.0 %all-to-all-start.11 = ((bf16[8,128,512]{2,1,0:T(8,128)(2,1)}), bf16[8,128,512]{2,1,0:T(8,128)(2,1)S(1)}, u32[]{:S(2)}, u32[]{:S(2)}) async-start(bf16[8,128,512]{2,1,0:T(8,128)(2,1)} %bitcast.97), calls=%async_computation.11 | async-start | bytes 2097152 | tf_op jit(solution)/shard_map/all_to_all | solution.py:62
  655.6 21.8 %collective-permute-start.10 = (bf16[2,128,2048]{2,1,0:T(8,128)(2,1)S(1)}, bf16[2,128,2048]{2,1,0:T(8,128)(2,1)}, u32[]{:S(2)}, u32[]{:S(2)}) collective-permute-start(bf16[2,128,2048]{2,1,0:T(8,128)(2,1)S(1)} %fusion.240), channel_id=1, source_target_pairs={{0,1},{1,0},{2,3},{3,2},{4,5},{5,4},{6,7},{7,6},{8,9},{9,8},{10,11... | collective-permute-start | bytes 3145736 | tf_op jit(solution)/shard_map/ppermute | solution.py:261
  671.2 29.9 %all-to-all-start.15 = ((bf16[8,128,512]{2,1,0:T(8,128)(2,1)}), bf16[8,128,512]{2,1,0:T(8,128)(2,1)}, u32[]{:S(2)}, u32[]{:S(2)}) async-start(bf16[8,128,512]{2,1,0:T(8,128)(2,1)} %bitcast.620), calls=%async_computation.15 | async-start | bytes 2097152 | tf_op jit(solution)/shard_map/all_to_all | solution.py:62
  681.8 101.9 %collective-permute-start.11 = (bf16[1,128,2048]{2,1,0:T(8,128)(2,1)}, bf16[1,128,2048]{2,1,0:T(8,128)(2,1)}, u32[]{:S(2)}, u32[]{:S(2)}) collective-permute-start(bf16[1,128,2048]{2,1,0:T(8,128)(2,1)} %dynamic-slice_convert_fusion.7), channel_id=1, source_target_pairs={{0,2},{1,3},{2,0},{3,1},{4,6},{5,7},{6,4},{7,5},{8,10},{9,11},{10,... | collective-permute-start | bytes 1572872 | tf_op jit(solution)/shard_map/ppermute | solution.py:261
  782.2 15.1 %collective-permute-start.15 = (bf16[1,512,512]{2,1,0:T(8,128)(2,1)}, bf16[1,512,512]{2,1,0:T(8,128)(2,1)}, u32[]{:S(2)}, u32[]{:S(2)}) collective-permute-start(bf16[1,512,512]{2,1,0:T(8,128)(2,1)} %dynamic-slice_convert_fusion.5), channel_id=1, source_target_pairs={{0,2},{1,3},{2,0},{3,1},{4,6},{5,7},{6,4},{7,5},{8,10},{9,11},{10,... | collective-permute-start | bytes 1572872 | tf_op jit(solution)/shard_map/ppermute | solution.py:261
  791.7 16.3 %collective-permute-start.1 = (bf16[1,128,2060]{1,2,0:T(8,128)(2,1)S(1)}, bf16[1,128,2060]{1,2,0:T(8,128)(2,1)S(1)}, u32[]{:S(2)}, u32[]{:S(2)}) collective-permute-start(bf16[1,128,2060]{1,2,0:T(8,128)(2,1)S(1)} %dynamic-slice_convert_fusion.3), channel_id=1, source_target_pairs={{0,2},{1,3},{2,0},{3,1},{4,6},{5,7},{6,4},{7,5},{8,10},{9,11},{10,... | collective-permute-start | bytes 1582088 | tf_op jit(solution)/shard_map/ppermute | solution.py:261
  (316 other events, 2098.8 us)
Sparse Core Ops, SparseCore 0:
  10.5 25.2 all-gather.12
  37.4 22.5 all-gather.14
  61.6 22.5 all-gather.16
  85.6 22.5 all-gather.10
  109.6 22.5 all-gather.18
  133.6 22.5 all-gather.20
  582.2 86.1 all-reduce.1

commit v11 on v10

--- a/solution.py
+++ b/solution.py
@@ -251,7 +251,7 @@
     me = lax.axis_index(axis_name)
     chunk = grad.shape[0] // size
     rest = grad.shape[1:]
-    total = grad.astype(jnp.float32).reshape(size, chunk, *rest)
+    total = grad.reshape(size, chunk, *rest)
     bit = 1
     while bit < size:
         pairs = total.reshape(total.shape[0] // 2, 2, chunk, *rest)
@@ -261,7 +261,7 @@
         got = lax.ppermute(
             give.astype(jnp.bfloat16), axis_name, [(i, i ^ bit) for i in range(size)]
         )
-        total = keep + got.astype(jnp.float32)
+        total = keep.astype(jnp.float32) + got.astype(jnp.float32)
         bit *= 2
     return total.reshape(chunk, *rest)
 
@@ -283,25 +283,35 @@
     return held.reshape((size * part.shape[0],) + part.shape[1:])
 
 
+def expert_sum(part):
+    owned = halving_scatter(part, "expert")
+    owned = lax.reduce_precision(owned, exponent_bits=8, mantissa_bits=7)
+    return doubling_gather(owned.astype(jnp.bfloat16), "expert").astype(jnp.float32)
+
+
 def reduce_layer(layer_grads, late):
     g_gain, g_shift, g_qkv, g_proj, g_router, g_in, g_out = layer_grads
     qkv_cols = g_qkv.shape[1]
     proj_cols = g_proj.shape[1]
     small = jnp.concatenate([g_gain.T, g_shift.T, g_router], axis=1)
-    shared = jnp.concatenate([g_qkv, g_proj, small], axis=1)
-    shared = halving_scatter(shared, "shard")
     if late:
-        owned = halving_scatter(shared, "expert")
-        owned = lax.reduce_precision(owned, exponent_bits=8, mantissa_bits=7)
-        shared = doubling_gather(owned.astype(jnp.bfloat16), "expert").astype(jnp.float32)
+        early = jnp.concatenate([g_proj, small], axis=1).astype(jnp.bfloat16)
+        early = expert_sum(halving_scatter(early, "shard"))
+        qkv = expert_sum(halving_scatter(g_qkv.astype(jnp.bfloat16), "shard"))
+        proj = early[:, :proj_cols]
+        tail = early[:, proj_cols:]
     else:
+        shared = jnp.concatenate([g_qkv, g_proj, small], axis=1)
+        shared = halving_scatter(shared, "shard")
         shared = lax.psum(shared.astype(jnp.bfloat16), "expert").astype(jnp.float32)
-    tail = shared[:, qkv_cols + proj_cols :]
+        qkv = shared[:, :qkv_cols]
+        proj = shared[:, qkv_cols : qkv_cols + proj_cols]
+        tail = shared[:, qkv_cols + proj_cols :]
     return [
         tail[:, 0:2].T,
         tail[:, 2:4].T,
-        shared[:, :qkv_cols],
-        shared[:, qkv_cols : qkv_cols + proj_cols],
+        qkv,
+        proj,
         tail[:, 4:],
         halving_scatter(g_in[0], "shard")[None],
         halving_scatter(g_out[0], "shard")[None],

time: 875 us -> 862 us (0.985)
  local copies, waits for them, and re-layouts: 191 us -> 170 us
  starting transfers between devices: 88.3 us -> 103 us
    unnamed x634 -> x651, local copies, waits for them, and re-layouts: 58.6 us -> 47.4 us
    ppermute x15 -> x20, starting transfers between devices: 10.4 us -> 18.5 us  [halving_scatter(): lax.ppermute(give.astype(jnp.bfloat16), axis_name, [(i, i ^ bit) for i in...]
    ppermute x15 -> x20, waiting for transfers between devices: 29.8 us -> 37.5 us  [halving_scatter(): lax.ppermute(give.astype(jnp.bfloat16), axis_name, [(i, i ^ bit) for i in...]
  transfers between devices with their start and end apart: 41 -> 49, of which waited for: 23 -> 29; matrix products, arithmetic and copies ran while one was open for 51% -> 43% of each run, Pallas kernels for 0% -> 0%
where the time goes in v11:
time: 862 us; the launch traced here: 849 us
  matrix products  298 us (35%)
  waiting for transfers between devices  189 us (22%)
  local copies, waits for them, and re-layouts  170 us (20%)
  starting transfers between devices  103 us (12%)
  other arithmetic  64.1 us (7%)
  between operations  18.8 us (2%)
    all_to_all x16, waiting for transfers between devices, exchange(): lax.all_to_all(blocks, axis_name, split_axis=0, concat_axis=0, tiled=True)  133 us
    dot_general x30, matrix products, dot_first(): lax.dot_general(left, right, (((0,), (0,)), ((), ())), preferred_element_...  92.6 us
    dot_general x20, matrix products, dot_last(): lax.dot_general(left, right, (((1,), (1,)), ((), ())), preferred_element_...  78.1 us
    all_to_all x16, starting transfers between devices, exchange(): lax.all_to_all(blocks, axis_name, split_axis=0, concat_axis=0, tiled=True)  77 us
    unnamed x651, local copies, waits for them, and re-layouts  47.4 us
    ppermute x20, waiting for transfers between devices, halving_scatter(): lax.ppermute(give.astype(jnp.bfloat16), axis_name, [(i, i ^ bit) for i in...  37.5 us
    dot_general x4, matrix products, forward_expert(): hidden_pre = jnp.dot(row_block, in_w[0], preferred_element_type=jnp.float32)  26.6 us
    dot_general x4, matrix products, forward_expert(): jnp.dot(hidden_act, out_w[0], preferred_element_type=jnp.float32)  24.4 us
  transfers between devices with their start and end apart: 49, of which 29 were waited for; matrix products, arithmetic and copies ran while one was open for 43% of the time, Pallas kernels for 0%

profile of v11, /device:TPU:0, one launch (start us, length us, event | category | flops | bytes accessed | tf_op | source)
XLA Modules:
  0.0 848.8 jit_solution(1676722861741683014)
XLA Ops:
  14.8 6.1 all_gather.21
  64.0 6.5 all-to-all-start
  101.5 6.0 all-to-all-start.4
  107.6 8.3 multiply_convert_fusion.3
  116.0 6.6 fusion.147
  122.5 10.9 %all-to-all-done.4 = bf16[8,128,512]{2,1,0:T(8,128)(2,1)} async-done(((bf16[8,128,512]{2,1,0:T(8,128)(2,1)}), bf16[8,128,512]{2,1,0:T(8,128)(2,1)}, u32[]{:S(2)}, u32[]{:S(2)}) %all-to-all-start.4) | async-done | bytes 1048608 | tf_op jit(solution)/shard_map/all_to_all | solution.py:62
  154.8 8.7 %all-to-all-done.1 = bf16[8,128,512]{2,1,0:T(8,128)(2,1)} async-done(((bf16[8,128,512]{2,1,0:T(8,128)(2,1)}), bf16[8,128,512]{2,1,0:T(8,128)(2,1)}, u32[]{:S(2)}, u32[]{:S(2)}) %all-to-all-start.1) | async-done | bytes 1048608 | tf_op jit(solution)/shard_map/all_to_all | solution.py:62
  193.5 6.4 all-to-all-start.2
  238.2 16.3 %all-to-all-done.8 = bf16[8,128,512]{2,1,0:T(8,128)(2,1)} async-done(((bf16[8,128,512]{2,1,0:T(8,128)(2,1)}), bf16[8,128,512]{2,1,0:T(8,128)(2,1)}, u32[]{:S(2)}, u32[]{:S(2)}) %all-to-all-start.8) | async-done | bytes 1048608 | tf_op jit(solution)/shard_map/all_to_all | solution.py:62
  264.1 19.9 %all-to-all-done.6 = bf16[8,128,512]{2,1,0:T(8,128)(2,1)S(1)} async-done(((bf16[8,128,512]{2,1,0:T(8,128)(2,1)}), bf16[8,128,512]{2,1,0:T(8,128)(2,1)S(1)}, u32[]{:S(2)}, u32[]{:S(2)}) %all-to-all-start.6) | async-done | bytes 1048608 | tf_op jit(solution)/shard_map/all_to_all | solution.py:62
  287.6 8.8 %multiply_convert_fusion.2 = (bf16[1024,2048]{1,0:T(8,128)(2,1)S(1)}, f32[1024,2048]{1,0:T(8,128)}) fusion(bf16[1024,512]{1,0:T(8,128)(2,1)} %bitcast.43, bf16[1,1,512,2048]{3,2,1,0:T(8,128)(2,1)} %all-gather.19.cloned.1.call-done), kind=kOutput, calls=%fused_computation.38 | convolution fusion | flops 2166358016 | bytes 15728640 | tf_op jit(solution)/shard_map/dot_general | solution.py:108
  296.5 5.7 fusion.81
  307.9 6.2 fusion.159
  314.0 6.2 all-to-all-start.3
  320.3 8.7 %convolution_add_fusion.2 = f32[2048,512]{1,0:T(8,128)S(1)} fusion(f32[2048,512]{1,0:T(8,128)} %fusion.397, bf16[1024,512]{1,0:T(8,128)(2,1)S(1)} %bitcast.648, f32[1024,2048]{1,0:T(8,128)} %fusion.81), kind=kOutput, calls=%fused_computation.82 | convolution fusion | flops 2167406592 | bytes 17825792 | tf_op jit(solution)/shard_map/dot_general | solution.py:31
  329.3 10.9 %fusion.27 = bf16[1024,2048]{1,0:T(8,128)(2,1)S(1)} fusion(f32[1024,2048]{1,0:T(8,128)} %fusion.81, bf16[1024,512]{1,0:T(8,128)(2,1)} %bitcast.649, bf16[1,1,2048,512]{3,2,1,0:T(8,128)(2,1)S(1)} %copy-done.310), kind=kOutput, calls=%fused_computation.35 | convolution fusion | flops 2189426688 | bytes 15728640 | tf_op jit(solution)/shard_map/dot_general | solution.py:37
  340.2 9.8 %fusion.13 = bf16[1024,2048]{1,0:T(8,128)(2,1)S(1)} fusion(f32[1024,2048]{1,0:T(8,128)S(1)} %bitcast.723, bf16[1024,512]{1,0:T(8,128)(2,1)} %bitcast.82, bf16[1,1,2048,512]{3,2,1,0:T(8,128)(2,1)S(1)} %copy-done.310), kind=kOutput, calls=%fused_computation.21 | convolution fusion | flops 2189426688 | bytes 15728640 | tf_op jit(solution)/shard_map/dot_general | solution.py:37
  362.8 6.0 all-to-all-start.9
  368.7 7.9 fusion.162
  382.8 12.5 %all-to-all-done.9 = bf16[8,128,512]{2,1,0:T(8,128)(2,1)} async-done(((bf16[8,128,512]{2,1,0:T(8,128)(2,1)}), bf16[8,128,512]{2,1,0:T(8,128)(2,1)}, u32[]{:S(2)}, u32[]{:S(2)}) %all-to-all-start.9) | async-done | bytes 1048608 | tf_op jit(solution)/shard_map/all_to_all | solution.py:62
  402.3 6.2 fusion.156
  418.4 6.7 all-to-all-done.7
  438.4 16.4 %all-to-all-done.13 = bf16[8,128,512]{2,1,0:T(8,128)(2,1)S(1)} async-done(((bf16[8,128,512]{2,1,0:T(8,128)(2,1)}), bf16[8,128,512]{2,1,0:T(8,128)(2,1)S(1)}, u32[]{:S(2)}, u32[]{:S(2)}) %all-to-all-start.13) | async-done | bytes 1048608 | tf_op jit(solution)/shard_map/all_to_all | solution.py:62
  580.2 6.9 fusion.396
  587.1 18.0 %all-to-all-done.14 = bf16[8,128,512]{2,1,0:T(8,128)(2,1)} async-done(((bf16[8,128,512]{2,1,0:T(8,128)(2,1)}), bf16[8,128,512]{2,1,0:T(8,128)(2,1)}, u32[]{:S(2)}, u32[]{:S(2)}) %all-to-all-start.14) | async-done | bytes 1048608 | tf_op jit(solution)/shard_map/all_to_all | solution.py:62
  605.0 9.1 %convolution_add_fusion.3 = f32[2048,512]{1,0:T(8,128)S(1)} fusion(f32[2048,512]{1,0:T(8,128)} %fusion.396, bf16[1024,512]{1,0:T(8,128)(2,1)} %bitcast.122, f32[1024,2048]{1,0:T(8,128)} %copy-done.311), kind=kOutput, calls=%fused_computation.83 | convolution fusion | flops 2167406592 | bytes 17825792 | tf_op jit(solution)/shard_map/dot_general | solution.py:31
  616.2 9.4 %fusion.6 = bf16[1024,2048]{1,0:T(8,128)(2,1)S(1)} fusion(f32[1024,2048]{1,0:T(8,128)} %get-tuple-element.242, bf16[1024,512]{1,0:T(8,128)(2,1)} %bitcast.96, bf16[1,1,2048,512]{3,2,1,0:T(8,128)(2,1)S(1)} %copy-done.307), kind=kOutput, calls=%fused_computation.14 | convolution fusion | flops 2189426688 | bytes 15728640 | tf_op jit(solution)/shard_map/dot_general | solution.py:37
  628.0 8.6 %fusion.20 = bf16[1024,2048]{1,0:T(8,128)(2,1)S(1)} fusion(f32[1024,2048]{1,0:T(8,128)S(1)} %bitcast.721, bf16[1024,512]{1,0:T(8,128)(2,1)} %bitcast.122, bf16[1,1,2048,512]{3,2,1,0:T(8,128)(2,1)S(1)} %copy-done.307), kind=kOutput, calls=%fused_computation.28 | convolution fusion | flops 2189426688 | bytes 15728640 | tf_op jit(solution)/shard_map/dot_general | solution.py:37
  650.8 6.2 fusion.144
  670.2 9.6 %all-to-all-done.11 = bf16[8,128,512]{2,1,0:T(8,128)(2,1)} async-done(((bf16[8,128,512]{2,1,0:T(8,128)(2,1)}), bf16[8,128,512]{2,1,0:T(8,128)(2,1)}, u32[]{:S(2)}, u32[]{:S(2)}) %all-to-all-start.11) | async-done | bytes 1048608 | tf_op jit(solution)/shard_map/all_to_all | solution.py:62
  691.1 8.3 collective-permute-done.19
  703.3 7.0 all-to-all-done.15
  (1109 shorter events, 539.3 us)
Async XLA Ops:
  7.2 30.7 %all-gather.13.cloned.1.call-start = ((), (), s32[]{:S(2)}) async-start(), calls=%async_computation.17 | async-start | bytes 2621440 | tf_op jit(solution)/shard_map/all_gather | solution.py:360
  10.4 97.2 %all-gather.15.cloned.1.call-start = ((), (), s32[]{:S(2)}) async-start(), calls=%async_computation.19 | async-start | bytes 2621440 | tf_op jit(solution)/shard_map/all_gather | solution.py:375
  11.6 104.4 %all-gather.17.cloned.1.call-start = ((), (), s32[]{:S(2)}) async-start(), calls=%async_computation.20 | async-start | bytes 2621440 | tf_op jit(solution)/shard_map/all_gather | solution.py:376
  12.7 126.6 %all-gather.11.cloned.1.call-start = ((), (), s32[]{:S(2)}) async-start(), calls=%async_computation.16 | async-start | bytes 2621440 | tf_op jit(solution)/shard_map/all_gather | solution.py:360
  13.6 274.0 %all-gather.19.cloned.1.call-start = ((), (), s32[]{:S(2)}) async-start(), calls=%async_computation.21 | async-start | bytes 2621440 | tf_op jit(solution)/shard_map/all_gather | solution.py:375
  14.2 293.7 %all-gather.21.cloned.1.call-start = ((), (), s32[]{:S(2)}) async-start(), calls=%async_computation.22 | async-start | bytes 2621440 | tf_op jit(solution)/shard_map/all_gather | solution.py:376
  64.0 37.5 %all-to-all-start = ((bf16[8,128,512]{2,1,0:T(8,128)(2,1)}), bf16[8,128,512]{2,1,0:T(8,128)(2,1)S(1)}, u32[]{:S(2)}, u32[]{:S(2)}) async-start(bf16[8,128,512]{2,1,0:T(8,128)(2,1)} %bitcast.643), calls=%async_computation | async-start | bytes 2097152 | tf_op jit(solution)/shard_map/all_to_all | solution.py:62
  101.5 31.9 %all-to-all-start.4 = ((bf16[8,128,512]{2,1,0:T(8,128)(2,1)}), bf16[8,128,512]{2,1,0:T(8,128)(2,1)}, u32[]{:S(2)}, u32[]{:S(2)}) async-start(bf16[8,128,512]{2,1,0:T(8,128)(2,1)} %bitcast.652), calls=%async_computation.4 | async-start | bytes 2097152 | tf_op jit(solution)/shard_map/all_to_all | solution.py:62
  133.4 30.1 %all-to-all-start.1 = ((bf16[8,128,512]{2,1,0:T(8,128)(2,1)}), bf16[8,128,512]{2,1,0:T(8,128)(2,1)}, u32[]{:S(2)}, u32[]{:S(2)}) async-start(bf16[8,128,512]{2,1,0:T(8,128)(2,1)} %bitcast.30), calls=%async_computation.1 | async-start | bytes 2097152 | tf_op jit(solution)/shard_map/all_to_all | solution.py:62
  163.5 29.9 %all-to-all-start.5 = ((bf16[8,128,512]{2,1,0:T(8,128)(2,1)}), bf16[8,128,512]{2,1,0:T(8,128)(2,1)}, u32[]{:S(2)}, u32[]{:S(2)}) async-start(bf16[8,128,512]{2,1,0:T(8,128)(2,1)} %bitcast.640), calls=%async_computation.5 | async-start | bytes 2097152 | tf_op jit(solution)/shard_map/all_to_all | solution.py:62
  193.5 31.3 %all-to-all-start.2 = ((bf16[8,128,512]{2,1,0:T(8,128)(2,1)}), bf16[8,128,512]{2,1,0:T(8,128)(2,1)}, u32[]{:S(2)}, u32[]{:S(2)}) async-start(bf16[8,128,512]{2,1,0:T(8,128)(2,1)} %bitcast.646), calls=%async_computation.2 | async-start | bytes 2097152 | tf_op jit(solution)/shard_map/all_to_all | solution.py:62
  224.8 29.7 %all-to-all-start.8 = ((bf16[8,128,512]{2,1,0:T(8,128)(2,1)}), bf16[8,128,512]{2,1,0:T(8,128)(2,1)}, u32[]{:S(2)}, u32[]{:S(2)}) async-start(bf16[8,128,512]{2,1,0:T(8,128)(2,1)} %bitcast.651), calls=%async_computation.8 | async-start | bytes 2097152 | tf_op jit(solution)/shard_map/all_to_all | solution.py:62
  254.5 29.5 %all-to-all-start.6 = ((bf16[8,128,512]{2,1,0:T(8,128)(2,1)}), bf16[8,128,512]{2,1,0:T(8,128)(2,1)S(1)}, u32[]{:S(2)}, u32[]{:S(2)}) async-start(bf16[8,128,512]{2,1,0:T(8,128)(2,1)} %bitcast.75), calls=%async_computation.6 | async-start | bytes 2097152 | tf_op jit(solution)/shard_map/all_to_all | solution.py:62
  284.0 30.1 %all-to-all-start.12 = ((bf16[8,128,512]{2,1,0:T(8,128)(2,1)}), bf16[8,128,512]{2,1,0:T(8,128)(2,1)S(1)}, u32[]{:S(2)}, u32[]{:S(2)}) async-start(bf16[8,128,512]{2,1,0:T(8,128)(2,1)} %bitcast.653), calls=%async_computation.12 | async-start | bytes 2097152 | tf_op jit(solution)/shard_map/all_to_all | solution.py:62
  314.0 48.7 %all-to-all-start.3 = ((bf16[8,128,512]{2,1,0:T(8,128)(2,1)}), bf16[8,128,512]{2,1,0:T(8,128)(2,1)}, u32[]{:S(2)}, u32[]{:S(2)}) async-start(bf16[8,128,512]{2,1,0:T(8,128)(2,1)} %bitcast.650), calls=%async_computation.3 | async-start | bytes 2097152 | tf_op jit(solution)/shard_map/all_to_all | solution.py:62
  329.2 47.4 %collective-permute-start.24 = (bf16[2,512,512]{2,1,0:T(8,128)(2,1)S(1)}, bf16[2,512,512]{2,1,0:T(8,128)(2,1)}, u32[]{:S(2)}, u32[]{:S(2)}) collective-permute-start(bf16[2,512,512]{2,1,0:T(8,128)(2,1)S(1)} %fusion.246), channel_id=1, source_target_pairs={{0,1},{1,0},{2,3},{3,2},{4,5},{5,4},{6,7},{7,6},{8,9},{9,8},{10,11... | collective-permute-start | bytes 3145736 | tf_op jit(solution)/shard_map/ppermute | solution.py:261
  359.4 20.6 %collective-permute-start.20 = (bf16[2,128,2048]{2,1,0:T(8,128)(2,1)}, bf16[2,128,2048]{2,1,0:T(8,128)(2,1)}, u32[]{:S(2)}, u32[]{:S(2)}) collective-permute-start(bf16[2,128,2048]{2,1,0:T(8,128)(2,1)} %fusion.244), channel_id=1, source_target_pairs={{0,1},{1,0},{2,3},{3,2},{4,5},{5,4},{6,7},{7,6},{8,9},{9,8},{10,11... | collective-permute-start | bytes 3145736 | tf_op jit(solution)/shard_map/ppermute | solution.py:261
  362.8 32.5 %all-to-all-start.9 = ((bf16[8,128,512]{2,1,0:T(8,128)(2,1)}), bf16[8,128,512]{2,1,0:T(8,128)(2,1)}, u32[]{:S(2)}, u32[]{:S(2)}) async-start(bf16[8,128,512]{2,1,0:T(8,128)(2,1)} %bitcast.83), calls=%async_computation.9 | async-start | bytes 2097152 | tf_op jit(solution)/shard_map/all_to_all | solution.py:62
  378.5 30.1 %collective-permute-start.25 = (bf16[1,512,512]{2,1,0:T(8,128)(2,1)S(1)}, bf16[1,512,512]{2,1,0:T(8,128)(2,1)}, u32[]{:S(2)}, u32[]{:S(2)}) collective-permute-start(bf16[1,512,512]{2,1,0:T(8,128)(2,1)S(1)} %dynamic-slice_convert_fusion.2), channel_id=1, source_target_pairs={{0,2},{1,3},{2,0},{3,1},{4,6},{5,7},{6,4},{7,5},{8,10},{9,11},{10,... | collective-permute-start | bytes 1572872 | tf_op jit(solution)/shard_map/ppermute | solution.py:261
  395.3 29.9 %all-to-all-start.7 = ((bf16[8,128,512]{2,1,0:T(8,128)(2,1)}), bf16[8,128,512]{2,1,0:T(8,128)(2,1)}, u32[]{:S(2)}, u32[]{:S(2)}) async-start(bf16[8,128,512]{2,1,0:T(8,128)(2,1)} %bitcast.644), calls=%async_computation.7 | async-start | bytes 2097152 | tf_op jit(solution)/shard_map/all_to_all | solution.py:62
  425.1 29.6 %all-to-all-start.13 = ((bf16[8,128,512]{2,1,0:T(8,128)(2,1)}), bf16[8,128,512]{2,1,0:T(8,128)(2,1)S(1)}, u32[]{:S(2)}, u32[]{:S(2)}) async-start(bf16[8,128,512]{2,1,0:T(8,128)(2,1)} %bitcast.111), calls=%async_computation.13 | async-start | bytes 2097152 | tf_op jit(solution)/shard_map/all_to_all | solution.py:62
  539.5 29.9 %all-to-all-start.10 = ((bf16[8,128,512]{2,1,0:T(8,128)(2,1)}), bf16[8,128,512]{2,1,0:T(8,128)(2,1)}, u32[]{:S(2)}, u32[]{:S(2)}) async-start(bf16[8,128,512]{2,1,0:T(8,128)(2,1)} %bitcast.642), calls=%async_computation.10 | async-start | bytes 2097152 | tf_op jit(solution)/shard_map/all_to_all | solution.py:62
  563.5 14.7 %collective-permute-start.9 = (bf16[1,128,2060]{1,2,0:T(8,128)(2,1)}, bf16[1,128,2060]{1,2,0:T(8,128)(2,1)}, u32[]{:S(2)}, u32[]{:S(2)}) collective-permute-start(bf16[1,128,2060]{1,2,0:T(8,128)(2,1)} %dynamic-slice_convert_fusion.1), channel_id=1, source_target_pairs={{0,2},{1,3},{2,0},{3,1},{4,6},{5,7},{6,4},{7,5},{8,10},{9,11},{10,... | collective-permute-start | bytes 1582088 | tf_op jit(solution)/shard_map/ppermute | solution.py:261
  569.4 35.7 %all-to-all-start.14 = ((bf16[8,128,512]{2,1,0:T(8,128)(2,1)}), bf16[8,128,512]{2,1,0:T(8,128)(2,1)}, u32[]{:S(2)}, u32[]{:S(2)}) async-start(bf16[8,128,512]{2,1,0:T(8,128)(2,1)} %bitcast.645), calls=%async_computation.14 | async-start | bytes 2097152 | tf_op jit(solution)/shard_map/all_to_all | solution.py:62
  573.8 85.9 %all-reduce.2.cloned.1.call-start = ((), (), s32[]{:S(2)}) async-start(), calls=%async_computation.18 | async-start | bytes 1056768 | tf_op jit(solution)/shard_map/psum | solution.py:306
  614.3 48.2 %collective-permute-start.22 = (bf16[2,512,512]{2,1,0:T(8,128)(2,1)S(1)}, bf16[2,512,512]{2,1,0:T(8,128)(2,1)}, u32[]{:S(2)}, u32[]{:S(2)}) collective-permute-start(bf16[2,512,512]{2,1,0:T(8,128)(2,1)S(1)} %fusion.245), channel_id=1, source_target_pairs={{0,1},{1,0},{2,3},{3,2},{4,5},{5,4},{6,7},{7,6},{8,9},{9,8},{10,11... | collective-permute-start | bytes 3145736 | tf_op jit(solution)/shard_map/ppermute | solution.py:261
  642.7 24.6 %collective-permute-start.18 = (bf16[2,128,2048]{2,1,0:T(8,128)(2,1)}, bf16[2,128,2048]{2,1,0:T(8,128)(2,1)}, u32[]{:S(2)}, u32[]{:S(2)}) collective-permute-start(bf16[2,128,2048]{2,1,0:T(8,128)(2,1)} %fusion.243), channel_id=1, source_target_pairs={{0,1},{1,0},{2,3},{3,2},{4,5},{5,4},{6,7},{7,6},{8,9},{9,8},{10,11... | collective-permute-start | bytes 3145736 | tf_op jit(solution)/shard_map/ppermute | solution.py:261
  646.1 33.6 %all-to-all-start.11 = ((bf16[8,128,512]{2,1,0:T(8,128)(2,1)}), bf16[8,128,512]{2,1,0:T(8,128)(2,1)}, u32[]{:S(2)}, u32[]{:S(2)}) async-start(bf16[8,128,512]{2,1,0:T(8,128)(2,1)} %bitcast.97), calls=%async_computation.11 | async-start | bytes 2097152 | tf_op jit(solution)/shard_map/all_to_all | solution.py:62
  665.8 22.4 %collective-permute-start.23 = (bf16[1,512,512]{2,1,0:T(8,128)(2,1)}, bf16[1,512,512]{2,1,0:T(8,128)(2,1)}, u32[]{:S(2)}, u32[]{:S(2)}) collective-permute-start(bf16[1,512,512]{2,1,0:T(8,128)(2,1)} %dynamic-slice_convert_fusion.3), channel_id=1, source_target_pairs={{0,2},{1,3},{2,0},{3,1},{4,6},{5,7},{6,4},{7,5},{8,10},{9,11},{10,... | collective-permute-start | bytes 1572872 | tf_op jit(solution)/shard_map/ppermute | solution.py:261
  679.7 30.6 %all-to-all-start.15 = ((bf16[8,128,512]{2,1,0:T(8,128)(2,1)}), bf16[8,128,512]{2,1,0:T(8,128)(2,1)}, u32[]{:S(2)}, u32[]{:S(2)}) async-start(bf16[8,128,512]{2,1,0:T(8,128)(2,1)} %bitcast.641), calls=%async_computation.15 | async-start | bytes 2097152 | tf_op jit(solution)/shard_map/all_to_all | solution.py:62
  685.4 14.0 %collective-permute-start.19 = (bf16[1,128,2048]{2,1,0:T(8,128)(2,1)S(1)}, bf16[1,128,2048]{2,1,0:T(8,128)(2,1)S(1)}, u32[]{:S(2)}, u32[]{:S(2)}) collective-permute-start(bf16[1,128,2048]{2,1,0:T(8,128)(2,1)S(1)} %dynamic-slice_convert_fusion.5), channel_id=1, source_target_pairs={{0,2},{1,3},{2,0},{3,1},{4,6},{5,7},{6,4},{7,5},{8,10},{9,11},{10,... | collective-permute-start | bytes 1572872 | tf_op jit(solution)/shard_map/ppermute | solution.py:261
  774.0 25.2 %collective-permute-start.10 = (bf16[2,128,1536]{2,1,0:T(8,128)(2,1)S(1)}, bf16[2,128,1536]{2,1,0:T(8,128)(2,1)S(1)}, u32[]{:S(2)}, u32[]{:S(2)}) collective-permute-start(bf16[2,128,1536]{2,1,0:T(8,128)(2,1)S(1)} %dynamic-slice_bitcast_fusion), channel_id=1, source_target_pairs={{0,1},{1,0},{2,3},{3,2},{4,5},{5,4},{6,7},{7,6},{8,9},{9,8},{10,11... | collective-permute-start | bytes 2359304 | tf_op jit(solution)/shard_map/ppermute | solution.py:261
  (334 other events, 2301.8 us)
Sparse Core Ops, SparseCore 0:
  10.5 25.2 all-gather.12
  37.4 22.5 all-gather.14
  61.6 22.5 all-gather.16
  85.6 22.5 all-gather.10
  109.6 22.5 all-gather.18
  133.6 22.5 all-gather.20
  580.3 79.4 all-reduce.1

commit v12 on v11

--- a/solution.py
+++ b/solution.py
@@ -37,6 +37,11 @@
     return lax.dot_general(
         left, right, (((1,), (1,)), ((), ())), preferred_element_type=jnp.float32
     )
+
+
+def same_image(tok_count):
+    image = jnp.arange(tok_count, dtype=jnp.int32) // SEQ
+    return image[:, None] == image[None, :]
 
 
 def slot_onehot(route_ids, prio_rank, experts, capacity):
@@ -66,18 +71,19 @@
     norm_gains, norm_shifts, qkv_w, proj_w, router_w, _, _ = weights
     _, token_hot, _ = tables
     tok_count = residual.shape[0]
-    seq_count = tok_count // SEQ
     score_scale = HEAD ** (-0.5)
     norm_scale = norm_gains.astype(jnp.float32)
     norm_shift = norm_shifts.astype(jnp.float32)
     normed = layer_norm(residual, norm_scale[0], norm_shift[0]).astype(jnp.bfloat16)
     qkv_rows = jnp.dot(normed, qkv_w, preferred_element_type=jnp.float32).astype(jnp.bfloat16)
-    heads = qkv_rows.reshape(seq_count, SEQ, 3, HEADS, HEAD)
-    scores = (
+    heads = qkv_rows.reshape(tok_count, 3, HEADS, HEAD)
+    scores = jnp.where(
+        same_image(tok_count),
         jnp.einsum(
-            "sqhd,skhd->shqk", heads[:, :, 0], heads[:, :, 1], preferred_element_type=jnp.float32
+            "thd,shd->hts", heads[:, 0], heads[:, 1], preferred_element_type=jnp.float32
         )
-        * score_scale
+        * score_scale,
+        -jnp.inf,
     )
     row_top = jnp.max(scores, axis=-1, keepdims=True)
     scores_exp = jnp.exp(scores - row_top)
@@ -85,9 +91,9 @@
     soft_scores = scores_exp / row_total
     log_total = row_top + jnp.log(row_total)
     mixed_heads = jnp.einsum(
-        "shqk,skhd->sqhd",
+        "hts,shd->thd",
         soft_scores.astype(jnp.bfloat16),
-        heads[:, :, 2],
+        heads[:, 2],
         preferred_element_type=jnp.float32,
     )
     mixed_heads = mixed_heads.astype(jnp.bfloat16).reshape(tok_count, D)
@@ -193,7 +199,6 @@
     pair_hot, _, _ = tables
     norm_gains, norm_shifts, qkv_w, proj_w, _, _, _ = weights
     tok_count = residual.shape[0]
-    seq_count = tok_count // SEQ
     score_scale = HEAD ** (-0.5)
     norm_scale = norm_gains.astype(jnp.float32)
     norm_shift = norm_shifts.astype(jnp.float32)
@@ -205,18 +210,20 @@
     d_middle = d_output + pulled_two[0]
     d_branch = d_middle.astype(jnp.bfloat16)
     g_proj = dot_first(mixed_heads, d_branch)
-    d_mixed = dot_last(d_branch, proj_w).astype(jnp.bfloat16).reshape(seq_count, SEQ, HEADS, HEAD)
-    query_heads = heads[:, :, 0]
-    key_heads = heads[:, :, 1]
-    value_heads = heads[:, :, 2]
-    scores = (
-        jnp.einsum("sqhd,skhd->shqk", query_heads, key_heads, preferred_element_type=jnp.float32)
-        * score_scale
+    d_mixed = dot_last(d_branch, proj_w).astype(jnp.bfloat16).reshape(tok_count, HEADS, HEAD)
+    query_heads = heads[:, 0]
+    key_heads = heads[:, 1]
+    value_heads = heads[:, 2]
+    scores = jnp.where(
+        same_image(tok_count),
+        jnp.einsum("thd,shd->hts", query_heads, key_heads, preferred_element_type=jnp.float32)
+        * score_scale,
+        -jnp.inf,
     )
     soft_scores = jnp.exp(scores - log_total)
-    d_soft = jnp.einsum("sqhd,skhd->shqk", d_mixed, value_heads, preferred_element_type=jnp.float32)
+    d_soft = jnp.einsum("thd,shd->hts", d_mixed, value_heads, preferred_element_type=jnp.float32)
     d_values = jnp.einsum(
-        "shqk,sqhd->skhd",
+        "hts,thd->shd",
         soft_scores.astype(jnp.bfloat16),
         d_mixed,
         preferred_element_type=jnp.float32,
@@ -225,15 +232,15 @@
         soft_scores * (d_soft - jnp.sum(soft_scores * d_soft, axis=-1, keepdims=True))
     ).astype(jnp.bfloat16)
     d_query = (
-        jnp.einsum("shqk,skhd->sqhd", d_scores, key_heads, preferred_element_type=jnp.float32)
+        jnp.einsum("hts,shd->thd", d_scores, key_heads, preferred_element_type=jnp.float32)
         * score_scale
     )
     d_keys = (
-        jnp.einsum("shqk,sqhd->skhd", d_scores, query_heads, preferred_element_type=jnp.float32)
+        jnp.einsum("hts,thd->shd", d_scores, query_heads, preferred_element_type=jnp.float32)
         * score_scale
     )
     d_qkv = (
-        jnp.stack([d_query, d_keys, d_values], axis=2)
+        jnp.stack([d_query, d_keys, d_values], axis=1)
         .reshape(tok_count, 3 * D)
         .astype(jnp.bfloat16)
     )

time: 862 us -> 825 us (0.957)
  local copies, waits for them, and re-layouts: 170 us -> 99 us
  matrix products: 298 us -> 317 us
  waiting for transfers between devices: 189 us -> 208 us
    reshape x16 -> x0, local copies, waits for them, and re-layouts: 34.8 us -> none  [the longest x8 18.9 us: backward_attend(): dot_last(d_branch, proj_w).astype(jnp.bfloat16)]
    dot_general x24, matrix products: 35.2 us -> 62.7 us  [the longest x4 19.7 us: backward_attend(): jnp.einsum('thd,shd->hts', d_mixed, value_heads, preferred_element_type=j...]
    all_to_all x16, waiting for transfers between devices: 133 us -> 148 us  [exchange(): lax.all_to_all(blocks, axis_name, split_axis=0, concat_axis=0, tiled=True)]
    unnamed x651 -> x559, local copies, waits for them, and re-layouts: 47.4 us -> 36.3 us
    slice x4 -> x0, local copies, waits for them, and re-layouts: 10.9 us -> none  [forward_attend(): heads[:, :, 2]]
  transfers between devices with their start and end apart: 49 -> 49, of which waited for: 29 -> 31; matrix products, arithmetic and copies ran while one was open for 43% -> 40% of each run, Pallas kernels for 0% -> 0%
where the time goes in v12:
time: 825 us; the launch traced here: 814 us
  matrix products  317 us (38%)
  waiting for transfers between devices  208 us (25%)
  starting transfers between devices  99.1 us (12%)
  local copies, waits for them, and re-layouts  99 us (12%)
  other arithmetic  66.4 us (8%)
  between operations  18.9 us (2%)
    all_to_all x16, waiting for transfers between devices, exchange(): lax.all_to_all(blocks, axis_name, split_axis=0, concat_axis=0, tiled=True)  148 us
    dot_general x30, matrix products, dot_first(): lax.dot_general(left, right, (((0,), (0,)), ((), ())), preferred_element_...  90.6 us
    dot_general x20, matrix products, dot_last(): lax.dot_general(left, right, (((1,), (1,)), ((), ())), preferred_element_...  73.7 us
    all_to_all x16, starting transfers between devices, exchange(): lax.all_to_all(blocks, axis_name, split_axis=0, concat_axis=0, tiled=True)  73.4 us
    ppermute x20, waiting for transfers between devices, halving_scatter(): lax.ppermute(give.astype(jnp.bfloat16), axis_name, [(i, i ^ bit) for i in...  39.8 us
    unnamed x559, local copies, waits for them, and re-layouts  36.3 us
    dot_general x4, matrix products, forward_expert(): hidden_pre = jnp.dot(row_block, in_w[0], preferred_element_type=jnp.float32)  27.1 us
    dot_general x4, matrix products, forward_expert(): jnp.dot(hidden_act, out_w[0], preferred_element_type=jnp.float32)  24 us
  transfers between devices with their start and end apart: 49, of which 31 were waited for; matrix products, arithmetic and copies ran while one was open for 40% of the time, Pallas kernels for 0%

profile of v12, /device:TPU:0, one launch (start us, length us, event | category | flops | bytes accessed | tf_op | source)
XLA Modules:
  0.0 814.0 jit_solution(3506964310460313928)
XLA Ops:
  14.8 6.1 all_gather.21
  54.6 6.7 all-to-all-start
  79.1 8.4 %all-to-all-done = bf16[8,128,512]{2,1,0:T(8,128)(2,1)} async-done(((bf16[8,128,512]{2,1,0:T(8,128)(2,1)}), bf16[8,128,512]{2,1,0:T(8,128)(2,1)}, u32[]{:S(2)}, u32[]{:S(2)}) %all-to-all-start) | async-done | bytes 1048608 | tf_op jit(solution)/shard_map/all_to_all | solution.py:67
  91.3 10.3 %multiply_convert_fusion.3 = (bf16[1024,2048]{1,0:T(8,128)(2,1)}, f32[1024,2048]{1,0:T(8,128)}) fusion(bf16[1024,512]{1,0:T(8,128)(2,1)} %bitcast.29, bf16[1,1,512,2048]{3,2,1,0:T(8,128)(2,1)} %all-gather.15.cloned.1.call-done), kind=kOutput, calls=%fused_computation.39 | convolution fusion | flops 2166358016 | bytes 15728640 | tf_op jit(solution)/shard_map/dot_general | solution.py:114
  101.6 6.2 fusion.143
  107.8 9.4 %all-to-all-done.4 = bf16[8,128,512]{2,1,0:T(8,128)(2,1)S(1)} async-done(((bf16[8,128,512]{2,1,0:T(8,128)(2,1)}), bf16[8,128,512]{2,1,0:T(8,128)(2,1)S(1)}, u32[]{:S(2)}, u32[]{:S(2)}) %all-to-all-start.4) | async-done | bytes 1048608 | tf_op jit(solution)/shard_map/all_to_all | solution.py:67
  137.7 9.5 %all-to-all-done.1 = bf16[8,128,512]{2,1,0:T(8,128)(2,1)} async-done(((bf16[8,128,512]{2,1,0:T(8,128)(2,1)}), bf16[8,128,512]{2,1,0:T(8,128)(2,1)}, u32[]{:S(2)}, u32[]{:S(2)}) %all-to-all-start.1) | async-done | bytes 1048608 | tf_op jit(solution)/shard_map/all_to_all | solution.py:67
  200.7 6.3 all-to-all-done.2
  219.0 17.7 %all-to-all-done.8 = bf16[8,128,512]{2,1,0:T(8,128)(2,1)} async-done(((bf16[8,128,512]{2,1,0:T(8,128)(2,1)}), bf16[8,128,512]{2,1,0:T(8,128)(2,1)}, u32[]{:S(2)}, u32[]{:S(2)}) %all-to-all-start.8) | async-done | bytes 1048608 | tf_op jit(solution)/shard_map/all_to_all | solution.py:67
  246.1 19.9 %all-to-all-done.6 = bf16[8,128,512]{2,1,0:T(8,128)(2,1)S(1)} async-done(((bf16[8,128,512]{2,1,0:T(8,128)(2,1)}), bf16[8,128,512]{2,1,0:T(8,128)(2,1)S(1)}, u32[]{:S(2)}, u32[]{:S(2)}) %all-to-all-start.6) | async-done | bytes 1048608 | tf_op jit(solution)/shard_map/all_to_all | solution.py:67
  270.5 8.8 %multiply_convert_fusion.2 = (bf16[1024,2048]{1,0:T(8,128)(2,1)S(1)}, f32[1024,2048]{1,0:T(8,128)}) fusion(bf16[1024,512]{1,0:T(8,128)(2,1)} %bitcast.47, bf16[1,1,512,2048]{3,2,1,0:T(8,128)(2,1)} %all-gather.19.cloned.1.call-done), kind=kOutput, calls=%fused_computation.38 | convolution fusion | flops 2166358016 | bytes 15728640 | tf_op jit(solution)/shard_map/dot_general | solution.py:114
  290.5 6.2 fusion.155
  296.7 6.2 all-to-all-start.3
  303.0 9.0 %convolution_add_fusion.2 = f32[2048,512]{1,0:T(8,128)S(1)} fusion(f32[2048,512]{1,0:T(8,128)} %fusion.356, bf16[1024,512]{1,0:T(8,128)(2,1)} %bitcast.122, f32[1024,2048]{1,0:T(8,128)} %fusion.97), kind=kOutput, calls=%fused_computation.106 | convolution fusion | flops 2167406592 | bytes 17825792 | tf_op jit(solution)/shard_map/dot_general | solution.py:31
  313.2 11.1 %fusion.27 = bf16[1024,2048]{1,0:T(8,128)(2,1)S(1)} fusion(f32[1024,2048]{1,0:T(8,128)} %fusion.97, bf16[1024,512]{1,0:T(8,128)(2,1)} %bitcast.122, bf16[1,1,2048,512]{3,2,1,0:T(8,128)(2,1)S(1)} %copy-done.262), kind=kOutput, calls=%fused_computation.35 | convolution fusion | flops 2189426688 | bytes 15728640 | tf_op jit(solution)/shard_map/dot_general | solution.py:37
  324.4 9.8 %fusion.13 = bf16[1024,2048]{1,0:T(8,128)(2,1)S(1)} fusion(f32[1024,2048]{1,0:T(8,128)S(1)} %bitcast.763, bf16[1024,512]{1,0:T(8,128)(2,1)} %bitcast.90, bf16[1,1,2048,512]{3,2,1,0:T(8,128)(2,1)S(1)} %copy-done.262), kind=kOutput, calls=%fused_computation.21 | convolution fusion | flops 2189426688 | bytes 15728640 | tf_op jit(solution)/shard_map/dot_general | solution.py:37
  345.9 6.0 all-to-all-start.9
  352.0 7.9 fusion.158
  367.3 11.2 %all-to-all-done.9 = bf16[8,128,512]{2,1,0:T(8,128)(2,1)} async-done(((bf16[8,128,512]{2,1,0:T(8,128)(2,1)}), bf16[8,128,512]{2,1,0:T(8,128)(2,1)}, u32[]{:S(2)}, u32[]{:S(2)}) %all-to-all-start.9) | async-done | bytes 1048608 | tf_op jit(solution)/shard_map/all_to_all | solution.py:67
  384.9 6.2 fusion.152
  401.7 6.3 all-to-all-done.7
  419.4 18.5 %all-to-all-done.13 = bf16[8,128,512]{2,1,0:T(8,128)(2,1)} async-done(((bf16[8,128,512]{2,1,0:T(8,128)(2,1)}), bf16[8,128,512]{2,1,0:T(8,128)(2,1)}, u32[]{:S(2)}, u32[]{:S(2)}) %all-to-all-start.13) | async-done | bytes 1048608 | tf_op jit(solution)/shard_map/all_to_all | solution.py:67
  497.4 6.0 concatenate.113
  557.1 6.8 fusion.355
  563.9 18.2 %all-to-all-done.14 = bf16[8,128,512]{2,1,0:T(8,128)(2,1)} async-done(((bf16[8,128,512]{2,1,0:T(8,128)(2,1)}), bf16[8,128,512]{2,1,0:T(8,128)(2,1)}, u32[]{:S(2)}, u32[]{:S(2)}) %all-to-all-start.14) | async-done | bytes 1048608 | tf_op jit(solution)/shard_map/all_to_all | solution.py:67
  582.1 9.1 %convolution_add_fusion.3 = f32[2048,512]{1,0:T(8,128)S(1)} fusion(f32[2048,512]{1,0:T(8,128)} %fusion.355, bf16[1024,512]{1,0:T(8,128)(2,1)} %bitcast.136, f32[1024,2048]{1,0:T(8,128)} %copy-done.263), kind=kOutput, calls=%fused_computation.107 | convolution fusion | flops 2167406592 | bytes 17825792 | tf_op jit(solution)/shard_map/dot_general | solution.py:31
  593.6 9.8 %fusion.6 = bf16[1024,2048]{1,0:T(8,128)(2,1)S(1)} fusion(f32[1024,2048]{1,0:T(8,128)} %get-tuple-element.230, bf16[1024,512]{1,0:T(8,128)(2,1)} %bitcast.106, bf16[1,1,2048,512]{3,2,1,0:T(8,128)(2,1)S(1)} %copy-done.259), kind=kOutput, calls=%fused_computation.14 | convolution fusion | flops 2189426688 | bytes 15728640 | tf_op jit(solution)/shard_map/dot_general | solution.py:37
  607.1 8.7 %fusion.20 = bf16[1024,2048]{1,0:T(8,128)(2,1)S(1)} fusion(f32[1024,2048]{1,0:T(8,128)S(1)} %bitcast.761, bf16[1024,512]{1,0:T(8,128)(2,1)} %bitcast.136, bf16[1,1,2048,512]{3,2,1,0:T(8,128)(2,1)S(1)} %copy-done.259), kind=kOutput, calls=%fused_computation.28 | convolution fusion | flops 2189426688 | bytes 15728640 | tf_op jit(solution)/shard_map/dot_general | solution.py:37
  627.3 6.2 fusion.140
  647.8 8.8 %all-to-all-done.11 = bf16[8,128,512]{2,1,0:T(8,128)(2,1)} async-done(((bf16[8,128,512]{2,1,0:T(8,128)(2,1)}), bf16[8,128,512]{2,1,0:T(8,128)(2,1)}, u32[]{:S(2)}, u32[]{:S(2)}) %all-to-all-start.11) | async-done | bytes 1048608 | tf_op jit(solution)/shard_map/all_to_all | solution.py:67
  667.1 9.2 %collective-permute-done.19 = bf16[1,128,2048]{2,1,0:T(8,128)(2,1)S(1)} collective-permute-done((bf16[1,128,2048]{2,1,0:T(8,128)(2,1)S(1)}, bf16[1,128,2048]{2,1,0:T(8,128)(2,1)S(1)}, u32[]{:S(2)}, u32[]{:S(2)}) %collective-permute-start.19) | collective-permute-done | bytes 524320 | tf_op jit(solution)/shard_map/ppermute | solution.py:268
  681.2 5.9 all-to-all-done.15
  (999 shorter events, 498.5 us)
Async XLA Ops:
  7.2 30.0 %all-gather.13.cloned.1.call-start = ((), (), s32[]{:S(2)}) async-start(), calls=%async_computation.17 | async-start | bytes 2621440 | tf_op jit(solution)/shard_map/all_gather | solution.py:367
  10.4 80.9 %all-gather.15.cloned.1.call-start = ((), (), s32[]{:S(2)}) async-start(), calls=%async_computation.19 | async-start | bytes 2621440 | tf_op jit(solution)/shard_map/all_gather | solution.py:382
  11.6 90.0 %all-gather.17.cloned.1.call-start = ((), (), s32[]{:S(2)}) async-start(), calls=%async_computation.20 | async-start | bytes 2621440 | tf_op jit(solution)/shard_map/all_gather | solution.py:383
  12.7 110.3 %all-gather.11.cloned.1.call-start = ((), (), s32[]{:S(2)}) async-start(), calls=%async_computation.16 | async-start | bytes 2621440 | tf_op jit(solution)/shard_map/all_gather | solution.py:367
  13.6 256.8 %all-gather.19.cloned.1.call-start = ((), (), s32[]{:S(2)}) async-start(), calls=%async_computation.21 | async-start | bytes 2621440 | tf_op jit(solution)/shard_map/all_gather | solution.py:382
  14.2 276.3 %all-gather.21.cloned.1.call-start = ((), (), s32[]{:S(2)}) async-start(), calls=%async_computation.22 | async-start | bytes 2621440 | tf_op jit(solution)/shard_map/all_gather | solution.py:383
  54.6 33.0 %all-to-all-start = ((bf16[8,128,512]{2,1,0:T(8,128)(2,1)}), bf16[8,128,512]{2,1,0:T(8,128)(2,1)}, u32[]{:S(2)}, u32[]{:S(2)}) async-start(bf16[8,128,512]{2,1,0:T(8,128)(2,1)} %bitcast.684), calls=%async_computation | async-start | bytes 2097152 | tf_op jit(solution)/shard_map/all_to_all | solution.py:67
  87.6 29.6 %all-to-all-start.4 = ((bf16[8,128,512]{2,1,0:T(8,128)(2,1)}), bf16[8,128,512]{2,1,0:T(8,128)(2,1)S(1)}, u32[]{:S(2)}, u32[]{:S(2)}) async-start(bf16[8,128,512]{2,1,0:T(8,128)(2,1)} %bitcast.691), calls=%async_computation.4 | async-start | bytes 2097152 | tf_op jit(solution)/shard_map/all_to_all | solution.py:67
  117.2 30.1 %all-to-all-start.1 = ((bf16[8,128,512]{2,1,0:T(8,128)(2,1)}), bf16[8,128,512]{2,1,0:T(8,128)(2,1)}, u32[]{:S(2)}, u32[]{:S(2)}) async-start(bf16[8,128,512]{2,1,0:T(8,128)(2,1)} %bitcast.693), calls=%async_computation.1 | async-start | bytes 2097152 | tf_op jit(solution)/shard_map/all_to_all | solution.py:67
  147.2 29.7 %all-to-all-start.5 = ((bf16[8,128,512]{2,1,0:T(8,128)(2,1)}), bf16[8,128,512]{2,1,0:T(8,128)(2,1)}, u32[]{:S(2)}, u32[]{:S(2)}) async-start(bf16[8,128,512]{2,1,0:T(8,128)(2,1)} %bitcast.681), calls=%async_computation.5 | async-start | bytes 2097152 | tf_op jit(solution)/shard_map/all_to_all | solution.py:67
  177.0 30.1 %all-to-all-start.2 = ((bf16[8,128,512]{2,1,0:T(8,128)(2,1)}), bf16[8,128,512]{2,1,0:T(8,128)(2,1)}, u32[]{:S(2)}, u32[]{:S(2)}) async-start(bf16[8,128,512]{2,1,0:T(8,128)(2,1)} %bitcast.686), calls=%async_computation.2 | async-start | bytes 2097152 | tf_op jit(solution)/shard_map/all_to_all | solution.py:67
  207.0 29.7 %all-to-all-start.8 = ((bf16[8,128,512]{2,1,0:T(8,128)(2,1)}), bf16[8,128,512]{2,1,0:T(8,128)(2,1)}, u32[]{:S(2)}, u32[]{:S(2)}) async-start(bf16[8,128,512]{2,1,0:T(8,128)(2,1)} %bitcast.688), calls=%async_computation.8 | async-start | bytes 2097152 | tf_op jit(solution)/shard_map/all_to_all | solution.py:67
  236.7 29.3 %all-to-all-start.6 = ((bf16[8,128,512]{2,1,0:T(8,128)(2,1)}), bf16[8,128,512]{2,1,0:T(8,128)(2,1)S(1)}, u32[]{:S(2)}, u32[]{:S(2)}) async-start(bf16[8,128,512]{2,1,0:T(8,128)(2,1)} %bitcast.689), calls=%async_computation.6 | async-start | bytes 2097152 | tf_op jit(solution)/shard_map/all_to_all | solution.py:67
  266.0 30.7 %all-to-all-start.12 = ((bf16[8,128,512]{2,1,0:T(8,128)(2,1)}), bf16[8,128,512]{2,1,0:T(8,128)(2,1)}, u32[]{:S(2)}, u32[]{:S(2)}) async-start(bf16[8,128,512]{2,1,0:T(8,128)(2,1)} %bitcast.692), calls=%async_computation.12 | async-start | bytes 2097152 | tf_op jit(solution)/shard_map/all_to_all | solution.py:67
  296.7 49.2 %all-to-all-start.3 = ((bf16[8,128,512]{2,1,0:T(8,128)(2,1)}), bf16[8,128,512]{2,1,0:T(8,128)(2,1)}, u32[]{:S(2)}, u32[]{:S(2)}) async-start(bf16[8,128,512]{2,1,0:T(8,128)(2,1)} %bitcast.687), calls=%async_computation.3 | async-start | bytes 2097152 | tf_op jit(solution)/shard_map/all_to_all | solution.py:67
  313.2 46.6 %collective-permute-start.24 = (bf16[2,512,512]{2,1,0:T(8,128)(2,1)}, bf16[2,512,512]{2,1,0:T(8,128)(2,1)}, u32[]{:S(2)}, u32[]{:S(2)}) collective-permute-start(bf16[2,512,512]{2,1,0:T(8,128)(2,1)} %fusion.238), channel_id=1, source_target_pairs={{0,1},{1,0},{2,3},{3,2},{4,5},{5,4},{6,7},{7,6},{8,9},{9,8},{10,11... | collective-permute-start | bytes 3145736 | tf_op jit(solution)/shard_map/ppermute | solution.py:268
  342.5 22.0 %collective-permute-start.20 = (bf16[2,128,2048]{2,1,0:T(8,128)(2,1)S(1)}, bf16[2,128,2048]{2,1,0:T(8,128)(2,1)}, u32[]{:S(2)}, u32[]{:S(2)}) collective-permute-start(bf16[2,128,2048]{2,1,0:T(8,128)(2,1)S(1)} %fusion.236), channel_id=1, source_target_pairs={{0,1},{1,0},{2,3},{3,2},{4,5},{5,4},{6,7},{7,6},{8,9},{9,8},{10,11... | collective-permute-start | bytes 3145736 | tf_op jit(solution)/shard_map/ppermute | solution.py:268
  345.9 32.5 %all-to-all-start.9 = ((bf16[8,128,512]{2,1,0:T(8,128)(2,1)}), bf16[8,128,512]{2,1,0:T(8,128)(2,1)}, u32[]{:S(2)}, u32[]{:S(2)}) async-start(bf16[8,128,512]{2,1,0:T(8,128)(2,1)} %bitcast.690), calls=%async_computation.9 | async-start | bytes 2097152 | tf_op jit(solution)/shard_map/all_to_all | solution.py:67
  362.9 28.2 %collective-permute-start.25 = (bf16[1,512,512]{2,1,0:T(8,128)(2,1)S(1)}, bf16[1,512,512]{2,1,0:T(8,128)(2,1)}, u32[]{:S(2)}, u32[]{:S(2)}) collective-permute-start(bf16[1,512,512]{2,1,0:T(8,128)(2,1)S(1)} %dynamic-slice_convert_fusion.2), channel_id=1, source_target_pairs={{0,2},{1,3},{2,0},{3,1},{4,6},{5,7},{6,4},{7,5},{8,10},{9,11},{10,... | collective-permute-start | bytes 1572872 | tf_op jit(solution)/shard_map/ppermute | solution.py:268
  378.5 29.6 %all-to-all-start.7 = ((bf16[8,128,512]{2,1,0:T(8,128)(2,1)}), bf16[8,128,512]{2,1,0:T(8,128)(2,1)S(1)}, u32[]{:S(2)}, u32[]{:S(2)}) async-start(bf16[8,128,512]{2,1,0:T(8,128)(2,1)} %bitcast.682), calls=%async_computation.7 | async-start | bytes 2097152 | tf_op jit(solution)/shard_map/all_to_all | solution.py:67
  408.1 29.8 %all-to-all-start.13 = ((bf16[8,128,512]{2,1,0:T(8,128)(2,1)}), bf16[8,128,512]{2,1,0:T(8,128)(2,1)}, u32[]{:S(2)}, u32[]{:S(2)}) async-start(bf16[8,128,512]{2,1,0:T(8,128)(2,1)} %bitcast.123), calls=%async_computation.13 | async-start | bytes 2097152 | tf_op jit(solution)/shard_map/all_to_all | solution.py:67
  516.9 29.7 %all-to-all-start.10 = ((bf16[8,128,512]{2,1,0:T(8,128)(2,1)}), bf16[8,128,512]{2,1,0:T(8,128)(2,1)}, u32[]{:S(2)}, u32[]{:S(2)}) async-start(bf16[8,128,512]{2,1,0:T(8,128)(2,1)} %bitcast.105), calls=%async_computation.10 | async-start | bytes 2097152 | tf_op jit(solution)/shard_map/all_to_all | solution.py:67
  541.7 14.4 %collective-permute-start.9 = (bf16[1,128,2060]{1,2,0:T(8,128)(2,1)}, bf16[1,128,2060]{1,2,0:T(8,128)(2,1)S(1)}, u32[]{:S(2)}, u32[]{:S(2)}) collective-permute-start(bf16[1,128,2060]{1,2,0:T(8,128)(2,1)} %dynamic-slice_convert_fusion.1), channel_id=1, source_target_pairs={{0,2},{1,3},{2,0},{3,1},{4,6},{5,7},{6,4},{7,5},{8,10},{9,11},{10,... | collective-permute-start | bytes 1582088 | tf_op jit(solution)/shard_map/ppermute | solution.py:268
  546.6 35.4 %all-to-all-start.14 = ((bf16[8,128,512]{2,1,0:T(8,128)(2,1)}), bf16[8,128,512]{2,1,0:T(8,128)(2,1)}, u32[]{:S(2)}, u32[]{:S(2)}) async-start(bf16[8,128,512]{2,1,0:T(8,128)(2,1)} %bitcast.683), calls=%async_computation.14 | async-start | bytes 2097152 | tf_op jit(solution)/shard_map/all_to_all | solution.py:67
  550.9 85.9 %all-reduce.2.cloned.1.call-start = ((), (), s32[]{:S(2)}) async-start(), calls=%async_computation.18 | async-start | bytes 1056768 | tf_op jit(solution)/shard_map/psum | solution.py:313
  592.4 47.2 %collective-permute-start.22 = (bf16[2,512,512]{2,1,0:T(8,128)(2,1)}, bf16[2,512,512]{2,1,0:T(8,128)(2,1)}, u32[]{:S(2)}, u32[]{:S(2)}) collective-permute-start(bf16[2,512,512]{2,1,0:T(8,128)(2,1)} %fusion.237), channel_id=1, source_target_pairs={{0,1},{1,0},{2,3},{3,2},{4,5},{5,4},{6,7},{7,6},{8,9},{9,8},{10,11... | collective-permute-start | bytes 3145736 | tf_op jit(solution)/shard_map/ppermute | solution.py:268
  619.7 25.2 %collective-permute-start.18 = (bf16[2,128,2048]{2,1,0:T(8,128)(2,1)}, bf16[2,128,2048]{2,1,0:T(8,128)(2,1)}, u32[]{:S(2)}, u32[]{:S(2)}) collective-permute-start(bf16[2,128,2048]{2,1,0:T(8,128)(2,1)} %fusion.235), channel_id=1, source_target_pairs={{0,1},{1,0},{2,3},{3,2},{4,5},{5,4},{6,7},{7,6},{8,9},{9,8},{10,11... | collective-permute-start | bytes 3145736 | tf_op jit(solution)/shard_map/ppermute | solution.py:268
  623.1 33.5 %all-to-all-start.11 = ((bf16[8,128,512]{2,1,0:T(8,128)(2,1)}), bf16[8,128,512]{2,1,0:T(8,128)(2,1)}, u32[]{:S(2)}, u32[]{:S(2)}) async-start(bf16[8,128,512]{2,1,0:T(8,128)(2,1)} %bitcast.107), calls=%async_computation.11 | async-start | bytes 2097152 | tf_op jit(solution)/shard_map/all_to_all | solution.py:67
  643.4 20.5 %collective-permute-start.23 = (bf16[1,512,512]{2,1,0:T(8,128)(2,1)S(1)}, bf16[1,512,512]{2,1,0:T(8,128)(2,1)}, u32[]{:S(2)}, u32[]{:S(2)}) collective-permute-start(bf16[1,512,512]{2,1,0:T(8,128)(2,1)S(1)} %dynamic-slice_convert_fusion.3), channel_id=1, source_target_pairs={{0,2},{1,3},{2,0},{3,1},{4,6},{5,7},{6,4},{7,5},{8,10},{9,11},{10,... | collective-permute-start | bytes 1572872 | tf_op jit(solution)/shard_map/ppermute | solution.py:268
  656.6 30.5 %all-to-all-start.15 = ((bf16[8,128,512]{2,1,0:T(8,128)(2,1)}), bf16[8,128,512]{2,1,0:T(8,128)(2,1)}, u32[]{:S(2)}, u32[]{:S(2)}) async-start(bf16[8,128,512]{2,1,0:T(8,128)(2,1)} %bitcast.680), calls=%async_computation.15 | async-start | bytes 2097152 | tf_op jit(solution)/shard_map/all_to_all | solution.py:67
  662.4 14.0 %collective-permute-start.19 = (bf16[1,128,2048]{2,1,0:T(8,128)(2,1)S(1)}, bf16[1,128,2048]{2,1,0:T(8,128)(2,1)S(1)}, u32[]{:S(2)}, u32[]{:S(2)}) collective-permute-start(bf16[1,128,2048]{2,1,0:T(8,128)(2,1)S(1)} %dynamic-slice_convert_fusion.5), channel_id=1, source_target_pairs={{0,2},{1,3},{2,0},{3,1},{4,6},{5,7},{6,4},{7,5},{8,10},{9,11},{10,... | collective-permute-start | bytes 1572872 | tf_op jit(solution)/shard_map/ppermute | solution.py:268
  738.9 25.2 %collective-permute-start.10 = (bf16[2,128,1536]{2,1,0:T(8,128)(2,1)S(1)}, bf16[2,128,1536]{2,1,0:T(8,128)(2,1)S(1)}, u32[]{:S(2)}, u32[]{:S(2)}) collective-permute-start(bf16[2,128,1536]{2,1,0:T(8,128)(2,1)S(1)} %dynamic-slice_bitcast_fusion), channel_id=1, source_target_pairs={{0,1},{1,0},{2,3},{3,2},{4,5},{5,4},{6,7},{7,6},{8,9},{9,8},{10,11... | collective-permute-start | bytes 2359304 | tf_op jit(solution)/shard_map/ppermute | solution.py:268
  (294 other events, 2320.9 us)
Sparse Core Ops, SparseCore 0:
  10.5 25.2 all-gather.12
  37.4 22.5 all-gather.14
  61.6 22.5 all-gather.16
  85.6 22.5 all-gather.10
  109.6 22.5 all-gather.18
  133.6 22.5 all-gather.20
  557.2 79.5 all-reduce.1

commit v13 on v12

--- a/solution.py
+++ b/solution.py
@@ -360,16 +360,14 @@
         ],
         axis=1,
     )
-    small = lax.all_gather(small, "shard", axis=0, tiled=True)
     qkv_cols = w_qkv.shape[2]
+    attn_cols = qkv_cols + w_proj.shape[2]
     all_weights = []
     for layer_index in range(LAYERS):
-        attn = lax.all_gather(
-            jnp.concatenate([w_qkv[layer_index], w_proj[layer_index]], axis=1),
-            "shard",
-            axis=0,
-            tiled=True,
-        )
+        parts = [w_qkv[layer_index], w_proj[layer_index]] + ([small] if layer_index == 0 else [])
+        attn = lax.all_gather(jnp.concatenate(parts, axis=1), "shard", axis=0, tiled=True)
+        if layer_index == 0:
+            small = attn[:, attn_cols:]
         shift_at = 2 * layer_count + 2 * layer_index
         router_at = 4 * layer_count + experts * layer_index
         all_weights.append(
@@ -377,7 +375,7 @@
                 small[:, 2 * layer_index : 2 * layer_index + 2].T,
                 small[:, shift_at : shift_at + 2].T,
                 attn[:, :qkv_cols],
-                attn[:, qkv_cols:],
+                attn[:, qkv_cols:attn_cols],
                 small[:, router_at : router_at + experts],
                 lax.all_gather(exp_in[layer_index], "shard", axis=1, tiled=True),
                 lax.all_gather(exp_out[layer_index], "shard", axis=1, tiled=True),

time: 825 us -> 859 us (1.041)
  waiting for transfers between devices: 208 us -> 233 us
    all_gather x2, waiting for transfers between devices: 0.01 us -> 26.9 us  [local(): lax.all_gather(jnp.concatenate(parts, axis=1), 'shard', axis=0, tiled=True)]
    unnamed x559 -> x543, local copies, waits for them, and re-layouts: 36.3 us -> 36.4 us
  transfers between devices with their start and end apart: 49 -> 49, of which waited for: 31 -> 33; matrix products, arithmetic and copies ran while one was open for 40% -> 40% of each run, Pallas kernels for 0% -> 0%
where the time goes in v13:
time: 859 us; the launch traced here: 847 us
  matrix products  322 us (37%)
  waiting for transfers between devices  233 us (27%)
  local copies, waits for them, and re-layouts  107 us (12%)
  starting transfers between devices  95.3 us (11%)
  other arithmetic  70.7 us (8%)
  between operations  18.8 us (2%)
    all_to_all x16, waiting for transfers between devices, exchange(): lax.all_to_all(blocks, axis_name, split_axis=0, concat_axis=0, tiled=True)  146 us
    dot_general x30, matrix products, dot_first(): lax.dot_general(left, right, (((0,), (0,)), ((), ())), preferred_element_...  89.3 us
    dot_general x20, matrix products, dot_last(): lax.dot_general(left, right, (((1,), (1,)), ((), ())), preferred_element_...  77.5 us
    all_to_all x16, starting transfers between devices, exchange(): lax.all_to_all(blocks, axis_name, split_axis=0, concat_axis=0, tiled=True)  72.3 us
    ppermute x20, waiting for transfers between devices, halving_scatter(): lax.ppermute(give.astype(jnp.bfloat16), axis_name, [(i, i ^ bit) for i in...  41.3 us
    unnamed x543, local copies, waits for them, and re-layouts  36.4 us
    dot_general x4, matrix products, forward_expert(): hidden_pre = jnp.dot(row_block, in_w[0], preferred_element_type=jnp.float32)  28.6 us
    all_gather x2, waiting for transfers between devices, local(): lax.all_gather(jnp.concatenate(parts, axis=1), 'shard', axis=0, tiled=True)  26.9 us
  transfers between devices with their start and end apart: 49, of which 33 were waited for; matrix products, arithmetic and copies ran while one was open for 40% of the time, Pallas kernels for 0%

profile of v13, /device:TPU:0, one launch (start us, length us, event | category | flops | bytes accessed | tf_op | source)
XLA Modules:
  0.0 847.4 jit_solution(7132615802512270565)
XLA Ops:
  29.9 6.0 all-gather.13.cloned.1.call-done
  40.5 20.9 %all-gather.11.cloned.1.call-done = bf16[512,2072]{1,0:T(8,128)(2,1)} async-done(((bf16[128,2072]{1,0:T(8,128)(2,1)}), bf16[512,2072]{1,0:T(8,128)(2,1)}) %all-gather.11.cloned.1.call-update) | async-done | bytes 2121744 | tf_op jit(solution)/shard_map/all_gather | solution.py:368
  110.3 7.5 all-to-all-done
  122.1 10.1 %multiply_convert_fusion.3 = (bf16[1024,2048]{1,0:T(8,128)(2,1)}, f32[1024,2048]{1,0:T(8,128)}) fusion(bf16[1024,512]{1,0:T(8,128)(2,1)} %bitcast.25, bf16[1,1,512,2048]{3,2,1,0:T(8,128)(2,1)} %all-gather.15.cloned.1.call-done), kind=kOutput, calls=%fused_computation.39 | convolution fusion | flops 2166358016 | bytes 15728640 | tf_op jit(solution)/shard_map/dot_general | solution.py:114
  132.1 6.2 fusion.143
  138.3 9.1 %all-to-all-done.4 = bf16[8,128,512]{2,1,0:T(8,128)(2,1)S(1)} async-done(((bf16[8,128,512]{2,1,0:T(8,128)(2,1)}), bf16[8,128,512]{2,1,0:T(8,128)(2,1)S(1)}, u32[]{:S(2)}, u32[]{:S(2)}) %all-to-all-start.4) | async-done | bytes 1048608 | tf_op jit(solution)/shard_map/all_to_all | solution.py:67
  164.2 13.3 %all-to-all-done.1 = bf16[8,128,512]{2,1,0:T(8,128)(2,1)} async-done(((bf16[8,128,512]{2,1,0:T(8,128)(2,1)}), bf16[8,128,512]{2,1,0:T(8,128)(2,1)}, u32[]{:S(2)}, u32[]{:S(2)}) %all-to-all-start.1) | async-done | bytes 1048608 | tf_op jit(solution)/shard_map/all_to_all | solution.py:67
  201.2 6.0 all-to-all-done.5
  249.1 17.8 %all-to-all-done.8 = bf16[8,128,512]{2,1,0:T(8,128)(2,1)} async-done(((bf16[8,128,512]{2,1,0:T(8,128)(2,1)}), bf16[8,128,512]{2,1,0:T(8,128)(2,1)}, u32[]{:S(2)}, u32[]{:S(2)}) %all-to-all-start.8) | async-done | bytes 1048608 | tf_op jit(solution)/shard_map/all_to_all | solution.py:67
  283.4 12.9 %all-to-all-done.6 = bf16[8,128,512]{2,1,0:T(8,128)(2,1)S(1)} async-done(((bf16[8,128,512]{2,1,0:T(8,128)(2,1)}), bf16[8,128,512]{2,1,0:T(8,128)(2,1)S(1)}, u32[]{:S(2)}, u32[]{:S(2)}) %all-to-all-start.6) | async-done | bytes 1048608 | tf_op jit(solution)/shard_map/all_to_all | solution.py:67
  300.7 8.8 %multiply_convert_fusion.2 = (bf16[1024,2048]{1,0:T(8,128)(2,1)S(1)}, f32[1024,2048]{1,0:T(8,128)}) fusion(bf16[1024,512]{1,0:T(8,128)(2,1)} %bitcast.39, bf16[1,1,512,2048]{3,2,1,0:T(8,128)(2,1)} %all-gather.19.cloned.1.call-done), kind=kOutput, calls=%fused_computation.38 | convolution fusion | flops 2166358016 | bytes 15728640 | tf_op jit(solution)/shard_map/dot_general | solution.py:114
  320.8 6.2 fusion.155
  326.9 6.1 all-to-all-start.3
  333.1 9.1 %convolution_add_fusion.2 = f32[2048,512]{1,0:T(8,128)S(1)} fusion(f32[2048,512]{1,0:T(8,128)} %fusion.346, bf16[1024,512]{1,0:T(8,128)(2,1)} %bitcast.102, f32[1024,2048]{1,0:T(8,128)} %fusion.97), kind=kOutput, calls=%fused_computation.106 | convolution fusion | flops 2167406592 | bytes 17825792 | tf_op jit(solution)/shard_map/dot_general | solution.py:31
  343.3 11.1 %fusion.27 = bf16[1024,2048]{1,0:T(8,128)(2,1)S(1)} fusion(f32[1024,2048]{1,0:T(8,128)} %fusion.97, bf16[1024,512]{1,0:T(8,128)(2,1)} %bitcast.102, bf16[1,1,2048,512]{3,2,1,0:T(8,128)(2,1)S(1)} %copy-done.254), kind=kOutput, calls=%fused_computation.35 | convolution fusion | flops 2189426688 | bytes 15728640 | tf_op jit(solution)/shard_map/dot_general | solution.py:37
  354.5 9.8 %fusion.13 = bf16[1024,2048]{1,0:T(8,128)(2,1)S(1)} fusion(f32[1024,2048]{1,0:T(8,128)S(1)} %bitcast.711, bf16[1024,512]{1,0:T(8,128)(2,1)} %bitcast.74, bf16[1,1,2048,512]{3,2,1,0:T(8,128)(2,1)S(1)} %copy-done.254), kind=kOutput, calls=%fused_computation.21 | convolution fusion | flops 2189426688 | bytes 15728640 | tf_op jit(solution)/shard_map/dot_general | solution.py:37
  376.1 6.0 all-to-all-start.9
  382.1 7.9 fusion.158
  396.6 12.0 %all-to-all-done.9 = bf16[8,128,512]{2,1,0:T(8,128)(2,1)} async-done(((bf16[8,128,512]{2,1,0:T(8,128)(2,1)}), bf16[8,128,512]{2,1,0:T(8,128)(2,1)}, u32[]{:S(2)}, u32[]{:S(2)}) %all-to-all-start.9) | async-done | bytes 1048608 | tf_op jit(solution)/shard_map/all_to_all | solution.py:67
  414.2 6.2 fusion.152
  431.9 6.3 all-to-all-done.7
  449.5 18.5 %all-to-all-done.13 = bf16[8,128,512]{2,1,0:T(8,128)(2,1)} async-done(((bf16[8,128,512]{2,1,0:T(8,128)(2,1)}), bf16[8,128,512]{2,1,0:T(8,128)(2,1)}, u32[]{:S(2)}, u32[]{:S(2)}) %all-to-all-start.13) | async-done | bytes 1048608 | tf_op jit(solution)/shard_map/all_to_all | solution.py:67
  529.5 6.0 concatenate.109
  589.1 6.8 fusion.345
  595.9 18.3 %all-to-all-done.14 = bf16[8,128,512]{2,1,0:T(8,128)(2,1)} async-done(((bf16[8,128,512]{2,1,0:T(8,128)(2,1)}), bf16[8,128,512]{2,1,0:T(8,128)(2,1)}, u32[]{:S(2)}, u32[]{:S(2)}) %all-to-all-start.14) | async-done | bytes 1048608 | tf_op jit(solution)/shard_map/all_to_all | solution.py:67
  614.1 9.1 %convolution_add_fusion.3 = f32[2048,512]{1,0:T(8,128)S(1)} fusion(f32[2048,512]{1,0:T(8,128)} %fusion.345, bf16[1024,512]{1,0:T(8,128)(2,1)} %bitcast.116, f32[1024,2048]{1,0:T(8,128)} %copy-done.255), kind=kOutput, calls=%fused_computation.107 | convolution fusion | flops 2167406592 | bytes 17825792 | tf_op jit(solution)/shard_map/dot_general | solution.py:31
  625.6 9.8 %fusion.6 = bf16[1024,2048]{1,0:T(8,128)(2,1)S(1)} fusion(f32[1024,2048]{1,0:T(8,128)} %get-tuple-element.230, bf16[1024,512]{1,0:T(8,128)(2,1)} %bitcast.88, bf16[1,1,2048,512]{3,2,1,0:T(8,128)(2,1)S(1)} %copy-done.251), kind=kOutput, calls=%fused_computation.14 | convolution fusion | flops 2189426688 | bytes 15728640 | tf_op jit(solution)/shard_map/dot_general | solution.py:37
  639.1 8.7 %fusion.20 = bf16[1024,2048]{1,0:T(8,128)(2,1)S(1)} fusion(f32[1024,2048]{1,0:T(8,128)S(1)} %bitcast.709, bf16[1024,512]{1,0:T(8,128)(2,1)} %bitcast.116, bf16[1,1,2048,512]{3,2,1,0:T(8,128)(2,1)S(1)} %copy-done.251), kind=kOutput, calls=%fused_computation.28 | convolution fusion | flops 2189426688 | bytes 15728640 | tf_op jit(solution)/shard_map/dot_general | solution.py:37
  659.4 6.2 fusion.140
  678.7 9.1 %all-to-all-done.11 = bf16[8,128,512]{2,1,0:T(8,128)(2,1)} async-done(((bf16[8,128,512]{2,1,0:T(8,128)(2,1)}), bf16[8,128,512]{2,1,0:T(8,128)(2,1)}, u32[]{:S(2)}, u32[]{:S(2)}) %all-to-all-start.11) | async-done | bytes 1048608 | tf_op jit(solution)/shard_map/all_to_all | solution.py:67
  698.2 9.3 %collective-permute-done.19 = bf16[1,128,2048]{2,1,0:T(8,128)(2,1)S(1)} collective-permute-done((bf16[1,128,2048]{2,1,0:T(8,128)(2,1)S(1)}, bf16[1,128,2048]{2,1,0:T(8,128)(2,1)S(1)}, u32[]{:S(2)}, u32[]{:S(2)}) %collective-permute-start.19) | collective-permute-done | bytes 524320 | tf_op jit(solution)/shard_map/ppermute | solution.py:268
  712.5 5.8 all-to-all-done.15
  (993 shorter events, 521.7 us)
Async XLA Ops:
  7.2 28.7 %all-gather.13.cloned.1.call-start = ((), (), s32[]{:S(2)}) async-start(), calls=%async_computation.17 | async-start | bytes 2621440 | tf_op jit(solution)/shard_map/all_gather | solution.py:368
  10.5 50.9 %all-gather.11.cloned.1.call-start = ((), (), s32[]{:S(2)}) async-start(), calls=%async_computation.16 | async-start | bytes 2785280 | tf_op jit(solution)/shard_map/all_gather | solution.py:368
  11.9 110.1 %all-gather.15.cloned.1.call-start = ((), (), s32[]{:S(2)}) async-start(), calls=%async_computation.19 | async-start | bytes 2621440 | tf_op jit(solution)/shard_map/all_gather | solution.py:380
  13.1 119.0 %all-gather.17.cloned.1.call-start = ((), (), s32[]{:S(2)}) async-start(), calls=%async_computation.20 | async-start | bytes 2621440 | tf_op jit(solution)/shard_map/all_gather | solution.py:381
  14.3 286.4 %all-gather.19.cloned.1.call-start = ((), (), s32[]{:S(2)}) async-start(), calls=%async_computation.21 | async-start | bytes 2621440 | tf_op jit(solution)/shard_map/all_gather | solution.py:380
  14.9 305.9 %all-gather.21.cloned.1.call-start = ((), (), s32[]{:S(2)}) async-start(), calls=%async_computation.22 | async-start | bytes 2621440 | tf_op jit(solution)/shard_map/all_gather | solution.py:381
  85.7 32.0 %all-to-all-start = ((bf16[8,128,512]{2,1,0:T(8,128)(2,1)}), bf16[8,128,512]{2,1,0:T(8,128)(2,1)}, u32[]{:S(2)}, u32[]{:S(2)}) async-start(bf16[8,128,512]{2,1,0:T(8,128)(2,1)} %bitcast.664), calls=%async_computation | async-start | bytes 2097152 | tf_op jit(solution)/shard_map/all_to_all | solution.py:67
  117.8 29.6 %all-to-all-start.4 = ((bf16[8,128,512]{2,1,0:T(8,128)(2,1)}), bf16[8,128,512]{2,1,0:T(8,128)(2,1)S(1)}, u32[]{:S(2)}, u32[]{:S(2)}) async-start(bf16[8,128,512]{2,1,0:T(8,128)(2,1)} %bitcast.671), calls=%async_computation.4 | async-start | bytes 2097152 | tf_op jit(solution)/shard_map/all_to_all | solution.py:67
  147.4 30.1 %all-to-all-start.1 = ((bf16[8,128,512]{2,1,0:T(8,128)(2,1)}), bf16[8,128,512]{2,1,0:T(8,128)(2,1)}, u32[]{:S(2)}, u32[]{:S(2)}) async-start(bf16[8,128,512]{2,1,0:T(8,128)(2,1)} %bitcast.673), calls=%async_computation.1 | async-start | bytes 2097152 | tf_op jit(solution)/shard_map/all_to_all | solution.py:67
  177.4 29.7 %all-to-all-start.5 = ((bf16[8,128,512]{2,1,0:T(8,128)(2,1)}), bf16[8,128,512]{2,1,0:T(8,128)(2,1)}, u32[]{:S(2)}, u32[]{:S(2)}) async-start(bf16[8,128,512]{2,1,0:T(8,128)(2,1)} %bitcast.661), calls=%async_computation.5 | async-start | bytes 2097152 | tf_op jit(solution)/shard_map/all_to_all | solution.py:67
  207.2 30.1 %all-to-all-start.2 = ((bf16[8,128,512]{2,1,0:T(8,128)(2,1)}), bf16[8,128,512]{2,1,0:T(8,128)(2,1)}, u32[]{:S(2)}, u32[]{:S(2)}) async-start(bf16[8,128,512]{2,1,0:T(8,128)(2,1)} %bitcast.666), calls=%async_computation.2 | async-start | bytes 2097152 | tf_op jit(solution)/shard_map/all_to_all | solution.py:67
  237.2 29.7 %all-to-all-start.8 = ((bf16[8,128,512]{2,1,0:T(8,128)(2,1)}), bf16[8,128,512]{2,1,0:T(8,128)(2,1)}, u32[]{:S(2)}, u32[]{:S(2)}) async-start(bf16[8,128,512]{2,1,0:T(8,128)(2,1)} %bitcast.669), calls=%async_computation.8 | async-start | bytes 2097152 | tf_op jit(solution)/shard_map/all_to_all | solution.py:67
  266.9 29.5 %all-to-all-start.6 = ((bf16[8,128,512]{2,1,0:T(8,128)(2,1)}), bf16[8,128,512]{2,1,0:T(8,128)(2,1)S(1)}, u32[]{:S(2)}, u32[]{:S(2)}) async-start(bf16[8,128,512]{2,1,0:T(8,128)(2,1)} %bitcast.667), calls=%async_computation.6 | async-start | bytes 2097152 | tf_op jit(solution)/shard_map/all_to_all | solution.py:67
  296.4 30.6 %all-to-all-start.12 = ((bf16[8,128,512]{2,1,0:T(8,128)(2,1)}), bf16[8,128,512]{2,1,0:T(8,128)(2,1)}, u32[]{:S(2)}, u32[]{:S(2)}) async-start(bf16[8,128,512]{2,1,0:T(8,128)(2,1)} %bitcast.672), calls=%async_computation.12 | async-start | bytes 2097152 | tf_op jit(solution)/shard_map/all_to_all | solution.py:67
  326.9 49.1 %all-to-all-start.3 = ((bf16[8,128,512]{2,1,0:T(8,128)(2,1)}), bf16[8,128,512]{2,1,0:T(8,128)(2,1)}, u32[]{:S(2)}, u32[]{:S(2)}) async-start(bf16[8,128,512]{2,1,0:T(8,128)(2,1)} %bitcast.668), calls=%async_computation.3 | async-start | bytes 2097152 | tf_op jit(solution)/shard_map/all_to_all | solution.py:67
  343.3 46.7 %collective-permute-start.24 = (bf16[2,512,512]{2,1,0:T(8,128)(2,1)}, bf16[2,512,512]{2,1,0:T(8,128)(2,1)}, u32[]{:S(2)}, u32[]{:S(2)}) collective-permute-start(bf16[2,512,512]{2,1,0:T(8,128)(2,1)} %fusion.238), channel_id=1, source_target_pairs={{0,1},{1,0},{2,3},{3,2},{4,5},{5,4},{6,7},{7,6},{8,9},{9,8},{10,11... | collective-permute-start | bytes 3145736 | tf_op jit(solution)/shard_map/ppermute | solution.py:268
  372.6 21.2 %collective-permute-start.20 = (bf16[2,128,2048]{2,1,0:T(8,128)(2,1)S(1)}, bf16[2,128,2048]{2,1,0:T(8,128)(2,1)}, u32[]{:S(2)}, u32[]{:S(2)}) collective-permute-start(bf16[2,128,2048]{2,1,0:T(8,128)(2,1)S(1)} %fusion.236), channel_id=1, source_target_pairs={{0,1},{1,0},{2,3},{3,2},{4,5},{5,4},{6,7},{7,6},{8,9},{9,8},{10,11... | collective-permute-start | bytes 3145736 | tf_op jit(solution)/shard_map/ppermute | solution.py:268
  376.1 32.5 %all-to-all-start.9 = ((bf16[8,128,512]{2,1,0:T(8,128)(2,1)}), bf16[8,128,512]{2,1,0:T(8,128)(2,1)}, u32[]{:S(2)}, u32[]{:S(2)}) async-start(bf16[8,128,512]{2,1,0:T(8,128)(2,1)} %bitcast.670), calls=%async_computation.9 | async-start | bytes 2097152 | tf_op jit(solution)/shard_map/all_to_all | solution.py:67
  393.1 27.3 %collective-permute-start.25 = (bf16[1,512,512]{2,1,0:T(8,128)(2,1)S(1)}, bf16[1,512,512]{2,1,0:T(8,128)(2,1)}, u32[]{:S(2)}, u32[]{:S(2)}) collective-permute-start(bf16[1,512,512]{2,1,0:T(8,128)(2,1)S(1)} %dynamic-slice_convert_fusion.2), channel_id=1, source_target_pairs={{0,2},{1,3},{2,0},{3,1},{4,6},{5,7},{6,4},{7,5},{8,10},{9,11},{10,... | collective-permute-start | bytes 1572872 | tf_op jit(solution)/shard_map/ppermute | solution.py:268
  408.6 29.6 %all-to-all-start.7 = ((bf16[8,128,512]{2,1,0:T(8,128)(2,1)}), bf16[8,128,512]{2,1,0:T(8,128)(2,1)S(1)}, u32[]{:S(2)}, u32[]{:S(2)}) async-start(bf16[8,128,512]{2,1,0:T(8,128)(2,1)} %bitcast.662), calls=%async_computation.7 | async-start | bytes 2097152 | tf_op jit(solution)/shard_map/all_to_all | solution.py:67
  438.2 29.8 %all-to-all-start.13 = ((bf16[8,128,512]{2,1,0:T(8,128)(2,1)}), bf16[8,128,512]{2,1,0:T(8,128)(2,1)}, u32[]{:S(2)}, u32[]{:S(2)}) async-start(bf16[8,128,512]{2,1,0:T(8,128)(2,1)} %bitcast.103), calls=%async_computation.13 | async-start | bytes 2097152 | tf_op jit(solution)/shard_map/all_to_all | solution.py:67
  549.0 29.7 %all-to-all-start.10 = ((bf16[8,128,512]{2,1,0:T(8,128)(2,1)}), bf16[8,128,512]{2,1,0:T(8,128)(2,1)}, u32[]{:S(2)}, u32[]{:S(2)}) async-start(bf16[8,128,512]{2,1,0:T(8,128)(2,1)} %bitcast.87), calls=%async_computation.10 | async-start | bytes 2097152 | tf_op jit(solution)/shard_map/all_to_all | solution.py:67
  573.7 14.5 %collective-permute-start.9 = (bf16[1,128,2060]{1,2,0:T(8,128)(2,1)}, bf16[1,128,2060]{1,2,0:T(8,128)(2,1)S(1)}, u32[]{:S(2)}, u32[]{:S(2)}) collective-permute-start(bf16[1,128,2060]{1,2,0:T(8,128)(2,1)} %dynamic-slice_convert_fusion.1), channel_id=1, source_target_pairs={{0,2},{1,3},{2,0},{3,1},{4,6},{5,7},{6,4},{7,5},{8,10},{9,11},{10,... | collective-permute-start | bytes 1582088 | tf_op jit(solution)/shard_map/ppermute | solution.py:268
  578.7 35.4 %all-to-all-start.14 = ((bf16[8,128,512]{2,1,0:T(8,128)(2,1)}), bf16[8,128,512]{2,1,0:T(8,128)(2,1)}, u32[]{:S(2)}, u32[]{:S(2)}) async-start(bf16[8,128,512]{2,1,0:T(8,128)(2,1)} %bitcast.663), calls=%async_computation.14 | async-start | bytes 2097152 | tf_op jit(solution)/shard_map/all_to_all | solution.py:67
  582.9 84.5 %all-reduce.2.cloned.1.call-start = ((), (), s32[]{:S(2)}) async-start(), calls=%async_computation.18 | async-start | bytes 1056768 | tf_op jit(solution)/shard_map/psum | solution.py:313
  624.6 45.7 %collective-permute-start.22 = (bf16[2,512,512]{2,1,0:T(8,128)(2,1)}, bf16[2,512,512]{2,1,0:T(8,128)(2,1)}, u32[]{:S(2)}, u32[]{:S(2)}) collective-permute-start(bf16[2,512,512]{2,1,0:T(8,128)(2,1)} %fusion.237), channel_id=1, source_target_pairs={{0,1},{1,0},{2,3},{3,2},{4,5},{5,4},{6,7},{7,6},{8,9},{9,8},{10,11... | collective-permute-start | bytes 3145736 | tf_op jit(solution)/shard_map/ppermute | solution.py:268
  651.7 24.2 %collective-permute-start.18 = (bf16[2,128,2048]{2,1,0:T(8,128)(2,1)}, bf16[2,128,2048]{2,1,0:T(8,128)(2,1)}, u32[]{:S(2)}, u32[]{:S(2)}) collective-permute-start(bf16[2,128,2048]{2,1,0:T(8,128)(2,1)} %fusion.235), channel_id=1, source_target_pairs={{0,1},{1,0},{2,3},{3,2},{4,5},{5,4},{6,7},{7,6},{8,9},{9,8},{10,11... | collective-permute-start | bytes 3145736 | tf_op jit(solution)/shard_map/ppermute | solution.py:268
  655.1 32.7 %all-to-all-start.11 = ((bf16[8,128,512]{2,1,0:T(8,128)(2,1)}), bf16[8,128,512]{2,1,0:T(8,128)(2,1)}, u32[]{:S(2)}, u32[]{:S(2)}) async-start(bf16[8,128,512]{2,1,0:T(8,128)(2,1)} %bitcast.89), calls=%async_computation.11 | async-start | bytes 2097152 | tf_op jit(solution)/shard_map/all_to_all | solution.py:67
  674.0 21.0 %collective-permute-start.23 = (bf16[1,512,512]{2,1,0:T(8,128)(2,1)S(1)}, bf16[1,512,512]{2,1,0:T(8,128)(2,1)}, u32[]{:S(2)}, u32[]{:S(2)}) collective-permute-start(bf16[1,512,512]{2,1,0:T(8,128)(2,1)S(1)} %dynamic-slice_convert_fusion.3), channel_id=1, source_target_pairs={{0,2},{1,3},{2,0},{3,1},{4,6},{5,7},{6,4},{7,5},{8,10},{9,11},{10,... | collective-permute-start | bytes 1572872 | tf_op jit(solution)/shard_map/ppermute | solution.py:268
  687.9 30.4 %all-to-all-start.15 = ((bf16[8,128,512]{2,1,0:T(8,128)(2,1)}), bf16[8,128,512]{2,1,0:T(8,128)(2,1)}, u32[]{:S(2)}, u32[]{:S(2)}) async-start(bf16[8,128,512]{2,1,0:T(8,128)(2,1)} %bitcast.660), calls=%async_computation.15 | async-start | bytes 2097152 | tf_op jit(solution)/shard_map/all_to_all | solution.py:67
  693.7 13.9 %collective-permute-start.19 = (bf16[1,128,2048]{2,1,0:T(8,128)(2,1)S(1)}, bf16[1,128,2048]{2,1,0:T(8,128)(2,1)S(1)}, u32[]{:S(2)}, u32[]{:S(2)}) collective-permute-start(bf16[1,128,2048]{2,1,0:T(8,128)(2,1)S(1)} %dynamic-slice_convert_fusion.5), channel_id=1, source_target_pairs={{0,2},{1,3},{2,0},{3,1},{4,6},{5,7},{6,4},{7,5},{8,10},{9,11},{10,... | collective-permute-start | bytes 1572872 | tf_op jit(solution)/shard_map/ppermute | solution.py:268
  772.1 25.5 %collective-permute-start.10 = (bf16[2,128,1536]{2,1,0:T(8,128)(2,1)S(1)}, bf16[2,128,1536]{2,1,0:T(8,128)(2,1)S(1)}, u32[]{:S(2)}, u32[]{:S(2)}) collective-permute-start(bf16[2,128,1536]{2,1,0:T(8,128)(2,1)S(1)} %dynamic-slice_bitcast_fusion), channel_id=1, source_target_pairs={{0,1},{1,0},{2,3},{3,2},{4,5},{5,4},{6,7},{7,6},{8,9},{9,8},{10,11... | collective-permute-start | bytes 2359304 | tf_op jit(solution)/shard_map/ppermute | solution.py:268
  (286 other events, 2677.1 us)
Sparse Core Ops, SparseCore 0:
  10.6 25.2 all-gather.12
  38.1 23.2 all-gather.10
  63.0 22.5 all-gather.14
  87.0 22.5 all-gather.16
  111.0 22.5 all-gather.18
  135.0 22.5 all-gather.20
  589.2 78.2 all-reduce.1
